TPU v7x, 32 devices: a whole 2x2x4 slice. The times are simulated.
32 devices in a mesh: dp: 8 (over y, x, core), tensor: 4 (over z).
Axes of the slice: x: 2, y: 2, z: 4, core: 2. Of those that a mesh axis runs over, the one named last changes fastest.
Arguments:
- teacher_master: float32 [256, 16384], P('dp', 'tensor'), as said below
- student_weight: bfloat16 [256, 16384], P('dp', 'tensor'), may hold values from -6 to 6
- teacher_feat: bfloat16 [2048, 256], P('dp'), as said below
- student_feat: bfloat16 [2048, 256], P('dp'), may hold values from -6 to 6
- center: float32 [16384], P('tensor'), may hold values from -0.3 to 0.3
Outputs:
- master_new: float32 [256, 16384], P('dp', 'tensor')
- student_grad: float32 [256, 16384], P('dp', 'tensor')
- new_center: float32 [16384], P('tensor')
Inputs may be any that keep to these rules, and one draw needn't show every extreme that they name: `teacher_feat`: rows of teacher features are real-valued and of order one. `teacher_master`: entries of the teacher master are real-valued and of order one.
All inputs are finite; a program needn't handle non-finite values.
Results may differ from a plain program's by a relative error of at most 0.014.
Values may be sent and summed in bfloat16 or wider, within the bound.
No kernel may reach another device: no remote copies, remote signals or barrier semaphores. Data moves between devices by JAX's collectives and lax.ppermute only.
A program may use at most 64 MiB of HBM per device.

v0:
```python
import jax
import jax.numpy as jnp
from jax import lax
from jax.sharding import PartitionSpec as P


def unit_rows(feat):
    wide = feat.astype(jnp.float32)
    return (wide * lax.rsqrt(jnp.sum(wide * wide, 1, keepdims=True) + 1e-06)).astype(jnp.bfloat16)


def shards(teacher_master, student_weight, teacher_feat, student_feat, center):
    zt = unit_rows(teacher_feat)
    zs = unit_rows(student_feat)
    images_all = teacher_feat.shape[0] * lax.axis_size("dp")
    student_full = lax.all_gather(student_weight, "dp", axis=0, tiled=True)
    master_new = 0.996 * teacher_master + 0.004 * student_weight.astype(jnp.float32)
    weight = lax.all_gather(master_new.astype(jnp.bfloat16), "dp", axis=0, tiled=True)
    feats = zt
    raw = jnp.dot(feats, weight, preferred_element_type=jnp.float32)
    squares = jnp.sum(jnp.square(weight.astype(jnp.float32)), 0)
    t_norm = jnp.sqrt(squares + 1e-06)
    t_cos = raw / t_norm
    s_norm = jnp.sqrt(jnp.sum(jnp.square(student_full.astype(jnp.float32)), 0) + 1e-06)
    s_cos = jnp.dot(zs, student_full, preferred_element_type=jnp.float32) / s_norm
    t_exp = jnp.exp((t_cos - center) / 0.04)
    s_exp = jnp.exp(s_cos / 0.1)
    t_total, s_total = lax.psum(
        (jnp.sum(t_exp, 1, keepdims=True), jnp.sum(s_exp, 1, keepdims=True)), "tensor"
    )
    cos_mean = lax.psum(jnp.sum(t_cos, 0), "dp") / images_all
    new_center = 0.5 * center + 0.5 * cos_mean
    dlog = ((s_exp / s_total - t_exp / t_total) / 0.1).astype(jnp.bfloat16)
    weighted = jnp.sum(dlog.astype(jnp.float32) * s_cos, 0)
    scaled = weighted / s_norm
    feats = zs
    product = lax.dot_general(
        feats, dlog, (((0,), (0,)), ((), ())), preferred_element_type=jnp.float32
    )
    student_grad = lax.psum_scatter(
        (product - student_full.astype(jnp.float32) * scaled) / s_norm,
        "dp",
        scatter_dimension=0,
        tiled=True,
    )
    return (master_new, student_grad, new_center)


def solution(mesh):
    placed = (P("dp", "tensor"), P("dp", "tensor"), P("dp", None), P("dp", None), P("tensor"))
    return jax.shard_map(
        shards,
        mesh=mesh,
        in_specs=placed,
        out_specs=(P("dp", "tensor"), P("dp", "tensor"), P("tensor")),
        check_vma=False,
    )
```

profile of v0, /device:TPU:0, one launch (start us, length us, event | category | flops | bytes accessed | tf_op | source)
XLA Modules:
  0.0 153.8 jit_solution(11268141412257356897)
XLA Ops:
  7.2 0.0 copy-start.3
  7.2 0.0 all-gather.3.cloned.1.call-start
  7.2 0.7 all-gather.3.cloned.1.call-update
  7.9 0.0 all-gather.5.cloned.1.call-start
  8.0 2.1 %fusion.13 = (bf16[32,4096]{1,0:T(8,128)(2,1)}, f32[32,4096]{1,0:T(8,128)}) fusion(bf16[32,4096]{1,0:T(8,128)(2,1)} %param.6, f32[32,4096]{1,0:T(8,128)} %param.5), kind=kLoop, calls=%fused_computation.31 | loop fusion | flops 655360 | bytes 1572864 | tf_op jit(solution)/shard_map/convert_element_type | solution.py:18
  10.0 0.0 all-gather.5.cloned.1.call-update
  10.1 0.0 reduce-scatter.2.cloned.1.call-start
  10.1 1.0 fusion.6
  11.1 1.0 fusion.4
  12.2 28.3 %all-gather.3.cloned.1.call-done = bf16[256,4096]{1,0:T(8,128)(2,1)} async-done(((bf16[32,4096]{1,0:T(8,128)(2,1)}), bf16[256,4096]{1,0:T(8,128)(2,1)}) %all-gather.3.cloned.1.call-update) | async-done | bytes 2097168 | tf_op jit(solution)/shard_map/all_gather | solution.py:16
  40.5 0.0 copy-start
  40.5 2.2 %fusion.1 = f32[4096]{0:T(1024)S(1)} fusion(bf16[256,4096]{1,0:T(8,128)(2,1)} %all-gather.3.cloned.1.call-done), kind=kLoop, calls=%fused_computation.6 | loop fusion | flops 3141632 | bytes 2113536 | tf_op jit(solution)/shard_map/reduce_sum | solution.py:24
  42.7 28.2 %all-gather.5.cloned.1.call-done = bf16[256,4096]{1,0:T(8,128)(2,1)} async-done(((bf16[32,4096]{1,0:T(8,128)(2,1)}), bf16[256,4096]{1,0:T(8,128)(2,1)}) %all-gather.5.cloned.1.call-update) | async-done | bytes 2097168 | tf_op jit(solution)/shard_map/all_gather | solution.py:18
  70.9 2.0 %multiply_reduce_fusion.1 = f32[4096]{0:T(1024)S(1)} fusion(bf16[256,4096]{1,0:T(8,128)(2,1)} %all-gather.5.cloned.1.call-done), kind=kLoop, calls=%fused_computation.10 | loop fusion | flops 3141632 | bytes 2113536 | tf_op jit(solution)/shard_map/reduce_sum | solution.py:21
  73.0 0.0 copy-done.3
  73.0 0.0 copy-done
  73.0 0.0 copy-start.1
  73.0 0.0 copy-start.2
  73.0 0.0 copy-start.4
  73.0 3.1 %fusion.2 = (f32[256]{0:T(256)S(1)}, f32[256,4096]{1,0:T(8,128)}) fusion(f32[4096]{0:T(1024)S(1)} %add_sqrt_fusion.1, bf16[256,4096]{1,0:T(8,128)(2,1)S(1)} %copy-done, bf16[256,256]{1,0:T(8,128)(2,1)S(1)} %copy-done.3, f32[256]{0:T(256)S(1)} %add_rsqrt_fusion.1), kind=kOutput, calls=%fused_computation.12 | convolution fusion | flops 540212992 | bytes 6440960 | tf_op jit(solution)/shard_map/dot_general | solution.py:25
  76.1 0.0 copy-done.1
  76.1 0.0 copy-done.2
  76.1 0.0 copy-done.4
  76.1 3.4 %fusion.12 = (f32[4096]{0:T(1024)S(1)}, f32[256]{0:T(256)S(1)}, f32[256,4096]{1,0:T(8,128)}) fusion(f32[4096]{0:T(1024)S(1)} %copy-done.4, f32[4096]{0:T(1024)S(1)} %add_sqrt_fusion, bf16[256,4096]{1,0:T(8,128)(2,1)S(1)} %copy-done.1, bf16[256,256]{1,0:T(8,128)(2,1)S(1)} %copy-done.2, f32[256]{0:T(256)S(1)} %add_rsqrt_fusion), kind=kOutput, calls=%fused_computation.30 | convolution fusion | flops 542306048 | bytes 6473728 | tf_op jit(solution)/shard_map/dot_general | solution.py:20
  79.5 11.7 %all-reduce = (f32[256]{0:T(256)S(1)}, f32[256]{0:T(256)S(1)}) all-reduce(f32[256]{0:T(256)S(1)} %get-tuple-element.4, f32[256]{0:T(256)S(1)} %get-tuple-element.12), channel_id=1, replica_groups=mesh['dp'=8,'tensor'=4] {'tensor'}, use_global_device_ids=true, to_apply=%region_7.0 | all-reduce | flops 512 | bytes 4096 | tf_op jit(solution)/shard_map/psum | solution.py:28
  91.1 4.5 %multiply_reduce_fusion = (f32[4096]{0:T(1024)S(1)}, bf16[256,4096]{1,0:T(8,128)(2,1)S(1)}) fusion(f32[256,4096]{1,0:T(8,128)} %get-tuple-element.13, f32[256]{0:T(256)S(1)} %get-tuple-element.5, f32[256,4096]{1,0:T(8,128)} %get-tuple-element.11, f32[4096]{0:T(1024)S(1)} %copy-done.4, f32[256]{0:T(256)S(1)} %get-tuple-element.6), kind=kLoop, calls=%fused_computation.7 | loop fusion | flops 11530240 | bytes 10520576 | tf_op jit(solution)/shard_map/reduce_sum | solution.py:34
  95.6 3.0 %fusion = f32[256,4096]{1,0:T(8,128)} fusion(bf16[256,4096]{1,0:T(8,128)(2,1)S(1)} %get-tuple-element.8, bf16[256,4096]{1,0:T(8,128)(2,1)S(1)} %copy-done, f32[4096]{0:T(1024)S(1)} %rsqrt_multiply_fusion, f32[4096]{0:T(1024)S(1)} %add_sqrt_fusion.1, bf16[256,256]{1,0:T(8,128)(2,1)S(1)} %copy-done.3, f32[256]{0:T(256)S(1)} %add_rsqrt_fusion.1), kind=kOutput, calls=%fused_computation.5 | convolution fusion | flops 541261824 | bytes 8553472 | tf_op jit(solution)/shard_map/dot_general | solution.py:37
  98.6 0.0 reduce-scatter.2.cloned.1.call-update
  98.6 22.4 %psum.23 = f32[4096]{0:T(1024)S(1)} all-reduce(f32[4096]{0:T(1024)S(1)} %get-tuple-element.3), channel_id=1, replica_groups=mesh['dp'=8,'tensor'=4] {'dp'}, use_global_device_ids=true, to_apply=%region_11.0 | all-reduce | flops 4096 | bytes 32768 | tf_op jit(solution)/shard_map/psum | solution.py:31
  121.0 0.6 multiply_add_fusion.1
  121.6 25.7 %reduce-scatter.2.cloned.1.call-done = f32[32,4096]{1,0:T(8,128)} async-done(((f32[256,4096]{1,0:T(8,128)}), f32[32,4096]{1,0:T(8,128)}) %reduce-scatter.2.cloned.1.call-update) | async-done | bytes 524304 | tf_op jit(solution)/shard_map/reduce_scatter | solution.py:40
  (5 shorter events, 0.0 us)
Async XLA Ops:
  7.2 65.8 %copy-start.3 = (bf16[256,256]{1,0:T(8,128)(2,1)S(1)}, bf16[256,256]{1,0:T(8,128)(2,1)}, u32[]{:S(2)}) copy-start(bf16[256,256]{1,0:T(8,128)(2,1)} %param.8) | copy-start | bytes 393220
  7.2 33.4 %all-gather.3.cloned.1.call-start = ((), (), s32[]{:S(2)}) async-start(), calls=%async_computation.1 | async-start | bytes 2359296 | tf_op jit(solution)/shard_map/all_gather | solution.py:16
  7.9 63.0 %all-gather.5.cloned.1.call-start = ((), (), s32[]{:S(2)}) async-start(), calls=%async_computation.2 | async-start | bytes 2359296 | tf_op jit(solution)/shard_map/all_gather | solution.py:18
  10.1 137.2 %reduce-scatter.2.cloned.1.call-start = ((), (), s32[]{:S(2)}) async-start(), calls=%async_computation.3 | async-start | bytes 4718592 | tf_op jit(solution)/shard_map/reduce_scatter | solution.py:40
  40.5 32.5 %copy-start = (bf16[256,4096]{1,0:T(8,128)(2,1)S(1)}, bf16[256,4096]{1,0:T(8,128)(2,1)}, u32[]{:S(2)}) copy-start(bf16[256,4096]{1,0:T(8,128)(2,1)} %all-gather.3.cloned.1.call-done) | copy-start | bytes 6291460
  73.0 3.1 %copy-start.1 = (bf16[256,4096]{1,0:T(8,128)(2,1)S(1)}, bf16[256,4096]{1,0:T(8,128)(2,1)}, u32[]{:S(2)}) copy-start(bf16[256,4096]{1,0:T(8,128)(2,1)} %all-gather.5.cloned.1.call-done) | copy-start | bytes 6291460
  73.0 3.1 %copy-start.2 = (bf16[256,256]{1,0:T(8,128)(2,1)S(1)}, bf16[256,256]{1,0:T(8,128)(2,1)}, u32[]{:S(2)}) copy-start(bf16[256,256]{1,0:T(8,128)(2,1)} %param.7) | copy-start | bytes 393220
  73.0 3.1 %copy-start.4 = (f32[4096]{0:T(1024)S(1)}, f32[4096]{0:T(1024)}, u32[]{:S(2)}) copy-start(f32[4096]{0:T(1024)} %param.9) | copy-start | bytes 49156
Sparse Core Ops, SparseCore 0:
  9.9 30.5 all-gather.2
  43.0 27.8 all-gather.4
  98.7 48.5 reduce-scatter.1
where the time goes:
time: 154 us
  waiting for transfers between devices  82.9 us (54%)
  blocking collectives  34.1 us (22%)
  between operations  13.9 us (9%)
  other arithmetic  13.4 us (9%)
  matrix products  9.39 us (6%)
    all_gather x1, waiting for transfers between devices, shards(): student_full = lax.all_gather(student_weight, 'dp', axis=0, tiled=True)  28.3 us
    all_gather x1, waiting for transfers between devices, shards(): lax.all_gather(master_new.astype(jnp.bfloat16), 'dp', axis=0, tiled=True)  28.2 us
    reduce_scatter x1, waiting for transfers between devices, shards(): lax.psum_scatter((product - student_full.astype(jnp.float32) * scaled) /...  25.7 us
    psum x1, blocking collectives, shards(): cos_mean = lax.psum(jnp.sum(t_cos, 0), 'dp') / images_all  22.4 us
    psum x1, blocking collectives, shards(): lax.psum((jnp.sum(t_exp, 1, keepdims=True), jnp.sum(s_exp, 1, keepdims=Tr...  11.7 us
    reduce_sum x1, other arithmetic, shards(): weighted = jnp.sum(dlog.astype(jnp.float32) * s_cos, 0)  4.47 us
    dot_general x1, matrix products, shards(): raw = jnp.dot(feats, weight, preferred_element_type=jnp.float32)  3.37 us
  transfers between devices with their start and end apart: 3, of which 3 were waited for; matrix products, arithmetic and copies ran while one was open for 5% of the time, Pallas kernels for 0%

commit v1 on v0

v1 whole, which is shorter than its diff:
```python
import jax
import jax.numpy as jnp
from jax import lax
from jax.sharding import PartitionSpec as P


def unit_rows(feat):
    wide = feat.astype(jnp.float32)
    return (wide * lax.rsqrt(jnp.sum(wide * wide, 1, keepdims=True) + 1e-06)).astype(jnp.bfloat16)


def weight_plan(teacher_master, student_weight, teacher_feat, student_feat, center):
    zt = unit_rows(teacher_feat)
    zs = unit_rows(student_feat)
    images_all = teacher_feat.shape[0] * lax.axis_size("dp")
    student_full = lax.all_gather(student_weight, "dp", axis=0, tiled=True)
    master_new = 0.996 * teacher_master + 0.004 * student_weight.astype(jnp.float32)
    weight = lax.all_gather(master_new.astype(jnp.bfloat16), "dp", axis=0, tiled=True)
    raw = jnp.dot(zt, weight, preferred_element_type=jnp.float32)
    t_norm = jnp.sqrt(jnp.sum(jnp.square(weight.astype(jnp.float32)), 0) + 1e-06)
    t_cos = raw / t_norm
    s_norm = jnp.sqrt(jnp.sum(jnp.square(student_full.astype(jnp.float32)), 0) + 1e-06)
    s_cos = jnp.dot(zs, student_full, preferred_element_type=jnp.float32) / s_norm
    t_exp = jnp.exp((t_cos - center) / 0.04)
    s_exp = jnp.exp(s_cos / 0.1)
    t_total, s_total = lax.psum(
        (jnp.sum(t_exp, 1, keepdims=True), jnp.sum(s_exp, 1, keepdims=True)), "tensor"
    )
    cos_mean = lax.psum(jnp.sum(t_cos, 0), "dp") / images_all
    new_center = 0.5 * center + 0.5 * cos_mean
    dlog = ((s_exp / s_total - t_exp / t_total) / 0.1).astype(jnp.bfloat16)
    scaled = jnp.sum(dlog.astype(jnp.float32) * s_cos, 0) / s_norm
    product = lax.dot_general(
        zs, dlog, (((0,), (0,)), ((), ())), preferred_element_type=jnp.float32
    )
    student_grad = lax.psum_scatter(
        (product - student_full.astype(jnp.float32) * scaled) / s_norm,
        "dp",
        scatter_dimension=0,
        tiled=True,
    )
    return (master_new, student_grad, new_center)


def feature_plan(teacher_master, student_weight, teacher_feat, student_feat, center):
    ndp = lax.axis_size("dp")
    bot = teacher_feat.shape[1]
    images_all = teacher_feat.shape[0] * ndp
    cols = center.shape[0] // ndp
    master_new = 0.996 * teacher_master + 0.004 * student_weight.astype(jnp.float32)
    both = jnp.stack([student_weight, master_new.astype(jnp.bfloat16)])
    both = lax.all_to_all(both, "dp", 2, 1, tiled=True)
    sw, tw = both[0], both[1]
    feats = jnp.concatenate([unit_rows(teacher_feat), unit_rows(student_feat)], axis=1)
    feats = lax.all_gather(feats, "dp", axis=0, tiled=True)
    zt, zs = feats[:, :bot], feats[:, bot:]
    c = lax.dynamic_slice_in_dim(center, lax.axis_index("dp") * cols, cols)
    t_norm = jnp.sqrt(jnp.sum(jnp.square(tw.astype(jnp.float32)), 0) + 1e-06)
    s_norm = jnp.sqrt(jnp.sum(jnp.square(sw.astype(jnp.float32)), 0) + 1e-06)
    t_cos = jnp.dot(zt, tw, preferred_element_type=jnp.float32) / t_norm
    s_cos = jnp.dot(zs, sw, preferred_element_type=jnp.float32) / s_norm
    t_exp = jnp.exp((t_cos - c) / 0.04)
    s_exp = jnp.exp(s_cos / 0.1)
    totals = lax.psum(
        jnp.stack([jnp.sum(t_exp, 1), jnp.sum(s_exp, 1)], axis=1), ("dp", "tensor")
    )
    t_total, s_total = totals[:, 0:1], totals[:, 1:2]
    part_center = 0.5 * c + 0.5 * (jnp.sum(t_cos, 0) / images_all)
    new_center = lax.all_gather(part_center, "dp", axis=0, tiled=True)
    dlog = ((s_exp / s_total - t_exp / t_total) / 0.1).astype(jnp.bfloat16)
    scaled = jnp.sum(dlog.astype(jnp.float32) * s_cos, 0) / s_norm
    product = lax.dot_general(
        zs, dlog, (((0,), (0,)), ((), ())), preferred_element_type=jnp.float32
    )
    grad = (product - sw.astype(jnp.float32) * scaled) / s_norm
    student_grad = lax.all_to_all(grad, "dp", 0, 1, tiled=True)
    return (master_new, student_grad, new_center)


def solution(mesh):
    placed = (P("dp", "tensor"), P("dp", "tensor"), P("dp", None), P("dp", None), P("tensor"))
    return jax.shard_map(
        shards_for(mesh),
        mesh=mesh,
        in_specs=placed,
        out_specs=(P("dp", "tensor"), P("dp", "tensor"), P("tensor")),
        check_vma=False,
    )


def shards_for(mesh):
    ndp = mesh.shape["dp"]

    def shards(teacher_master, student_weight, teacher_feat, student_feat, center):
        images_all = teacher_feat.shape[0] * ndp
        cols = center.shape[0]
        if images_all < cols and cols % ndp == 0:
            return feature_plan(teacher_master, student_weight, teacher_feat, student_feat, center)
        return weight_plan(teacher_master, student_weight, teacher_feat, student_feat, center)

    return shards
```

time: 154 us -> 121 us (0.79)
  waiting for transfers between devices: 82.9 us -> 13.8 us
  blocking collectives: 34.1 us -> 51.6 us
  local copies, waits for them, and re-layouts: 0.03 us -> 10.1 us
  starting transfers between devices: 0.12 us -> 9.6 us
    all_gather x2 -> x1, waiting for transfers between devices: 56.5 us -> 4.81 us  [feature_plan(): feats = lax.all_gather(feats, 'dp', axis=0, tiled=True)]
    reduce_scatter x1 -> x0, waiting for transfers between devices: 25.7 us -> none  [shards(): lax.psum_scatter((product - student_full.astype(jnp.float32) * scaled) /...]
    all_gather x0 -> x1, blocking collectives: none -> 12.1 us  [feature_plan(): new_center = lax.all_gather(part_center, 'dp', axis=0, tiled=True)]
    all_to_all x0 -> x2, starting transfers between devices: none -> 9.56 us  [the longest x1 5.17 us: feature_plan(): both = lax.all_to_all(both, 'dp', 2, 1, tiled=True)]
    all_to_all x0 -> x2, waiting for transfers between devices: none -> 8.99 us  [the longest x1 8.99 us: feature_plan(): both = lax.all_to_all(both, 'dp', 2, 1, tiled=True)]
    psum x2 -> x1, blocking collectives: 34.1 us -> 39.5 us  [feature_plan(): lax.psum(jnp.stack([jnp.sum(t_exp, 1), jnp.sum(s_exp, 1)], axis=1), ('dp'...]
    unnamed x10 -> x5, local copies, waits for them, and re-layouts: 0.03 us -> 4.31 us
    reduce_sum x3 -> x2, other arithmetic: 8.68 us -> 4.65 us  [the longest x1 4.52 us: feature_plan(): scaled = jnp.sum(dlog.astype(jnp.float32) * s_cos, 0) / s_norm]
  transfers between devices with their start and end apart: 3 -> 3, of which waited for: 3 -> 2; matrix products, arithmetic and copies ran while one was open for 5% -> 10% of each run, Pallas kernels for 0% -> 0%
where the time goes in v1:
time: 121 us; the launch traced here: 120 us
  blocking collectives  51.6 us (43%)
  between operations  14.1 us (12%)
  waiting for transfers between devices  13.8 us (11%)
  other arithmetic  12.3 us (10%)
  local copies, waits for them, and re-layouts  10.1 us (8%)
  starting transfers between devices  9.6 us (8%)
  matrix products  8.79 us (7%)
    psum x1, blocking collectives, feature_plan(): lax.psum(jnp.stack([jnp.sum(t_exp, 1), jnp.sum(s_exp, 1)], axis=1), ('dp'...  39.5 us
    all_gather x1, blocking collectives, feature_plan(): new_center = lax.all_gather(part_center, 'dp', axis=0, tiled=True)  12.1 us
    all_to_all x1, waiting for transfers between devices, feature_plan(): both = lax.all_to_all(both, 'dp', 2, 1, tiled=True)  8.99 us
    all_to_all x1, starting transfers between devices, feature_plan(): both = lax.all_to_all(both, 'dp', 2, 1, tiled=True)  5.17 us
    all_gather x1, waiting for transfers between devices, feature_plan(): feats = lax.all_gather(feats, 'dp', axis=0, tiled=True)  4.81 us
    reduce_sum x1, other arithmetic, feature_plan(): scaled = jnp.sum(dlog.astype(jnp.float32) * s_cos, 0) / s_norm  4.52 us
    all_to_all x1, starting transfers between devices, feature_plan(): student_grad = lax.all_to_all(grad, 'dp', 0, 1, tiled=True)  4.39 us
    unnamed x5, local copies, waits for them, and re-layouts  4.31 us
  transfers between devices with their start and end apart: 3, of which 2 were waited for; matrix products, arithmetic and copies ran while one was open for 10% of the time, Pallas kernels for 0%

profile of v1, /device:TPU:0, one launch (start us, length us, event | category | flops | bytes accessed | tf_op | source)
XLA Modules:
  0.0 120.3 jit_solution(14048190160954956227)
XLA Ops:
  7.2 0.0 all-gather.3.cloned.1.call-start
  7.2 1.0 fusion.6
  8.2 1.0 fusion.8
  9.3 1.1 fusion.7
  10.4 0.7 pad_maximum_fusion.1
  11.1 0.0 all-gather.3.cloned.1.call-update
  11.1 2.0 %convert_bitcast_fusion = (bf16[1,32,4096]{2,1,0:T(8,128)(2,1)S(1)}, f32[32,4096]{1,0:T(8,128)}) fusion(bf16[32,4096]{1,0:T(8,128)(2,1)} %param.6, f32[32,4096]{1,0:T(8,128)} %param.5), kind=kLoop, calls=%fused_computation.26 | loop fusion | flops 655360 | bytes 1572864 | tf_op jit(solution)/shard_map/stack | solution.py:51
  13.1 1.0 pad_maximum_fusion
  14.1 2.8 %copy.18 = bf16[2,32,4096]{1,0,2:T(2,128)(2,1)S(1)} copy(bf16[2,32,4096]{2,1,0:T(8,128)(2,1)S(1)} %pad_maximum_fusion) | data formatting | bytes 1048576 | tf_op jit(solution)/shard_map/stack | solution.py:51
  16.9 2.7 %reshape.42 = bf16[8,2,16384]{2,1,0:T(2,128)(2,1)} reshape(bf16[4096,2,32]{2,1,0:T(2,128)(2,1)S(1)} %bitcast.22) | data formatting | bytes 1048576
  19.6 5.2 %all-to-all-start = ((bf16[8,2,16384]{2,1,0:T(2,128)(2,1)}), bf16[8,2,16384]{2,1,0:T(2,128)(2,1)S(1)}, u32[]{:S(2)}, u32[]{:S(2)}) async-start(bf16[8,2,16384]{2,1,0:T(2,128)(2,1)} %reshape.42), calls=%async_computation | async-start | bytes 1048576 | tf_op jit(solution)/shard_map/all_to_all | solution.py:52
  24.7 0.8 dynamic_slice.3
  25.5 9.0 %all-to-all-done = bf16[8,2,16384]{2,1,0:T(2,128)(2,1)S(1)} async-done(((bf16[8,2,16384]{2,1,0:T(2,128)(2,1)}), bf16[8,2,16384]{2,1,0:T(2,128)(2,1)S(1)}, u32[]{:S(2)}, u32[]{:S(2)}) %all-to-all-start) | async-done | bytes 524320 | tf_op jit(solution)/shard_map/all_to_all | solution.py:52
  34.5 1.0 reshape.43
  35.5 1.3 %copy.19 = bf16[2,32,8,512]{3,1,2,0:T(8,128)(2,1)S(1)} copy(bf16[2,32,8,512]{1,0,3,2:T(2,128)(2,1)S(1)} %bitcast.23) | data formatting | bytes 1048576 | tf_op jit(solution)/shard_map/all_to_all | solution.py:52
  36.9 0.1 multiply_reduce_fusion.1
  37.1 4.8 %all-gather.3.cloned.1.call-done = bf16[2048,512]{1,0:T(8,128)(2,1)} async-done(((bf16[256,512]{1,0:T(8,128)(2,1)}), bf16[2048,512]{1,0:T(8,128)(2,1)}) %all-gather.3.cloned.1.call-update) | async-done | bytes 2097168 | tf_op jit(solution)/shard_map/all_gather | solution.py:55
  41.9 0.0 copy-start
  41.9 4.1 %fusion = (f32[2048]{0:T(1024)S(1)}, f32[2048,512]{1,0:T(8,128)}) fusion(f32[512]{0:T(512)S(1)} %get-tuple-element.22, bf16[256,512]{1,0:T(8,128)(2,1)S(1)} %bitcast.29, bf16[2048,512]{1,0:T(8,128)(2,1)} %all-gather.3.cloned.1.call-done), kind=kOutput, calls=%fused_computation.4 | convolution fusion | flops 540014592 | bytes 5515264 | tf_op jit(solution)/shard_map/dot_general | solution.py:61
  46.0 0.0 copy-done
  46.0 3.1 %fusion.10 = (f32[512]{0:T(512)S(1)}, f32[2048]{0:T(1024)S(1)}, f32[2048,512]{1,0:T(8,128)}) fusion(f32[512]{0:T(512)S(1)} %dynamic_slice.3, f32[512]{0:T(512)S(1)} %get-tuple-element.21, bf16[256,512]{1,0:T(8,128)(2,1)S(1)} %bitcast.31, bf16[2048,512]{1,0:T(8,128)(2,1)S(1)} %copy-done), kind=kOutput, calls=%fused_computation.34 | convolution fusion | flops 542111232 | bytes 5519360 | tf_op jit(solution)/shard_map/dot_general | solution.py:60
  49.2 39.5 %psum.7 = f32[2048,2]{0,1:T(2,128)S(1)} all-reduce(f32[2048,2]{0,1:T(2,128)S(1)} %pad_maximum_fusion.2), channel_id=1, replica_groups=mesh['dp'=8,'tensor'=4] {'dp','tensor'}, use_global_device_ids=true, to_apply=%region_6.0 | all-reduce | flops 4096 | bytes 32768 | tf_op jit(solution)/shard_map/psum | solution.py:64
  88.7 4.5 %multiply_reduce_fusion = (f32[512]{0:T(512)S(1)}, bf16[2048,512]{1,0:T(8,128)(2,1)S(1)}) fusion(f32[2048,512]{1,0:T(8,128)} %get-tuple-element.19, f32[2048]{0:T(1024)S(1)} %bitcast.34, f32[2048,512]{1,0:T(8,128)} %get-tuple-element.20, f32[512]{0:T(512)S(1)} %dynamic_slice.3, f32[2048]{0:T(1024)S(1)} %bitcast.33), kind=kLoop, calls=%fused_computation | loop fusion | flops 11533824 | bytes 10506240 | tf_op jit(solution)/shard_map/reduce_sum | solution.py:71
  93.2 1.5 %fusion.2 = f32[256,512]{1,0:T(8,128)} fusion(bf16[2048,512]{1,0:T(8,128)(2,1)S(1)} %get-tuple-element.11, bf16[2048,512]{1,0:T(8,128)(2,1)S(1)} %copy-done, bf16[256,512]{1,0:T(8,128)(2,1)S(1)} %bitcast.30, f32[512]{0:T(512)S(1)} %get-tuple-element.22, f32[512]{0:T(512)S(1)} %rsqrt_multiply_fusion), kind=kOutput, calls=%fused_computation.9 | convolution fusion | flops 537395200 | bytes 3936256 | tf_op jit(solution)/shard_map/dot_general | solution.py:72
  94.8 4.4 %all-to-all-start.1 = ((f32[8,32,512]{2,1,0:T(8,128)}), f32[8,32,512]{2,1,0:T(8,128)S(1)}, u32[]{:S(2)}, u32[]{:S(2)}) async-start(f32[8,32,512]{2,1,0:T(8,128)} %bitcast.10), calls=%async_computation.1 | async-start | bytes 1048576 | tf_op jit(solution)/shard_map/all_to_all | solution.py:76
  99.2 0.8 multiply_add_fusion.1
  99.9 12.1 %all-gather = f32[8,1,512]{2,1,0:T(1,128)S(1)} all-gather(f32[1,1,512]{2,1,0:T(1,128)S(1)} %bitcast.35), channel_id=1, replica_groups=mesh['dp'=8,'tensor'=4] {'dp'}, dimensions={0}, use_global_device_ids=true | all-gather | bytes 18432 | tf_op jit(solution)/shard_map/all_gather | solution.py:69
  112.0 0.0 all-to-all-done.1
  112.0 0.8 copy.21
  112.8 0.6 copy.23
  (7 shorter events, 0.1 us)
Async XLA Ops:
  7.2 34.7 %all-gather.3.cloned.1.call-start = ((), (), s32[]{:S(2)}) async-start(), calls=%async_computation.2 | async-start | bytes 2359296 | tf_op jit(solution)/shard_map/all_gather | solution.py:55
  19.6 14.9 %all-to-all-start = ((bf16[8,2,16384]{2,1,0:T(2,128)(2,1)}), bf16[8,2,16384]{2,1,0:T(2,128)(2,1)S(1)}, u32[]{:S(2)}, u32[]{:S(2)}) async-start(bf16[8,2,16384]{2,1,0:T(2,128)(2,1)} %reshape.42), calls=%async_computation | async-start | bytes 1048576 | tf_op jit(solution)/shard_map/all_to_all | solution.py:52
  41.9 4.1 %copy-start = (bf16[2048,512]{1,0:T(8,128)(2,1)S(1)}, bf16[2048,512]{1,0:T(8,128)(2,1)}, u32[]{:S(2)}) copy-start(bf16[2048,512]{1,0:T(8,128)(2,1)} %all-gather.3.cloned.1.call-done) | copy-start | bytes 6291460
  94.8 17.2 %all-to-all-start.1 = ((f32[8,32,512]{2,1,0:T(8,128)}), f32[8,32,512]{2,1,0:T(8,128)S(1)}, u32[]{:S(2)}, u32[]{:S(2)}) async-start(f32[8,32,512]{2,1,0:T(8,128)} %bitcast.10), calls=%async_computation.1 | async-start | bytes 1048576 | tf_op jit(solution)/shard_map/all_to_all | solution.py:76
Sparse Core Ops, SparseCore 0:
  11.2 30.5 all-gather.2

commit v2 on v1

--- a/solution.py
+++ b/solution.py
@@ -61,20 +61,22 @@
     s_cos = jnp.dot(zs, sw, preferred_element_type=jnp.float32) / s_norm
     t_exp = jnp.exp((t_cos - c) / 0.04)
     s_exp = jnp.exp(s_cos / 0.1)
-    totals = lax.psum(
-        jnp.stack([jnp.sum(t_exp, 1), jnp.sum(s_exp, 1)], axis=1), ("dp", "tensor")
-    )
-    t_total, s_total = totals[:, 0:1], totals[:, 1:2]
+    totals = lax.psum(jnp.stack([jnp.sum(t_exp, 1), jnp.sum(s_exp, 1)]), ("dp", "tensor"))
+    t_total, s_total = totals[0][:, None], totals[1][:, None]
     part_center = 0.5 * c + 0.5 * (jnp.sum(t_cos, 0) / images_all)
-    new_center = lax.all_gather(part_center, "dp", axis=0, tiled=True)
     dlog = ((s_exp / s_total - t_exp / t_total) / 0.1).astype(jnp.bfloat16)
     scaled = jnp.sum(dlog.astype(jnp.float32) * s_cos, 0) / s_norm
     product = lax.dot_general(
         zs, dlog, (((0,), (0,)), ((), ())), preferred_element_type=jnp.float32
     )
     grad = (product - sw.astype(jnp.float32) * scaled) / s_norm
-    student_grad = lax.all_to_all(grad, "dp", 0, 1, tiled=True)
-    return (master_new, student_grad, new_center)
+    rows = grad.shape[0] // ndp
+    sent = jnp.concatenate(
+        [grad.reshape(ndp, rows, cols), jnp.broadcast_to(part_center, (ndp, 1, cols))], axis=1
+    )
+    got = lax.all_to_all(sent, "dp", 0, 2, tiled=True)
+    got = got.reshape(rows + 1, ndp * cols)
+    return (master_new, got[:rows], got[rows])
 
 
 def solution(mesh):

time: 121 us -> 119 us (0.983)
  starting transfers between devices: 9.6 us -> 5.21 us
  blocking collectives: 51.6 us -> 54.9 us
    all_to_all x0 -> x1, blocking collectives: none -> 15.3 us  [feature_plan(): got = lax.all_to_all(sent, 'dp', 0, 2, tiled=True)]
    all_gather x1 -> x0, blocking collectives: 12.1 us -> none  [feature_plan(): new_center = lax.all_gather(part_center, 'dp', axis=0, tiled=True)]
    all_to_all x1 -> x0, starting transfers between devices: 4.39 us -> none  [feature_plan(): student_grad = lax.all_to_all(grad, 'dp', 0, 1, tiled=True)]
    unnamed x5 -> x6, local copies, waits for them, and re-layouts: 4.31 us -> 4.57 us
  transfers between devices with their start and end apart: 3 -> 2, of which waited for: 2 -> 2; matrix products, arithmetic and copies ran while one was open for 10% -> 10% of each run, Pallas kernels for 0% -> 0%
where the time goes in v2:
time: 119 us
  blocking collectives  54.9 us (46%)
  between operations  14.2 us (12%)
  waiting for transfers between devices  13.8 us (12%)
  other arithmetic  12.4 us (10%)
  local copies, waits for them, and re-layouts  10.1 us (8%)
  matrix products  7.99 us (7%)
  starting transfers between devices  5.21 us (4%)
    psum x1, blocking collectives, feature_plan(): lax.psum(jnp.stack([jnp.sum(t_exp, 1), jnp.sum(s_exp, 1)]), ('dp', 'tenso...  39.5 us
    all_to_all x1, blocking collectives, feature_plan(): got = lax.all_to_all(sent, 'dp', 0, 2, tiled=True)  15.3 us
    all_to_all x1, waiting for transfers between devices, feature_plan(): both = lax.all_to_all(both, 'dp', 2, 1, tiled=True)  8.99 us
    all_to_all x1, starting transfers between devices, feature_plan(): both = lax.all_to_all(both, 'dp', 2, 1, tiled=True)  5.17 us
    all_gather x1, waiting for transfers between devices, feature_plan(): feats = lax.all_gather(feats, 'dp', axis=0, tiled=True)  4.82 us
    unnamed x6, local copies, waits for them, and re-layouts  4.57 us
    reduce_sum x1, other arithmetic, feature_plan(): scaled = jnp.sum(dlog.astype(jnp.float32) * s_cos, 0) / s_norm  4.52 us
    dot_general x1, matrix products, feature_plan(): s_cos = jnp.dot(zs, sw, preferred_element_type=jnp.float32) / s_norm  4.14 us
  transfers between devices with their start and end apart: 2, of which 2 were waited for; matrix products, arithmetic and copies ran while one was open for 10% of the time, Pallas kernels for 0%

profile of v2, /device:TPU:0, one launch (start us, length us, event | category | flops | bytes accessed | tf_op | source)
XLA Modules:
  0.0 118.5 jit_solution(6791389335047282275)
XLA Ops:
  7.2 0.0 all-gather.2.cloned.1.call-start
  7.2 1.0 fusion.8
  8.2 1.0 fusion.6
  9.3 1.1 fusion.7
  10.4 0.7 pad_maximum_fusion.2
  11.1 0.0 all-gather.2.cloned.1.call-update
  11.1 2.0 %convert_bitcast_fusion = (bf16[1,32,4096]{2,1,0:T(8,128)(2,1)S(1)}, f32[32,4096]{1,0:T(8,128)}) fusion(bf16[32,4096]{1,0:T(8,128)(2,1)} %param.6, f32[32,4096]{1,0:T(8,128)} %param.5), kind=kLoop, calls=%fused_computation.27 | loop fusion | flops 655360 | bytes 1572864 | tf_op jit(solution)/shard_map/stack | solution.py:51
  13.1 1.0 pad_maximum_fusion.1
  14.1 2.8 %copy.16 = bf16[2,32,4096]{1,0,2:T(2,128)(2,1)S(1)} copy(bf16[2,32,4096]{2,1,0:T(8,128)(2,1)S(1)} %pad_maximum_fusion.1) | data formatting | bytes 1048576 | tf_op jit(solution)/shard_map/stack | solution.py:51
  16.9 2.7 %reshape.48 = bf16[8,2,16384]{2,1,0:T(2,128)(2,1)} reshape(bf16[4096,2,32]{2,1,0:T(2,128)(2,1)S(1)} %bitcast.26) | data formatting | bytes 1048576
  19.6 5.2 %all-to-all-start = ((bf16[8,2,16384]{2,1,0:T(2,128)(2,1)}), bf16[8,2,16384]{2,1,0:T(2,128)(2,1)S(1)}, u32[]{:S(2)}, u32[]{:S(2)}) async-start(bf16[8,2,16384]{2,1,0:T(2,128)(2,1)} %reshape.48), calls=%async_computation | async-start | bytes 1048576 | tf_op jit(solution)/shard_map/all_to_all | solution.py:52
  24.7 0.8 dynamic_slice.3
  25.5 9.0 %all-to-all-done = bf16[8,2,16384]{2,1,0:T(2,128)(2,1)S(1)} async-done(((bf16[8,2,16384]{2,1,0:T(2,128)(2,1)}), bf16[8,2,16384]{2,1,0:T(2,128)(2,1)S(1)}, u32[]{:S(2)}, u32[]{:S(2)}) %all-to-all-start) | async-done | bytes 524320 | tf_op jit(solution)/shard_map/all_to_all | solution.py:52
  34.5 1.0 reshape.49
  35.5 1.3 %copy.17 = bf16[2,32,8,512]{3,1,2,0:T(8,128)(2,1)S(1)} copy(bf16[2,32,8,512]{1,0,3,2:T(2,128)(2,1)S(1)} %bitcast.27) | data formatting | bytes 1048576 | tf_op jit(solution)/shard_map/all_to_all | solution.py:52
  36.9 0.1 multiply_reduce_fusion.2
  37.1 4.8 %all-gather.2.cloned.1.call-done = bf16[2048,512]{1,0:T(8,128)(2,1)} async-done(((bf16[256,512]{1,0:T(8,128)(2,1)}), bf16[2048,512]{1,0:T(8,128)(2,1)}) %all-gather.2.cloned.1.call-update) | async-done | bytes 2097168 | tf_op jit(solution)/shard_map/all_gather | solution.py:55
  41.9 0.0 copy-start
  41.9 4.1 %fusion = (f32[2048]{0:T(1024)S(1)}, f32[2048,512]{1,0:T(8,128)}) fusion(f32[512]{0:T(512)S(1)} %get-tuple-element.22, bf16[256,512]{1,0:T(8,128)(2,1)S(1)} %bitcast.35, bf16[2048,512]{1,0:T(8,128)(2,1)} %all-gather.2.cloned.1.call-done), kind=kOutput, calls=%fused_computation.4 | convolution fusion | flops 540014592 | bytes 5515264 | tf_op jit(solution)/shard_map/dot_general | solution.py:61
  46.0 0.0 copy-done
  46.0 3.1 %fusion.1 = (f32[2048]{0:T(1024)S(1)}, f32[512]{0:T(512)S(1)}, f32[2048,512]{1,0:T(8,128)}) fusion(f32[512]{0:T(512)S(1)} %dynamic_slice.3, f32[512]{0:T(512)S(1)} %get-tuple-element.21, bf16[256,512]{1,0:T(8,128)(2,1)S(1)} %bitcast.37, bf16[2048,512]{1,0:T(8,128)(2,1)S(1)} %copy-done), kind=kOutput, calls=%fused_computation.5 | convolution fusion | flops 542111232 | bytes 5519360 | tf_op jit(solution)/shard_map/dot_general | solution.py:60
  49.2 39.5 %psum.7 = f32[2,2048]{1,0:T(2,128)S(1)} all-reduce(f32[2,2048]{1,0:T(2,128)S(1)} %pad_maximum_fusion.3), channel_id=1, replica_groups=mesh['dp'=8,'tensor'=4] {'dp','tensor'}, use_global_device_ids=true, to_apply=%region_6.0 | all-reduce | flops 4096 | bytes 32768 | tf_op jit(solution)/shard_map/psum | solution.py:64
  88.7 4.5 %multiply_reduce_fusion = (f32[512]{0:T(512)S(1)}, bf16[2048,512]{1,0:T(8,128)(2,1)S(1)}) fusion(f32[2048,512]{1,0:T(8,128)} %get-tuple-element.20, f32[2048]{0:T(1024)S(1)} %bitcast.39, f32[2048,512]{1,0:T(8,128)} %get-tuple-element.18, f32[512]{0:T(512)S(1)} %dynamic_slice.3, f32[2048]{0:T(1024)S(1)} %bitcast.38), kind=kLoop, calls=%fused_computation | loop fusion | flops 11533824 | bytes 10506240 | tf_op jit(solution)/shard_map/reduce_sum | solution.py:68
  93.3 0.8 multiply_add_fusion.1
  94.0 0.7 fusion.2
  94.8 0.1 pad_maximum_fusion
  94.8 15.3 %all_to_all.30 = f32[8,33,512]{2,1,0:T(8,128)S(1)} all-to-all(f32[8,33,512]{2,1,0:T(8,128)S(1)} %pad_maximum_fusion), channel_id=1, replica_groups=mesh['dp'=8,'tensor'=4] {'dp'}, dimensions={0} | all-to-all | bytes 1081344 | tf_op jit(solution)/shard_map/all_to_all | solution.py:77
  110.2 0.6 slice.46
  110.8 0.8 copy.19
  (9 shorter events, 0.1 us)
Async XLA Ops:
  7.2 34.7 %all-gather.2.cloned.1.call-start = ((), (), s32[]{:S(2)}) async-start(), calls=%async_computation.2 | async-start | bytes 2359296 | tf_op jit(solution)/shard_map/all_gather | solution.py:55
  19.6 14.9 %all-to-all-start = ((bf16[8,2,16384]{2,1,0:T(2,128)(2,1)}), bf16[8,2,16384]{2,1,0:T(2,128)(2,1)S(1)}, u32[]{:S(2)}, u32[]{:S(2)}) async-start(bf16[8,2,16384]{2,1,0:T(2,128)(2,1)} %reshape.48), calls=%async_computation | async-start | bytes 1048576 | tf_op jit(solution)/shard_map/all_to_all | solution.py:52
  41.9 4.1 %copy-start = (bf16[2048,512]{1,0:T(8,128)(2,1)S(1)}, bf16[2048,512]{1,0:T(8,128)(2,1)}, u32[]{:S(2)}) copy-start(bf16[2048,512]{1,0:T(8,128)(2,1)} %all-gather.2.cloned.1.call-done) | copy-start | bytes 6291460
Sparse Core Ops, SparseCore 0:
  11.2 30.5 all-gather.1

commit v3 on v2

--- a/solution.py
+++ b/solution.py
@@ -42,6 +42,16 @@
     return (master_new, student_grad, new_center)
 
 
+def exchange_sum(x, axis, n):
+    if n & (n - 1):
+        return lax.psum(x, axis)
+    step = 1
+    while step < n:
+        x = x + lax.ppermute(x, axis, [(i, i ^ step) for i in range(n)])
+        step *= 2
+    return x
+
+
 def feature_plan(teacher_master, student_weight, teacher_feat, student_feat, center):
     ndp = lax.axis_size("dp")
     bot = teacher_feat.shape[1]
@@ -61,7 +71,8 @@
     s_cos = jnp.dot(zs, sw, preferred_element_type=jnp.float32) / s_norm
     t_exp = jnp.exp((t_cos - c) / 0.04)
     s_exp = jnp.exp(s_cos / 0.1)
-    totals = lax.psum(jnp.stack([jnp.sum(t_exp, 1), jnp.sum(s_exp, 1)]), ("dp", "tensor"))
+    totals = jnp.stack([jnp.sum(t_exp, 1), jnp.sum(s_exp, 1)])
+    totals = exchange_sum(exchange_sum(totals, "dp", ndp), "tensor", lax.axis_size("tensor"))
     t_total, s_total = totals[0][:, None], totals[1][:, None]
     part_center = 0.5 * c + 0.5 * (jnp.sum(t_cos, 0) / images_all)
     dlog = ((s_exp / s_total - t_exp / t_total) / 0.1).astype(jnp.bfloat16)

time: 119 us -> 88.6 us (0.74)
  blocking collectives: 54.9 us -> 13.7 us
  waiting for transfers between devices: 13.8 us -> 23.1 us
  starting transfers between devices: 5.21 us -> 12.6 us
  matrix products: 7.99 us -> 4.29 us
  other arithmetic: 12.4 us -> 10.3 us
    psum x1 -> x0, blocking collectives: 39.5 us -> none  [feature_plan(): lax.psum(jnp.stack([jnp.sum(t_exp, 1), jnp.sum(s_exp, 1)]), ('dp', 'tenso...]
    ppermute x0 -> x5, waiting for transfers between devices: none -> 9.25 us  [exchange_sum(): x = x + lax.ppermute(x, axis, [(i, i ^ step) for i in range(n)])]
    ppermute x0 -> x5, starting transfers between devices: none -> 7.35 us  [exchange_sum(): x = x + lax.ppermute(x, axis, [(i, i ^ step) for i in range(n)])]
    reduce_sum x1, other arithmetic: 4.52 us -> 2.37 us  [feature_plan(): scaled = jnp.sum(dlog.astype(jnp.float32) * s_cos, 0) / s_norm]
    dot_general x1, matrix products: 3.12 us -> 1.23 us  [feature_plan(): t_cos = jnp.dot(zt, tw, preferred_element_type=jnp.float32) / t_norm]
    dot_general x1, matrix products: 4.14 us -> 2.32 us  [feature_plan(): s_cos = jnp.dot(zs, sw, preferred_element_type=jnp.float32) / s_norm]
    all_to_all x1, blocking collectives: 15.3 us -> 13.7 us  [feature_plan(): got = lax.all_to_all(sent, 'dp', 0, 2, tiled=True)]
  transfers between devices with their start and end apart: 2 -> 7, of which waited for: 2 -> 7; matrix products, arithmetic and copies ran while one was open for 10% -> 14% of each run, Pallas kernels for 0% -> 0%
where the time goes in v3:
time: 88.6 us; the launch traced here: 88.2 us
  waiting for transfers between devices  23.1 us (26%)
  between operations  14.2 us (16%)
  blocking collectives  13.7 us (15%)
  starting transfers between devices  12.6 us (14%)
  other arithmetic  10.3 us (12%)
  local copies, waits for them, and re-layouts  10.1 us (11%)
  matrix products  4.29 us (5%)
    all_to_all x1, blocking collectives, feature_plan(): got = lax.all_to_all(sent, 'dp', 0, 2, tiled=True)  13.7 us
    ppermute x5, waiting for transfers between devices, exchange_sum(): x = x + lax.ppermute(x, axis, [(i, i ^ step) for i in range(n)])  9.25 us
    all_to_all x1, waiting for transfers between devices, feature_plan(): both = lax.all_to_all(both, 'dp', 2, 1, tiled=True)  8.99 us
    ppermute x5, starting transfers between devices, exchange_sum(): x = x + lax.ppermute(x, axis, [(i, i ^ step) for i in range(n)])  7.35 us
    all_to_all x1, starting transfers between devices, feature_plan(): both = lax.all_to_all(both, 'dp', 2, 1, tiled=True)  5.17 us
    all_gather x1, waiting for transfers between devices, feature_plan(): feats = lax.all_gather(feats, 'dp', axis=0, tiled=True)  4.83 us
    unnamed x6, local copies, waits for them, and re-layouts  4.57 us
    another operation x2, other arithmetic, feature_plan(): both = jnp.stack([student_weight, master_new.astype(jnp.bfloat16)])  3 us
  transfers between devices with their start and end apart: 7, of which 7 were waited for; matrix products, arithmetic and copies ran while one was open for 14% of the time, Pallas kernels for 0%

profile of v3, /device:TPU:0, one launch (start us, length us, event | category | flops | bytes accessed | tf_op | source)
XLA Modules:
  0.0 88.2 jit_solution(17118919411496583706)
XLA Ops:
  7.2 1.0 %fusion.8 = f32[256]{0:T(256)S(1)} fusion(bf16[256,256]{1,0:T(8,128)(2,1)} %param.8), kind=kLoop, calls=%fused_computation.24 | loop fusion | flops 196352 | bytes 132096 | tf_op jit(solution)/shard_map/reduce_sum | solution.py:9
  8.2 1.0 %fusion.6 = f32[256]{0:T(256)S(1)} fusion(bf16[256,256]{1,0:T(8,128)(2,1)} %param.7), kind=kLoop, calls=%fused_computation.22 | loop fusion | flops 196352 | bytes 132096 | tf_op jit(solution)/shard_map/reduce_sum | solution.py:9
  9.3 1.1 %fusion.7 = (bf16[256,256]{1,0:T(8,128)(2,1)S(1)}, bf16[256,256]{1,0:T(8,128)(2,1)S(1)}) fusion(bf16[256,256]{1,0:T(8,128)(2,1)} %param.7, f32[256]{0:T(256)S(1)} %add_rsqrt_fusion.1, f32[256]{0:T(256)S(1)} %add_rsqrt_fusion, bf16[256,256]{1,0:T(8,128)(2,1)} %param.8), kind=kLoop, calls=%fused_computation.23 | loop fusion | flops 393216 | bytes 526336 | tf_op jit(solution)/shard_map/convert_element_type | solution.py:9
  10.4 0.7 pad_maximum_fusion.2
  11.2 2.0 %convert_bitcast_fusion = (bf16[1,32,4096]{2,1,0:T(8,128)(2,1)S(1)}, f32[32,4096]{1,0:T(8,128)}) fusion(bf16[32,4096]{1,0:T(8,128)(2,1)} %param.6, f32[32,4096]{1,0:T(8,128)} %param.5), kind=kLoop, calls=%fused_computation.27 | loop fusion | flops 655360 | bytes 1572864 | tf_op jit(solution)/shard_map/stack | solution.py:61
  13.2 1.0 %pad_maximum_fusion.1 = bf16[2,32,4096]{2,1,0:T(8,128)(2,1)S(1)} fusion(bf16[1,32,4096]{2,1,0:T(8,128)(2,1)S(1)} %get-tuple-element.12, bf16[1,32,4096]{2,1,0:T(8,128)(2,1)} %bitcast.32), kind=kLoop, calls=%fused_computation.14 | loop fusion | flops 262144 | bytes 1048576 | tf_op jit(solution)/shard_map/stack | solution.py:61
  14.2 2.8 %copy.16 = bf16[2,32,4096]{1,0,2:T(2,128)(2,1)S(1)} copy(bf16[2,32,4096]{2,1,0:T(8,128)(2,1)S(1)} %pad_maximum_fusion.1) | data formatting | bytes 1048576 | tf_op jit(solution)/shard_map/stack | solution.py:61
  16.9 2.7 %reshape.48 = bf16[8,2,16384]{2,1,0:T(2,128)(2,1)} reshape(bf16[4096,2,32]{2,1,0:T(2,128)(2,1)S(1)} %bitcast.26) | data formatting | bytes 1048576
  19.6 5.2 %all-to-all-start = ((bf16[8,2,16384]{2,1,0:T(2,128)(2,1)}), bf16[8,2,16384]{2,1,0:T(2,128)(2,1)S(1)}, u32[]{:S(2)}, u32[]{:S(2)}) async-start(bf16[8,2,16384]{2,1,0:T(2,128)(2,1)} %reshape.48), calls=%async_computation | async-start | bytes 1048576 | tf_op jit(solution)/shard_map/all_to_all | solution.py:62
  24.8 0.8 dynamic_slice.3
  25.5 9.0 %all-to-all-done = bf16[8,2,16384]{2,1,0:T(2,128)(2,1)S(1)} async-done(((bf16[8,2,16384]{2,1,0:T(2,128)(2,1)}), bf16[8,2,16384]{2,1,0:T(2,128)(2,1)S(1)}, u32[]{:S(2)}, u32[]{:S(2)}) %all-to-all-start) | async-done | bytes 524320 | tf_op jit(solution)/shard_map/all_to_all | solution.py:62
  34.5 1.0 %reshape.49 = bf16[4096,2,32]{2,1,0:T(2,128)(2,1)S(1)} reshape(bf16[8,2,16384]{2,1,0:T(2,128)(2,1)S(1)} %all-to-all-done) | data formatting | bytes 1048576
  35.6 1.3 %copy.17 = bf16[2,32,8,512]{3,1,2,0:T(8,128)(2,1)S(1)} copy(bf16[2,32,8,512]{1,0,3,2:T(2,128)(2,1)S(1)} %bitcast.27) | data formatting | bytes 1048576 | tf_op jit(solution)/shard_map/all_to_all | solution.py:62
  37.1 4.8 %all-gather.2.cloned.1.call-done = bf16[2048,512]{1,0:T(8,128)(2,1)} async-done(((bf16[256,512]{1,0:T(8,128)(2,1)}), bf16[2048,512]{1,0:T(8,128)(2,1)}) %all-gather.2.cloned.1.call-update) | async-done | bytes 2097168 | tf_op jit(solution)/shard_map/all_gather | solution.py:65
  41.9 2.3 %fusion = (f32[2048]{0:T(1024)S(1)}, f32[2048,512]{1,0:T(8,128)S(1)}) fusion(f32[512]{0:T(512)S(1)} %get-tuple-element.22, bf16[256,512]{1,0:T(8,128)(2,1)S(1)} %bitcast.35, bf16[2048,512]{1,0:T(8,128)(2,1)} %all-gather.2.cloned.1.call-done), kind=kOutput, calls=%fused_computation.4 | convolution fusion | flops 540014592 | bytes 5515264 | tf_op jit(solution)/shard_map/dot_general | solution.py:71
  44.2 1.2 %fusion.1 = (f32[2048]{0:T(1024)S(1)}, f32[512]{0:T(512)S(1)}, f32[2048,512]{1,0:T(8,128)S(1)}) fusion(f32[512]{0:T(512)S(1)} %dynamic_slice.3, f32[512]{0:T(512)S(1)} %get-tuple-element.21, bf16[256,512]{1,0:T(8,128)(2,1)S(1)} %bitcast.37, bf16[2048,512]{1,0:T(8,128)(2,1)S(1)} %copy-done), kind=kOutput, calls=%fused_computation.5 | convolution fusion | flops 542111232 | bytes 5519360 | tf_op jit(solution)/shard_map/dot_general | solution.py:70
  45.5 0.3 collective-permute-start
  45.8 0.9 %collective-permute-done = f32[2,2048]{1,0:T(2,128)S(1)} collective-permute-done((f32[2,2048]{1,0:T(2,128)S(1)}, f32[2,2048]{1,0:T(2,128)S(1)}, u32[]{:S(2)}, u32[]{:S(2)}) %collective-permute-start) | collective-permute-done | bytes 16416 | tf_op jit(solution)/shard_map/ppermute | solution.py:50
  46.8 1.5 %collective-permute-start.1 = (f32[2,2048]{1,0:T(2,128)S(1)}, f32[2,2048]{1,0:T(2,128)S(1)}, u32[]{:S(2)}, u32[]{:S(2)}) collective-permute-start(f32[2,2048]{1,0:T(2,128)S(1)} %fusion.10), channel_id=1, source_target_pairs={{0,8},{4,12},{8,0},{12,4},{16,24},{20,28},{24,16},{28,20},{1,9},{5... | collective-permute-start | bytes 49160 | tf_op jit(solution)/shard_map/ppermute | solution.py:50
  48.3 2.3 %collective-permute-done.1 = f32[2,2048]{1,0:T(2,128)S(1)} collective-permute-done((f32[2,2048]{1,0:T(2,128)S(1)}, f32[2,2048]{1,0:T(2,128)S(1)}, u32[]{:S(2)}, u32[]{:S(2)}) %collective-permute-start.1) | collective-permute-done | bytes 16416 | tf_op jit(solution)/shard_map/ppermute | solution.py:50
  50.6 1.5 %collective-permute-start.2 = (f32[2,2048]{1,0:T(2,128)S(1)}, f32[2,2048]{1,0:T(2,128)S(1)}, u32[]{:S(2)}, u32[]{:S(2)}) collective-permute-start(f32[2,2048]{1,0:T(2,128)S(1)} %fusion.16), channel_id=1, source_target_pairs={{0,16},{4,20},{8,24},{12,28},{16,0},{20,4},{24,8},{28,12},{1,17},{... | collective-permute-start | bytes 49160 | tf_op jit(solution)/shard_map/ppermute | solution.py:50
  52.1 2.3 %collective-permute-done.2 = f32[2,2048]{1,0:T(2,128)S(1)} collective-permute-done((f32[2,2048]{1,0:T(2,128)S(1)}, f32[2,2048]{1,0:T(2,128)S(1)}, u32[]{:S(2)}, u32[]{:S(2)}) %collective-permute-start.2) | collective-permute-done | bytes 16416 | tf_op jit(solution)/shard_map/ppermute | solution.py:50
  54.4 1.5 %collective-permute-start.3 = (f32[2,2048]{1,0:T(2,128)S(1)}, f32[2,2048]{1,0:T(2,128)S(1)}, u32[]{:S(2)}, u32[]{:S(2)}) collective-permute-start(f32[2,2048]{1,0:T(2,128)S(1)} %add.65), channel_id=1, source_target_pairs={{0,1},{1,0},{2,3},{3,2},{4,5},{5,4},{6,7},{7,6},{8,9},{9,8},{10,11... | collective-permute-start | bytes 49160 | tf_op jit(solution)/shard_map/ppermute | solution.py:50
  56.0 2.3 %collective-permute-done.3 = f32[2,2048]{1,0:T(2,128)S(1)} collective-permute-done((f32[2,2048]{1,0:T(2,128)S(1)}, f32[2,2048]{1,0:T(2,128)S(1)}, u32[]{:S(2)}, u32[]{:S(2)}) %collective-permute-start.3) | collective-permute-done | bytes 16416 | tf_op jit(solution)/shard_map/ppermute | solution.py:50
  58.2 2.5 %collective-permute-start.4 = (f32[2,2048]{1,0:T(2,128)S(1)}, f32[2,2048]{1,0:T(2,128)S(1)}, u32[]{:S(2)}, u32[]{:S(2)}) collective-permute-start(f32[2,2048]{1,0:T(2,128)S(1)} %add.66), channel_id=1, source_target_pairs={{0,2},{1,3},{2,0},{3,1},{4,6},{5,7},{6,4},{7,5},{8,10},{9,11},{10,... | collective-permute-start | bytes 49160 | tf_op jit(solution)/shard_map/ppermute | solution.py:50
  60.7 0.8 multiply_add_fusion.1
  61.5 1.4 %collective-permute-done.4 = f32[2,2048]{1,0:T(2,128)S(1)} collective-permute-done((f32[2,2048]{1,0:T(2,128)S(1)}, f32[2,2048]{1,0:T(2,128)S(1)}, u32[]{:S(2)}, u32[]{:S(2)}) %collective-permute-start.4) | collective-permute-done | bytes 16416 | tf_op jit(solution)/shard_map/ppermute | solution.py:50
  63.0 2.4 %multiply_reduce_fusion = (f32[512]{0:T(512)S(1)}, bf16[2048,512]{1,0:T(8,128)(2,1)S(1)}) fusion(f32[2048,512]{1,0:T(8,128)S(1)} %get-tuple-element.20, f32[2048]{0:T(1024)S(1)} %bitcast.45, f32[2048,512]{1,0:T(8,128)S(1)} %get-tuple-element.18, f32[512]{0:T(512)S(1)} %dynamic_slice.3, f32[2048]{0:T(1024)S(1)} %bitcast.44), kind=kLoop, calls=%fused_computation | loop fusion | flops 11533824 | bytes 10506240 | tf_op jit(solution)/shard_map/reduce_sum | solution.py:79
  65.4 0.7 fusion.2
  66.2 13.7 %all_to_all.30 = f32[8,33,512]{2,1,0:T(8,128)S(1)} all-to-all(f32[8,33,512]{2,1,0:T(8,128)S(1)} %pad_maximum_fusion), channel_id=1, replica_groups=mesh['dp'=8,'tensor'=4] {'dp'}, dimensions={0} | all-to-all | bytes 1081344 | tf_op jit(solution)/shard_map/all_to_all | solution.py:88
  79.9 0.6 slice.46
  80.6 0.8 copy.19
  (20 shorter events, 0.5 us)
Async XLA Ops:
  7.2 34.7 %all-gather.2.cloned.1.call-start = ((), (), s32[]{:S(2)}) async-start(), calls=%async_computation.2 | async-start | bytes 2359296 | tf_op jit(solution)/shard_map/all_gather | solution.py:65
  19.6 14.9 %all-to-all-start = ((bf16[8,2,16384]{2,1,0:T(2,128)(2,1)}), bf16[8,2,16384]{2,1,0:T(2,128)(2,1)S(1)}, u32[]{:S(2)}, u32[]{:S(2)}) async-start(bf16[8,2,16384]{2,1,0:T(2,128)(2,1)} %reshape.48), calls=%async_computation | async-start | bytes 1048576 | tf_op jit(solution)/shard_map/all_to_all | solution.py:62
  41.9 2.3 %copy-start = (bf16[2048,512]{1,0:T(8,128)(2,1)S(1)}, bf16[2048,512]{1,0:T(8,128)(2,1)}, u32[]{:S(2)}) copy-start(bf16[2048,512]{1,0:T(8,128)(2,1)} %all-gather.2.cloned.1.call-done) | copy-start | bytes 6291460
  45.5 1.2 %collective-permute-start = (f32[2,2048]{1,0:T(2,128)S(1)}, f32[2,2048]{1,0:T(2,128)S(1)}, u32[]{:S(2)}, u32[]{:S(2)}) collective-permute-start(f32[2,2048]{1,0:T(2,128)S(1)} %pad_maximum_fusion.3), channel_id=1, source_target_pairs={{0,4},{4,0},{8,12},{12,8},{16,20},{20,16},{24,28},{28,24},{1,5},{5... | collective-permute-start | bytes 49160 | tf_op jit(solution)/shard_map/ppermute | solution.py:50
  46.8 3.8 %collective-permute-start.1 = (f32[2,2048]{1,0:T(2,128)S(1)}, f32[2,2048]{1,0:T(2,128)S(1)}, u32[]{:S(2)}, u32[]{:S(2)}) collective-permute-start(f32[2,2048]{1,0:T(2,128)S(1)} %fusion.10), channel_id=1, source_target_pairs={{0,8},{4,12},{8,0},{12,4},{16,24},{20,28},{24,16},{28,20},{1,9},{5... | collective-permute-start | bytes 49160 | tf_op jit(solution)/shard_map/ppermute | solution.py:50
  50.6 3.8 %collective-permute-start.2 = (f32[2,2048]{1,0:T(2,128)S(1)}, f32[2,2048]{1,0:T(2,128)S(1)}, u32[]{:S(2)}, u32[]{:S(2)}) collective-permute-start(f32[2,2048]{1,0:T(2,128)S(1)} %fusion.16), channel_id=1, source_target_pairs={{0,16},{4,20},{8,24},{12,28},{16,0},{20,4},{24,8},{28,12},{1,17},{... | collective-permute-start | bytes 49160 | tf_op jit(solution)/shard_map/ppermute | solution.py:50
  54.4 3.8 %collective-permute-start.3 = (f32[2,2048]{1,0:T(2,128)S(1)}, f32[2,2048]{1,0:T(2,128)S(1)}, u32[]{:S(2)}, u32[]{:S(2)}) collective-permute-start(f32[2,2048]{1,0:T(2,128)S(1)} %add.65), channel_id=1, source_target_pairs={{0,1},{1,0},{2,3},{3,2},{4,5},{5,4},{6,7},{7,6},{8,9},{9,8},{10,11... | collective-permute-start | bytes 49160 | tf_op jit(solution)/shard_map/ppermute | solution.py:50
  58.2 4.7 %collective-permute-start.4 = (f32[2,2048]{1,0:T(2,128)S(1)}, f32[2,2048]{1,0:T(2,128)S(1)}, u32[]{:S(2)}, u32[]{:S(2)}) collective-permute-start(f32[2,2048]{1,0:T(2,128)S(1)} %add.66), channel_id=1, source_target_pairs={{0,2},{1,3},{2,0},{3,1},{4,6},{5,7},{6,4},{7,5},{8,10},{9,11},{10,... | collective-permute-start | bytes 49160 | tf_op jit(solution)/shard_map/ppermute | solution.py:50
Sparse Core Ops, SparseCore 0:
  11.3 30.5 all-gather.1

commit v4 on v3

--- a/solution.py
+++ b/solution.py
@@ -53,18 +53,27 @@
 
 
 def feature_plan(teacher_master, student_weight, teacher_feat, student_feat, center):
-    ndp = lax.axis_size("dp")
+    n = lax.axis_size("dp")
+    me = lax.axis_index("dp")
+    rows, width = teacher_master.shape
     bot = teacher_feat.shape[1]
-    images_all = teacher_feat.shape[0] * ndp
-    cols = center.shape[0] // ndp
+    images = teacher_feat.shape[0]
+    cols = width // n
     master_new = 0.996 * teacher_master + 0.004 * student_weight.astype(jnp.float32)
-    both = jnp.stack([student_weight, master_new.astype(jnp.bfloat16)])
-    both = lax.all_to_all(both, "dp", 2, 1, tiled=True)
+    local = jnp.stack([student_weight, master_new.astype(jnp.bfloat16)])
+    feat = jnp.concatenate([unit_rows(teacher_feat), unit_rows(student_feat)], axis=1)
+    feats, blocks = [feat], [lax.dynamic_slice_in_dim(local, me * cols, cols, axis=2)]
+    for k in range(1, n):
+        part = lax.dynamic_slice_in_dim(local, (me ^ k) * cols, cols, axis=2)
+        got_feat, got_part = lax.ppermute((feat, part), "dp", [(i, i ^ k) for i in range(n)])
+        feats.append(got_feat)
+        blocks.append(got_part)
+    feats = jnp.concatenate(feats, axis=0)
+    order = me ^ jnp.arange(n)
+    both = jnp.take(jnp.stack(blocks, axis=1), order, axis=1).reshape(2, n * rows, cols)
     sw, tw = both[0], both[1]
-    feats = jnp.concatenate([unit_rows(teacher_feat), unit_rows(student_feat)], axis=1)
-    feats = lax.all_gather(feats, "dp", axis=0, tiled=True)
     zt, zs = feats[:, :bot], feats[:, bot:]
-    c = lax.dynamic_slice_in_dim(center, lax.axis_index("dp") * cols, cols)
+    c = lax.dynamic_slice_in_dim(center, me * cols, cols)
     t_norm = jnp.sqrt(jnp.sum(jnp.square(tw.astype(jnp.float32)), 0) + 1e-06)
     s_norm = jnp.sqrt(jnp.sum(jnp.square(sw.astype(jnp.float32)), 0) + 1e-06)
     t_cos = jnp.dot(zt, tw, preferred_element_type=jnp.float32) / t_norm
@@ -72,21 +81,28 @@
     t_exp = jnp.exp((t_cos - c) / 0.04)
     s_exp = jnp.exp(s_cos / 0.1)
     totals = jnp.stack([jnp.sum(t_exp, 1), jnp.sum(s_exp, 1)])
-    totals = exchange_sum(exchange_sum(totals, "dp", ndp), "tensor", lax.axis_size("tensor"))
+    step = 1
+    while step < n:
+        got = lax.ppermute(totals, "dp", [(i, i ^ step) for i in range(n)])
+        got = got.reshape(2, n // (2 * step), 2, step, images)[:, :, ::-1]
+        totals = totals + got.reshape(2, n * images)
+        step *= 2
+    totals = exchange_sum(totals, "tensor", lax.axis_size("tensor"))
     t_total, s_total = totals[0][:, None], totals[1][:, None]
-    part_center = 0.5 * c + 0.5 * (jnp.sum(t_cos, 0) / images_all)
+    part_center = 0.5 * c + 0.5 * (jnp.sum(t_cos, 0) / (images * n))
     dlog = ((s_exp / s_total - t_exp / t_total) / 0.1).astype(jnp.bfloat16)
     scaled = jnp.sum(dlog.astype(jnp.float32) * s_cos, 0) / s_norm
     product = lax.dot_general(
         zs, dlog, (((0,), (0,)), ((), ())), preferred_element_type=jnp.float32
     )
     grad = (product - sw.astype(jnp.float32) * scaled) / s_norm
-    rows = grad.shape[0] // ndp
     sent = jnp.concatenate(
-        [grad.reshape(ndp, rows, cols), jnp.broadcast_to(part_center, (ndp, 1, cols))], axis=1
+        [grad.reshape(n, rows, cols), jnp.broadcast_to(part_center, (n, 1, cols))], axis=1
     )
-    got = lax.all_to_all(sent, "dp", 0, 2, tiled=True)
-    got = got.reshape(rows + 1, ndp * cols)
+    back = [sent[me]]
+    for k in range(1, n):
+        back.append(lax.ppermute(sent[me ^ k], "dp", [(i, i ^ k) for i in range(n)]))
+    got = jnp.take(jnp.stack(back, axis=1), order, axis=1).reshape(rows + 1, n * cols)
     return (master_new, got[:rows], got[rows])
 
 
@@ -107,7 +123,7 @@
     def shards(teacher_master, student_weight, teacher_feat, student_feat, center):
         images_all = teacher_feat.shape[0] * ndp
         cols = center.shape[0]
-        if images_all < cols and cols % ndp == 0:
+        if images_all < cols and cols % ndp == 0 and ndp & (ndp - 1) == 0:
             return feature_plan(teacher_master, student_weight, teacher_feat, student_feat, center)
         return weight_plan(teacher_master, student_weight, teacher_feat, student_feat, center)
 

time: 88.6 us -> 109 us (1.23)
  waiting for transfers between devices: 23.1 us -> 54.6 us
  starting transfers between devices: 12.6 us -> 29.9 us
  blocking collectives: 13.7 us -> 0 us
  between operations: 14.2 us -> 1.09 us
  local copies, waits for them, and re-layouts: 10.1 us -> 4.05 us
  matrix products: 4.29 us -> 6.67 us
  other arithmetic: 10.3 us -> 12 us
    ppermute x0 -> x24, waiting for transfers between devices: none -> 51.7 us  [the longest x14 39 us: feature_plan(): lax.ppermute((feat, part), 'dp', [(i, i ^ k) for i in range(n)])]
    ppermute x0 -> x24, starting transfers between devices: none -> 25.1 us  [the longest x14 16.3 us: feature_plan(): lax.ppermute((feat, part), 'dp', [(i, i ^ k) for i in range(n)])]
    all_to_all x1 -> x0, blocking collectives: 13.7 us -> none  [feature_plan(): got = lax.all_to_all(sent, 'dp', 0, 2, tiled=True)]
    all_to_all x1 -> x0, waiting for transfers between devices: 8.99 us -> none  [feature_plan(): both = lax.all_to_all(both, 'dp', 2, 1, tiled=True)]
    ppermute x5 -> x2, waiting for transfers between devices: 9.25 us -> 2.94 us  [exchange_sum(): x = x + lax.ppermute(x, axis, [(i, i ^ step) for i in range(n)])]
    all_to_all x1 -> x0, starting transfers between devices: 5.17 us -> none  [feature_plan(): both = lax.all_to_all(both, 'dp', 2, 1, tiled=True)]
    all_gather x1 -> x0, waiting for transfers between devices: 4.83 us -> none  [feature_plan(): feats = lax.all_gather(feats, 'dp', axis=0, tiled=True)]
    unnamed x6 -> x27, local copies, waits for them, and re-layouts: 4.57 us -> 0.29 us
  transfers between devices with their start and end apart: 7 -> 26, of which waited for: 7 -> 18; matrix products, arithmetic and copies ran while one was open for 14% -> 4% of each run, Pallas kernels for 0% -> 0%
where the time goes in v4:
time: 109 us; the launch traced here: 108 us
  waiting for transfers between devices  54.6 us (50%)
  starting transfers between devices  29.9 us (27%)
  other arithmetic  12 us (11%)
  matrix products  6.67 us (6%)
  local copies, waits for them, and re-layouts  4.05 us (4%)
  between operations  1.09 us (1%)
    ppermute x14, waiting for transfers between devices, feature_plan(): lax.ppermute((feat, part), 'dp', [(i, i ^ k) for i in range(n)])  39 us
    ppermute x14, starting transfers between devices, feature_plan(): lax.ppermute((feat, part), 'dp', [(i, i ^ k) for i in range(n)])  16.3 us
    ppermute x7, waiting for transfers between devices, feature_plan(): lax.ppermute(sent[me ^ k], 'dp', [(i, i ^ k) for i in range(n)])  7.01 us
    ppermute x3, waiting for transfers between devices, feature_plan(): got = lax.ppermute(totals, 'dp', [(i, i ^ step) for i in range(n)])  5.7 us
    ppermute x7, starting transfers between devices, feature_plan(): lax.ppermute(sent[me ^ k], 'dp', [(i, i ^ k) for i in range(n)])  5.58 us
    ppermute x2, starting transfers between devices, exchange_sum(): x = x + lax.ppermute(x, axis, [(i, i ^ step) for i in range(n)])  4.8 us
    reduce_sum x1, other arithmetic, feature_plan(): scaled = jnp.sum(dlog.astype(jnp.float32) * s_cos, 0) / s_norm  4.65 us
    ppermute x3, starting transfers between devices, feature_plan(): got = lax.ppermute(totals, 'dp', [(i, i ^ step) for i in range(n)])  3.15 us
  transfers between devices with their start and end apart: 26, of which 18 were waited for; matrix products, arithmetic and copies ran while one was open for 4% of the time, Pallas kernels for 0%

profile of v4, /device:TPU:0, one launch (start us, length us, event | category | flops | bytes accessed | tf_op | source)
XLA Modules:
  0.0 108.3 jit_solution(1076531389265483037)
XLA Ops:
  2.8 1.1 %fusion.7 = (bf16[256,256]{1,0:T(8,128)(2,1)S(1)}, bf16[256,256]{1,0:T(8,128)(2,1)S(1)}) fusion(bf16[256,256]{1,0:T(8,128)(2,1)} %param.7, f32[256]{0:T(256)S(1)} %add_rsqrt_fusion.1, f32[256]{0:T(256)S(1)} %add_rsqrt_fusion, bf16[256,256]{1,0:T(8,128)(2,1)} %param.8), kind=kLoop, calls=%fused_computation.58 | loop fusion | flops 393216 | bytes 526336 | tf_op jit(solution)/shard_map/convert_element_type | solution.py:9
  5.1 2.5 %collective-permute-start.1 = (bf16[256,512]{1,0:T(8,128)(2,1)S(1)}, bf16[256,512]{1,0:T(8,128)(2,1)S(1)}, u32[]{:S(2)}, u32[]{:S(2)}) collective-permute-start(bf16[256,512]{1,0:T(8,128)(2,1)S(1)} %get-tuple-element.25), channel_id=1, source_target_pairs={{0,8},{4,12},{8,0},{12,4},{16,24},{20,28},{24,16},{28,20},{1,9},{5... | collective-permute-start | bytes 786440 | tf_op jit(solution)/shard_map/ppermute | solution.py:68
  7.7 1.7 %collective-permute-start.3 = (bf16[256,512]{1,0:T(8,128)(2,1)S(1)}, bf16[256,512]{1,0:T(8,128)(2,1)S(1)}, u32[]{:S(2)}, u32[]{:S(2)}) collective-permute-start(bf16[256,512]{1,0:T(8,128)(2,1)S(1)} %get-tuple-element.25), channel_id=1, source_target_pairs={{0,16},{4,20},{8,24},{12,28},{16,0},{20,4},{24,8},{28,12},{1,17},{... | collective-permute-start | bytes 786440 | tf_op jit(solution)/shard_map/ppermute | solution.py:68
  9.4 2.0 %convert_bitcast_fusion = (bf16[1,32,4096]{2,1,0:T(8,128)(2,1)S(1)}, f32[32,4096]{1,0:T(8,128)}) fusion(bf16[32,4096]{1,0:T(8,128)(2,1)} %param.6, f32[32,4096]{1,0:T(8,128)} %param.5), kind=kLoop, calls=%fused_computation.62 | loop fusion | flops 655360 | bytes 1572864 | tf_op jit(solution)/shard_map/stack | solution.py:63
  12.8 1.5 %collective-permute-start.8 = (bf16[2,32,512]{2,1,0:T(8,128)(2,1)S(1)}, bf16[2,32,512]{2,1,0:T(8,128)(2,1)S(1)}, u32[]{:S(2)}, u32[]{:S(2)}) collective-permute-start(bf16[2,32,512]{2,1,0:T(8,128)(2,1)S(1)} %get-tuple-element.21), channel_id=1, source_target_pairs={{0,8},{4,12},{8,0},{12,4},{16,24},{20,28},{24,16},{28,20},{1,9},{5... | collective-permute-start | bytes 196616 | tf_op jit(solution)/shard_map/ppermute | solution.py:68
  14.3 7.3 %collective-permute-done.8 = bf16[2,32,512]{2,1,0:T(8,128)(2,1)S(1)} collective-permute-done((bf16[2,32,512]{2,1,0:T(8,128)(2,1)S(1)}, bf16[2,32,512]{2,1,0:T(8,128)(2,1)S(1)}, u32[]{:S(2)}, u32[]{:S(2)}) %collective-permute-start.8) | collective-permute-done | bytes 65568 | tf_op jit(solution)/shard_map/ppermute | solution.py:68
  21.5 1.1 collective-permute-start.9
  22.6 3.0 %collective-permute-done.9 = bf16[2,32,512]{2,1,0:T(8,128)(2,1)S(1)} collective-permute-done((bf16[2,32,512]{2,1,0:T(8,128)(2,1)S(1)}, bf16[2,32,512]{2,1,0:T(8,128)(2,1)S(1)}, u32[]{:S(2)}, u32[]{:S(2)}) %collective-permute-start.9) | collective-permute-done | bytes 65568 | tf_op jit(solution)/shard_map/ppermute | solution.py:68
  25.6 2.0 %collective-permute-start.10 = (bf16[2,32,512]{2,1,0:T(8,128)(2,1)S(1)}, bf16[2,32,512]{2,1,0:T(8,128)(2,1)S(1)}, u32[]{:S(2)}, u32[]{:S(2)}) collective-permute-start(bf16[2,32,512]{2,1,0:T(8,128)(2,1)S(1)} %get-tuple-element.23), channel_id=1, source_target_pairs={{0,16},{4,20},{8,24},{12,28},{16,0},{20,4},{24,8},{28,12},{1,17},{... | collective-permute-start | bytes 196616 | tf_op jit(solution)/shard_map/ppermute | solution.py:68
  27.7 2.4 %collective-permute-done.10 = bf16[2,32,512]{2,1,0:T(8,128)(2,1)S(1)} collective-permute-done((bf16[2,32,512]{2,1,0:T(8,128)(2,1)S(1)}, bf16[2,32,512]{2,1,0:T(8,128)(2,1)S(1)}, u32[]{:S(2)}, u32[]{:S(2)}) %collective-permute-start.10) | collective-permute-done | bytes 65568 | tf_op jit(solution)/shard_map/ppermute | solution.py:68
  30.5 3.6 %collective-permute-done.11 = bf16[2,32,512]{2,1,0:T(8,128)(2,1)S(1)} collective-permute-done((bf16[2,32,512]{2,1,0:T(8,128)(2,1)S(1)}, bf16[2,32,512]{2,1,0:T(8,128)(2,1)S(1)}, u32[]{:S(2)}, u32[]{:S(2)}) %collective-permute-start.11) | collective-permute-done | bytes 65568 | tf_op jit(solution)/shard_map/ppermute | solution.py:68
  34.1 2.4 %collective-permute-start.12 = (bf16[2,32,512]{2,1,0:T(8,128)(2,1)S(1)}, bf16[2,32,512]{2,1,0:T(8,128)(2,1)S(1)}, u32[]{:S(2)}, u32[]{:S(2)}) collective-permute-start(bf16[2,32,512]{2,1,0:T(8,128)(2,1)S(1)} %fusion.34), channel_id=1, source_target_pairs={{0,24},{4,28},{8,16},{12,20},{16,8},{20,12},{24,0},{28,4},{1,25},{... | collective-permute-start | bytes 196616 | tf_op jit(solution)/shard_map/ppermute | solution.py:68
  36.5 2.7 %collective-permute-done.12 = bf16[2,32,512]{2,1,0:T(8,128)(2,1)S(1)} collective-permute-done((bf16[2,32,512]{2,1,0:T(8,128)(2,1)S(1)}, bf16[2,32,512]{2,1,0:T(8,128)(2,1)S(1)}, u32[]{:S(2)}, u32[]{:S(2)}) %collective-permute-start.12) | collective-permute-done | bytes 65568 | tf_op jit(solution)/shard_map/ppermute | solution.py:68
  39.2 5.2 %collective-permute-done.13 = bf16[2,32,512]{2,1,0:T(8,128)(2,1)S(1)} collective-permute-done((bf16[2,32,512]{2,1,0:T(8,128)(2,1)S(1)}, bf16[2,32,512]{2,1,0:T(8,128)(2,1)S(1)}, u32[]{:S(2)}, u32[]{:S(2)}) %collective-permute-start.13) | collective-permute-done | bytes 65568 | tf_op jit(solution)/shard_map/ppermute | solution.py:68
  46.0 1.2 %collective-permute-start.5 = (bf16[256,512]{1,0:T(8,128)(2,1)S(1)}, bf16[256,512]{1,0:T(8,128)(2,1)S(1)}, u32[]{:S(2)}, u32[]{:S(2)}) collective-permute-start(bf16[256,512]{1,0:T(8,128)(2,1)S(1)} %get-tuple-element.25), channel_id=1, source_target_pairs={{0,24},{4,28},{8,16},{12,20},{16,8},{20,12},{24,0},{28,4},{1,25},{... | collective-permute-start | bytes 786440 | tf_op jit(solution)/shard_map/ppermute | solution.py:68
  47.3 2.0 %collective-permute-start.6 = (bf16[256,512]{1,0:T(8,128)(2,1)S(1)}, bf16[256,512]{1,0:T(8,128)(2,1)S(1)}, u32[]{:S(2)}, u32[]{:S(2)}) collective-permute-start(bf16[256,512]{1,0:T(8,128)(2,1)S(1)} %get-tuple-element.25), channel_id=1, source_target_pairs={{0,28},{4,24},{8,20},{12,16},{16,12},{20,8},{24,4},{28,0},{1,29},{... | collective-permute-start | bytes 786440 | tf_op jit(solution)/shard_map/ppermute | solution.py:68
  49.5 14.5 %collective-permute-done.4 = bf16[256,512]{1,0:T(8,128)(2,1)S(1)} collective-permute-done((bf16[256,512]{1,0:T(8,128)(2,1)S(1)}, bf16[256,512]{1,0:T(8,128)(2,1)S(1)}, u32[]{:S(2)}, u32[]{:S(2)}) %collective-permute-start.4) | collective-permute-done | bytes 262176 | tf_op jit(solution)/shard_map/ppermute | solution.py:68
  64.1 2.8 %fusion = (f32[2048]{0:T(1024)S(1)}, f32[2048,512]{1,0:T(8,128)}) fusion(f32[512]{0:T(512)S(1)} %get-tuple-element.33, bf16[256,512]{1,0:T(8,128)(2,1)S(1)} %bitcast.82, bf16[2048,512]{1,0:T(8,128)(2,1)S(1)} %constant_dynamic-update-slice_fusion), kind=kOutput, calls=%fused_computation.6 | convolution fusion | flops 540014592 | bytes 5515264 | tf_op jit(solution)/shard_map/dot_general | solution.py:80
  66.9 3.1 %fusion.1 = (f32[2048]{0:T(1024)S(1)}, f32[512]{0:T(512)S(1)}, f32[2048,512]{1,0:T(8,128)}) fusion(f32[512]{0:T(512)S(1)} %dynamic_slice.59, f32[512]{0:T(512)S(1)} %get-tuple-element.32, bf16[256,512]{1,0:T(8,128)(2,1)S(1)} %bitcast.84, bf16[2048,512]{1,0:T(8,128)(2,1)S(1)} %constant_dynamic-update-slice_fusion), kind=kOutput, calls=%fused_computation.7 | convolution fusion | flops 542111232 | bytes 5519360 | tf_op jit(solution)/shard_map/dot_general | solution.py:79
  70.2 1.1 collective-permute-done.14
  71.5 1.3 %collective-permute-start.15 = (f32[2,2048]{1,0:T(2,128)S(1)}, f32[2,2048]{1,0:T(2,128)S(1)}, u32[]{:S(2)}, u32[]{:S(2)}) collective-permute-start(f32[2,2048]{1,0:T(2,128)S(1)} %fusion.36), channel_id=1, source_target_pairs={{0,8},{4,12},{8,0},{12,4},{16,24},{20,28},{24,16},{28,20},{1,9},{5... | collective-permute-start | bytes 49160 | tf_op jit(solution)/shard_map/ppermute | solution.py:86
  72.8 2.5 %collective-permute-done.15 = f32[2,2048]{1,0:T(2,128)S(1)} collective-permute-done((f32[2,2048]{1,0:T(2,128)S(1)}, f32[2,2048]{1,0:T(2,128)S(1)}, u32[]{:S(2)}, u32[]{:S(2)}) %collective-permute-start.15) | collective-permute-done | bytes 16416 | tf_op jit(solution)/shard_map/ppermute | solution.py:86
  75.4 1.6 %collective-permute-start.16 = (f32[2,2048]{1,0:T(2,128)S(1)}, f32[2,2048]{1,0:T(2,128)S(1)}, u32[]{:S(2)}, u32[]{:S(2)}) collective-permute-start(f32[2,2048]{1,0:T(2,128)S(1)} %fusion.42), channel_id=1, source_target_pairs={{0,16},{4,20},{8,24},{12,28},{16,0},{20,4},{24,8},{28,12},{1,17},{... | collective-permute-start | bytes 49160 | tf_op jit(solution)/shard_map/ppermute | solution.py:86
  77.1 2.2 %collective-permute-done.16 = f32[2,2048]{1,0:T(2,128)S(1)} collective-permute-done((f32[2,2048]{1,0:T(2,128)S(1)}, f32[2,2048]{1,0:T(2,128)S(1)}, u32[]{:S(2)}, u32[]{:S(2)}) %collective-permute-start.16) | collective-permute-done | bytes 16416 | tf_op jit(solution)/shard_map/ppermute | solution.py:86
  79.3 1.9 %collective-permute-start.17 = (f32[2,2048]{1,0:T(2,128)S(1)}, f32[2,2048]{1,0:T(2,128)S(1)}, u32[]{:S(2)}, u32[]{:S(2)}) collective-permute-start(f32[2,2048]{1,0:T(2,128)S(1)} %add.137), channel_id=1, source_target_pairs={{0,1},{1,0},{2,3},{3,2},{4,5},{5,4},{6,7},{7,6},{8,9},{9,8},{10,11... | collective-permute-start | bytes 49160 | tf_op jit(solution)/shard_map/ppermute | solution.py:50
  81.2 1.9 %collective-permute-done.17 = f32[2,2048]{1,0:T(2,128)S(1)} collective-permute-done((f32[2,2048]{1,0:T(2,128)S(1)}, f32[2,2048]{1,0:T(2,128)S(1)}, u32[]{:S(2)}, u32[]{:S(2)}) %collective-permute-start.17) | collective-permute-done | bytes 16416 | tf_op jit(solution)/shard_map/ppermute | solution.py:50
  83.1 2.9 %collective-permute-start.18 = (f32[2,2048]{1,0:T(2,128)S(1)}, f32[2,2048]{1,0:T(2,128)S(1)}, u32[]{:S(2)}, u32[]{:S(2)}) collective-permute-start(f32[2,2048]{1,0:T(2,128)S(1)} %add.138), channel_id=1, source_target_pairs={{0,2},{1,3},{2,0},{3,1},{4,6},{5,7},{6,4},{7,5},{8,10},{9,11},{10,... | collective-permute-start | bytes 49160 | tf_op jit(solution)/shard_map/ppermute | solution.py:50
  87.9 4.7 %multiply_reduce_fusion = (f32[512]{0:T(512)S(1)}, bf16[2048,512]{1,0:T(8,128)(2,1)S(1)}) fusion(f32[2048,512]{1,0:T(8,128)} %get-tuple-element.31, f32[2048]{0:T(1024)S(1)} %bitcast.92, f32[2048,512]{1,0:T(8,128)} %get-tuple-element.29, f32[512]{0:T(512)S(1)} %dynamic_slice.59, f32[2048]{0:T(1024)S(1)} %bitcast.91), kind=kLoop, calls=%fused_computation.2 | loop fusion | flops 11533824 | bytes 10506240 | tf_op jit(solution)/shard_map/reduce_sum | solution.py:94
  93.3 1.9 %collective-permute-start.24 = (f32[33,512]{1,0:T(8,128)S(1)}, f32[33,512]{1,0:T(8,128)S(1)}, u32[]{:S(2)}, u32[]{:S(2)}) collective-permute-start(f32[33,512]{1,0:T(8,128)S(1)} %fusion.18), channel_id=1, source_target_pairs={{0,24},{4,28},{8,16},{12,20},{16,8},{20,12},{24,0},{28,4},{1,25},{... | collective-permute-start | bytes 202760 | tf_op jit(solution)/shard_map/ppermute | solution.py:104
  95.3 1.3 %collective-permute-start.20 = (f32[33,512]{1,0:T(8,128)S(1)}, f32[33,512]{1,0:T(8,128)S(1)}, u32[]{:S(2)}, u32[]{:S(2)}) collective-permute-start(f32[33,512]{1,0:T(8,128)S(1)} %get-tuple-element.13), channel_id=1, source_target_pairs={{0,8},{4,12},{8,0},{12,4},{16,24},{20,28},{24,16},{28,20},{1,9},{5... | collective-permute-start | bytes 202760 | tf_op jit(solution)/shard_map/ppermute | solution.py:104
  99.0 2.1 %collective-permute-done.20 = f32[33,512]{1,0:T(8,128)S(1)} collective-permute-done((f32[33,512]{1,0:T(8,128)S(1)}, f32[33,512]{1,0:T(8,128)S(1)}, u32[]{:S(2)}, u32[]{:S(2)}) %collective-permute-start.20) | collective-permute-done | bytes 67616 | tf_op jit(solution)/shard_map/ppermute | solution.py:104
  103.1 2.9 %collective-permute-done.25 = f32[33,512]{1,0:T(8,128)S(1)} collective-permute-done((f32[33,512]{1,0:T(8,128)S(1)}, f32[33,512]{1,0:T(8,128)S(1)}, u32[]{:S(2)}, u32[]{:S(2)}) %collective-permute-start.25) | collective-permute-done | bytes 67616 | tf_op jit(solution)/shard_map/ppermute | solution.py:104
  (99 shorter events, 16.8 us)
Async XLA Ops:
  0.6 10.8 %copy-start = (bf16[32,4096]{1,0:T(8,128)(2,1)S(1)}, bf16[32,4096]{1,0:T(8,128)(2,1)}, u32[]{:S(2)}) copy-start(bf16[32,4096]{1,0:T(8,128)(2,1)} %param.6) | copy-start | bytes 786436
  4.6 41.4 %collective-permute-start = (bf16[256,512]{1,0:T(8,128)(2,1)S(1)}, bf16[256,512]{1,0:T(8,128)(2,1)S(1)}, u32[]{:S(2)}, u32[]{:S(2)}) collective-permute-start(bf16[256,512]{1,0:T(8,128)(2,1)S(1)} %get-tuple-element.25), channel_id=1, source_target_pairs={{0,4},{4,0},{8,12},{12,8},{16,20},{20,16},{24,28},{28,24},{1,5},{5... | collective-permute-start | bytes 786440 | tf_op jit(solution)/shard_map/ppermute | solution.py:68
  5.1 42.3 %collective-permute-start.1 = (bf16[256,512]{1,0:T(8,128)(2,1)S(1)}, bf16[256,512]{1,0:T(8,128)(2,1)S(1)}, u32[]{:S(2)}, u32[]{:S(2)}) collective-permute-start(bf16[256,512]{1,0:T(8,128)(2,1)S(1)} %get-tuple-element.25), channel_id=1, source_target_pairs={{0,8},{4,12},{8,0},{12,4},{16,24},{20,28},{24,16},{28,20},{1,9},{5... | collective-permute-start | bytes 786440 | tf_op jit(solution)/shard_map/ppermute | solution.py:68
  7.5 41.9 %collective-permute-start.2 = (bf16[256,512]{1,0:T(8,128)(2,1)S(1)}, bf16[256,512]{1,0:T(8,128)(2,1)S(1)}, u32[]{:S(2)}, u32[]{:S(2)}) collective-permute-start(bf16[256,512]{1,0:T(8,128)(2,1)S(1)} %get-tuple-element.25), channel_id=1, source_target_pairs={{0,12},{4,8},{8,4},{12,0},{16,28},{20,24},{24,20},{28,16},{1,13},{... | collective-permute-start | bytes 786440 | tf_op jit(solution)/shard_map/ppermute | solution.py:68
  7.7 41.8 %collective-permute-start.3 = (bf16[256,512]{1,0:T(8,128)(2,1)S(1)}, bf16[256,512]{1,0:T(8,128)(2,1)S(1)}, u32[]{:S(2)}, u32[]{:S(2)}) collective-permute-start(bf16[256,512]{1,0:T(8,128)(2,1)S(1)} %get-tuple-element.25), channel_id=1, source_target_pairs={{0,16},{4,20},{8,24},{12,28},{16,0},{20,4},{24,8},{28,12},{1,17},{... | collective-permute-start | bytes 786440 | tf_op jit(solution)/shard_map/ppermute | solution.py:68
  11.5 1.3 %collective-permute-start.7 = (bf16[2,32,512]{2,1,0:T(8,128)(2,1)S(1)}, bf16[2,32,512]{2,1,0:T(8,128)(2,1)S(1)}, u32[]{:S(2)}, u32[]{:S(2)}) collective-permute-start(bf16[2,32,512]{2,1,0:T(8,128)(2,1)S(1)} %get-tuple-element.20), channel_id=1, source_target_pairs={{0,4},{4,0},{8,12},{12,8},{16,20},{20,16},{24,28},{28,24},{1,5},{5... | collective-permute-start | bytes 196616 | tf_op jit(solution)/shard_map/ppermute | solution.py:68
  12.8 8.8 %collective-permute-start.8 = (bf16[2,32,512]{2,1,0:T(8,128)(2,1)S(1)}, bf16[2,32,512]{2,1,0:T(8,128)(2,1)S(1)}, u32[]{:S(2)}, u32[]{:S(2)}) collective-permute-start(bf16[2,32,512]{2,1,0:T(8,128)(2,1)S(1)} %get-tuple-element.21), channel_id=1, source_target_pairs={{0,8},{4,12},{8,0},{12,4},{16,24},{20,28},{24,16},{28,20},{1,9},{5... | collective-permute-start | bytes 196616 | tf_op jit(solution)/shard_map/ppermute | solution.py:68
  21.5 4.1 %collective-permute-start.9 = (bf16[2,32,512]{2,1,0:T(8,128)(2,1)S(1)}, bf16[2,32,512]{2,1,0:T(8,128)(2,1)S(1)}, u32[]{:S(2)}, u32[]{:S(2)}) collective-permute-start(bf16[2,32,512]{2,1,0:T(8,128)(2,1)S(1)} %get-tuple-element.22), channel_id=1, source_target_pairs={{0,12},{4,8},{8,4},{12,0},{16,28},{20,24},{24,20},{28,16},{1,13},{... | collective-permute-start | bytes 196616 | tf_op jit(solution)/shard_map/ppermute | solution.py:68
  25.6 4.4 %collective-permute-start.10 = (bf16[2,32,512]{2,1,0:T(8,128)(2,1)S(1)}, bf16[2,32,512]{2,1,0:T(8,128)(2,1)S(1)}, u32[]{:S(2)}, u32[]{:S(2)}) collective-permute-start(bf16[2,32,512]{2,1,0:T(8,128)(2,1)S(1)} %get-tuple-element.23), channel_id=1, source_target_pairs={{0,16},{4,20},{8,24},{12,28},{16,0},{20,4},{24,8},{28,12},{1,17},{... | collective-permute-start | bytes 196616 | tf_op jit(solution)/shard_map/ppermute | solution.py:68
  30.0 4.0 %collective-permute-start.11 = (bf16[2,32,512]{2,1,0:T(8,128)(2,1)S(1)}, bf16[2,32,512]{2,1,0:T(8,128)(2,1)S(1)}, u32[]{:S(2)}, u32[]{:S(2)}) collective-permute-start(bf16[2,32,512]{2,1,0:T(8,128)(2,1)S(1)} %get-tuple-element.24), channel_id=1, source_target_pairs={{0,20},{4,16},{8,28},{12,24},{16,4},{20,0},{24,12},{28,8},{1,21},{... | collective-permute-start | bytes 196616 | tf_op jit(solution)/shard_map/ppermute | solution.py:68
  34.1 5.2 %collective-permute-start.12 = (bf16[2,32,512]{2,1,0:T(8,128)(2,1)S(1)}, bf16[2,32,512]{2,1,0:T(8,128)(2,1)S(1)}, u32[]{:S(2)}, u32[]{:S(2)}) collective-permute-start(bf16[2,32,512]{2,1,0:T(8,128)(2,1)S(1)} %fusion.34), channel_id=1, source_target_pairs={{0,24},{4,28},{8,16},{12,20},{16,8},{20,12},{24,0},{28,4},{1,25},{... | collective-permute-start | bytes 196616 | tf_op jit(solution)/shard_map/ppermute | solution.py:68
  39.2 5.2 %collective-permute-start.13 = (bf16[2,32,512]{2,1,0:T(8,128)(2,1)S(1)}, bf16[2,32,512]{2,1,0:T(8,128)(2,1)S(1)}, u32[]{:S(2)}, u32[]{:S(2)}) collective-permute-start(bf16[2,32,512]{2,1,0:T(8,128)(2,1)S(1)} %get-tuple-element.19), channel_id=1, source_target_pairs={{0,28},{4,24},{8,20},{12,16},{16,12},{20,8},{24,4},{28,0},{1,29},{... | collective-permute-start | bytes 196616 | tf_op jit(solution)/shard_map/ppermute | solution.py:68
  44.4 19.5 %collective-permute-start.4 = (bf16[256,512]{1,0:T(8,128)(2,1)S(1)}, bf16[256,512]{1,0:T(8,128)(2,1)S(1)}, u32[]{:S(2)}, u32[]{:S(2)}) collective-permute-start(bf16[256,512]{1,0:T(8,128)(2,1)S(1)} %get-tuple-element.25), channel_id=1, source_target_pairs={{0,20},{4,16},{8,28},{12,24},{16,4},{20,0},{24,12},{28,8},{1,21},{... | collective-permute-start | bytes 786440 | tf_op jit(solution)/shard_map/ppermute | solution.py:68
  45.7 1.6 %copy-start.1 = (bf16[2048,512]{1,0:T(8,128)(2,1)S(1)}, bf16[2048,512]{1,0:T(8,128)(2,1)}, u32[]{:S(2)}) copy-start(bf16[2048,512]{1,0:T(8,128)(2,1)} %get-tuple-element.26) | copy-start | bytes 6291460
  46.0 18.0 %collective-permute-start.5 = (bf16[256,512]{1,0:T(8,128)(2,1)S(1)}, bf16[256,512]{1,0:T(8,128)(2,1)S(1)}, u32[]{:S(2)}, u32[]{:S(2)}) collective-permute-start(bf16[256,512]{1,0:T(8,128)(2,1)S(1)} %get-tuple-element.25), channel_id=1, source_target_pairs={{0,24},{4,28},{8,16},{12,20},{16,8},{20,12},{24,0},{28,4},{1,25},{... | collective-permute-start | bytes 786440 | tf_op jit(solution)/shard_map/ppermute | solution.py:68
  47.3 16.7 %collective-permute-start.6 = (bf16[256,512]{1,0:T(8,128)(2,1)S(1)}, bf16[256,512]{1,0:T(8,128)(2,1)S(1)}, u32[]{:S(2)}, u32[]{:S(2)}) collective-permute-start(bf16[256,512]{1,0:T(8,128)(2,1)S(1)} %get-tuple-element.25), channel_id=1, source_target_pairs={{0,28},{4,24},{8,20},{12,16},{16,12},{20,8},{24,4},{28,0},{1,29},{... | collective-permute-start | bytes 786440 | tf_op jit(solution)/shard_map/ppermute | solution.py:68
  64.1 2.9 %copy-start.2 = (bf16[2048,512]{1,0:T(8,128)(2,1)}, bf16[2048,512]{1,0:T(8,128)(2,1)S(1)}, u32[]{:S(2)}) copy-start(bf16[2048,512]{1,0:T(8,128)(2,1)S(1)} %constant_dynamic-update-slice_fusion) | copy-start | bytes 6291460
  70.1 1.2 %collective-permute-start.14 = (f32[2,2048]{1,0:T(2,128)S(1)}, f32[2,2048]{1,0:T(2,128)S(1)}, u32[]{:S(2)}, u32[]{:S(2)}) collective-permute-start(f32[2,2048]{1,0:T(2,128)S(1)} %pad_maximum_fusion.1), channel_id=1, source_target_pairs={{0,4},{4,0},{8,12},{12,8},{16,20},{20,16},{24,28},{28,24},{1,5},{5... | collective-permute-start | bytes 49160 | tf_op jit(solution)/shard_map/ppermute | solution.py:86
  71.5 3.8 %collective-permute-start.15 = (f32[2,2048]{1,0:T(2,128)S(1)}, f32[2,2048]{1,0:T(2,128)S(1)}, u32[]{:S(2)}, u32[]{:S(2)}) collective-permute-start(f32[2,2048]{1,0:T(2,128)S(1)} %fusion.36), channel_id=1, source_target_pairs={{0,8},{4,12},{8,0},{12,4},{16,24},{20,28},{24,16},{28,20},{1,9},{5... | collective-permute-start | bytes 49160 | tf_op jit(solution)/shard_map/ppermute | solution.py:86
  75.4 3.8 %collective-permute-start.16 = (f32[2,2048]{1,0:T(2,128)S(1)}, f32[2,2048]{1,0:T(2,128)S(1)}, u32[]{:S(2)}, u32[]{:S(2)}) collective-permute-start(f32[2,2048]{1,0:T(2,128)S(1)} %fusion.42), channel_id=1, source_target_pairs={{0,16},{4,20},{8,24},{12,28},{16,0},{20,4},{24,8},{28,12},{1,17},{... | collective-permute-start | bytes 49160 | tf_op jit(solution)/shard_map/ppermute | solution.py:86
  79.3 3.8 %collective-permute-start.17 = (f32[2,2048]{1,0:T(2,128)S(1)}, f32[2,2048]{1,0:T(2,128)S(1)}, u32[]{:S(2)}, u32[]{:S(2)}) collective-permute-start(f32[2,2048]{1,0:T(2,128)S(1)} %add.137), channel_id=1, source_target_pairs={{0,1},{1,0},{2,3},{3,2},{4,5},{5,4},{6,7},{7,6},{8,9},{9,8},{10,11... | collective-permute-start | bytes 49160 | tf_op jit(solution)/shard_map/ppermute | solution.py:50
  83.1 4.7 %collective-permute-start.18 = (f32[2,2048]{1,0:T(2,128)S(1)}, f32[2,2048]{1,0:T(2,128)S(1)}, u32[]{:S(2)}, u32[]{:S(2)}) collective-permute-start(f32[2,2048]{1,0:T(2,128)S(1)} %add.138), channel_id=1, source_target_pairs={{0,2},{1,3},{2,0},{3,1},{4,6},{5,7},{6,4},{7,5},{8,10},{9,11},{10,... | collective-permute-start | bytes 49160 | tf_op jit(solution)/shard_map/ppermute | solution.py:50
  87.9 4.7 %copy-start.3 = (bf16[2048,512]{1,0:T(8,128)(2,1)S(1)}, bf16[2048,512]{1,0:T(8,128)(2,1)}, u32[]{:S(2)}) copy-start(bf16[2048,512]{1,0:T(8,128)(2,1)} %copy-done.2) | copy-start | bytes 6291460
  93.3 9.8 %collective-permute-start.24 = (f32[33,512]{1,0:T(8,128)S(1)}, f32[33,512]{1,0:T(8,128)S(1)}, u32[]{:S(2)}, u32[]{:S(2)}) collective-permute-start(f32[33,512]{1,0:T(8,128)S(1)} %fusion.18), channel_id=1, source_target_pairs={{0,24},{4,28},{8,16},{12,20},{16,8},{20,12},{24,0},{28,4},{1,25},{... | collective-permute-start | bytes 202760 | tf_op jit(solution)/shard_map/ppermute | solution.py:104
  95.3 2.9 %collective-permute-start.19 = (f32[33,512]{1,0:T(8,128)S(1)}, f32[33,512]{1,0:T(8,128)S(1)}, u32[]{:S(2)}, u32[]{:S(2)}) collective-permute-start(f32[33,512]{1,0:T(8,128)S(1)} %get-tuple-element.12), channel_id=1, source_target_pairs={{0,4},{4,0},{8,12},{12,8},{16,20},{20,16},{24,28},{28,24},{1,5},{5... | collective-permute-start | bytes 202760 | tf_op jit(solution)/shard_map/ppermute | solution.py:104
  95.3 5.8 %collective-permute-start.20 = (f32[33,512]{1,0:T(8,128)S(1)}, f32[33,512]{1,0:T(8,128)S(1)}, u32[]{:S(2)}, u32[]{:S(2)}) collective-permute-start(f32[33,512]{1,0:T(8,128)S(1)} %get-tuple-element.13), channel_id=1, source_target_pairs={{0,8},{4,12},{8,0},{12,4},{16,24},{20,28},{24,16},{28,20},{1,9},{5... | collective-permute-start | bytes 202760 | tf_op jit(solution)/shard_map/ppermute | solution.py:104
  96.6 5.2 %collective-permute-start.21 = (f32[33,512]{1,0:T(8,128)S(1)}, f32[33,512]{1,0:T(8,128)S(1)}, u32[]{:S(2)}, u32[]{:S(2)}) collective-permute-start(f32[33,512]{1,0:T(8,128)S(1)} %get-tuple-element.14), channel_id=1, source_target_pairs={{0,12},{4,8},{8,4},{12,0},{16,28},{20,24},{24,20},{28,16},{1,13},{... | collective-permute-start | bytes 202760 | tf_op jit(solution)/shard_map/ppermute | solution.py:104
  97.2 5.3 %collective-permute-start.22 = (f32[33,512]{1,0:T(8,128)S(1)}, f32[33,512]{1,0:T(8,128)S(1)}, u32[]{:S(2)}, u32[]{:S(2)}) collective-permute-start(f32[33,512]{1,0:T(8,128)S(1)} %get-tuple-element.15), channel_id=1, source_target_pairs={{0,16},{4,20},{8,24},{12,28},{16,0},{20,4},{24,8},{28,12},{1,17},{... | collective-permute-start | bytes 202760 | tf_op jit(solution)/shard_map/ppermute | solution.py:104
  98.1 5.0 %collective-permute-start.23 = (f32[33,512]{1,0:T(8,128)S(1)}, f32[33,512]{1,0:T(8,128)S(1)}, u32[]{:S(2)}, u32[]{:S(2)}) collective-permute-start(f32[33,512]{1,0:T(8,128)S(1)} %get-tuple-element.16), channel_id=1, source_target_pairs={{0,20},{4,16},{8,28},{12,24},{16,4},{20,0},{24,12},{28,8},{1,21},{... | collective-permute-start | bytes 202760 | tf_op jit(solution)/shard_map/ppermute | solution.py:104
  101.1 5.0 %collective-permute-start.25 = (f32[33,512]{1,0:T(8,128)S(1)}, f32[33,512]{1,0:T(8,128)S(1)}, u32[]{:S(2)}, u32[]{:S(2)}) collective-permute-start(f32[33,512]{1,0:T(8,128)S(1)} %get-tuple-element.11), channel_id=1, source_target_pairs={{0,28},{4,24},{8,20},{12,16},{16,12},{20,8},{24,4},{28,0},{1,29},{... | collective-permute-start | bytes 202760 | tf_op jit(solution)/shard_map/ppermute | solution.py:104

commit v5 on v3

--- a/solution.py
+++ b/solution.py
@@ -52,6 +52,13 @@
     return x
 
 
+def exchange_all(x, axis, n):
+    total = x
+    for k in range(1, n):
+        total = total + lax.ppermute(x, axis, [(i, (i + k) % n) for i in range(n)])
+    return total
+
+
 def feature_plan(teacher_master, student_weight, teacher_feat, student_feat, center):
     ndp = lax.axis_size("dp")
     bot = teacher_feat.shape[1]
@@ -72,7 +79,7 @@
     t_exp = jnp.exp((t_cos - c) / 0.04)
     s_exp = jnp.exp(s_cos / 0.1)
     totals = jnp.stack([jnp.sum(t_exp, 1), jnp.sum(s_exp, 1)])
-    totals = exchange_sum(exchange_sum(totals, "dp", ndp), "tensor", lax.axis_size("tensor"))
+    totals = exchange_all(exchange_all(totals, "dp", ndp), "tensor", lax.axis_size("tensor"))
     t_total, s_total = totals[0][:, None], totals[1][:, None]
     part_center = 0.5 * c + 0.5 * (jnp.sum(t_cos, 0) / images_all)
     dlog = ((s_exp / s_total - t_exp / t_total) / 0.1).astype(jnp.bfloat16)
@@ -82,12 +89,18 @@
     )
     grad = (product - sw.astype(jnp.float32) * scaled) / s_norm
     rows = grad.shape[0] // ndp
+    high = part_center.astype(jnp.bfloat16)
+    low = (part_center - high.astype(jnp.float32)).astype(jnp.bfloat16)
     sent = jnp.concatenate(
-        [grad.reshape(ndp, rows, cols), jnp.broadcast_to(part_center, (ndp, 1, cols))], axis=1
+        [
+            grad.astype(jnp.bfloat16).reshape(ndp, rows, cols),
+            jnp.broadcast_to(jnp.stack([high, low]), (ndp, 2, cols)),
+        ],
+        axis=1,
     )
     got = lax.all_to_all(sent, "dp", 0, 2, tiled=True)
-    got = got.reshape(rows + 1, ndp * cols)
-    return (master_new, got[:rows], got[rows])
+    got = got.reshape(rows + 2, ndp * cols).astype(jnp.float32)
+    return (master_new, got[:rows], got[rows] + got[rows + 1])
 
 
 def solution(mesh):

time: 88.6 us -> 84.9 us (0.958)
  waiting for transfers between devices: 23.1 us -> 16.7 us
  starting transfers between devices: 12.6 us -> 18.8 us
  blocking collectives: 13.7 us -> 10 us
    ppermute x5 -> x10, waiting for transfers between devices: 9.25 us -> 2.93 us  [exchange_all(): total = total + lax.ppermute(x, axis, [(i, (i + k) % n) for i in range(n)])]
    ppermute x5 -> x10, starting transfers between devices: 7.35 us -> 13.6 us  [exchange_all(): total = total + lax.ppermute(x, axis, [(i, (i + k) % n) for i in range(n)])]
    all_to_all x1, blocking collectives: 13.7 us -> 10 us  [feature_plan(): got = lax.all_to_all(sent, 'dp', 0, 2, tiled=True)]
  transfers between devices with their start and end apart: 7 -> 12, of which waited for: 7 -> 6; matrix products, arithmetic and copies ran while one was open for 14% -> 15% of each run, Pallas kernels for 0% -> 0%
where the time goes in v5:
time: 84.9 us; the launch traced here: 84.5 us
  starting transfers between devices  18.8 us (22%)
  waiting for transfers between devices  16.7 us (20%)
  between operations  14.2 us (17%)
  other arithmetic  11 us (13%)
  blocking collectives  10 us (12%)
  local copies, waits for them, and re-layouts  9.56 us (11%)
  matrix products  4.27 us (5%)
    ppermute x10, starting transfers between devices, exchange_all(): total = total + lax.ppermute(x, axis, [(i, (i + k) % n) for i in range(n)])  13.6 us
    all_to_all x1, blocking collectives, feature_plan(): got = lax.all_to_all(sent, 'dp', 0, 2, tiled=True)  10 us
    all_to_all x1, waiting for transfers between devices, feature_plan(): both = lax.all_to_all(both, 'dp', 2, 1, tiled=True)  8.99 us
    all_to_all x1, starting transfers between devices, feature_plan(): both = lax.all_to_all(both, 'dp', 2, 1, tiled=True)  5.17 us
    all_gather x1, waiting for transfers between devices, feature_plan(): feats = lax.all_gather(feats, 'dp', axis=0, tiled=True)  4.76 us
    unnamed x6, local copies, waits for them, and re-layouts  4.63 us
    another operation x2, other arithmetic, feature_plan(): both = jnp.stack([student_weight, master_new.astype(jnp.bfloat16)])  3 us
    ppermute x10, waiting for transfers between devices, exchange_all(): total = total + lax.ppermute(x, axis, [(i, (i + k) % n) for i in range(n)])  2.93 us
  transfers between devices with their start and end apart: 12, of which 6 were waited for; matrix products, arithmetic and copies ran while one was open for 15% of the time, Pallas kernels for 0%

profile of v5, /device:TPU:0, one launch (start us, length us, event | category | flops | bytes accessed | tf_op | source)
XLA Modules:
  0.0 84.5 jit_solution(8413575921019581863)
XLA Ops:
  7.2 1.0 %fusion.9 = f32[256]{0:T(256)S(1)} fusion(bf16[256,256]{1,0:T(8,128)(2,1)} %param.8), kind=kLoop, calls=%fused_computation.26 | loop fusion | flops 196352 | bytes 132096 | tf_op jit(solution)/shard_map/reduce_sum | solution.py:9
  8.2 1.0 %fusion.7 = f32[256]{0:T(256)S(1)} fusion(bf16[256,256]{1,0:T(8,128)(2,1)} %param.7), kind=kLoop, calls=%fused_computation.24 | loop fusion | flops 196352 | bytes 132096 | tf_op jit(solution)/shard_map/reduce_sum | solution.py:9
  9.3 1.1 %fusion.8 = (bf16[256,256]{1,0:T(8,128)(2,1)S(1)}, bf16[256,256]{1,0:T(8,128)(2,1)S(1)}) fusion(bf16[256,256]{1,0:T(8,128)(2,1)} %param.7, f32[256]{0:T(256)S(1)} %add_rsqrt_fusion.1, f32[256]{0:T(256)S(1)} %add_rsqrt_fusion, bf16[256,256]{1,0:T(8,128)(2,1)} %param.8), kind=kLoop, calls=%fused_computation.25 | loop fusion | flops 393216 | bytes 526336 | tf_op jit(solution)/shard_map/convert_element_type | solution.py:9
  10.4 0.7 pad_maximum_fusion.2
  11.2 2.0 %convert_bitcast_fusion.1 = (bf16[1,32,4096]{2,1,0:T(8,128)(2,1)S(1)}, f32[32,4096]{1,0:T(8,128)}) fusion(bf16[32,4096]{1,0:T(8,128)(2,1)} %param.6, f32[32,4096]{1,0:T(8,128)} %param.5), kind=kLoop, calls=%fused_computation.29 | loop fusion | flops 655360 | bytes 1572864 | tf_op jit(solution)/shard_map/stack | solution.py:68
  13.2 1.0 %pad_maximum_fusion = bf16[2,32,4096]{2,1,0:T(8,128)(2,1)S(1)} fusion(bf16[1,32,4096]{2,1,0:T(8,128)(2,1)S(1)} %get-tuple-element.12, bf16[1,32,4096]{2,1,0:T(8,128)(2,1)} %bitcast.32), kind=kLoop, calls=%fused_computation.15 | loop fusion | flops 262144 | bytes 1048576 | tf_op jit(solution)/shard_map/stack | solution.py:68
  14.2 2.8 %copy.16 = bf16[2,32,4096]{1,0,2:T(2,128)(2,1)S(1)} copy(bf16[2,32,4096]{2,1,0:T(8,128)(2,1)S(1)} %pad_maximum_fusion) | data formatting | bytes 1048576 | tf_op jit(solution)/shard_map/stack | solution.py:68
  16.9 2.7 %reshape.55 = bf16[8,2,16384]{2,1,0:T(2,128)(2,1)} reshape(bf16[4096,2,32]{2,1,0:T(2,128)(2,1)S(1)} %bitcast.28) | data formatting | bytes 1048576
  19.7 5.2 %all-to-all-start = ((bf16[8,2,16384]{2,1,0:T(2,128)(2,1)}), bf16[8,2,16384]{2,1,0:T(2,128)(2,1)S(1)}, u32[]{:S(2)}, u32[]{:S(2)}) async-start(bf16[8,2,16384]{2,1,0:T(2,128)(2,1)} %reshape.55), calls=%async_computation | async-start | bytes 1048576 | tf_op jit(solution)/shard_map/all_to_all | solution.py:69
  24.8 0.8 dynamic_slice.3
  25.6 9.0 %all-to-all-done = bf16[8,2,16384]{2,1,0:T(2,128)(2,1)S(1)} async-done(((bf16[8,2,16384]{2,1,0:T(2,128)(2,1)}), bf16[8,2,16384]{2,1,0:T(2,128)(2,1)S(1)}, u32[]{:S(2)}, u32[]{:S(2)}) %all-to-all-start) | async-done | bytes 524320 | tf_op jit(solution)/shard_map/all_to_all | solution.py:69
  34.6 1.0 %reshape.56 = bf16[4096,2,32]{2,1,0:T(2,128)(2,1)S(1)} reshape(bf16[8,2,16384]{2,1,0:T(2,128)(2,1)S(1)} %all-to-all-done) | data formatting | bytes 1048576
  35.6 1.3 %copy.17 = bf16[2,32,8,512]{3,1,2,0:T(8,128)(2,1)S(1)} copy(bf16[2,32,8,512]{1,0,3,2:T(2,128)(2,1)S(1)} %bitcast.29) | data formatting | bytes 1048576 | tf_op jit(solution)/shard_map/all_to_all | solution.py:69
  37.1 4.8 %all-gather.2.cloned.1.call-done = bf16[2048,512]{1,0:T(8,128)(2,1)} async-done(((bf16[256,512]{1,0:T(8,128)(2,1)}), bf16[2048,512]{1,0:T(8,128)(2,1)}) %all-gather.2.cloned.1.call-update) | async-done | bytes 2097168 | tf_op jit(solution)/shard_map/all_gather | solution.py:72
  41.9 2.3 %fusion = (f32[2048]{0:T(1024)S(1)}, f32[2048,512]{1,0:T(8,128)S(1)}) fusion(f32[512]{0:T(512)S(1)} %get-tuple-element.24, bf16[256,512]{1,0:T(8,128)(2,1)S(1)} %bitcast.35, bf16[2048,512]{1,0:T(8,128)(2,1)} %all-gather.2.cloned.1.call-done), kind=kOutput, calls=%fused_computation.4 | convolution fusion | flops 540014592 | bytes 5515264 | tf_op jit(solution)/shard_map/dot_general | solution.py:78
  44.2 1.2 %fusion.1 = (f32[2048]{0:T(1024)S(1)}, f32[512]{0:T(512)S(1)}, f32[2048,512]{1,0:T(8,128)S(1)}) fusion(f32[512]{0:T(512)S(1)} %dynamic_slice.3, f32[512]{0:T(512)S(1)} %get-tuple-element.23, bf16[256,512]{1,0:T(8,128)(2,1)S(1)} %bitcast.37, bf16[2048,512]{1,0:T(8,128)(2,1)S(1)} %copy-done), kind=kOutput, calls=%fused_computation.5 | convolution fusion | flops 542111232 | bytes 5519360 | tf_op jit(solution)/shard_map/dot_general | solution.py:77
  45.8 1.5 %collective-permute-start.1 = (f32[2,2048]{1,0:T(2,128)S(1)}, f32[2,2048]{1,0:T(2,128)S(1)}, u32[]{:S(2)}, u32[]{:S(2)}) collective-permute-start(f32[2,2048]{1,0:T(2,128)S(1)} %pad_maximum_fusion.3), channel_id=1, source_target_pairs={{0,8},{4,12},{8,16},{12,20},{16,24},{20,28},{24,0},{28,4},{1,9},{5... | collective-permute-start | bytes 49160 | tf_op jit(solution)/shard_map/ppermute | solution.py:58
  47.3 1.2 %collective-permute-start.2 = (f32[2,2048]{1,0:T(2,128)S(1)}, f32[2,2048]{1,0:T(2,128)S(1)}, u32[]{:S(2)}, u32[]{:S(2)}) collective-permute-start(f32[2,2048]{1,0:T(2,128)S(1)} %pad_maximum_fusion.3), channel_id=1, source_target_pairs={{0,12},{4,16},{8,20},{12,24},{16,28},{20,0},{24,4},{28,8},{1,13},{... | collective-permute-start | bytes 49160 | tf_op jit(solution)/shard_map/ppermute | solution.py:58
  48.5 1.5 %collective-permute-start.3 = (f32[2,2048]{1,0:T(2,128)S(1)}, f32[2,2048]{1,0:T(2,128)S(1)}, u32[]{:S(2)}, u32[]{:S(2)}) collective-permute-start(f32[2,2048]{1,0:T(2,128)S(1)} %pad_maximum_fusion.3), channel_id=1, source_target_pairs={{0,16},{4,20},{8,24},{12,28},{16,0},{20,4},{24,8},{28,12},{1,17},{... | collective-permute-start | bytes 49160 | tf_op jit(solution)/shard_map/ppermute | solution.py:58
  49.9 1.6 %collective-permute-start.5 = (f32[2,2048]{1,0:T(2,128)S(1)}, f32[2,2048]{1,0:T(2,128)S(1)}, u32[]{:S(2)}, u32[]{:S(2)}) collective-permute-start(f32[2,2048]{1,0:T(2,128)S(1)} %pad_maximum_fusion.3), channel_id=1, source_target_pairs={{0,24},{4,28},{8,0},{12,4},{16,8},{20,12},{24,16},{28,20},{1,25},{... | collective-permute-start | bytes 49160 | tf_op jit(solution)/shard_map/ppermute | solution.py:58
  51.5 2.1 %collective-permute-start.6 = (f32[2,2048]{1,0:T(2,128)S(1)}, f32[2,2048]{1,0:T(2,128)S(1)}, u32[]{:S(2)}, u32[]{:S(2)}) collective-permute-start(f32[2,2048]{1,0:T(2,128)S(1)} %pad_maximum_fusion.3), channel_id=1, source_target_pairs={{0,28},{4,0},{8,4},{12,8},{16,12},{20,16},{24,20},{28,24},{1,29},{... | collective-permute-start | bytes 49160 | tf_op jit(solution)/shard_map/ppermute | solution.py:58
  53.7 0.8 fusion.11
  54.5 0.6 collective-permute-done.6
  55.2 1.5 %collective-permute-start.7 = (f32[2,2048]{1,0:T(2,128)S(1)}, f32[2,2048]{1,0:T(2,128)S(1)}, u32[]{:S(2)}, u32[]{:S(2)}) collective-permute-start(f32[2,2048]{1,0:T(2,128)S(1)} %add_add_fusion.1), channel_id=1, source_target_pairs={{0,1},{1,2},{2,3},{3,0},{4,5},{5,6},{6,7},{7,4},{8,9},{9,10},{10,1... | collective-permute-start | bytes 49160 | tf_op jit(solution)/shard_map/ppermute | solution.py:58
  56.7 2.4 %collective-permute-start.8 = (f32[2,2048]{1,0:T(2,128)S(1)}, f32[2,2048]{1,0:T(2,128)S(1)}, u32[]{:S(2)}, u32[]{:S(2)}) collective-permute-start(f32[2,2048]{1,0:T(2,128)S(1)} %add_add_fusion.1), channel_id=1, source_target_pairs={{0,2},{1,3},{2,0},{3,1},{4,6},{5,7},{6,4},{7,5},{8,10},{9,11},{10,... | collective-permute-start | bytes 49160 | tf_op jit(solution)/shard_map/ppermute | solution.py:58
  59.1 1.4 %collective-permute-start.9 = (f32[2,2048]{1,0:T(2,128)S(1)}, f32[2,2048]{1,0:T(2,128)S(1)}, u32[]{:S(2)}, u32[]{:S(2)}) collective-permute-start(f32[2,2048]{1,0:T(2,128)S(1)} %add_add_fusion.1), channel_id=1, source_target_pairs={{0,3},{1,0},{2,1},{3,2},{4,7},{5,4},{6,5},{7,6},{8,11},{9,8},{10,9... | collective-permute-start | bytes 49160 | tf_op jit(solution)/shard_map/ppermute | solution.py:58
  61.4 1.5 %collective-permute-done.9 = f32[2,2048]{1,0:T(2,128)S(1)} collective-permute-done((f32[2,2048]{1,0:T(2,128)S(1)}, f32[2,2048]{1,0:T(2,128)S(1)}, u32[]{:S(2)}, u32[]{:S(2)}) %collective-permute-start.9) | collective-permute-done | bytes 16416 | tf_op jit(solution)/shard_map/ppermute | solution.py:58
  62.9 2.4 %multiply_reduce_fusion = (f32[512]{0:T(512)S(1)}, bf16[2048,512]{1,0:T(8,128)(2,1)S(1)}) fusion(f32[2048,512]{1,0:T(8,128)S(1)} %get-tuple-element.22, f32[2048]{0:T(1024)S(1)} %bitcast.39, f32[2048,512]{1,0:T(8,128)S(1)} %get-tuple-element.20, f32[512]{0:T(512)S(1)} %dynamic_slice.3, f32[2048]{0:T(1024)S(1)} %bitcast.38), kind=kLoop, calls=%fused_computation | loop fusion | flops 11533824 | bytes 10506240 | tf_op jit(solution)/shard_map/reduce_sum | solution.py:86
  65.3 0.7 fusion.3
  66.1 10.0 %all_to_all.24 = bf16[8,34,512]{2,1,0:T(8,128)(2,1)S(1)} all-to-all(bf16[8,34,512]{2,1,0:T(8,128)(2,1)S(1)} %pad_maximum_fusion.1), channel_id=1, replica_groups=mesh['dp'=8,'tensor'=4] {'dp'}, dimensions={0} | all-to-all | bytes 557056 | tf_op jit(solution)/shard_map/all_to_all | solution.py:101
  76.2 0.6 slice_add_fusion
  76.9 0.8 copy.19
  (31 shorter events, 1.6 us)
Async XLA Ops:
  7.2 34.7 %all-gather.2.cloned.1.call-start = ((), (), s32[]{:S(2)}) async-start(), calls=%async_computation.2 | async-start | bytes 2359296 | tf_op jit(solution)/shard_map/all_gather | solution.py:72
  19.7 14.9 %all-to-all-start = ((bf16[8,2,16384]{2,1,0:T(2,128)(2,1)}), bf16[8,2,16384]{2,1,0:T(2,128)(2,1)S(1)}, u32[]{:S(2)}, u32[]{:S(2)}) async-start(bf16[8,2,16384]{2,1,0:T(2,128)(2,1)} %reshape.55), calls=%async_computation | async-start | bytes 1048576 | tf_op jit(solution)/shard_map/all_to_all | solution.py:69
  41.9 2.3 %copy-start = (bf16[2048,512]{1,0:T(8,128)(2,1)S(1)}, bf16[2048,512]{1,0:T(8,128)(2,1)}, u32[]{:S(2)}) copy-start(bf16[2048,512]{1,0:T(8,128)(2,1)} %all-gather.2.cloned.1.call-done) | copy-start | bytes 6291460
  45.5 4.4 %collective-permute-start = (f32[2,2048]{1,0:T(2,128)S(1)}, f32[2,2048]{1,0:T(2,128)S(1)}, u32[]{:S(2)}, u32[]{:S(2)}) collective-permute-start(f32[2,2048]{1,0:T(2,128)S(1)} %pad_maximum_fusion.3), channel_id=1, source_target_pairs={{0,4},{4,8},{8,12},{12,16},{16,20},{20,24},{24,28},{28,0},{1,5},{5... | collective-permute-start | bytes 49160 | tf_op jit(solution)/shard_map/ppermute | solution.py:58
  45.8 5.8 %collective-permute-start.1 = (f32[2,2048]{1,0:T(2,128)S(1)}, f32[2,2048]{1,0:T(2,128)S(1)}, u32[]{:S(2)}, u32[]{:S(2)}) collective-permute-start(f32[2,2048]{1,0:T(2,128)S(1)} %pad_maximum_fusion.3), channel_id=1, source_target_pairs={{0,8},{4,12},{8,16},{12,20},{16,24},{20,28},{24,0},{28,4},{1,9},{5... | collective-permute-start | bytes 49160 | tf_op jit(solution)/shard_map/ppermute | solution.py:58
  47.3 7.2 %collective-permute-start.2 = (f32[2,2048]{1,0:T(2,128)S(1)}, f32[2,2048]{1,0:T(2,128)S(1)}, u32[]{:S(2)}, u32[]{:S(2)}) collective-permute-start(f32[2,2048]{1,0:T(2,128)S(1)} %pad_maximum_fusion.3), channel_id=1, source_target_pairs={{0,12},{4,16},{8,20},{12,24},{16,28},{20,0},{24,4},{28,8},{1,13},{... | collective-permute-start | bytes 49160 | tf_op jit(solution)/shard_map/ppermute | solution.py:58
  48.5 6.0 %collective-permute-start.3 = (f32[2,2048]{1,0:T(2,128)S(1)}, f32[2,2048]{1,0:T(2,128)S(1)}, u32[]{:S(2)}, u32[]{:S(2)}) collective-permute-start(f32[2,2048]{1,0:T(2,128)S(1)} %pad_maximum_fusion.3), channel_id=1, source_target_pairs={{0,16},{4,20},{8,24},{12,28},{16,0},{20,4},{24,8},{28,12},{1,17},{... | collective-permute-start | bytes 49160 | tf_op jit(solution)/shard_map/ppermute | solution.py:58
  49.9 4.6 %collective-permute-start.4 = (f32[2,2048]{1,0:T(2,128)S(1)}, f32[2,2048]{1,0:T(2,128)S(1)}, u32[]{:S(2)}, u32[]{:S(2)}) collective-permute-start(f32[2,2048]{1,0:T(2,128)S(1)} %pad_maximum_fusion.3), channel_id=1, source_target_pairs={{0,20},{4,24},{8,28},{12,0},{16,4},{20,8},{24,12},{28,16},{1,21},{... | collective-permute-start | bytes 49160 | tf_op jit(solution)/shard_map/ppermute | solution.py:58
  49.9 4.6 %collective-permute-start.5 = (f32[2,2048]{1,0:T(2,128)S(1)}, f32[2,2048]{1,0:T(2,128)S(1)}, u32[]{:S(2)}, u32[]{:S(2)}) collective-permute-start(f32[2,2048]{1,0:T(2,128)S(1)} %pad_maximum_fusion.3), channel_id=1, source_target_pairs={{0,24},{4,28},{8,0},{12,4},{16,8},{20,12},{24,16},{28,20},{1,25},{... | collective-permute-start | bytes 49160 | tf_op jit(solution)/shard_map/ppermute | solution.py:58
  51.5 3.6 %collective-permute-start.6 = (f32[2,2048]{1,0:T(2,128)S(1)}, f32[2,2048]{1,0:T(2,128)S(1)}, u32[]{:S(2)}, u32[]{:S(2)}) collective-permute-start(f32[2,2048]{1,0:T(2,128)S(1)} %pad_maximum_fusion.3), channel_id=1, source_target_pairs={{0,28},{4,0},{8,4},{12,8},{16,12},{20,16},{24,20},{28,24},{1,29},{... | collective-permute-start | bytes 49160 | tf_op jit(solution)/shard_map/ppermute | solution.py:58
  55.2 5.7 %collective-permute-start.7 = (f32[2,2048]{1,0:T(2,128)S(1)}, f32[2,2048]{1,0:T(2,128)S(1)}, u32[]{:S(2)}, u32[]{:S(2)}) collective-permute-start(f32[2,2048]{1,0:T(2,128)S(1)} %add_add_fusion.1), channel_id=1, source_target_pairs={{0,1},{1,2},{2,3},{3,0},{4,5},{5,6},{6,7},{7,4},{8,9},{9,10},{10,1... | collective-permute-start | bytes 49160 | tf_op jit(solution)/shard_map/ppermute | solution.py:58
  56.7 4.6 %collective-permute-start.8 = (f32[2,2048]{1,0:T(2,128)S(1)}, f32[2,2048]{1,0:T(2,128)S(1)}, u32[]{:S(2)}, u32[]{:S(2)}) collective-permute-start(f32[2,2048]{1,0:T(2,128)S(1)} %add_add_fusion.1), channel_id=1, source_target_pairs={{0,2},{1,3},{2,0},{3,1},{4,6},{5,7},{6,4},{7,5},{8,10},{9,11},{10,... | collective-permute-start | bytes 49160 | tf_op jit(solution)/shard_map/ppermute | solution.py:58
  59.1 3.7 %collective-permute-start.9 = (f32[2,2048]{1,0:T(2,128)S(1)}, f32[2,2048]{1,0:T(2,128)S(1)}, u32[]{:S(2)}, u32[]{:S(2)}) collective-permute-start(f32[2,2048]{1,0:T(2,128)S(1)} %add_add_fusion.1), channel_id=1, source_target_pairs={{0,3},{1,0},{2,1},{3,2},{4,7},{5,4},{6,5},{7,6},{8,11},{9,8},{10,9... | collective-permute-start | bytes 49160 | tf_op jit(solution)/shard_map/ppermute | solution.py:58
Sparse Core Ops, SparseCore 0:
  11.3 30.5 all-gather.1

commit v6 on v5

--- a/solution.py
+++ b/solution.py
@@ -79,7 +79,9 @@
     t_exp = jnp.exp((t_cos - c) / 0.04)
     s_exp = jnp.exp(s_cos / 0.1)
     totals = jnp.stack([jnp.sum(t_exp, 1), jnp.sum(s_exp, 1)])
-    totals = exchange_all(exchange_all(totals, "dp", ndp), "tensor", lax.axis_size("tensor"))
+    everyone = ndp * lax.axis_size("tensor")
+    totals = jnp.broadcast_to(totals[None], (everyone,) + totals.shape)
+    totals = jnp.sum(lax.all_to_all(totals, ("dp", "tensor"), 0, 0, tiled=True), 0)
     t_total, s_total = totals[0][:, None], totals[1][:, None]
     part_center = 0.5 * c + 0.5 * (jnp.sum(t_cos, 0) / images_all)
     dlog = ((s_exp / s_total - t_exp / t_total) / 0.1).astype(jnp.bfloat16)

time: 84.9 us -> 94.6 us (1.11)
  waiting for transfers between devices: 16.7 us -> 27.4 us
  starting transfers between devices: 18.8 us -> 9.81 us
  matrix products: 4.27 us -> 7.98 us
  other arithmetic: 11 us -> 13.2 us
  blocking collectives: 10 us -> 11 us
    ppermute x10 -> x0, starting transfers between devices: 13.6 us -> none  [exchange_all(): total = total + lax.ppermute(x, axis, [(i, (i + k) % n) for i in range(n)])]
    all_to_all x0 -> x1, waiting for transfers between devices: none -> 13.6 us  [feature_plan(): lax.all_to_all(totals, ('dp', 'tensor'), 0, 0, tiled=True)]
    all_to_all x0 -> x1, starting transfers between devices: none -> 4.6 us  [feature_plan(): lax.all_to_all(totals, ('dp', 'tensor'), 0, 0, tiled=True)]
    ppermute x10 -> x0, waiting for transfers between devices: 2.93 us -> none  [exchange_all(): total = total + lax.ppermute(x, axis, [(i, (i + k) % n) for i in range(n)])]
    reduce_sum x1, other arithmetic: 2.37 us -> 4.52 us  [feature_plan(): scaled = jnp.sum(dlog.astype(jnp.float32) * s_cos, 0) / s_norm]
    dot_general x1, matrix products: 1.21 us -> 3.09 us  [feature_plan(): t_cos = jnp.dot(zt, tw, preferred_element_type=jnp.float32) / t_norm]
    dot_general x1, matrix products: 2.32 us -> 4.14 us  [feature_plan(): s_cos = jnp.dot(zs, sw, preferred_element_type=jnp.float32) / s_norm]
    broadcast_in_dim x0 -> x1, local copies, waits for them, and re-layouts: none -> 1.03 us  [feature_plan(): totals = jnp.broadcast_to(totals[None], (everyone,) + totals.shape)]
  transfers between devices with their start and end apart: 12 -> 3, of which waited for: 6 -> 3; matrix products, arithmetic and copies ran while one was open for 15% -> 13% of each run, Pallas kernels for 0% -> 0%
where the time goes in v6:
time: 94.6 us; the launch traced here: 94.1 us
  waiting for transfers between devices  27.4 us (29%)
  between operations  14.2 us (15%)
  other arithmetic  13.2 us (14%)
  blocking collectives  11 us (12%)
  local copies, waits for them, and re-layouts  10.5 us (11%)
  starting transfers between devices  9.81 us (10%)
  matrix products  7.98 us (8%)
    all_to_all x1, waiting for transfers between devices, feature_plan(): lax.all_to_all(totals, ('dp', 'tensor'), 0, 0, tiled=True)  13.6 us
    all_to_all x1, blocking collectives, feature_plan(): got = lax.all_to_all(sent, 'dp', 0, 2, tiled=True)  11 us
    all_to_all x1, waiting for transfers between devices, feature_plan(): both = lax.all_to_all(both, 'dp', 2, 1, tiled=True)  8.99 us
    all_to_all x1, starting transfers between devices, feature_plan(): both = lax.all_to_all(both, 'dp', 2, 1, tiled=True)  5.17 us
    all_gather x1, waiting for transfers between devices, feature_plan(): feats = lax.all_gather(feats, 'dp', axis=0, tiled=True)  4.82 us
    all_to_all x1, starting transfers between devices, feature_plan(): lax.all_to_all(totals, ('dp', 'tensor'), 0, 0, tiled=True)  4.6 us
    unnamed x6, local copies, waits for them, and re-layouts  4.58 us
    reduce_sum x1, other arithmetic, feature_plan(): scaled = jnp.sum(dlog.astype(jnp.float32) * s_cos, 0) / s_norm  4.52 us
  transfers between devices with their start and end apart: 3, of which 3 were waited for; matrix products, arithmetic and copies ran while one was open for 13% of the time, Pallas kernels for 0%

profile of v6, /device:TPU:0, one launch (start us, length us, event | category | flops | bytes accessed | tf_op | source)
XLA Modules:
  0.0 94.1 jit_solution(12908241086278702082)
XLA Ops:
  7.2 0.0 all-gather.2.cloned.1.call-start
  7.2 1.0 %fusion.9 = f32[256]{0:T(256)S(1)} fusion(bf16[256,256]{1,0:T(8,128)(2,1)} %param.8), kind=kLoop, calls=%fused_computation.26 | loop fusion | flops 196352 | bytes 132096 | tf_op jit(solution)/shard_map/reduce_sum | solution.py:9
  8.2 1.0 %fusion.7 = f32[256]{0:T(256)S(1)} fusion(bf16[256,256]{1,0:T(8,128)(2,1)} %param.7), kind=kLoop, calls=%fused_computation.24 | loop fusion | flops 196352 | bytes 132096 | tf_op jit(solution)/shard_map/reduce_sum | solution.py:9
  9.3 1.1 %fusion.8 = (bf16[256,256]{1,0:T(8,128)(2,1)S(1)}, bf16[256,256]{1,0:T(8,128)(2,1)S(1)}) fusion(bf16[256,256]{1,0:T(8,128)(2,1)} %param.7, f32[256]{0:T(256)S(1)} %add_rsqrt_fusion.1, f32[256]{0:T(256)S(1)} %add_rsqrt_fusion, bf16[256,256]{1,0:T(8,128)(2,1)} %param.8), kind=kLoop, calls=%fused_computation.25 | loop fusion | flops 393216 | bytes 526336 | tf_op jit(solution)/shard_map/convert_element_type | solution.py:9
  10.4 0.7 pad_maximum_fusion.2
  11.1 0.0 all-gather.2.cloned.1.call-update
  11.1 2.0 %convert_bitcast_fusion.1 = (bf16[1,32,4096]{2,1,0:T(8,128)(2,1)S(1)}, f32[32,4096]{1,0:T(8,128)}) fusion(bf16[32,4096]{1,0:T(8,128)(2,1)} %param.6, f32[32,4096]{1,0:T(8,128)} %param.5), kind=kLoop, calls=%fused_computation.29 | loop fusion | flops 655360 | bytes 1572864 | tf_op jit(solution)/shard_map/stack | solution.py:68
  13.1 1.0 %pad_maximum_fusion = bf16[2,32,4096]{2,1,0:T(8,128)(2,1)S(1)} fusion(bf16[1,32,4096]{2,1,0:T(8,128)(2,1)S(1)} %get-tuple-element.12, bf16[1,32,4096]{2,1,0:T(8,128)(2,1)} %bitcast.32), kind=kLoop, calls=%fused_computation.15 | loop fusion | flops 262144 | bytes 1048576 | tf_op jit(solution)/shard_map/stack | solution.py:68
  14.1 2.8 %copy.22 = bf16[2,32,4096]{1,0,2:T(2,128)(2,1)S(1)} copy(bf16[2,32,4096]{2,1,0:T(8,128)(2,1)S(1)} %pad_maximum_fusion) | data formatting | bytes 1048576 | tf_op jit(solution)/shard_map/stack | solution.py:68
  16.9 2.7 %reshape.56 = bf16[8,2,16384]{2,1,0:T(2,128)(2,1)} reshape(bf16[4096,2,32]{2,1,0:T(2,128)(2,1)S(1)} %bitcast.28) | data formatting | bytes 1048576
  19.6 5.2 %all-to-all-start = ((bf16[8,2,16384]{2,1,0:T(2,128)(2,1)}), bf16[8,2,16384]{2,1,0:T(2,128)(2,1)S(1)}, u32[]{:S(2)}, u32[]{:S(2)}) async-start(bf16[8,2,16384]{2,1,0:T(2,128)(2,1)} %reshape.56), calls=%async_computation | async-start | bytes 1048576 | tf_op jit(solution)/shard_map/all_to_all | solution.py:69
  24.7 0.8 dynamic_slice.3
  25.5 9.0 %all-to-all-done = bf16[8,2,16384]{2,1,0:T(2,128)(2,1)S(1)} async-done(((bf16[8,2,16384]{2,1,0:T(2,128)(2,1)}), bf16[8,2,16384]{2,1,0:T(2,128)(2,1)S(1)}, u32[]{:S(2)}, u32[]{:S(2)}) %all-to-all-start) | async-done | bytes 524320 | tf_op jit(solution)/shard_map/all_to_all | solution.py:69
  34.5 1.0 %reshape.57 = bf16[4096,2,32]{2,1,0:T(2,128)(2,1)S(1)} reshape(bf16[8,2,16384]{2,1,0:T(2,128)(2,1)S(1)} %all-to-all-done) | data formatting | bytes 1048576
  35.5 1.3 %copy.23 = bf16[2,32,8,512]{3,1,2,0:T(8,128)(2,1)S(1)} copy(bf16[2,32,8,512]{1,0,3,2:T(2,128)(2,1)S(1)} %bitcast.29) | data formatting | bytes 1048576 | tf_op jit(solution)/shard_map/all_to_all | solution.py:69
  36.9 0.1 multiply_reduce_fusion.2
  37.1 4.8 %all-gather.2.cloned.1.call-done = bf16[2048,512]{1,0:T(8,128)(2,1)} async-done(((bf16[256,512]{1,0:T(8,128)(2,1)}), bf16[2048,512]{1,0:T(8,128)(2,1)}) %all-gather.2.cloned.1.call-update) | async-done | bytes 2097168 | tf_op jit(solution)/shard_map/all_gather | solution.py:72
  41.9 0.0 copy-start
  41.9 4.1 %fusion = (f32[2048]{0:T(1024)S(1)}, f32[2048,512]{1,0:T(8,128)}) fusion(f32[512]{0:T(512)S(1)} %get-tuple-element.24, bf16[256,512]{1,0:T(8,128)(2,1)S(1)} %bitcast.35, bf16[2048,512]{1,0:T(8,128)(2,1)} %all-gather.2.cloned.1.call-done), kind=kOutput, calls=%fused_computation.4 | convolution fusion | flops 540014592 | bytes 5515264 | tf_op jit(solution)/shard_map/dot_general | solution.py:78
  46.0 0.0 copy-done
  46.0 3.1 %fusion.1 = (f32[2048]{0:T(1024)S(1)}, f32[512]{0:T(512)S(1)}, f32[2048,512]{1,0:T(8,128)}) fusion(f32[512]{0:T(512)S(1)} %dynamic_slice.3, f32[512]{0:T(512)S(1)} %get-tuple-element.23, bf16[256,512]{1,0:T(8,128)(2,1)S(1)} %bitcast.37, bf16[2048,512]{1,0:T(8,128)(2,1)S(1)} %copy-done), kind=kOutput, calls=%fused_computation.5 | convolution fusion | flops 542111232 | bytes 5519360 | tf_op jit(solution)/shard_map/dot_general | solution.py:77
  49.1 1.0 %broadcast_in_dim.4 = f32[32,2,2048]{2,1,0:T(2,128)} broadcast(f32[2,2048]{1,0:T(2,128)S(1)} %pad_maximum_fusion.3), dimensions={1,2} | broadcast | bytes 540672 | tf_op jit(solution)/shard_map/broadcast_in_dim | solution.py:83
  50.2 4.6 %all-to-all-start.1 = ((f32[32,2,2048]{2,1,0:T(2,128)}), f32[32,2,2048]{2,1,0:T(2,128)S(1)}, u32[]{:S(2)}, u32[]{:S(2)}) async-start(f32[32,2,2048]{2,1,0:T(2,128)} %broadcast_in_dim.4), calls=%async_computation.1 | async-start | bytes 1048576 | tf_op jit(solution)/shard_map/all_to_all | solution.py:84
  54.8 0.8 fusion.11
  55.6 13.6 %all-to-all-done.1 = f32[32,2,2048]{2,1,0:T(2,128)S(1)} async-done(((f32[32,2,2048]{2,1,0:T(2,128)}), f32[32,2,2048]{2,1,0:T(2,128)S(1)}, u32[]{:S(2)}, u32[]{:S(2)}) %all-to-all-start.1) | async-done | bytes 524320 | tf_op jit(solution)/shard_map/all_to_all | solution.py:84
  69.1 0.2 reduce_sum.87
  69.3 4.5 %multiply_reduce_fusion = (f32[512]{0:T(512)S(1)}, bf16[2048,512]{1,0:T(8,128)(2,1)S(1)}) fusion(f32[2048,512]{1,0:T(8,128)} %get-tuple-element.22, f32[2048]{0:T(1024)S(1)} %bitcast.39, f32[2048,512]{1,0:T(8,128)} %get-tuple-element.20, f32[512]{0:T(512)S(1)} %dynamic_slice.3, f32[2048]{0:T(1024)S(1)} %bitcast.38), kind=kLoop, calls=%fused_computation | loop fusion | flops 11533824 | bytes 10506240 | tf_op jit(solution)/shard_map/reduce_sum | solution.py:88
  73.9 0.7 fusion.3
  74.7 11.0 %all_to_all.29 = bf16[8,34,512]{2,1,0:T(8,128)(2,1)S(1)} all-to-all(bf16[8,34,512]{2,1,0:T(8,128)(2,1)S(1)} %pad_maximum_fusion.1), channel_id=1, replica_groups=mesh['dp'=8,'tensor'=4] {'dp'}, dimensions={0} | all-to-all | bytes 557056 | tf_op jit(solution)/shard_map/all_to_all | solution.py:103
  85.7 0.1 convert_bitcast_fusion
  85.8 0.6 slice_add_fusion
  86.4 0.8 copy.29
  (13 shorter events, 0.2 us)
Async XLA Ops:
  7.2 34.7 %all-gather.2.cloned.1.call-start = ((), (), s32[]{:S(2)}) async-start(), calls=%async_computation.3 | async-start | bytes 2359296 | tf_op jit(solution)/shard_map/all_gather | solution.py:72
  19.6 14.9 %all-to-all-start = ((bf16[8,2,16384]{2,1,0:T(2,128)(2,1)}), bf16[8,2,16384]{2,1,0:T(2,128)(2,1)S(1)}, u32[]{:S(2)}, u32[]{:S(2)}) async-start(bf16[8,2,16384]{2,1,0:T(2,128)(2,1)} %reshape.56), calls=%async_computation | async-start | bytes 1048576 | tf_op jit(solution)/shard_map/all_to_all | solution.py:69
  41.9 4.1 %copy-start = (bf16[2048,512]{1,0:T(8,128)(2,1)S(1)}, bf16[2048,512]{1,0:T(8,128)(2,1)}, u32[]{:S(2)}) copy-start(bf16[2048,512]{1,0:T(8,128)(2,1)} %all-gather.2.cloned.1.call-done) | copy-start | bytes 6291460
  50.2 19.0 %all-to-all-start.1 = ((f32[32,2,2048]{2,1,0:T(2,128)}), f32[32,2,2048]{2,1,0:T(2,128)S(1)}, u32[]{:S(2)}, u32[]{:S(2)}) async-start(f32[32,2,2048]{2,1,0:T(2,128)} %broadcast_in_dim.4), calls=%async_computation.1 | async-start | bytes 1048576 | tf_op jit(solution)/shard_map/all_to_all | solution.py:84
Sparse Core Ops, SparseCore 0:
  11.2 30.5 all-gather.1

commit v7 on v5

--- a/solution.py
+++ b/solution.py
@@ -65,9 +65,12 @@
     images_all = teacher_feat.shape[0] * ndp
     cols = center.shape[0] // ndp
     master_new = 0.996 * teacher_master + 0.004 * student_weight.astype(jnp.float32)
+    rows = teacher_master.shape[0]
     both = jnp.stack([student_weight, master_new.astype(jnp.bfloat16)])
-    both = lax.all_to_all(both, "dp", 2, 1, tiled=True)
-    sw, tw = both[0], both[1]
+    both = both.reshape(2, rows, ndp, cols).transpose(2, 0, 1, 3).reshape(ndp, 2 * rows, cols)
+    both = lax.all_to_all(both, "dp", 0, 0, tiled=True)
+    sw = both[:, :rows].reshape(ndp * rows, cols)
+    tw = both[:, rows:].reshape(ndp * rows, cols)
     feats = jnp.concatenate([unit_rows(teacher_feat), unit_rows(student_feat)], axis=1)
     feats = lax.all_gather(feats, "dp", axis=0, tiled=True)
     zt, zs = feats[:, :bot], feats[:, bot:]
@@ -88,7 +91,6 @@
         zs, dlog, (((0,), (0,)), ((), ())), preferred_element_type=jnp.float32
     )
     grad = (product - sw.astype(jnp.float32) * scaled) / s_norm
-    rows = grad.shape[0] // ndp
     high = part_center.astype(jnp.bfloat16)
     low = (part_center - high.astype(jnp.float32)).astype(jnp.bfloat16)
     sent = jnp.concatenate(

time: 84.9 us -> 90.3 us (1.064)
  waiting for transfers between devices: 16.7 us -> 28.8 us
  local copies, waits for them, and re-layouts: 9.56 us -> 3.78 us
  other arithmetic: 11 us -> 10 us
    all_gather x1, waiting for transfers between devices: 4.76 us -> 14 us  [feature_plan(): feats = lax.all_gather(feats, 'dp', axis=0, tiled=True)]
    another operation x2 -> x0, other arithmetic: 3 us -> none  [feature_plan(): both = jnp.stack([student_weight, master_new.astype(jnp.bfloat16)])]
    all_to_all x1, waiting for transfers between devices: 8.99 us -> 11.8 us  [feature_plan(): both = lax.all_to_all(both, 'dp', 0, 0, tiled=True)]
    another operation x1 -> x0, local copies, waits for them, and re-layouts: 2.77 us -> none  [feature_plan(): both = jnp.stack([student_weight, master_new.astype(jnp.bfloat16)])]
    unnamed x6, local copies, waits for them, and re-layouts: 4.63 us -> 1.99 us
    convert_element_type x0 -> x1, other arithmetic: none -> 2 us  [feature_plan(): both = jnp.stack([student_weight, master_new.astype(jnp.bfloat16)])]
    all_to_all x1 -> x0, local copies, waits for them, and re-layouts: 1.32 us -> none  [feature_plan(): both = lax.all_to_all(both, 'dp', 2, 1, tiled=True)]
    transpose x0 -> x1, local copies, waits for them, and re-layouts: none -> 0.95 us  [feature_plan(): both.reshape(2, rows, ndp, cols).transpose(2, 0, 1, 3)]
  transfers between devices with their start and end apart: 12 -> 12, of which waited for: 6 -> 6; matrix products, arithmetic and copies ran while one was open for 15% -> 6% of each run, Pallas kernels for 0% -> 0%
where the time goes in v7:
time: 90.3 us; the launch traced here: 89.9 us
  waiting for transfers between devices  28.8 us (32%)
  starting transfers between devices  18.8 us (21%)
  between operations  14.2 us (16%)
  other arithmetic  10 us (11%)
  blocking collectives  10 us (11%)
  matrix products  4.28 us (5%)
  local copies, waits for them, and re-layouts  3.78 us (4%)
    all_gather x1, waiting for transfers between devices, feature_plan(): feats = lax.all_gather(feats, 'dp', axis=0, tiled=True)  14 us
    ppermute x10, starting transfers between devices, exchange_all(): total = total + lax.ppermute(x, axis, [(i, (i + k) % n) for i in range(n)])  13.6 us
    all_to_all x1, waiting for transfers between devices, feature_plan(): both = lax.all_to_all(both, 'dp', 0, 0, tiled=True)  11.8 us
    all_to_all x1, blocking collectives, feature_plan(): got = lax.all_to_all(sent, 'dp', 0, 2, tiled=True)  10 us
    all_to_all x1, starting transfers between devices, feature_plan(): both = lax.all_to_all(both, 'dp', 0, 0, tiled=True)  5.17 us
    ppermute x10, waiting for transfers between devices, exchange_all(): total = total + lax.ppermute(x, axis, [(i, (i + k) % n) for i in range(n)])  2.94 us
    reduce_sum x1, other arithmetic, feature_plan(): scaled = jnp.sum(dlog.astype(jnp.float32) * s_cos, 0) / s_norm  2.36 us
    dot_general x1, matrix products, feature_plan(): s_cos = jnp.dot(zs, sw, preferred_element_type=jnp.float32) / s_norm  2.32 us
  transfers between devices with their start and end apart: 12, of which 6 were waited for; matrix products, arithmetic and copies ran while one was open for 6% of the time, Pallas kernels for 0%

profile of v7, /device:TPU:0, one launch (start us, length us, event | category | flops | bytes accessed | tf_op | source)
XLA Modules:
  0.0 89.9 jit_solution(3417104444621411995)
XLA Ops:
  7.2 1.0 %fusion.9 = f32[256]{0:T(256)S(1)} fusion(bf16[256,256]{1,0:T(8,128)(2,1)} %param.8), kind=kLoop, calls=%fused_computation.26 | loop fusion | flops 196352 | bytes 132096 | tf_op jit(solution)/shard_map/reduce_sum | solution.py:9
  8.2 1.0 %fusion.7 = f32[256]{0:T(256)S(1)} fusion(bf16[256,256]{1,0:T(8,128)(2,1)} %param.7), kind=kLoop, calls=%fused_computation.24 | loop fusion | flops 196352 | bytes 132096 | tf_op jit(solution)/shard_map/reduce_sum | solution.py:9
  9.3 1.1 %fusion.8 = (bf16[256,256]{1,0:T(8,128)(2,1)S(1)}, bf16[256,256]{1,0:T(8,128)(2,1)S(1)}) fusion(bf16[256,256]{1,0:T(8,128)(2,1)} %param.7, f32[256]{0:T(256)S(1)} %add_rsqrt_fusion.1, f32[256]{0:T(256)S(1)} %add_rsqrt_fusion, bf16[256,256]{1,0:T(8,128)(2,1)} %param.8), kind=kLoop, calls=%fused_computation.25 | loop fusion | flops 393216 | bytes 526336 | tf_op jit(solution)/shard_map/convert_element_type | solution.py:9
  10.4 0.7 pad_maximum_fusion.1
  11.2 2.0 %fusion.12 = (bf16[32,4096]{1,0:T(8,128)(2,1)S(1)}, f32[32,4096]{1,0:T(8,128)}) fusion(bf16[32,4096]{1,0:T(8,128)(2,1)} %param.6, f32[32,4096]{1,0:T(8,128)} %param.5), kind=kLoop, calls=%fused_computation.42 | loop fusion | flops 655360 | bytes 1572864 | tf_op jit(solution)/shard_map/convert_element_type | solution.py:69
  13.2 1.0 %copy.10 = bf16[4,8,8,512]{3,2,1,0:T(8,128)(2,1)S(1)} copy(bf16[4,8,8,512]{3,1,2,0:T(8,128)(2,1)} %bitcast.30) | data formatting | bytes 524288
  14.3 0.9 %copy.8 = bf16[8,2,32,512]{3,2,1,0:T(8,128)(2,1)} copy(bf16[8,2,32,512]{3,0,2,1:T(8,128)(2,1)S(1)} %maximum_bitcast_fusion) | data formatting | bytes 1048576 | tf_op jit(solution)/shard_map/transpose | solution.py:70
  15.3 5.2 %all-to-all-start = ((bf16[8,64,512]{2,1,0:T(8,128)(2,1)}), bf16[8,64,512]{2,1,0:T(8,128)(2,1)S(1)}, u32[]{:S(2)}, u32[]{:S(2)}) async-start(bf16[8,64,512]{2,1,0:T(8,128)(2,1)} %bitcast.1), calls=%async_computation | async-start | bytes 1048576 | tf_op jit(solution)/shard_map/all_to_all | solution.py:71
  20.5 0.8 dynamic_slice.3
  21.2 11.8 %all-to-all-done = bf16[8,64,512]{2,1,0:T(8,128)(2,1)S(1)} async-done(((bf16[8,64,512]{2,1,0:T(8,128)(2,1)}), bf16[8,64,512]{2,1,0:T(8,128)(2,1)S(1)}, u32[]{:S(2)}, u32[]{:S(2)}) %all-to-all-start) | async-done | bytes 524320 | tf_op jit(solution)/shard_map/all_to_all | solution.py:71
  33.2 14.0 %all-gather.2.cloned.1.call-done = bf16[2048,512]{1,0:T(8,128)(2,1)} async-done(((bf16[256,512]{1,0:T(8,128)(2,1)}), bf16[2048,512]{1,0:T(8,128)(2,1)}) %all-gather.2.cloned.1.call-update) | async-done | bytes 2097168 | tf_op jit(solution)/shard_map/all_gather | solution.py:75
  47.3 2.3 %fusion = (f32[2048]{0:T(1024)S(1)}, f32[2048,512]{1,0:T(8,128)S(1)}) fusion(f32[512]{0:T(512)S(1)} %get-tuple-element.21, bf16[256,512]{1,0:T(8,128)(2,1)S(1)} %bitcast.36, bf16[2048,512]{1,0:T(8,128)(2,1)} %all-gather.2.cloned.1.call-done), kind=kOutput, calls=%fused_computation.4 | convolution fusion | flops 540014592 | bytes 5515264 | tf_op jit(solution)/shard_map/dot_general | solution.py:81
  49.6 1.2 %fusion.1 = (f32[2048]{0:T(1024)S(1)}, f32[512]{0:T(512)S(1)}, f32[2048,512]{1,0:T(8,128)S(1)}) fusion(f32[512]{0:T(512)S(1)} %dynamic_slice.3, f32[512]{0:T(512)S(1)} %get-tuple-element.20, bf16[256,512]{1,0:T(8,128)(2,1)S(1)} %bitcast.38, bf16[2048,512]{1,0:T(8,128)(2,1)S(1)} %copy-done), kind=kOutput, calls=%fused_computation.5 | convolution fusion | flops 542111232 | bytes 5519360 | tf_op jit(solution)/shard_map/dot_general | solution.py:80
  50.8 0.3 collective-permute-start
  51.2 1.5 %collective-permute-start.1 = (f32[2,2048]{1,0:T(2,128)S(1)}, f32[2,2048]{1,0:T(2,128)S(1)}, u32[]{:S(2)}, u32[]{:S(2)}) collective-permute-start(f32[2,2048]{1,0:T(2,128)S(1)} %pad_maximum_fusion.2), channel_id=1, source_target_pairs={{0,8},{4,12},{8,16},{12,20},{16,24},{20,28},{24,0},{28,4},{1,9},{5... | collective-permute-start | bytes 49160 | tf_op jit(solution)/shard_map/ppermute | solution.py:58
  52.6 1.2 %collective-permute-start.2 = (f32[2,2048]{1,0:T(2,128)S(1)}, f32[2,2048]{1,0:T(2,128)S(1)}, u32[]{:S(2)}, u32[]{:S(2)}) collective-permute-start(f32[2,2048]{1,0:T(2,128)S(1)} %pad_maximum_fusion.2), channel_id=1, source_target_pairs={{0,12},{4,16},{8,20},{12,24},{16,28},{20,0},{24,4},{28,8},{1,13},{... | collective-permute-start | bytes 49160 | tf_op jit(solution)/shard_map/ppermute | solution.py:58
  53.8 1.5 %collective-permute-start.3 = (f32[2,2048]{1,0:T(2,128)S(1)}, f32[2,2048]{1,0:T(2,128)S(1)}, u32[]{:S(2)}, u32[]{:S(2)}) collective-permute-start(f32[2,2048]{1,0:T(2,128)S(1)} %pad_maximum_fusion.2), channel_id=1, source_target_pairs={{0,16},{4,20},{8,24},{12,28},{16,0},{20,4},{24,8},{28,12},{1,17},{... | collective-permute-start | bytes 49160 | tf_op jit(solution)/shard_map/ppermute | solution.py:58
  55.3 1.6 %collective-permute-start.5 = (f32[2,2048]{1,0:T(2,128)S(1)}, f32[2,2048]{1,0:T(2,128)S(1)}, u32[]{:S(2)}, u32[]{:S(2)}) collective-permute-start(f32[2,2048]{1,0:T(2,128)S(1)} %pad_maximum_fusion.2), channel_id=1, source_target_pairs={{0,24},{4,28},{8,0},{12,4},{16,8},{20,12},{24,16},{28,20},{1,25},{... | collective-permute-start | bytes 49160 | tf_op jit(solution)/shard_map/ppermute | solution.py:58
  56.9 2.1 %collective-permute-start.6 = (f32[2,2048]{1,0:T(2,128)S(1)}, f32[2,2048]{1,0:T(2,128)S(1)}, u32[]{:S(2)}, u32[]{:S(2)}) collective-permute-start(f32[2,2048]{1,0:T(2,128)S(1)} %pad_maximum_fusion.2), channel_id=1, source_target_pairs={{0,28},{4,0},{8,4},{12,8},{16,12},{20,16},{24,20},{28,24},{1,29},{... | collective-permute-start | bytes 49160 | tf_op jit(solution)/shard_map/ppermute | solution.py:58
  59.1 0.8 fusion.11
  59.9 0.6 collective-permute-done.6
  60.5 1.5 %collective-permute-start.7 = (f32[2,2048]{1,0:T(2,128)S(1)}, f32[2,2048]{1,0:T(2,128)S(1)}, u32[]{:S(2)}, u32[]{:S(2)}) collective-permute-start(f32[2,2048]{1,0:T(2,128)S(1)} %add_add_fusion.1), channel_id=1, source_target_pairs={{0,1},{1,2},{2,3},{3,0},{4,5},{5,6},{6,7},{7,4},{8,9},{9,10},{10,1... | collective-permute-start | bytes 49160 | tf_op jit(solution)/shard_map/ppermute | solution.py:58
  62.1 2.4 %collective-permute-start.8 = (f32[2,2048]{1,0:T(2,128)S(1)}, f32[2,2048]{1,0:T(2,128)S(1)}, u32[]{:S(2)}, u32[]{:S(2)}) collective-permute-start(f32[2,2048]{1,0:T(2,128)S(1)} %add_add_fusion.1), channel_id=1, source_target_pairs={{0,2},{1,3},{2,0},{3,1},{4,6},{5,7},{6,4},{7,5},{8,10},{9,11},{10,... | collective-permute-start | bytes 49160 | tf_op jit(solution)/shard_map/ppermute | solution.py:58
  64.5 1.4 %collective-permute-start.9 = (f32[2,2048]{1,0:T(2,128)S(1)}, f32[2,2048]{1,0:T(2,128)S(1)}, u32[]{:S(2)}, u32[]{:S(2)}) collective-permute-start(f32[2,2048]{1,0:T(2,128)S(1)} %add_add_fusion.1), channel_id=1, source_target_pairs={{0,3},{1,0},{2,1},{3,2},{4,7},{5,4},{6,5},{7,6},{8,11},{9,8},{10,9... | collective-permute-start | bytes 49160 | tf_op jit(solution)/shard_map/ppermute | solution.py:58
  65.9 0.3 collective-permute-done.7
  66.2 0.5 collective-permute-done.8
  66.7 1.5 %collective-permute-done.9 = f32[2,2048]{1,0:T(2,128)S(1)} collective-permute-done((f32[2,2048]{1,0:T(2,128)S(1)}, f32[2,2048]{1,0:T(2,128)S(1)}, u32[]{:S(2)}, u32[]{:S(2)}) %collective-permute-start.9) | collective-permute-done | bytes 16416 | tf_op jit(solution)/shard_map/ppermute | solution.py:58
  68.3 2.4 %multiply_reduce_fusion = (f32[512]{0:T(512)S(1)}, bf16[2048,512]{1,0:T(8,128)(2,1)S(1)}) fusion(f32[2048,512]{1,0:T(8,128)S(1)} %get-tuple-element.19, f32[2048]{0:T(1024)S(1)} %bitcast.40, f32[2048,512]{1,0:T(8,128)S(1)} %get-tuple-element.17, f32[512]{0:T(512)S(1)} %dynamic_slice.3, f32[2048]{0:T(1024)S(1)} %bitcast.39), kind=kLoop, calls=%fused_computation | loop fusion | flops 11533824 | bytes 10506240 | tf_op jit(solution)/shard_map/reduce_sum | solution.py:89
  70.7 0.7 fusion.3
  71.5 10.0 %all_to_all.14 = bf16[8,34,512]{2,1,0:T(8,128)(2,1)S(1)} all-to-all(bf16[8,34,512]{2,1,0:T(8,128)(2,1)S(1)} %pad_maximum_fusion), channel_id=1, replica_groups=mesh['dp'=8,'tensor'=4] {'dp'}, dimensions={0} | all-to-all | bytes 557056 | tf_op jit(solution)/shard_map/all_to_all | solution.py:103
  81.6 0.6 slice_add_fusion
  82.2 0.8 copy.12
  (30 shorter events, 0.7 us)
Async XLA Ops:
  7.2 40.1 %all-gather.2.cloned.1.call-start = ((), (), s32[]{:S(2)}) async-start(), calls=%async_computation.2 | async-start | bytes 2359296 | tf_op jit(solution)/shard_map/all_gather | solution.py:75
  15.3 17.7 %all-to-all-start = ((bf16[8,64,512]{2,1,0:T(8,128)(2,1)}), bf16[8,64,512]{2,1,0:T(8,128)(2,1)S(1)}, u32[]{:S(2)}, u32[]{:S(2)}) async-start(bf16[8,64,512]{2,1,0:T(8,128)(2,1)} %bitcast.1), calls=%async_computation | async-start | bytes 1048576 | tf_op jit(solution)/shard_map/all_to_all | solution.py:71
  47.2 2.3 %copy-start = (bf16[2048,512]{1,0:T(8,128)(2,1)S(1)}, bf16[2048,512]{1,0:T(8,128)(2,1)}, u32[]{:S(2)}) copy-start(bf16[2048,512]{1,0:T(8,128)(2,1)} %all-gather.2.cloned.1.call-done) | copy-start | bytes 6291460
  50.8 4.4 %collective-permute-start = (f32[2,2048]{1,0:T(2,128)S(1)}, f32[2,2048]{1,0:T(2,128)S(1)}, u32[]{:S(2)}, u32[]{:S(2)}) collective-permute-start(f32[2,2048]{1,0:T(2,128)S(1)} %pad_maximum_fusion.2), channel_id=1, source_target_pairs={{0,4},{4,8},{8,12},{12,16},{16,20},{20,24},{24,28},{28,0},{1,5},{5... | collective-permute-start | bytes 49160 | tf_op jit(solution)/shard_map/ppermute | solution.py:58
  51.2 5.8 %collective-permute-start.1 = (f32[2,2048]{1,0:T(2,128)S(1)}, f32[2,2048]{1,0:T(2,128)S(1)}, u32[]{:S(2)}, u32[]{:S(2)}) collective-permute-start(f32[2,2048]{1,0:T(2,128)S(1)} %pad_maximum_fusion.2), channel_id=1, source_target_pairs={{0,8},{4,12},{8,16},{12,20},{16,24},{20,28},{24,0},{28,4},{1,9},{5... | collective-permute-start | bytes 49160 | tf_op jit(solution)/shard_map/ppermute | solution.py:58
  52.6 7.2 %collective-permute-start.2 = (f32[2,2048]{1,0:T(2,128)S(1)}, f32[2,2048]{1,0:T(2,128)S(1)}, u32[]{:S(2)}, u32[]{:S(2)}) collective-permute-start(f32[2,2048]{1,0:T(2,128)S(1)} %pad_maximum_fusion.2), channel_id=1, source_target_pairs={{0,12},{4,16},{8,20},{12,24},{16,28},{20,0},{24,4},{28,8},{1,13},{... | collective-permute-start | bytes 49160 | tf_op jit(solution)/shard_map/ppermute | solution.py:58
  53.8 6.0 %collective-permute-start.3 = (f32[2,2048]{1,0:T(2,128)S(1)}, f32[2,2048]{1,0:T(2,128)S(1)}, u32[]{:S(2)}, u32[]{:S(2)}) collective-permute-start(f32[2,2048]{1,0:T(2,128)S(1)} %pad_maximum_fusion.2), channel_id=1, source_target_pairs={{0,16},{4,20},{8,24},{12,28},{16,0},{20,4},{24,8},{28,12},{1,17},{... | collective-permute-start | bytes 49160 | tf_op jit(solution)/shard_map/ppermute | solution.py:58
  55.3 4.6 %collective-permute-start.4 = (f32[2,2048]{1,0:T(2,128)S(1)}, f32[2,2048]{1,0:T(2,128)S(1)}, u32[]{:S(2)}, u32[]{:S(2)}) collective-permute-start(f32[2,2048]{1,0:T(2,128)S(1)} %pad_maximum_fusion.2), channel_id=1, source_target_pairs={{0,20},{4,24},{8,28},{12,0},{16,4},{20,8},{24,12},{28,16},{1,21},{... | collective-permute-start | bytes 49160 | tf_op jit(solution)/shard_map/ppermute | solution.py:58
  55.3 4.6 %collective-permute-start.5 = (f32[2,2048]{1,0:T(2,128)S(1)}, f32[2,2048]{1,0:T(2,128)S(1)}, u32[]{:S(2)}, u32[]{:S(2)}) collective-permute-start(f32[2,2048]{1,0:T(2,128)S(1)} %pad_maximum_fusion.2), channel_id=1, source_target_pairs={{0,24},{4,28},{8,0},{12,4},{16,8},{20,12},{24,16},{28,20},{1,25},{... | collective-permute-start | bytes 49160 | tf_op jit(solution)/shard_map/ppermute | solution.py:58
  56.9 3.6 %collective-permute-start.6 = (f32[2,2048]{1,0:T(2,128)S(1)}, f32[2,2048]{1,0:T(2,128)S(1)}, u32[]{:S(2)}, u32[]{:S(2)}) collective-permute-start(f32[2,2048]{1,0:T(2,128)S(1)} %pad_maximum_fusion.2), channel_id=1, source_target_pairs={{0,28},{4,0},{8,4},{12,8},{16,12},{20,16},{24,20},{28,24},{1,29},{... | collective-permute-start | bytes 49160 | tf_op jit(solution)/shard_map/ppermute | solution.py:58
  60.5 5.7 %collective-permute-start.7 = (f32[2,2048]{1,0:T(2,128)S(1)}, f32[2,2048]{1,0:T(2,128)S(1)}, u32[]{:S(2)}, u32[]{:S(2)}) collective-permute-start(f32[2,2048]{1,0:T(2,128)S(1)} %add_add_fusion.1), channel_id=1, source_target_pairs={{0,1},{1,2},{2,3},{3,0},{4,5},{5,6},{6,7},{7,4},{8,9},{9,10},{10,1... | collective-permute-start | bytes 49160 | tf_op jit(solution)/shard_map/ppermute | solution.py:58
  62.1 4.6 %collective-permute-start.8 = (f32[2,2048]{1,0:T(2,128)S(1)}, f32[2,2048]{1,0:T(2,128)S(1)}, u32[]{:S(2)}, u32[]{:S(2)}) collective-permute-start(f32[2,2048]{1,0:T(2,128)S(1)} %add_add_fusion.1), channel_id=1, source_target_pairs={{0,2},{1,3},{2,0},{3,1},{4,6},{5,7},{6,4},{7,5},{8,10},{9,11},{10,... | collective-permute-start | bytes 49160 | tf_op jit(solution)/shard_map/ppermute | solution.py:58
  64.5 3.7 %collective-permute-start.9 = (f32[2,2048]{1,0:T(2,128)S(1)}, f32[2,2048]{1,0:T(2,128)S(1)}, u32[]{:S(2)}, u32[]{:S(2)}) collective-permute-start(f32[2,2048]{1,0:T(2,128)S(1)} %add_add_fusion.1), channel_id=1, source_target_pairs={{0,3},{1,0},{2,1},{3,2},{4,7},{5,4},{6,5},{7,6},{8,11},{9,8},{10,9... | collective-permute-start | bytes 49160 | tf_op jit(solution)/shard_map/ppermute | solution.py:58
Sparse Core Ops, SparseCore 0:
  11.3 35.9 all-gather.1

commit v8 on v7

--- a/solution.py
+++ b/solution.py
@@ -72,7 +72,9 @@
     sw = both[:, :rows].reshape(ndp * rows, cols)
     tw = both[:, rows:].reshape(ndp * rows, cols)
     feats = jnp.concatenate([unit_rows(teacher_feat), unit_rows(student_feat)], axis=1)
-    feats = lax.all_gather(feats, "dp", axis=0, tiled=True)
+    groups = [[2 * t + core for t in range(ndp // 2)] for core in range(2)]
+    half = lax.all_gather(feats, "dp", axis=0, tiled=True, axis_index_groups=groups)
+    feats = jnp.concatenate([half, lax.ppermute(half, "dp", [(i, i ^ 1) for i in range(ndp)])])
     zt, zs = feats[:, :bot], feats[:, bot:]
     c = lax.dynamic_slice_in_dim(center, lax.axis_index("dp") * cols, cols)
     t_norm = jnp.sqrt(jnp.sum(jnp.square(tw.astype(jnp.float32)), 0) + 1e-06)
@@ -82,7 +84,13 @@
     t_exp = jnp.exp((t_cos - c) / 0.04)
     s_exp = jnp.exp(s_cos / 0.1)
     totals = jnp.stack([jnp.sum(t_exp, 1), jnp.sum(s_exp, 1)])
-    totals = exchange_all(exchange_all(totals, "dp", ndp), "tensor", lax.axis_size("tensor"))
+    summed = totals
+    for k in range(1, ndp):
+        got = lax.ppermute(totals, "dp", [(i, i ^ k) for i in range(ndp)])
+        if k % 2:
+            got = got.reshape(2, 2, -1)[:, ::-1].reshape(totals.shape)
+        summed = summed + got
+    totals = exchange_all(summed, "tensor", lax.axis_size("tensor"))
     t_total, s_total = totals[0][:, None], totals[1][:, None]
     part_center = 0.5 * c + 0.5 * (jnp.sum(t_cos, 0) / images_all)
     dlog = ((s_exp / s_total - t_exp / t_total) / 0.1).astype(jnp.bfloat16)
@@ -122,7 +130,7 @@
     def shards(teacher_master, student_weight, teacher_feat, student_feat, center):
         images_all = teacher_feat.shape[0] * ndp
         cols = center.shape[0]
-        if images_all < cols and cols % ndp == 0:
+        if images_all < cols and cols % ndp == 0 and ndp > 1 and ndp & (ndp - 1) == 0:
             return feature_plan(teacher_master, student_weight, teacher_feat, student_feat, center)
         return weight_plan(teacher_master, student_weight, teacher_feat, student_feat, center)
 

time: 90.3 us -> 98.5 us (1.091)
  waiting for transfers between devices: 28.8 us -> 31.8 us
  local copies, waits for them, and re-layouts: 3.78 us -> 6.28 us
  matrix products: 4.28 us -> 6.64 us
  other arithmetic: 10 us -> 12.3 us
  starting transfers between devices: 18.8 us -> 16.6 us
    all_to_all x1, waiting for transfers between devices: 11.8 us -> 0.01 us  [feature_plan(): both = lax.all_to_all(both, 'dp', 0, 0, tiled=True)]
    all_gather x1, waiting for transfers between devices: 14 us -> 25.5 us  [feature_plan(): lax.all_gather(feats, 'dp', axis=0, tiled=True, axis_index_groups=groups)]
    ppermute x10 -> x3, starting transfers between devices: 13.6 us -> 4.48 us  [exchange_all(): total = total + lax.ppermute(x, axis, [(i, (i + k) % n) for i in range(n)])]
    ppermute x0 -> x8, starting transfers between devices: none -> 6.88 us  [the longest x7 6.88 us: feature_plan(): got = lax.ppermute(totals, 'dp', [(i, i ^ k) for i in range(ndp)])]
    reduce_sum x1, other arithmetic: 2.36 us -> 4.66 us  [feature_plan(): scaled = jnp.sum(dlog.astype(jnp.float32) * s_cos, 0) / s_norm]
    dot_general x1, matrix products: 1.23 us -> 3.09 us  [feature_plan(): t_cos = jnp.dot(zt, tw, preferred_element_type=jnp.float32) / t_norm]
    ppermute x0 -> x8, waiting for transfers between devices: none -> 1.8 us  [the longest x7 1.18 us: feature_plan(): got = lax.ppermute(totals, 'dp', [(i, i ^ k) for i in range(ndp)])]
    ppermute x10 -> x3, waiting for transfers between devices: 2.94 us -> 4.42 us  [exchange_all(): total = total + lax.ppermute(x, axis, [(i, (i + k) % n) for i in range(n)])]
  transfers between devices with their start and end apart: 12 -> 13, of which waited for: 6 -> 5; matrix products, arithmetic and copies ran while one was open for 6% -> 8% of each run, Pallas kernels for 0% -> 0%
where the time goes in v8:
time: 98.5 us; the launch traced here: 98 us
  waiting for transfers between devices  31.8 us (32%)
  starting transfers between devices  16.6 us (17%)
  between operations  14.3 us (15%)
  other arithmetic  12.3 us (12%)
  blocking collectives  10.2 us (10%)
  matrix products  6.64 us (7%)
  local copies, waits for them, and re-layouts  6.28 us (6%)
    all_gather x1, waiting for transfers between devices, feature_plan(): lax.all_gather(feats, 'dp', axis=0, tiled=True, axis_index_groups=groups)  25.5 us
    all_to_all x1, blocking collectives, feature_plan(): got = lax.all_to_all(sent, 'dp', 0, 2, tiled=True)  10.2 us
    ppermute x7, starting transfers between devices, feature_plan(): got = lax.ppermute(totals, 'dp', [(i, i ^ k) for i in range(ndp)])  6.88 us
    all_to_all x1, starting transfers between devices, feature_plan(): both = lax.all_to_all(both, 'dp', 0, 0, tiled=True)  5.17 us
    reduce_sum x1, other arithmetic, feature_plan(): scaled = jnp.sum(dlog.astype(jnp.float32) * s_cos, 0) / s_norm  4.66 us
    ppermute x3, starting transfers between devices, exchange_all(): total = total + lax.ppermute(x, axis, [(i, (i + k) % n) for i in range(n)])  4.48 us
    ppermute x3, waiting for transfers between devices, exchange_all(): total = total + lax.ppermute(x, axis, [(i, (i + k) % n) for i in range(n)])  4.42 us
    unnamed x13, local copies, waits for them, and re-layouts  3.33 us
  transfers between devices with their start and end apart: 13, of which 5 were waited for; matrix products, arithmetic and copies ran while one was open for 8% of the time, Pallas kernels for 0%

profile of v8, /device:TPU:0, one launch (start us, length us, event | category | flops | bytes accessed | tf_op | source)
XLA Modules:
  0.0 98.0 jit_solution(1523427379619167689)
XLA Ops:
  7.2 1.0 %fusion.9 = f32[256]{0:T(256)S(1)} fusion(bf16[256,256]{1,0:T(8,128)(2,1)} %param.8), kind=kLoop, calls=%fused_computation.26 | loop fusion | flops 196352 | bytes 132096 | tf_op jit(solution)/shard_map/reduce_sum | solution.py:9
  8.2 1.0 %fusion.7 = f32[256]{0:T(256)S(1)} fusion(bf16[256,256]{1,0:T(8,128)(2,1)} %param.7), kind=kLoop, calls=%fused_computation.24 | loop fusion | flops 196352 | bytes 132096 | tf_op jit(solution)/shard_map/reduce_sum | solution.py:9
  9.3 1.1 %fusion.8 = (bf16[256,256]{1,0:T(8,128)(2,1)S(1)}, bf16[256,256]{1,0:T(8,128)(2,1)S(1)}) fusion(bf16[256,256]{1,0:T(8,128)(2,1)} %param.7, f32[256]{0:T(256)S(1)} %add_rsqrt_fusion.1, f32[256]{0:T(256)S(1)} %add_rsqrt_fusion, bf16[256,256]{1,0:T(8,128)(2,1)} %param.8), kind=kLoop, calls=%fused_computation.25 | loop fusion | flops 393216 | bytes 526336 | tf_op jit(solution)/shard_map/convert_element_type | solution.py:9
  10.4 0.7 pad_maximum_fusion.1
  11.1 2.0 %fusion.12 = (bf16[32,4096]{1,0:T(8,128)(2,1)S(1)}, f32[32,4096]{1,0:T(8,128)}) fusion(bf16[32,4096]{1,0:T(8,128)(2,1)} %param.6, f32[32,4096]{1,0:T(8,128)} %param.5), kind=kLoop, calls=%fused_computation.44 | loop fusion | flops 655360 | bytes 1572864 | tf_op jit(solution)/shard_map/convert_element_type | solution.py:69
  13.2 1.0 %copy.10 = bf16[4,8,8,512]{3,2,1,0:T(8,128)(2,1)S(1)} copy(bf16[4,8,8,512]{3,1,2,0:T(8,128)(2,1)} %bitcast.38) | data formatting | bytes 524288
  14.3 0.9 copy.8
  15.3 5.2 %all-to-all-start = ((bf16[8,64,512]{2,1,0:T(8,128)(2,1)}), bf16[8,64,512]{2,1,0:T(8,128)(2,1)S(1)}, u32[]{:S(2)}, u32[]{:S(2)}) async-start(bf16[8,64,512]{2,1,0:T(8,128)(2,1)} %bitcast.1), calls=%async_computation | async-start | bytes 1048576 | tf_op jit(solution)/shard_map/all_to_all | solution.py:71
  20.4 25.5 %all-gather.2.cloned.1.call-done = bf16[1024,512]{1,0:T(8,128)(2,1)} async-done(((bf16[256,512]{1,0:T(8,128)(2,1)}), bf16[1024,512]{1,0:T(8,128)(2,1)}) %all-gather.2.cloned.1.call-update) | async-done | bytes 1048592 | tf_op jit(solution)/shard_map/all_gather | solution.py:76
  46.0 0.8 dynamic_slice.3
  46.9 1.3 %constant_dynamic-update-slice_fusion.1 = bf16[2048,512]{1,0:T(8,128)(2,1)S(1)} fusion(bf16[1024,512]{1,0:T(8,128)(2,1)} %all-gather.2.cloned.1.call-done), kind=kLoop, calls=%fused_computation.34 | loop fusion | bytes 2097152
  48.2 0.6 collective-permute-done
  48.9 2.8 %fusion = (f32[2048]{0:T(1024)S(1)}, f32[2048,512]{1,0:T(8,128)}) fusion(f32[512]{0:T(512)S(1)} %get-tuple-element.21, bf16[256,512]{1,0:T(8,128)(2,1)S(1)} %bitcast.44, bf16[2048,512]{1,0:T(8,128)(2,1)S(1)} %constant_dynamic-update-slice_fusion), kind=kOutput, calls=%fused_computation.4 | convolution fusion | flops 540014592 | bytes 5515264 | tf_op jit(solution)/shard_map/dot_general | solution.py:83
  51.7 3.1 %fusion.1 = (f32[2048]{0:T(1024)S(1)}, f32[512]{0:T(512)S(1)}, f32[2048,512]{1,0:T(8,128)}) fusion(f32[512]{0:T(512)S(1)} %dynamic_slice.3, f32[512]{0:T(512)S(1)} %get-tuple-element.20, bf16[256,512]{1,0:T(8,128)(2,1)S(1)} %bitcast.46, bf16[2048,512]{1,0:T(8,128)(2,1)S(1)} %constant_dynamic-update-slice_fusion), kind=kOutput, calls=%fused_computation.5 | convolution fusion | flops 542111232 | bytes 5519360 | tf_op jit(solution)/shard_map/dot_general | solution.py:82
  55.1 1.4 %collective-permute-start.3 = (f32[2,2048]{1,0:T(2,128)S(1)}, f32[2,2048]{1,0:T(2,128)S(1)}, u32[]{:S(2)}, u32[]{:S(2)}) collective-permute-start(f32[2,2048]{1,0:T(2,128)S(1)} %pad_maximum_fusion.2), channel_id=1, source_target_pairs={{0,12},{4,8},{8,4},{12,0},{16,28},{20,24},{24,20},{28,16},{1,13},{... | collective-permute-start | bytes 49160 | tf_op jit(solution)/shard_map/ppermute | solution.py:89
  56.5 0.3 collective-permute-start.5
  56.8 1.4 %collective-permute-start.7 = (f32[2,2048]{1,0:T(2,128)S(1)}, f32[2,2048]{1,0:T(2,128)S(1)}, u32[]{:S(2)}, u32[]{:S(2)}) collective-permute-start(f32[2,2048]{1,0:T(2,128)S(1)} %pad_maximum_fusion.2), channel_id=1, source_target_pairs={{0,28},{4,24},{8,20},{12,16},{16,12},{20,8},{24,4},{28,0},{1,29},{... | collective-permute-start | bytes 49160 | tf_op jit(solution)/shard_map/ppermute | solution.py:89
  58.2 1.5 %collective-permute-start.2 = (f32[2,2048]{1,0:T(2,128)S(1)}, f32[2,2048]{1,0:T(2,128)S(1)}, u32[]{:S(2)}, u32[]{:S(2)}) collective-permute-start(f32[2,2048]{1,0:T(2,128)S(1)} %pad_maximum_fusion.2), channel_id=1, source_target_pairs={{0,8},{4,12},{8,0},{12,4},{16,24},{20,28},{24,16},{28,20},{1,9},{5... | collective-permute-start | bytes 49160 | tf_op jit(solution)/shard_map/ppermute | solution.py:89
  59.7 0.6 collective-permute-start.4
  60.3 1.4 %collective-permute-start.6 = (f32[2,2048]{1,0:T(2,128)S(1)}, f32[2,2048]{1,0:T(2,128)S(1)}, u32[]{:S(2)}, u32[]{:S(2)}) collective-permute-start(f32[2,2048]{1,0:T(2,128)S(1)} %pad_maximum_fusion.2), channel_id=1, source_target_pairs={{0,24},{4,28},{8,16},{12,20},{16,8},{20,12},{24,0},{28,4},{1,25},{... | collective-permute-start | bytes 49160 | tf_op jit(solution)/shard_map/ppermute | solution.py:89
  61.7 0.8 fusion.11
  62.5 0.2 rev.12
  63.8 1.2 %collective-permute-done.6 = f32[2,2048]{1,0:T(2,128)S(1)} collective-permute-done((f32[2,2048]{1,0:T(2,128)S(1)}, f32[2,2048]{1,0:T(2,128)S(1)}, u32[]{:S(2)}, u32[]{:S(2)}) %collective-permute-start.6) | collective-permute-done | bytes 16416 | tf_op jit(solution)/shard_map/ppermute | solution.py:89
  65.0 3.4 %collective-permute-start.10 = (f32[2,2048]{1,0:T(2,128)S(1)}, f32[2,2048]{1,0:T(2,128)S(1)}, u32[]{:S(2)}, u32[]{:S(2)}) collective-permute-start(f32[2,2048]{1,0:T(2,128)S(1)} %add_add_fusion.1), channel_id=1, source_target_pairs={{0,3},{1,0},{2,1},{3,2},{4,7},{5,4},{6,5},{7,6},{8,11},{9,8},{10,9... | collective-permute-start | bytes 49160 | tf_op jit(solution)/shard_map/ppermute | solution.py:58
  68.4 1.1 %collective-permute-start.9 = (f32[2,2048]{1,0:T(2,128)S(1)}, f32[2,2048]{1,0:T(2,128)S(1)}, u32[]{:S(2)}, u32[]{:S(2)}) collective-permute-start(f32[2,2048]{1,0:T(2,128)S(1)} %add_add_fusion.1), channel_id=1, source_target_pairs={{0,2},{1,3},{2,0},{3,1},{4,6},{5,7},{6,4},{7,5},{8,10},{9,11},{10,... | collective-permute-start | bytes 49160 | tf_op jit(solution)/shard_map/ppermute | solution.py:58
  69.5 0.3 collective-permute-done.10
  69.8 4.1 %collective-permute-done.8 = f32[2,2048]{1,0:T(2,128)S(1)} collective-permute-done((f32[2,2048]{1,0:T(2,128)S(1)}, f32[2,2048]{1,0:T(2,128)S(1)}, u32[]{:S(2)}, u32[]{:S(2)}) %collective-permute-start.8) | collective-permute-done | bytes 16416 | tf_op jit(solution)/shard_map/ppermute | solution.py:58
  73.9 4.7 %multiply_reduce_fusion = (f32[512]{0:T(512)S(1)}, bf16[2048,512]{1,0:T(8,128)(2,1)S(1)}) fusion(f32[2048,512]{1,0:T(8,128)} %get-tuple-element.19, f32[2048]{0:T(1024)S(1)} %bitcast.56, f32[2048,512]{1,0:T(8,128)} %get-tuple-element.17, f32[512]{0:T(512)S(1)} %dynamic_slice.3, f32[2048]{0:T(1024)S(1)} %bitcast.55), kind=kLoop, calls=%fused_computation | loop fusion | flops 11533824 | bytes 10506240 | tf_op jit(solution)/shard_map/reduce_sum | solution.py:97
  78.6 0.7 fusion.3
  79.4 10.2 %all_to_all.14 = bf16[8,34,512]{2,1,0:T(8,128)(2,1)S(1)} all-to-all(bf16[8,34,512]{2,1,0:T(8,128)(2,1)S(1)} %pad_maximum_fusion), channel_id=1, replica_groups=mesh['dp'=8,'tensor'=4] {'dp'}, dimensions={0} | all-to-all | bytes 557056 | tf_op jit(solution)/shard_map/all_to_all | solution.py:111
  89.7 0.6 slice_add_fusion
  90.3 0.8 copy.16
  (48 shorter events, 1.8 us)
Async XLA Ops:
  7.2 38.8 %all-gather.2.cloned.1.call-start = ((), (), s32[]{:S(2)}) async-start(), calls=%async_computation.2 | async-start | bytes 1310720 | tf_op jit(solution)/shard_map/all_gather | solution.py:76
  15.3 31.5 %all-to-all-start = ((bf16[8,64,512]{2,1,0:T(8,128)(2,1)}), bf16[8,64,512]{2,1,0:T(8,128)(2,1)S(1)}, u32[]{:S(2)}, u32[]{:S(2)}) async-start(bf16[8,64,512]{2,1,0:T(8,128)(2,1)} %bitcast.1), calls=%async_computation | async-start | bytes 1048576 | tf_op jit(solution)/shard_map/all_to_all | solution.py:71
  46.0 2.9 %collective-permute-start = (bf16[1024,512]{1,0:T(8,128)(2,1)}, bf16[1024,512]{1,0:T(8,128)(2,1)S(1)}, u32[]{:S(2)}, u32[]{:S(2)}) collective-permute-start(bf16[1024,512]{1,0:T(8,128)(2,1)} %all-gather.2.cloned.1.call-done), channel_id=1, source_target_pairs={{0,4},{4,0},{8,12},{12,8},{16,20},{20,16},{24,28},{28,24},{1,5},{5... | collective-permute-start | bytes 3145736 | tf_op jit(solution)/shard_map/ppermute | solution.py:77
  48.9 2.8 %copy-start = (bf16[2048,512]{1,0:T(8,128)(2,1)}, bf16[2048,512]{1,0:T(8,128)(2,1)S(1)}, u32[]{:S(2)}) copy-start(bf16[2048,512]{1,0:T(8,128)(2,1)S(1)} %constant_dynamic-update-slice_fusion) | copy-start | bytes 6291460
  54.8 4.9 %collective-permute-start.1 = (f32[2,2048]{1,0:T(2,128)S(1)}, f32[2,2048]{1,0:T(2,128)S(1)}, u32[]{:S(2)}, u32[]{:S(2)}) collective-permute-start(f32[2,2048]{1,0:T(2,128)S(1)} %pad_maximum_fusion.2), channel_id=1, source_target_pairs={{0,4},{4,0},{8,12},{12,8},{16,20},{20,16},{24,28},{28,24},{1,5},{5... | collective-permute-start | bytes 49160 | tf_op jit(solution)/shard_map/ppermute | solution.py:89
  55.1 5.2 %collective-permute-start.3 = (f32[2,2048]{1,0:T(2,128)S(1)}, f32[2,2048]{1,0:T(2,128)S(1)}, u32[]{:S(2)}, u32[]{:S(2)}) collective-permute-start(f32[2,2048]{1,0:T(2,128)S(1)} %pad_maximum_fusion.2), channel_id=1, source_target_pairs={{0,12},{4,8},{8,4},{12,0},{16,28},{20,24},{24,20},{28,16},{1,13},{... | collective-permute-start | bytes 49160 | tf_op jit(solution)/shard_map/ppermute | solution.py:89
  56.5 6.6 %collective-permute-start.5 = (f32[2,2048]{1,0:T(2,128)S(1)}, f32[2,2048]{1,0:T(2,128)S(1)}, u32[]{:S(2)}, u32[]{:S(2)}) collective-permute-start(f32[2,2048]{1,0:T(2,128)S(1)} %pad_maximum_fusion.2), channel_id=1, source_target_pairs={{0,20},{4,16},{8,28},{12,24},{16,4},{20,0},{24,12},{28,8},{1,21},{... | collective-permute-start | bytes 49160 | tf_op jit(solution)/shard_map/ppermute | solution.py:89
  56.8 6.6 %collective-permute-start.7 = (f32[2,2048]{1,0:T(2,128)S(1)}, f32[2,2048]{1,0:T(2,128)S(1)}, u32[]{:S(2)}, u32[]{:S(2)}) collective-permute-start(f32[2,2048]{1,0:T(2,128)S(1)} %pad_maximum_fusion.2), channel_id=1, source_target_pairs={{0,28},{4,24},{8,20},{12,16},{16,12},{20,8},{24,4},{28,0},{1,29},{... | collective-permute-start | bytes 49160 | tf_op jit(solution)/shard_map/ppermute | solution.py:89
  58.2 5.5 %collective-permute-start.2 = (f32[2,2048]{1,0:T(2,128)S(1)}, f32[2,2048]{1,0:T(2,128)S(1)}, u32[]{:S(2)}, u32[]{:S(2)}) collective-permute-start(f32[2,2048]{1,0:T(2,128)S(1)} %pad_maximum_fusion.2), channel_id=1, source_target_pairs={{0,8},{4,12},{8,0},{12,4},{16,24},{20,28},{24,16},{28,20},{1,9},{5... | collective-permute-start | bytes 49160 | tf_op jit(solution)/shard_map/ppermute | solution.py:89
  59.7 4.1 %collective-permute-start.4 = (f32[2,2048]{1,0:T(2,128)S(1)}, f32[2,2048]{1,0:T(2,128)S(1)}, u32[]{:S(2)}, u32[]{:S(2)}) collective-permute-start(f32[2,2048]{1,0:T(2,128)S(1)} %pad_maximum_fusion.2), channel_id=1, source_target_pairs={{0,16},{4,20},{8,24},{12,28},{16,0},{20,4},{24,8},{28,12},{1,17},{... | collective-permute-start | bytes 49160 | tf_op jit(solution)/shard_map/ppermute | solution.py:89
  60.3 4.6 %collective-permute-start.6 = (f32[2,2048]{1,0:T(2,128)S(1)}, f32[2,2048]{1,0:T(2,128)S(1)}, u32[]{:S(2)}, u32[]{:S(2)}) collective-permute-start(f32[2,2048]{1,0:T(2,128)S(1)} %pad_maximum_fusion.2), channel_id=1, source_target_pairs={{0,24},{4,28},{8,16},{12,20},{16,8},{20,12},{24,0},{28,4},{1,25},{... | collective-permute-start | bytes 49160 | tf_op jit(solution)/shard_map/ppermute | solution.py:89
  65.0 4.8 %collective-permute-start.10 = (f32[2,2048]{1,0:T(2,128)S(1)}, f32[2,2048]{1,0:T(2,128)S(1)}, u32[]{:S(2)}, u32[]{:S(2)}) collective-permute-start(f32[2,2048]{1,0:T(2,128)S(1)} %add_add_fusion.1), channel_id=1, source_target_pairs={{0,3},{1,0},{2,1},{3,2},{4,7},{5,4},{6,5},{7,6},{8,11},{9,8},{10,9... | collective-permute-start | bytes 49160 | tf_op jit(solution)/shard_map/ppermute | solution.py:58
  68.4 5.5 %collective-permute-start.8 = (f32[2,2048]{1,0:T(2,128)S(1)}, f32[2,2048]{1,0:T(2,128)S(1)}, u32[]{:S(2)}, u32[]{:S(2)}) collective-permute-start(f32[2,2048]{1,0:T(2,128)S(1)} %add_add_fusion.1), channel_id=1, source_target_pairs={{0,1},{1,2},{2,3},{3,0},{4,5},{5,6},{6,7},{7,4},{8,9},{9,10},{10,1... | collective-permute-start | bytes 49160 | tf_op jit(solution)/shard_map/ppermute | solution.py:58
  68.4 5.5 %collective-permute-start.9 = (f32[2,2048]{1,0:T(2,128)S(1)}, f32[2,2048]{1,0:T(2,128)S(1)}, u32[]{:S(2)}, u32[]{:S(2)}) collective-permute-start(f32[2,2048]{1,0:T(2,128)S(1)} %add_add_fusion.1), channel_id=1, source_target_pairs={{0,2},{1,3},{2,0},{3,1},{4,6},{5,7},{6,4},{7,5},{8,10},{9,11},{10,... | collective-permute-start | bytes 49160 | tf_op jit(solution)/shard_map/ppermute | solution.py:58
  73.9 4.7 %copy-start.1 = (bf16[2048,512]{1,0:T(8,128)(2,1)S(1)}, bf16[2048,512]{1,0:T(8,128)(2,1)}, u32[]{:S(2)}) copy-start(bf16[2048,512]{1,0:T(8,128)(2,1)} %copy-done) | copy-start | bytes 6291460
Sparse Core Ops, SparseCore 0:
  11.2 34.6 all-gather.1

commit v9 on v5

--- a/solution.py
+++ b/solution.py
@@ -60,18 +60,41 @@
 
 
 def feature_plan(teacher_master, student_weight, teacher_feat, student_feat, center):
-    ndp = lax.axis_size("dp")
+    n = lax.axis_size("dp")
+    me = lax.axis_index("dp")
+    rows, width = teacher_master.shape
     bot = teacher_feat.shape[1]
-    images_all = teacher_feat.shape[0] * ndp
-    cols = center.shape[0] // ndp
+    images = teacher_feat.shape[0]
+    cols = width // n
+    nbits = n.bit_length() - 1
     master_new = 0.996 * teacher_master + 0.004 * student_weight.astype(jnp.float32)
     both = jnp.stack([student_weight, master_new.astype(jnp.bfloat16)])
-    both = lax.all_to_all(both, "dp", 2, 1, tiled=True)
-    sw, tw = both[0], both[1]
+    both = both.reshape(2, rows, n, cols).transpose(2, 0, 1, 3).reshape(n, 2 * rows, cols)
+    order = me ^ jnp.arange(n)
+    held = jnp.take(both, order, axis=0).reshape((2,) * nbits + (2 * rows, cols))
     feats = jnp.concatenate([unit_rows(teacher_feat), unit_rows(student_feat)], axis=1)
-    feats = lax.all_gather(feats, "dp", axis=0, tiled=True)
+    bits = list(range(1, nbits)) + [0]
+    for b in bits:
+        dim = nbits - 1 - b
+        keep = lax.index_in_dim(held, 0, dim, keepdims=False)
+        away = lax.index_in_dim(held, 1, dim, keepdims=False)
+        flat_feats = feats.reshape(-1, 2 * bot)
+        pairs = [(i, i ^ (1 << b)) for i in range(n)]
+        if 2 * bot == cols:
+            payload = jnp.concatenate([flat_feats, away.reshape(-1, cols)], axis=0)
+            got = lax.ppermute(payload, "dp", pairs)
+            got_feats = got[: flat_feats.shape[0]].reshape(feats.shape)
+            got_held = got[flat_feats.shape[0]:].reshape(away.shape)
+        else:
+            got_feats, got_held = lax.ppermute((feats, away), "dp", pairs)
+        feats = jnp.stack([feats, got_feats])
+        held = jnp.stack([keep, got_held], axis=dim)
+    feats = feats.reshape(-1, 2 * bot)
+    held = jnp.take(held.reshape(n, 2 * rows, cols), order, axis=0)
+    sw = held[:, :rows].reshape(n * rows, cols)
+    tw = held[:, rows:].reshape(n * rows, cols)
     zt, zs = feats[:, :bot], feats[:, bot:]
-    c = lax.dynamic_slice_in_dim(center, lax.axis_index("dp") * cols, cols)
+    c = lax.dynamic_slice_in_dim(center, me * cols, cols)
     t_norm = jnp.sqrt(jnp.sum(jnp.square(tw.astype(jnp.float32)), 0) + 1e-06)
     s_norm = jnp.sqrt(jnp.sum(jnp.square(sw.astype(jnp.float32)), 0) + 1e-06)
     t_cos = jnp.dot(zt, tw, preferred_element_type=jnp.float32) / t_norm
@@ -79,27 +102,31 @@
     t_exp = jnp.exp((t_cos - c) / 0.04)
     s_exp = jnp.exp(s_cos / 0.1)
     totals = jnp.stack([jnp.sum(t_exp, 1), jnp.sum(s_exp, 1)])
-    totals = exchange_all(exchange_all(totals, "dp", ndp), "tensor", lax.axis_size("tensor"))
+    round_dims = {b: nbits - 1 - pos for pos, b in enumerate(bits)}
+    for b in bits:
+        got = lax.ppermute(totals, "dp", [(i, i ^ (1 << b)) for i in range(n)])
+        got = jnp.flip(got.reshape((2,) + (2,) * nbits + (images,)), 1 + round_dims[b])
+        totals = totals + got.reshape(totals.shape)
+    totals = exchange_all(totals, "tensor", lax.axis_size("tensor"))
     t_total, s_total = totals[0][:, None], totals[1][:, None]
-    part_center = 0.5 * c + 0.5 * (jnp.sum(t_cos, 0) / images_all)
+    part_center = 0.5 * c + 0.5 * (jnp.sum(t_cos, 0) / (images * n))
     dlog = ((s_exp / s_total - t_exp / t_total) / 0.1).astype(jnp.bfloat16)
     scaled = jnp.sum(dlog.astype(jnp.float32) * s_cos, 0) / s_norm
     product = lax.dot_general(
         zs, dlog, (((0,), (0,)), ((), ())), preferred_element_type=jnp.float32
     )
     grad = (product - sw.astype(jnp.float32) * scaled) / s_norm
-    rows = grad.shape[0] // ndp
     high = part_center.astype(jnp.bfloat16)
     low = (part_center - high.astype(jnp.float32)).astype(jnp.bfloat16)
     sent = jnp.concatenate(
         [
-            grad.astype(jnp.bfloat16).reshape(ndp, rows, cols),
-            jnp.broadcast_to(jnp.stack([high, low]), (ndp, 2, cols)),
+            grad.astype(jnp.bfloat16).reshape(n, rows, cols),
+            jnp.broadcast_to(jnp.stack([high, low]), (n, 2, cols)),
         ],
         axis=1,
     )
     got = lax.all_to_all(sent, "dp", 0, 2, tiled=True)
-    got = got.reshape(rows + 2, ndp * cols).astype(jnp.float32)
+    got = got.reshape(rows + 2, n * cols).astype(jnp.float32)
     return (master_new, got[:rows], got[rows] + got[rows + 1])
 
 
@@ -120,7 +147,7 @@
     def shards(teacher_master, student_weight, teacher_feat, student_feat, center):
         images_all = teacher_feat.shape[0] * ndp
         cols = center.shape[0]
-        if images_all < cols and cols % ndp == 0:
+        if images_all < cols and cols % ndp == 0 and ndp > 1 and ndp & (ndp - 1) == 0:
             return feature_plan(teacher_master, student_weight, teacher_feat, student_feat, center)
         return weight_plan(teacher_master, student_weight, teacher_feat, student_feat, center)
 

time: 84.9 us -> 86.8 us (1.022)
  waiting for transfers between devices: 16.7 us -> 38.7 us
  between operations: 14.2 us -> 1.08 us
  starting transfers between devices: 18.8 us -> 13.4 us
  local copies, waits for them, and re-layouts: 9.56 us -> 4.71 us
  matrix products: 4.27 us -> 6.63 us
  blocking collectives: 10 us -> 11.2 us
    ppermute x0 -> x6, waiting for transfers between devices: none -> 36.3 us  [the longest x3 31.3 us: feature_plan(): got = lax.ppermute(payload, 'dp', pairs)]
    all_to_all x1 -> x0, waiting for transfers between devices: 8.99 us -> none  [feature_plan(): both = lax.all_to_all(both, 'dp', 2, 1, tiled=True)]
    ppermute x10 -> x3, starting transfers between devices: 13.6 us -> 5.49 us  [exchange_all(): total = total + lax.ppermute(x, axis, [(i, (i + k) % n) for i in range(n)])]
    ppermute x0 -> x6, starting transfers between devices: none -> 7.91 us  [the longest x3 4.84 us: feature_plan(): got = lax.ppermute(payload, 'dp', pairs)]
    all_to_all x1 -> x0, starting transfers between devices: 5.17 us -> none  [feature_plan(): both = lax.all_to_all(both, 'dp', 2, 1, tiled=True)]
    all_gather x1 -> x0, waiting for transfers between devices: 4.76 us -> none  [feature_plan(): feats = lax.all_gather(feats, 'dp', axis=0, tiled=True)]
    another operation x2 -> x1, other arithmetic: 3 us -> 0.05 us  [feature_plan(): both = jnp.stack([student_weight, master_new.astype(jnp.bfloat16)])]
    unnamed x6 -> x12, local copies, waits for them, and re-layouts: 4.63 us -> 2.01 us
  transfers between devices with their start and end apart: 12 -> 9, of which waited for: 6 -> 9; matrix products, arithmetic and copies ran while one was open for 15% -> 2% of each run, Pallas kernels for 0% -> 0%
where the time goes in v9:
time: 86.8 us; the launch traced here: 86.5 us
  waiting for transfers between devices  38.7 us (45%)
  starting transfers between devices  13.4 us (15%)
  blocking collectives  11.2 us (13%)
  other arithmetic  10.8 us (12%)
  matrix products  6.63 us (8%)
  local copies, waits for them, and re-layouts  4.71 us (5%)
  between operations  1.08 us (1%)
    ppermute x3, waiting for transfers between devices, feature_plan(): got = lax.ppermute(payload, 'dp', pairs)  31.3 us
    all_to_all x1, blocking collectives, feature_plan(): got = lax.all_to_all(sent, 'dp', 0, 2, tiled=True)  11.2 us
    ppermute x3, starting transfers between devices, exchange_all(): total = total + lax.ppermute(x, axis, [(i, (i + k) % n) for i in range(n)])  5.49 us
    ppermute x3, waiting for transfers between devices, feature_plan(): got = lax.ppermute(totals, 'dp', [(i, i ^ 1 << b) for i in range(n)])  4.99 us
    ppermute x3, starting transfers between devices, feature_plan(): got = lax.ppermute(payload, 'dp', pairs)  4.84 us
    reduce_sum x1, other arithmetic, feature_plan(): scaled = jnp.sum(dlog.astype(jnp.float32) * s_cos, 0) / s_norm  4.56 us
    ppermute x3, starting transfers between devices, feature_plan(): got = lax.ppermute(totals, 'dp', [(i, i ^ 1 << b) for i in range(n)])  3.07 us
    dot_general x1, matrix products, feature_plan(): t_cos = jnp.dot(zt, tw, preferred_element_type=jnp.float32) / t_norm  3.06 us
  transfers between devices with their start and end apart: 9, of which 9 were waited for; matrix products, arithmetic and copies ran while one was open for 2% of the time, Pallas kernels for 0%

profile of v9, /device:TPU:0, one launch (start us, length us, event | category | flops | bytes accessed | tf_op | source)
XLA Modules:
  0.0 86.5 jit_solution(3203039228790035890)
XLA Ops:
  0.7 2.1 %fusion.20 = (bf16[32,4096]{1,0:T(8,128)(2,1)S(1)}, f32[32,4096]{1,0:T(8,128)}) fusion(bf16[32,4096]{1,0:T(8,128)(2,1)} %param.8, f32[32,4096]{1,0:T(8,128)} %param.7), kind=kLoop, calls=%fused_computation.67 | loop fusion | flops 655360 | bytes 1572864 | tf_op jit(solution)/shard_map/convert_element_type | solution.py:71
  2.9 1.0 %copy.13 = bf16[4,8,8,512]{3,2,1,0:T(8,128)(2,1)S(1)} copy(bf16[4,8,8,512]{3,1,2,0:T(8,128)(2,1)} %bitcast.70) | data formatting | bytes 524288
  4.1 0.6 gather_fusion
  5.1 0.1 fusion.12
  5.3 3.0 %collective-permute-start = (bf16[512,512]{1,0:T(8,128)(2,1)S(1)}, bf16[512,512]{1,0:T(8,128)(2,1)S(1)}, u32[]{:S(2)}, u32[]{:S(2)}) collective-permute-start(bf16[512,512]{1,0:T(8,128)(2,1)S(1)} %pad_maximum_fusion.5), channel_id=1, source_target_pairs={{0,8},{4,12},{8,0},{12,4},{16,24},{20,28},{24,16},{28,20},{1,9},{5... | collective-permute-start | bytes 1572872 | tf_op jit(solution)/shard_map/ppermute | solution.py:85
  8.4 11.9 %collective-permute-done = bf16[512,512]{1,0:T(8,128)(2,1)S(1)} collective-permute-done((bf16[512,512]{1,0:T(8,128)(2,1)S(1)}, bf16[512,512]{1,0:T(8,128)(2,1)S(1)}, u32[]{:S(2)}, u32[]{:S(2)}) %collective-permute-start) | collective-permute-done | bytes 524320 | tf_op jit(solution)/shard_map/ppermute | solution.py:85
  20.5 1.8 %collective-permute-start.1 = (bf16[768,512]{1,0:T(8,128)(2,1)S(1)}, bf16[768,512]{1,0:T(8,128)(2,1)S(1)}, u32[]{:S(2)}, u32[]{:S(2)}) collective-permute-start(bf16[768,512]{1,0:T(8,128)(2,1)S(1)} %pad_maximum_fusion.3), channel_id=1, source_target_pairs={{0,16},{4,20},{8,24},{12,28},{16,0},{20,4},{24,8},{28,12},{1,17},{... | collective-permute-start | bytes 2359304 | tf_op jit(solution)/shard_map/ppermute | solution.py:85
  22.3 17.0 %collective-permute-done.1 = bf16[768,512]{1,0:T(8,128)(2,1)S(1)} collective-permute-done((bf16[768,512]{1,0:T(8,128)(2,1)S(1)}, bf16[768,512]{1,0:T(8,128)(2,1)S(1)}, u32[]{:S(2)}, u32[]{:S(2)}) %collective-permute-start.1) | collective-permute-done | bytes 786464 | tf_op jit(solution)/shard_map/ppermute | solution.py:85
  39.4 0.1 fusion.19
  39.6 1.1 %pad_maximum_fusion.1 = bf16[1280,512]{1,0:T(8,128)(2,1)} fusion(bf16[256,512]{1,0:T(8,128)(2,1)S(1)} %bitcast.66, bf16[1024,512]{1,0:T(8,128)(2,1)S(1)} %bitcast.53), kind=kLoop, calls=%fused_computation.11 | loop fusion | flops 2621440 | bytes 2621440 | tf_op jit(solution)/shard_map/concatenate | solution.py:84
  40.7 0.8 dynamic_slice.3
  41.5 2.5 %collective-permute-done.2 = bf16[1280,512]{1,0:T(8,128)(2,1)S(1)} collective-permute-done((bf16[1280,512]{1,0:T(8,128)(2,1)}, bf16[1280,512]{1,0:T(8,128)(2,1)S(1)}, u32[]{:S(2)}, u32[]{:S(2)}) %collective-permute-start.2) | collective-permute-done | bytes 1310752 | tf_op jit(solution)/shard_map/ppermute | solution.py:85
  44.1 0.6 gather_fusion.1
  45.1 0.2 pad_maximum_fusion
  45.3 2.8 %fusion = (f32[2048]{0:T(1024)S(1)}, f32[2048,512]{1,0:T(8,128)}) fusion(f32[512]{0:T(512)S(1)} %add_sqrt_fusion.1, bf16[256,512]{1,0:T(8,128)(2,1)S(1)} %bitcast.76, bf16[2048,512]{1,0:T(8,128)(2,1)S(1)} %bitcast.58), kind=kOutput, calls=%fused_computation.6 | convolution fusion | flops 540014592 | bytes 5515264 | tf_op jit(solution)/shard_map/dot_general | solution.py:101
  48.1 3.1 %fusion.1 = (f32[2048]{0:T(1024)S(1)}, f32[512]{0:T(512)S(1)}, f32[2048,512]{1,0:T(8,128)}) fusion(f32[512]{0:T(512)S(1)} %dynamic_slice.3, f32[512]{0:T(512)S(1)} %add_sqrt_fusion, bf16[256,512]{1,0:T(8,128)(2,1)S(1)} %bitcast.78, bf16[2048,512]{1,0:T(8,128)(2,1)S(1)} %bitcast.59), kind=kOutput, calls=%fused_computation.7 | convolution fusion | flops 542111232 | bytes 5519360 | tf_op jit(solution)/shard_map/dot_general | solution.py:100
  51.2 1.5 %collective-permute-start.3 = (f32[2,2048]{1,0:T(2,128)S(1)}, f32[2,2048]{1,0:T(2,128)S(1)}, u32[]{:S(2)}, u32[]{:S(2)}) collective-permute-start(f32[2,2048]{1,0:T(2,128)S(1)} %pad_maximum_fusion.9), channel_id=1, source_target_pairs={{0,8},{4,12},{8,0},{12,4},{16,24},{20,28},{24,16},{28,20},{1,9},{5... | collective-permute-start | bytes 49160 | tf_op jit(solution)/shard_map/ppermute | solution.py:107
  52.7 2.3 %collective-permute-done.3 = f32[2,2048]{1,0:T(2,128)S(1)} collective-permute-done((f32[2,2048]{1,0:T(2,128)S(1)}, f32[2,2048]{1,0:T(2,128)S(1)}, u32[]{:S(2)}, u32[]{:S(2)}) %collective-permute-start.3) | collective-permute-done | bytes 16416 | tf_op jit(solution)/shard_map/ppermute | solution.py:107
  55.2 1.5 %collective-permute-start.4 = (f32[2,2048]{1,0:T(2,128)S(1)}, f32[2,2048]{1,0:T(2,128)S(1)}, u32[]{:S(2)}, u32[]{:S(2)}) collective-permute-start(f32[2,2048]{1,0:T(2,128)S(1)} %fusion.17), channel_id=1, source_target_pairs={{0,16},{4,20},{8,24},{12,28},{16,0},{20,4},{24,8},{28,12},{1,17},{... | collective-permute-start | bytes 49160 | tf_op jit(solution)/shard_map/ppermute | solution.py:107
  56.7 2.3 %collective-permute-done.4 = f32[2,2048]{1,0:T(2,128)S(1)} collective-permute-done((f32[2,2048]{1,0:T(2,128)S(1)}, f32[2,2048]{1,0:T(2,128)S(1)}, u32[]{:S(2)}, u32[]{:S(2)}) %collective-permute-start.4) | collective-permute-done | bytes 16416 | tf_op jit(solution)/shard_map/ppermute | solution.py:107
  59.2 0.8 fusion.16
  60.0 0.4 collective-permute-done.5
  60.4 1.6 %collective-permute-start.6 = (f32[2,2048]{1,0:T(2,128)S(1)}, f32[2,2048]{1,0:T(2,128)S(1)}, u32[]{:S(2)}, u32[]{:S(2)}) collective-permute-start(f32[2,2048]{1,0:T(2,128)S(1)} %add.78), channel_id=1, source_target_pairs={{0,1},{1,2},{2,3},{3,0},{4,5},{5,6},{6,7},{7,4},{8,9},{9,10},{10,1... | collective-permute-start | bytes 49160 | tf_op jit(solution)/shard_map/ppermute | solution.py:58
  62.0 2.6 %collective-permute-start.7 = (f32[2,2048]{1,0:T(2,128)S(1)}, f32[2,2048]{1,0:T(2,128)S(1)}, u32[]{:S(2)}, u32[]{:S(2)}) collective-permute-start(f32[2,2048]{1,0:T(2,128)S(1)} %add.78), channel_id=1, source_target_pairs={{0,2},{1,3},{2,0},{3,1},{4,6},{5,7},{6,4},{7,5},{8,10},{9,11},{10,... | collective-permute-start | bytes 49160 | tf_op jit(solution)/shard_map/ppermute | solution.py:58
  64.6 1.4 %collective-permute-start.8 = (f32[2,2048]{1,0:T(2,128)S(1)}, f32[2,2048]{1,0:T(2,128)S(1)}, u32[]{:S(2)}, u32[]{:S(2)}) collective-permute-start(f32[2,2048]{1,0:T(2,128)S(1)} %add.78), channel_id=1, source_target_pairs={{0,3},{1,0},{2,1},{3,2},{4,7},{5,4},{6,5},{7,6},{8,11},{9,8},{10,9... | collective-permute-start | bytes 49160 | tf_op jit(solution)/shard_map/ppermute | solution.py:58
  66.0 0.9 %collective-permute-done.7 = f32[2,2048]{1,0:T(2,128)S(1)} collective-permute-done((f32[2,2048]{1,0:T(2,128)S(1)}, f32[2,2048]{1,0:T(2,128)S(1)}, u32[]{:S(2)}, u32[]{:S(2)}) %collective-permute-start.7) | collective-permute-done | bytes 16416 | tf_op jit(solution)/shard_map/ppermute | solution.py:58
  66.9 1.4 %collective-permute-done.8 = f32[2,2048]{1,0:T(2,128)S(1)} collective-permute-done((f32[2,2048]{1,0:T(2,128)S(1)}, f32[2,2048]{1,0:T(2,128)S(1)}, u32[]{:S(2)}, u32[]{:S(2)}) %collective-permute-start.8) | collective-permute-done | bytes 16416 | tf_op jit(solution)/shard_map/ppermute | solution.py:58
  68.4 4.6 %multiply_reduce_fusion = (f32[512]{0:T(512)S(1)}, bf16[2048,512]{1,0:T(8,128)(2,1)S(1)}) fusion(f32[2048,512]{1,0:T(8,128)} %get-tuple-element.30, f32[2048]{0:T(1024)S(1)} %bitcast.86, f32[2048,512]{1,0:T(8,128)} %get-tuple-element.28, f32[512]{0:T(512)S(1)} %dynamic_slice.3, f32[2048]{0:T(1024)S(1)} %bitcast.85), kind=kLoop, calls=%fused_computation.2 | loop fusion | flops 11533824 | bytes 10506240 | tf_op jit(solution)/shard_map/reduce_sum | solution.py:114
  73.0 0.7 fusion.3
  73.8 11.2 %all_to_all.4 = bf16[8,34,512]{2,1,0:T(8,128)(2,1)S(1)} all-to-all(bf16[8,34,512]{2,1,0:T(8,128)(2,1)S(1)} %pad_maximum_fusion.8), channel_id=1, replica_groups=mesh['dp'=8,'tensor'=4] {'dp'}, dimensions={0} | all-to-all | bytes 557056 | tf_op jit(solution)/shard_map/all_to_all | solution.py:128
  85.0 0.6 slice_add_fusion
  85.7 0.8 copy.15
  (65 shorter events, 2.3 us)
Async XLA Ops:
  0.6 4.2 %copy-start.1 = (bf16[256,256]{1,0:T(8,128)(2,1)S(1)}, bf16[256,256]{1,0:T(8,128)(2,1)}, u32[]{:S(2)}) copy-start(bf16[256,256]{1,0:T(8,128)(2,1)} %param.10) | copy-start | bytes 393220
  0.6 4.4 %copy-start = (bf16[256,256]{1,0:T(8,128)(2,1)S(1)}, bf16[256,256]{1,0:T(8,128)(2,1)}, u32[]{:S(2)}) copy-start(bf16[256,256]{1,0:T(8,128)(2,1)} %param.9) | copy-start | bytes 393220
  5.3 14.9 %collective-permute-start = (bf16[512,512]{1,0:T(8,128)(2,1)S(1)}, bf16[512,512]{1,0:T(8,128)(2,1)S(1)}, u32[]{:S(2)}, u32[]{:S(2)}) collective-permute-start(bf16[512,512]{1,0:T(8,128)(2,1)S(1)} %pad_maximum_fusion.5), channel_id=1, source_target_pairs={{0,8},{4,12},{8,0},{12,4},{16,24},{20,28},{24,16},{28,20},{1,9},{5... | collective-permute-start | bytes 1572872 | tf_op jit(solution)/shard_map/ppermute | solution.py:85
  20.5 18.8 %collective-permute-start.1 = (bf16[768,512]{1,0:T(8,128)(2,1)S(1)}, bf16[768,512]{1,0:T(8,128)(2,1)S(1)}, u32[]{:S(2)}, u32[]{:S(2)}) collective-permute-start(bf16[768,512]{1,0:T(8,128)(2,1)S(1)} %pad_maximum_fusion.3), channel_id=1, source_target_pairs={{0,16},{4,20},{8,24},{12,28},{16,0},{20,4},{24,8},{28,12},{1,17},{... | collective-permute-start | bytes 2359304 | tf_op jit(solution)/shard_map/ppermute | solution.py:85
  40.7 3.2 %collective-permute-start.2 = (bf16[1280,512]{1,0:T(8,128)(2,1)}, bf16[1280,512]{1,0:T(8,128)(2,1)S(1)}, u32[]{:S(2)}, u32[]{:S(2)}) collective-permute-start(bf16[1280,512]{1,0:T(8,128)(2,1)} %pad_maximum_fusion.1), channel_id=1, source_target_pairs={{0,4},{4,0},{8,12},{12,8},{16,20},{20,16},{24,28},{28,24},{1,5},{5... | collective-permute-start | bytes 3932168 | tf_op jit(solution)/shard_map/ppermute | solution.py:85
  44.8 3.3 %copy-start.2 = (bf16[8,32,512]{2,1,0:T(8,128)(2,1)}, bf16[8,32,512]{2,1,0:T(8,128)(2,1)S(1)}, u32[]{:S(2)}) copy-start(bf16[8,32,512]{2,1,0:T(8,128)(2,1)S(1)} %get-tuple-element.14) | copy-start | bytes 786436
  51.2 3.8 %collective-permute-start.3 = (f32[2,2048]{1,0:T(2,128)S(1)}, f32[2,2048]{1,0:T(2,128)S(1)}, u32[]{:S(2)}, u32[]{:S(2)}) collective-permute-start(f32[2,2048]{1,0:T(2,128)S(1)} %pad_maximum_fusion.9), channel_id=1, source_target_pairs={{0,8},{4,12},{8,0},{12,4},{16,24},{20,28},{24,16},{28,20},{1,9},{5... | collective-permute-start | bytes 49160 | tf_op jit(solution)/shard_map/ppermute | solution.py:107
  55.2 3.8 %collective-permute-start.4 = (f32[2,2048]{1,0:T(2,128)S(1)}, f32[2,2048]{1,0:T(2,128)S(1)}, u32[]{:S(2)}, u32[]{:S(2)}) collective-permute-start(f32[2,2048]{1,0:T(2,128)S(1)} %fusion.17), channel_id=1, source_target_pairs={{0,16},{4,20},{8,24},{12,28},{16,0},{20,4},{24,8},{28,12},{1,17},{... | collective-permute-start | bytes 49160 | tf_op jit(solution)/shard_map/ppermute | solution.py:107
  59.1 1.2 %collective-permute-start.5 = (f32[2,2048]{1,0:T(2,128)S(1)}, f32[2,2048]{1,0:T(2,128)S(1)}, u32[]{:S(2)}, u32[]{:S(2)}) collective-permute-start(f32[2,2048]{1,0:T(2,128)S(1)} %fusion.28), channel_id=1, source_target_pairs={{0,4},{4,0},{8,12},{12,8},{16,20},{20,16},{24,28},{28,24},{1,5},{5... | collective-permute-start | bytes 49160 | tf_op jit(solution)/shard_map/ppermute | solution.py:107
  60.4 5.6 %collective-permute-start.6 = (f32[2,2048]{1,0:T(2,128)S(1)}, f32[2,2048]{1,0:T(2,128)S(1)}, u32[]{:S(2)}, u32[]{:S(2)}) collective-permute-start(f32[2,2048]{1,0:T(2,128)S(1)} %add.78), channel_id=1, source_target_pairs={{0,1},{1,2},{2,3},{3,0},{4,5},{5,6},{6,7},{7,4},{8,9},{9,10},{10,1... | collective-permute-start | bytes 49160 | tf_op jit(solution)/shard_map/ppermute | solution.py:58
  62.0 4.9 %collective-permute-start.7 = (f32[2,2048]{1,0:T(2,128)S(1)}, f32[2,2048]{1,0:T(2,128)S(1)}, u32[]{:S(2)}, u32[]{:S(2)}) collective-permute-start(f32[2,2048]{1,0:T(2,128)S(1)} %add.78), channel_id=1, source_target_pairs={{0,2},{1,3},{2,0},{3,1},{4,6},{5,7},{6,4},{7,5},{8,10},{9,11},{10,... | collective-permute-start | bytes 49160 | tf_op jit(solution)/shard_map/ppermute | solution.py:58
  64.6 3.7 %collective-permute-start.8 = (f32[2,2048]{1,0:T(2,128)S(1)}, f32[2,2048]{1,0:T(2,128)S(1)}, u32[]{:S(2)}, u32[]{:S(2)}) collective-permute-start(f32[2,2048]{1,0:T(2,128)S(1)} %add.78), channel_id=1, source_target_pairs={{0,3},{1,0},{2,1},{3,2},{4,7},{5,4},{6,5},{7,6},{8,11},{9,8},{10,9... | collective-permute-start | bytes 49160 | tf_op jit(solution)/shard_map/ppermute | solution.py:58
  68.4 4.6 %copy-start.3 = (bf16[8,32,512]{2,1,0:T(8,128)(2,1)S(1)}, bf16[8,32,512]{2,1,0:T(8,128)(2,1)}, u32[]{:S(2)}) copy-start(bf16[8,32,512]{2,1,0:T(8,128)(2,1)} %copy-done.2) | copy-start | bytes 786436

commit v10 on v9

--- a/solution.py
+++ b/solution.py
@@ -67,30 +67,52 @@
     images = teacher_feat.shape[0]
     cols = width // n
     nbits = n.bit_length() - 1
+    odd = me % 2
+    up = list(range(1, nbits))
+    down = up[::-1]
+    dim_bits = [jnp.where(odd == 1, down[r], up[r]) for r in range(nbits - 1)][::-1]
     master_new = 0.996 * teacher_master + 0.004 * student_weight.astype(jnp.float32)
     both = jnp.stack([student_weight, master_new.astype(jnp.bfloat16)])
     both = both.reshape(2, rows, n, cols).transpose(2, 0, 1, 3).reshape(n, 2 * rows, cols)
-    order = me ^ jnp.arange(n)
-    held = jnp.take(both, order, axis=0).reshape((2,) * nbits + (2 * rows, cols))
+    pos = jnp.arange(n)
+    rel = (pos >> (nbits - 1)) & 1
+    for d, bit in enumerate(dim_bits):
+        rel = rel | (((pos >> (nbits - 2 - d)) & 1) << bit)
+    held = jnp.take(both, me ^ rel, axis=0).reshape((2,) * nbits + (2 * rows, cols))
     feats = jnp.concatenate([unit_rows(teacher_feat), unit_rows(student_feat)], axis=1)
-    bits = list(range(1, nbits)) + [0]
-    for b in bits:
-        dim = nbits - 1 - b
+    cross_rev = list(range(nbits - 2, -1, -1))
+
+    def swap(pairs_up, pairs_down):
+        return [(i, i ^ (1 << (pairs_down if i % 2 else pairs_up))) for i in range(n)]
+
+    for r in range(nbits):
+        last = r == nbits - 1
+        dim = 0 if last else nbits - 1 - r
         keep = lax.index_in_dim(held, 0, dim, keepdims=False)
         away = lax.index_in_dim(held, 1, dim, keepdims=False)
-        flat_feats = feats.reshape(-1, 2 * bot)
-        pairs = [(i, i ^ (1 << b)) for i in range(n)]
+        if last:
+            pairs = [(i, i ^ 1) for i in range(n)]
+        else:
+            pairs = swap(up[r], down[r])
         if 2 * bot == cols:
+            flat_feats = feats.reshape(-1, 2 * bot)
             payload = jnp.concatenate([flat_feats, away.reshape(-1, cols)], axis=0)
             got = lax.ppermute(payload, "dp", pairs)
             got_feats = got[: flat_feats.shape[0]].reshape(feats.shape)
             got_held = got[flat_feats.shape[0]:].reshape(away.shape)
         else:
             got_feats, got_held = lax.ppermute((feats, away), "dp", pairs)
+        if last:
+            got_feats = jnp.transpose(got_feats, cross_rev + [nbits - 1, nbits])
+            got_held = jnp.transpose(got_held, cross_rev + [nbits - 1, nbits])
         feats = jnp.stack([feats, got_feats])
         held = jnp.stack([keep, got_held], axis=dim)
     feats = feats.reshape(-1, 2 * bot)
-    held = jnp.take(held.reshape(n, 2 * rows, cols), order, axis=0)
+    src = me ^ pos
+    where = src & 1
+    for d, bit in enumerate(dim_bits):
+        where = (where << 1) | ((src >> bit) & 1)
+    held = jnp.take(held.reshape(n, 2 * rows, cols), where, axis=0)
     sw = held[:, :rows].reshape(n * rows, cols)
     tw = held[:, rows:].reshape(n * rows, cols)
     zt, zs = feats[:, :bot], feats[:, bot:]
@@ -102,10 +124,14 @@
     t_exp = jnp.exp((t_cos - c) / 0.04)
     s_exp = jnp.exp(s_cos / 0.1)
     totals = jnp.stack([jnp.sum(t_exp, 1), jnp.sum(s_exp, 1)])
-    round_dims = {b: nbits - 1 - pos for pos, b in enumerate(bits)}
-    for b in bits:
-        got = lax.ppermute(totals, "dp", [(i, i ^ (1 << b)) for i in range(n)])
-        got = jnp.flip(got.reshape((2,) + (2,) * nbits + (images,)), 1 + round_dims[b])
+    shape = (2,) + (2,) * nbits + (images,)
+    for r in range(nbits):
+        if r == nbits - 1:
+            got = lax.ppermute(totals, "dp", [(i, i ^ 1) for i in range(n)]).reshape(shape)
+            got = jnp.flip(jnp.transpose(got, [0, 1] + [2 + d for d in cross_rev] + [nbits + 1]), 1)
+        else:
+            got = lax.ppermute(totals, "dp", swap(up[r], down[r])).reshape(shape)
+            got = jnp.flip(got, nbits - r)
         totals = totals + got.reshape(totals.shape)
     totals = exchange_all(totals, "tensor", lax.axis_size("tensor"))
     t_total, s_total = totals[0][:, None], totals[1][:, None]

time: 86.8 us -> 76.2 us (0.88)
  waiting for transfers between devices: 38.7 us -> 25.8 us
  starting transfers between devices: 13.4 us -> 15.4 us
    ppermute x3, waiting for transfers between devices: 31.3 us -> 19.6 us  [feature_plan(): got = lax.ppermute(payload, 'dp', pairs)]
    ppermute x3, starting transfers between devices: 3.07 us -> 4.21 us  [the longest x2 4.14 us: feature_plan(): got = lax.ppermute(totals, 'dp', swap(up[r], down[r])).reshape(shape)]
    ppermute x3, waiting for transfers between devices: 4.99 us -> 3.86 us  [the longest x2 3.48 us: feature_plan(): got = lax.ppermute(totals, 'dp', swap(up[r], down[r])).reshape(shape)]
  transfers between devices with their start and end apart: 9 -> 9, of which waited for: 9 -> 8; matrix products, arithmetic and copies ran while one was open for 2% -> 2% of each run, Pallas kernels for 0% -> 0%
where the time goes in v10:
time: 76.2 us; the launch traced here: 75.9 us
  waiting for transfers between devices  25.8 us (34%)
  starting transfers between devices  15.4 us (20%)
  blocking collectives  11.2 us (15%)
  other arithmetic  10.8 us (14%)
  matrix products  6.62 us (9%)
  local copies, waits for them, and re-layouts  5 us (7%)
  between operations  1.11 us (1%)
    ppermute x3, waiting for transfers between devices, feature_plan(): got = lax.ppermute(payload, 'dp', pairs)  19.6 us
    all_to_all x1, blocking collectives, feature_plan(): got = lax.all_to_all(sent, 'dp', 0, 2, tiled=True)  11.2 us
    ppermute x3, starting transfers between devices, exchange_all(): total = total + lax.ppermute(x, axis, [(i, (i + k) % n) for i in range(n)])  6.06 us
    ppermute x3, starting transfers between devices, feature_plan(): got = lax.ppermute(payload, 'dp', pairs)  5.12 us
    reduce_sum x1, other arithmetic, feature_plan(): scaled = jnp.sum(dlog.astype(jnp.float32) * s_cos, 0) / s_norm  4.56 us
    ppermute x2, starting transfers between devices, feature_plan(): got = lax.ppermute(totals, 'dp', swap(up[r], down[r])).reshape(shape)  4.14 us
    ppermute x2, waiting for transfers between devices, feature_plan(): got = lax.ppermute(totals, 'dp', swap(up[r], down[r])).reshape(shape)  3.48 us
    dot_general x1, matrix products, feature_plan(): t_cos = jnp.dot(zt, tw, preferred_element_type=jnp.float32) / t_norm  3.06 us
  transfers between devices with their start and end apart: 9, of which 8 were waited for; matrix products, arithmetic and copies ran while one was open for 2% of the time, Pallas kernels for 0%

profile of v10, /device:TPU:0, one launch (start us, length us, event | category | flops | bytes accessed | tf_op | source)
XLA Modules:
  0.0 75.9 jit_solution(8593512070237458696)
XLA Ops:
  0.7 2.0 %fusion.20 = (bf16[32,4096]{1,0:T(8,128)(2,1)S(1)}, f32[32,4096]{1,0:T(8,128)}) fusion(bf16[32,4096]{1,0:T(8,128)(2,1)} %param.8, f32[32,4096]{1,0:T(8,128)} %param.7), kind=kLoop, calls=%fused_computation.73 | loop fusion | flops 655360 | bytes 1572864 | tf_op jit(solution)/shard_map/convert_element_type | solution.py:75
  2.9 1.0 %copy.23 = bf16[4,8,8,512]{3,2,1,0:T(8,128)(2,1)S(1)} copy(bf16[4,8,8,512]{3,1,2,0:T(8,128)(2,1)} %bitcast.85) | data formatting | bytes 524288
  4.1 0.6 gather_fusion
  5.1 0.1 fusion.12
  5.3 3.0 %collective-permute-start = (bf16[512,512]{1,0:T(8,128)(2,1)S(1)}, bf16[512,512]{1,0:T(8,128)(2,1)S(1)}, u32[]{:S(2)}, u32[]{:S(2)}) collective-permute-start(bf16[512,512]{1,0:T(8,128)(2,1)S(1)} %pad_maximum_fusion.5), channel_id=1, source_target_pairs={{0,8},{4,20},{8,0},{12,28},{16,24},{20,4},{24,16},{28,12},{1,9},{5... | collective-permute-start | bytes 1572872 | tf_op jit(solution)/shard_map/ppermute | solution.py:100
  8.4 7.1 %collective-permute-done = bf16[512,512]{1,0:T(8,128)(2,1)S(1)} collective-permute-done((bf16[512,512]{1,0:T(8,128)(2,1)S(1)}, bf16[512,512]{1,0:T(8,128)(2,1)S(1)}, u32[]{:S(2)}, u32[]{:S(2)}) %collective-permute-start) | collective-permute-done | bytes 524320 | tf_op jit(solution)/shard_map/ppermute | solution.py:100
  15.7 2.1 %collective-permute-start.1 = (bf16[768,512]{1,0:T(8,128)(2,1)S(1)}, bf16[768,512]{1,0:T(8,128)(2,1)S(1)}, u32[]{:S(2)}, u32[]{:S(2)}) collective-permute-start(bf16[768,512]{1,0:T(8,128)(2,1)S(1)} %pad_maximum_fusion.3), channel_id=1, source_target_pairs={{0,16},{4,12},{8,24},{12,4},{16,0},{20,28},{24,8},{28,20},{1,17},{... | collective-permute-start | bytes 2359304 | tf_op jit(solution)/shard_map/ppermute | solution.py:100
  17.8 10.0 %collective-permute-done.1 = bf16[768,512]{1,0:T(8,128)(2,1)S(1)} collective-permute-done((bf16[768,512]{1,0:T(8,128)(2,1)S(1)}, bf16[768,512]{1,0:T(8,128)(2,1)S(1)}, u32[]{:S(2)}, u32[]{:S(2)}) %collective-permute-start.1) | collective-permute-done | bytes 786464 | tf_op jit(solution)/shard_map/ppermute | solution.py:100
  28.1 1.2 %pad_maximum_fusion.1 = bf16[1280,512]{1,0:T(8,128)(2,1)} fusion(bf16[256,512]{1,0:T(8,128)(2,1)S(1)} %bitcast.80, bf16[1024,512]{1,0:T(8,128)(2,1)S(1)} %bitcast.66), kind=kLoop, calls=%fused_computation.11 | loop fusion | flops 2621440 | bytes 2621440 | tf_op jit(solution)/shard_map/concatenate | solution.py:99
  29.3 0.8 %dynamic_slice.3 = f32[512]{0:T(512)S(1)} dynamic-slice(f32[4096]{0:T(1024)} %param.11, s32[]{:T(128)S(6)} %select_n.27), dynamic_slice_sizes={512} | dynamic-slice | bytes 4100 | tf_op jit(solution)/shard_map/dynamic_slice | solution.py:119
  30.0 2.5 %collective-permute-done.2 = bf16[1280,512]{1,0:T(8,128)(2,1)S(1)} collective-permute-done((bf16[1280,512]{1,0:T(8,128)(2,1)}, bf16[1280,512]{1,0:T(8,128)(2,1)S(1)}, u32[]{:S(2)}, u32[]{:S(2)}) %collective-permute-start.2) | collective-permute-done | bytes 1310752 | tf_op jit(solution)/shard_map/ppermute | solution.py:100
  32.6 0.6 gather_fusion.1
  33.7 0.2 pad_maximum_fusion
  33.9 0.2 copy-done.2
  34.1 2.8 %fusion = (f32[2048]{0:T(1024)S(1)}, f32[2048,512]{1,0:T(8,128)}) fusion(f32[512]{0:T(512)S(1)} %add_sqrt_fusion.1, bf16[256,512]{1,0:T(8,128)(2,1)S(1)} %bitcast.91, bf16[2048,512]{1,0:T(8,128)(2,1)S(1)} %bitcast.72), kind=kOutput, calls=%fused_computation.6 | convolution fusion | flops 540014592 | bytes 5515264 | tf_op jit(solution)/shard_map/dot_general | solution.py:123
  36.9 3.1 %fusion.1 = (f32[2048]{0:T(1024)S(1)}, f32[512]{0:T(512)S(1)}, f32[2048,512]{1,0:T(8,128)}) fusion(f32[512]{0:T(512)S(1)} %dynamic_slice.3, f32[512]{0:T(512)S(1)} %add_sqrt_fusion, bf16[256,512]{1,0:T(8,128)(2,1)S(1)} %bitcast.93, bf16[2048,512]{1,0:T(8,128)(2,1)S(1)} %bitcast.73), kind=kOutput, calls=%fused_computation.7 | convolution fusion | flops 542111232 | bytes 5519360 | tf_op jit(solution)/shard_map/dot_general | solution.py:122
  40.0 2.0 %collective-permute-start.3 = (f32[2,2048]{1,0:T(2,128)S(1)}, f32[2,2048]{1,0:T(2,128)S(1)}, u32[]{:S(2)}, u32[]{:S(2)}) collective-permute-start(f32[2,2048]{1,0:T(2,128)S(1)} %pad_maximum_fusion.9), channel_id=1, source_target_pairs={{0,8},{4,20},{8,0},{12,28},{16,24},{20,4},{24,16},{28,12},{1,9},{5... | collective-permute-start | bytes 49160 | tf_op jit(solution)/shard_map/ppermute | solution.py:133
  42.0 1.8 %collective-permute-done.3 = f32[2,2048]{1,0:T(2,128)S(1)} collective-permute-done((f32[2,2048]{1,0:T(2,128)S(1)}, f32[2,2048]{1,0:T(2,128)S(1)}, u32[]{:S(2)}, u32[]{:S(2)}) %collective-permute-start.3) | collective-permute-done | bytes 16416 | tf_op jit(solution)/shard_map/ppermute | solution.py:133
  44.0 2.1 %collective-permute-start.4 = (f32[2,2048]{1,0:T(2,128)S(1)}, f32[2,2048]{1,0:T(2,128)S(1)}, u32[]{:S(2)}, u32[]{:S(2)}) collective-permute-start(f32[2,2048]{1,0:T(2,128)S(1)} %fusion.17), channel_id=1, source_target_pairs={{0,16},{4,12},{8,24},{12,4},{16,0},{20,28},{24,8},{28,20},{1,17},{... | collective-permute-start | bytes 49160 | tf_op jit(solution)/shard_map/ppermute | solution.py:133
  46.1 1.7 %collective-permute-done.4 = f32[2,2048]{1,0:T(2,128)S(1)} collective-permute-done((f32[2,2048]{1,0:T(2,128)S(1)}, f32[2,2048]{1,0:T(2,128)S(1)}, u32[]{:S(2)}, u32[]{:S(2)}) %collective-permute-start.4) | collective-permute-done | bytes 16416 | tf_op jit(solution)/shard_map/ppermute | solution.py:133
  48.0 0.8 %fusion.16 = (bf16[512]{0:T(512)(128)(2,1)S(1)}, bf16[512]{0:T(512)(128)(2,1)S(1)}) fusion(f32[512]{0:T(512)S(1)} %get-tuple-element.5, f32[4096]{0:T(1024)} %param.11, s32[]{:T(128)S(6)} %select_n.27), kind=kLoop, calls=%fused_computation.69 | loop fusion | flops 3584 | bytes 6148 | tf_op jit(solution)/shard_map/convert_element_type | solution.py:145
  48.8 0.4 collective-permute-done.5
  49.3 2.1 %collective-permute-start.6 = (f32[2,2048]{1,0:T(2,128)S(1)}, f32[2,2048]{1,0:T(2,128)S(1)}, u32[]{:S(2)}, u32[]{:S(2)}) collective-permute-start(f32[2,2048]{1,0:T(2,128)S(1)} %add.83), channel_id=1, source_target_pairs={{0,1},{1,2},{2,3},{3,0},{4,5},{5,6},{6,7},{7,4},{8,9},{9,10},{10,1... | collective-permute-start | bytes 49160 | tf_op jit(solution)/shard_map/ppermute | solution.py:58
  51.4 2.6 %collective-permute-start.7 = (f32[2,2048]{1,0:T(2,128)S(1)}, f32[2,2048]{1,0:T(2,128)S(1)}, u32[]{:S(2)}, u32[]{:S(2)}) collective-permute-start(f32[2,2048]{1,0:T(2,128)S(1)} %add.83), channel_id=1, source_target_pairs={{0,2},{1,3},{2,0},{3,1},{4,6},{5,7},{6,4},{7,5},{8,10},{9,11},{10,... | collective-permute-start | bytes 49160 | tf_op jit(solution)/shard_map/ppermute | solution.py:58
  54.0 1.4 %collective-permute-start.8 = (f32[2,2048]{1,0:T(2,128)S(1)}, f32[2,2048]{1,0:T(2,128)S(1)}, u32[]{:S(2)}, u32[]{:S(2)}) collective-permute-start(f32[2,2048]{1,0:T(2,128)S(1)} %add.83), channel_id=1, source_target_pairs={{0,3},{1,0},{2,1},{3,2},{4,7},{5,4},{6,5},{7,6},{8,11},{9,8},{10,9... | collective-permute-start | bytes 49160 | tf_op jit(solution)/shard_map/ppermute | solution.py:58
  55.4 0.9 %collective-permute-done.7 = f32[2,2048]{1,0:T(2,128)S(1)} collective-permute-done((f32[2,2048]{1,0:T(2,128)S(1)}, f32[2,2048]{1,0:T(2,128)S(1)}, u32[]{:S(2)}, u32[]{:S(2)}) %collective-permute-start.7) | collective-permute-done | bytes 16416 | tf_op jit(solution)/shard_map/ppermute | solution.py:58
  56.3 1.4 %collective-permute-done.8 = f32[2,2048]{1,0:T(2,128)S(1)} collective-permute-done((f32[2,2048]{1,0:T(2,128)S(1)}, f32[2,2048]{1,0:T(2,128)S(1)}, u32[]{:S(2)}, u32[]{:S(2)}) %collective-permute-start.8) | collective-permute-done | bytes 16416 | tf_op jit(solution)/shard_map/ppermute | solution.py:58
  57.8 4.6 %multiply_reduce_fusion = (f32[512]{0:T(512)S(1)}, bf16[2048,512]{1,0:T(8,128)(2,1)S(1)}) fusion(f32[2048,512]{1,0:T(8,128)} %get-tuple-element.34, f32[2048]{0:T(1024)S(1)} %bitcast.102, f32[2048,512]{1,0:T(8,128)} %get-tuple-element.32, f32[512]{0:T(512)S(1)} %dynamic_slice.3, f32[2048]{0:T(1024)S(1)} %bitcast.101), kind=kLoop, calls=%fused_computation.2 | loop fusion | flops 11533824 | bytes 10506240 | tf_op jit(solution)/shard_map/reduce_sum | solution.py:140
  62.4 0.7 fusion.3
  63.2 11.2 %all_to_all.4 = bf16[8,34,512]{2,1,0:T(8,128)(2,1)S(1)} all-to-all(bf16[8,34,512]{2,1,0:T(8,128)(2,1)S(1)} %pad_maximum_fusion.8), channel_id=1, replica_groups=mesh['dp'=8,'tensor'=4] {'dp'}, dimensions={0} | all-to-all | bytes 557056 | tf_op jit(solution)/shard_map/all_to_all | solution.py:154
  74.5 0.6 slice_add_fusion
  75.1 0.8 %copy.25 = f32[4,8,8,512]{3,1,2,0:T(8,128)} copy(f32[4,8,8,512]{3,1,0,2:T(8,128)S(1)} %slice_bitcast_fusion.1) | data formatting | bytes 1048576
  (68 shorter events, 2.4 us)
Async XLA Ops:
  0.6 4.2 %copy-start.1 = (bf16[256,256]{1,0:T(8,128)(2,1)S(1)}, bf16[256,256]{1,0:T(8,128)(2,1)}, u32[]{:S(2)}) copy-start(bf16[256,256]{1,0:T(8,128)(2,1)} %param.10) | copy-start | bytes 393220
  0.6 4.4 %copy-start = (bf16[256,256]{1,0:T(8,128)(2,1)S(1)}, bf16[256,256]{1,0:T(8,128)(2,1)}, u32[]{:S(2)}) copy-start(bf16[256,256]{1,0:T(8,128)(2,1)} %param.9) | copy-start | bytes 393220
  5.3 10.2 %collective-permute-start = (bf16[512,512]{1,0:T(8,128)(2,1)S(1)}, bf16[512,512]{1,0:T(8,128)(2,1)S(1)}, u32[]{:S(2)}, u32[]{:S(2)}) collective-permute-start(bf16[512,512]{1,0:T(8,128)(2,1)S(1)} %pad_maximum_fusion.5), channel_id=1, source_target_pairs={{0,8},{4,20},{8,0},{12,28},{16,24},{20,4},{24,16},{28,12},{1,9},{5... | collective-permute-start | bytes 1572872 | tf_op jit(solution)/shard_map/ppermute | solution.py:100
  15.7 12.1 %collective-permute-start.1 = (bf16[768,512]{1,0:T(8,128)(2,1)S(1)}, bf16[768,512]{1,0:T(8,128)(2,1)S(1)}, u32[]{:S(2)}, u32[]{:S(2)}) collective-permute-start(bf16[768,512]{1,0:T(8,128)(2,1)S(1)} %pad_maximum_fusion.3), channel_id=1, source_target_pairs={{0,16},{4,12},{8,24},{12,4},{16,0},{20,28},{24,8},{28,20},{1,17},{... | collective-permute-start | bytes 2359304 | tf_op jit(solution)/shard_map/ppermute | solution.py:100
  29.3 3.2 %collective-permute-start.2 = (bf16[1280,512]{1,0:T(8,128)(2,1)}, bf16[1280,512]{1,0:T(8,128)(2,1)S(1)}, u32[]{:S(2)}, u32[]{:S(2)}) collective-permute-start(bf16[1280,512]{1,0:T(8,128)(2,1)} %pad_maximum_fusion.1), channel_id=1, source_target_pairs={{0,4},{4,0},{8,12},{12,8},{16,20},{20,16},{24,28},{28,24},{1,5},{5... | collective-permute-start | bytes 3932168 | tf_op jit(solution)/shard_map/ppermute | solution.py:100
  33.4 0.7 copy-start.2
  40.0 3.8 %collective-permute-start.3 = (f32[2,2048]{1,0:T(2,128)S(1)}, f32[2,2048]{1,0:T(2,128)S(1)}, u32[]{:S(2)}, u32[]{:S(2)}) collective-permute-start(f32[2,2048]{1,0:T(2,128)S(1)} %pad_maximum_fusion.9), channel_id=1, source_target_pairs={{0,8},{4,20},{8,0},{12,28},{16,24},{20,4},{24,16},{28,12},{1,9},{5... | collective-permute-start | bytes 49160 | tf_op jit(solution)/shard_map/ppermute | solution.py:133
  44.0 3.8 %collective-permute-start.4 = (f32[2,2048]{1,0:T(2,128)S(1)}, f32[2,2048]{1,0:T(2,128)S(1)}, u32[]{:S(2)}, u32[]{:S(2)}) collective-permute-start(f32[2,2048]{1,0:T(2,128)S(1)} %fusion.17), channel_id=1, source_target_pairs={{0,16},{4,12},{8,24},{12,4},{16,0},{20,28},{24,8},{28,20},{1,17},{... | collective-permute-start | bytes 49160 | tf_op jit(solution)/shard_map/ppermute | solution.py:133
  47.9 1.2 %collective-permute-start.5 = (f32[2,2048]{1,0:T(2,128)S(1)}, f32[2,2048]{1,0:T(2,128)S(1)}, u32[]{:S(2)}, u32[]{:S(2)}) collective-permute-start(f32[2,2048]{1,0:T(2,128)S(1)} %fusion.28), channel_id=1, source_target_pairs={{0,4},{4,0},{8,12},{12,8},{16,20},{20,16},{24,28},{28,24},{1,5},{5... | collective-permute-start | bytes 49160 | tf_op jit(solution)/shard_map/ppermute | solution.py:130
  49.3 6.1 %collective-permute-start.6 = (f32[2,2048]{1,0:T(2,128)S(1)}, f32[2,2048]{1,0:T(2,128)S(1)}, u32[]{:S(2)}, u32[]{:S(2)}) collective-permute-start(f32[2,2048]{1,0:T(2,128)S(1)} %add.83), channel_id=1, source_target_pairs={{0,1},{1,2},{2,3},{3,0},{4,5},{5,6},{6,7},{7,4},{8,9},{9,10},{10,1... | collective-permute-start | bytes 49160 | tf_op jit(solution)/shard_map/ppermute | solution.py:58
  51.4 4.9 %collective-permute-start.7 = (f32[2,2048]{1,0:T(2,128)S(1)}, f32[2,2048]{1,0:T(2,128)S(1)}, u32[]{:S(2)}, u32[]{:S(2)}) collective-permute-start(f32[2,2048]{1,0:T(2,128)S(1)} %add.83), channel_id=1, source_target_pairs={{0,2},{1,3},{2,0},{3,1},{4,6},{5,7},{6,4},{7,5},{8,10},{9,11},{10,... | collective-permute-start | bytes 49160 | tf_op jit(solution)/shard_map/ppermute | solution.py:58
  54.0 3.7 %collective-permute-start.8 = (f32[2,2048]{1,0:T(2,128)S(1)}, f32[2,2048]{1,0:T(2,128)S(1)}, u32[]{:S(2)}, u32[]{:S(2)}) collective-permute-start(f32[2,2048]{1,0:T(2,128)S(1)} %add.83), channel_id=1, source_target_pairs={{0,3},{1,0},{2,1},{3,2},{4,7},{5,4},{6,5},{7,6},{8,11},{9,8},{10,9... | collective-permute-start | bytes 49160 | tf_op jit(solution)/shard_map/ppermute | solution.py:58
  57.8 4.6 %copy-start.3 = (bf16[8,32,512]{2,1,0:T(8,128)(2,1)S(1)}, bf16[8,32,512]{2,1,0:T(8,128)(2,1)}, u32[]{:S(2)}) copy-start(bf16[8,32,512]{2,1,0:T(8,128)(2,1)} %copy-done.2) | copy-start | bytes 786436

commit v11 on v10

--- a/solution.py
+++ b/solution.py
@@ -137,11 +137,12 @@
     t_total, s_total = totals[0][:, None], totals[1][:, None]
     part_center = 0.5 * c + 0.5 * (jnp.sum(t_cos, 0) / (images * n))
     dlog = ((s_exp / s_total - t_exp / t_total) / 0.1).astype(jnp.bfloat16)
-    scaled = jnp.sum(dlog.astype(jnp.float32) * s_cos, 0) / s_norm
     product = lax.dot_general(
         zs, dlog, (((0,), (0,)), ((), ())), preferred_element_type=jnp.float32
     )
-    grad = (product - sw.astype(jnp.float32) * scaled) / s_norm
+    wide = sw.astype(jnp.float32)
+    scaled = jnp.sum(wide * product, 0) / s_norm / s_norm
+    grad = (product - wide * scaled) / s_norm
     high = part_center.astype(jnp.bfloat16)
     low = (part_center - high.astype(jnp.float32)).astype(jnp.bfloat16)
     sent = jnp.concatenate(

time: 76.2 us -> 76.3 us (level)
  matrix products: 6.62 us -> 11.2 us
  other arithmetic: 10.8 us -> 6.37 us
    reduce_sum x1 -> x0, other arithmetic: 4.56 us -> none  [feature_plan(): scaled = jnp.sum(dlog.astype(jnp.float32) * s_cos, 0) / s_norm]
    dot_general x1, matrix products: 0.74 us -> 5.09 us  [feature_plan(): lax.dot_general(zs, dlog, (((0,), (0,)), ((), ())), preferred_element_typ...]
where the time goes in v11:
time: 76.3 us; the launch traced here: 76 us
  waiting for transfers between devices  25.8 us (34%)
  starting transfers between devices  15.4 us (20%)
  matrix products  11.2 us (15%)
  blocking collectives  11.2 us (15%)
  other arithmetic  6.37 us (8%)
  local copies, waits for them, and re-layouts  5 us (7%)
  between operations  1.11 us (1%)
    ppermute x3, waiting for transfers between devices, feature_plan(): got = lax.ppermute(payload, 'dp', pairs)  19.6 us
    all_to_all x1, blocking collectives, feature_plan(): got = lax.all_to_all(sent, 'dp', 0, 2, tiled=True)  11.2 us
    ppermute x3, starting transfers between devices, exchange_all(): total = total + lax.ppermute(x, axis, [(i, (i + k) % n) for i in range(n)])  6.06 us
    ppermute x3, starting transfers between devices, feature_plan(): got = lax.ppermute(payload, 'dp', pairs)  5.12 us
    dot_general x1, matrix products, feature_plan(): lax.dot_general(zs, dlog, (((0,), (0,)), ((), ())), preferred_element_typ...  5.09 us
    ppermute x2, starting transfers between devices, feature_plan(): got = lax.ppermute(totals, 'dp', swap(up[r], down[r])).reshape(shape)  4.12 us
    ppermute x2, waiting for transfers between devices, feature_plan(): got = lax.ppermute(totals, 'dp', swap(up[r], down[r])).reshape(shape)  3.48 us
    dot_general x1, matrix products, feature_plan(): t_cos = jnp.dot(zt, tw, preferred_element_type=jnp.float32) / t_norm  3.17 us
  transfers between devices with their start and end apart: 9, of which 8 were waited for; matrix products, arithmetic and copies ran while one was open for 2% of the time, Pallas kernels for 0%

profile of v11, /device:TPU:0, one launch (start us, length us, event | category | flops | bytes accessed | tf_op | source)
XLA Modules:
  0.0 76.0 jit_solution(314487377995135101)
XLA Ops:
  0.7 2.0 %fusion.24 = (bf16[32,4096]{1,0:T(8,128)(2,1)S(1)}, f32[32,4096]{1,0:T(8,128)}) fusion(bf16[32,4096]{1,0:T(8,128)(2,1)} %param.8, f32[32,4096]{1,0:T(8,128)} %param.7), kind=kLoop, calls=%fused_computation.76 | loop fusion | flops 655360 | bytes 1572864 | tf_op jit(solution)/shard_map/convert_element_type | solution.py:75
  2.9 1.0 %copy.27 = bf16[4,8,8,512]{3,2,1,0:T(8,128)(2,1)S(1)} copy(bf16[4,8,8,512]{3,1,2,0:T(8,128)(2,1)} %bitcast.87) | data formatting | bytes 524288
  4.1 0.6 gather_fusion
  5.1 0.1 fusion.14
  5.3 3.0 %collective-permute-start = (bf16[512,512]{1,0:T(8,128)(2,1)S(1)}, bf16[512,512]{1,0:T(8,128)(2,1)S(1)}, u32[]{:S(2)}, u32[]{:S(2)}) collective-permute-start(bf16[512,512]{1,0:T(8,128)(2,1)S(1)} %pad_maximum_fusion.5), channel_id=1, source_target_pairs={{0,8},{4,20},{8,0},{12,28},{16,24},{20,4},{24,16},{28,12},{1,9},{5... | collective-permute-start | bytes 1572872 | tf_op jit(solution)/shard_map/ppermute | solution.py:100
  8.4 7.1 %collective-permute-done = bf16[512,512]{1,0:T(8,128)(2,1)S(1)} collective-permute-done((bf16[512,512]{1,0:T(8,128)(2,1)S(1)}, bf16[512,512]{1,0:T(8,128)(2,1)S(1)}, u32[]{:S(2)}, u32[]{:S(2)}) %collective-permute-start) | collective-permute-done | bytes 524320 | tf_op jit(solution)/shard_map/ppermute | solution.py:100
  15.7 2.1 %collective-permute-start.1 = (bf16[768,512]{1,0:T(8,128)(2,1)S(1)}, bf16[768,512]{1,0:T(8,128)(2,1)S(1)}, u32[]{:S(2)}, u32[]{:S(2)}) collective-permute-start(bf16[768,512]{1,0:T(8,128)(2,1)S(1)} %pad_maximum_fusion.3), channel_id=1, source_target_pairs={{0,16},{4,12},{8,24},{12,4},{16,0},{20,28},{24,8},{28,20},{1,17},{... | collective-permute-start | bytes 2359304 | tf_op jit(solution)/shard_map/ppermute | solution.py:100
  17.8 10.0 %collective-permute-done.1 = bf16[768,512]{1,0:T(8,128)(2,1)S(1)} collective-permute-done((bf16[768,512]{1,0:T(8,128)(2,1)S(1)}, bf16[768,512]{1,0:T(8,128)(2,1)S(1)}, u32[]{:S(2)}, u32[]{:S(2)}) %collective-permute-start.1) | collective-permute-done | bytes 786464 | tf_op jit(solution)/shard_map/ppermute | solution.py:100
  28.0 0.1 fusion.23
  28.1 1.2 %pad_maximum_fusion.1 = bf16[1280,512]{1,0:T(8,128)(2,1)} fusion(bf16[256,512]{1,0:T(8,128)(2,1)S(1)} %bitcast.81, bf16[1024,512]{1,0:T(8,128)(2,1)S(1)} %bitcast.67), kind=kLoop, calls=%fused_computation.9 | loop fusion | flops 2621440 | bytes 2621440 | tf_op jit(solution)/shard_map/concatenate | solution.py:99
  29.3 0.8 dynamic_slice.3
  30.0 2.5 %collective-permute-done.2 = bf16[1280,512]{1,0:T(8,128)(2,1)S(1)} collective-permute-done((bf16[1280,512]{1,0:T(8,128)(2,1)}, bf16[1280,512]{1,0:T(8,128)(2,1)S(1)}, u32[]{:S(2)}, u32[]{:S(2)}) %collective-permute-start.2) | collective-permute-done | bytes 1310752 | tf_op jit(solution)/shard_map/ppermute | solution.py:100
  32.6 0.6 gather_fusion.1
  33.7 0.2 pad_maximum_fusion
  33.9 0.2 copy-done
  34.1 2.9 %fusion.29 = (f32[2048]{0:T(1024)S(1)}, f32[2048,512]{0,1:T(8,128)}) fusion(f32[512]{0:T(512)S(1)} %add_sqrt_fusion.1, bf16[256,512]{1,0:T(8,128)(2,1)S(1)} %bitcast.90, bf16[2048,512]{1,0:T(8,128)(2,1)S(1)} %bitcast.73), kind=kOutput, calls=%fused_computation.81 | convolution fusion | flops 540014592 | bytes 5515264 | tf_op jit(solution)/shard_map/dot_general | solution.py:123
  37.0 3.2 %fusion = (f32[2048]{0:T(1024)S(1)}, f32[512]{0:T(512)S(1)}, f32[2048,512]{0,1:T(8,128)}) fusion(f32[512]{0:T(512)S(1)} %dynamic_slice.3, f32[512]{0:T(512)S(1)} %add_sqrt_fusion, bf16[256,512]{1,0:T(8,128)(2,1)S(1)} %bitcast.93, bf16[2048,512]{1,0:T(8,128)(2,1)S(1)} %bitcast.74), kind=kOutput, calls=%fused_computation.5 | convolution fusion | flops 542111232 | bytes 5519360 | tf_op jit(solution)/shard_map/dot_general | solution.py:122
  40.2 2.0 %collective-permute-start.3 = (f32[2,2048]{1,0:T(2,128)S(1)}, f32[2,2048]{1,0:T(2,128)S(1)}, u32[]{:S(2)}, u32[]{:S(2)}) collective-permute-start(f32[2,2048]{1,0:T(2,128)S(1)} %pad_maximum_fusion.9), channel_id=1, source_target_pairs={{0,8},{4,20},{8,0},{12,28},{16,24},{20,4},{24,16},{28,12},{1,9},{5... | collective-permute-start | bytes 49160 | tf_op jit(solution)/shard_map/ppermute | solution.py:133
  42.3 1.8 %collective-permute-done.3 = f32[2,2048]{1,0:T(2,128)S(1)} collective-permute-done((f32[2,2048]{1,0:T(2,128)S(1)}, f32[2,2048]{1,0:T(2,128)S(1)}, u32[]{:S(2)}, u32[]{:S(2)}) %collective-permute-start.3) | collective-permute-done | bytes 16416 | tf_op jit(solution)/shard_map/ppermute | solution.py:133
  44.2 2.1 %collective-permute-start.4 = (f32[2,2048]{1,0:T(2,128)S(1)}, f32[2,2048]{1,0:T(2,128)S(1)}, u32[]{:S(2)}, u32[]{:S(2)}) collective-permute-start(f32[2,2048]{1,0:T(2,128)S(1)} %fusion.21), channel_id=1, source_target_pairs={{0,16},{4,12},{8,24},{12,4},{16,0},{20,28},{24,8},{28,20},{1,17},{... | collective-permute-start | bytes 49160 | tf_op jit(solution)/shard_map/ppermute | solution.py:133
  46.3 1.7 %collective-permute-done.4 = f32[2,2048]{1,0:T(2,128)S(1)} collective-permute-done((f32[2,2048]{1,0:T(2,128)S(1)}, f32[2,2048]{1,0:T(2,128)S(1)}, u32[]{:S(2)}, u32[]{:S(2)}) %collective-permute-start.4) | collective-permute-done | bytes 16416 | tf_op jit(solution)/shard_map/ppermute | solution.py:133
  48.2 0.8 %fusion.18 = (bf16[512]{0:T(512)(128)(2,1)S(1)}, bf16[512]{0:T(512)(128)(2,1)S(1)}) fusion(f32[512]{0:T(512)S(1)} %get-tuple-element.5, f32[4096]{0:T(1024)} %param.11, s32[]{:T(128)S(6)} %select_n.27), kind=kLoop, calls=%fused_computation.70 | loop fusion | flops 3584 | bytes 6148 | tf_op jit(solution)/shard_map/convert_element_type | solution.py:146
  49.0 0.4 collective-permute-done.5
  49.5 2.1 %collective-permute-start.6 = (f32[2,2048]{1,0:T(2,128)S(1)}, f32[2,2048]{1,0:T(2,128)S(1)}, u32[]{:S(2)}, u32[]{:S(2)}) collective-permute-start(f32[2,2048]{1,0:T(2,128)S(1)} %add.83), channel_id=1, source_target_pairs={{0,1},{1,2},{2,3},{3,0},{4,5},{5,6},{6,7},{7,4},{8,9},{9,10},{10,1... | collective-permute-start | bytes 49160 | tf_op jit(solution)/shard_map/ppermute | solution.py:58
  51.6 2.6 %collective-permute-start.7 = (f32[2,2048]{1,0:T(2,128)S(1)}, f32[2,2048]{1,0:T(2,128)S(1)}, u32[]{:S(2)}, u32[]{:S(2)}) collective-permute-start(f32[2,2048]{1,0:T(2,128)S(1)} %add.83), channel_id=1, source_target_pairs={{0,2},{1,3},{2,0},{3,1},{4,6},{5,7},{6,4},{7,5},{8,10},{9,11},{10,... | collective-permute-start | bytes 49160 | tf_op jit(solution)/shard_map/ppermute | solution.py:58
  54.2 1.3 %collective-permute-start.8 = (f32[2,2048]{1,0:T(2,128)S(1)}, f32[2,2048]{1,0:T(2,128)S(1)}, u32[]{:S(2)}, u32[]{:S(2)}) collective-permute-start(f32[2,2048]{1,0:T(2,128)S(1)} %add.83), channel_id=1, source_target_pairs={{0,3},{1,0},{2,1},{3,2},{4,7},{5,4},{6,5},{7,6},{8,11},{9,8},{10,9... | collective-permute-start | bytes 49160 | tf_op jit(solution)/shard_map/ppermute | solution.py:58
  55.6 0.9 %collective-permute-done.7 = f32[2,2048]{1,0:T(2,128)S(1)} collective-permute-done((f32[2,2048]{1,0:T(2,128)S(1)}, f32[2,2048]{1,0:T(2,128)S(1)}, u32[]{:S(2)}, u32[]{:S(2)}) %collective-permute-start.7) | collective-permute-done | bytes 16416 | tf_op jit(solution)/shard_map/ppermute | solution.py:58
  56.5 1.4 %collective-permute-done.8 = f32[2,2048]{1,0:T(2,128)S(1)} collective-permute-done((f32[2,2048]{1,0:T(2,128)S(1)}, f32[2,2048]{1,0:T(2,128)S(1)}, u32[]{:S(2)}, u32[]{:S(2)}) %collective-permute-start.8) | collective-permute-done | bytes 16416 | tf_op jit(solution)/shard_map/ppermute | solution.py:58
  58.0 5.1 %fusion.7 = (f32[512]{0:T(512)S(1)}, f32[256,512]{1,0:T(8,128)S(1)}) fusion(bf16[8,32,512]{2,1,0:T(8,128)(2,1)S(1)} %copy-done.1, f32[2048,512]{0,1:T(8,128)} %get-tuple-element.32, f32[2048,512]{0,1:T(8,128)} %get-tuple-element.30, f32[2048]{0:T(1024)S(1)} %bitcast.103, f32[2048]{0:T(1024)S(1)} %bitcast.102, f32[512]{0:T(512)S(1)} %dynamic_slice.3, ...), kind=kOutput, calls=%fused_computation.24 | convolution fusion | flops 544603648 | bytes 10244096 | tf_op jit(solution)/shard_map/dot_general | solution.py:140
  63.3 11.2 %all_to_all.4 = bf16[8,34,512]{2,1,0:T(8,128)(2,1)S(1)} all-to-all(bf16[8,34,512]{2,1,0:T(8,128)(2,1)S(1)} %pad_maximum_fusion.8), channel_id=1, replica_groups=mesh['dp'=8,'tensor'=4] {'dp'}, dimensions={0} | all-to-all | bytes 557056 | tf_op jit(solution)/shard_map/all_to_all | solution.py:155
  74.6 0.6 slice_add_fusion
  75.2 0.8 %copy.29 = f32[4,8,8,512]{3,1,2,0:T(8,128)} copy(f32[4,8,8,512]{3,1,0,2:T(8,128)S(1)} %slice_bitcast_fusion.1) | data formatting | bytes 1048576
  (68 shorter events, 2.4 us)
Async XLA Ops:
  0.6 4.2 %copy-start.3 = (bf16[256,256]{1,0:T(8,128)(2,1)S(1)}, bf16[256,256]{1,0:T(8,128)(2,1)}, u32[]{:S(2)}) copy-start(bf16[256,256]{1,0:T(8,128)(2,1)} %param.10) | copy-start | bytes 393220
  0.6 4.4 %copy-start.2 = (bf16[256,256]{1,0:T(8,128)(2,1)S(1)}, bf16[256,256]{1,0:T(8,128)(2,1)}, u32[]{:S(2)}) copy-start(bf16[256,256]{1,0:T(8,128)(2,1)} %param.9) | copy-start | bytes 393220
  5.3 10.2 %collective-permute-start = (bf16[512,512]{1,0:T(8,128)(2,1)S(1)}, bf16[512,512]{1,0:T(8,128)(2,1)S(1)}, u32[]{:S(2)}, u32[]{:S(2)}) collective-permute-start(bf16[512,512]{1,0:T(8,128)(2,1)S(1)} %pad_maximum_fusion.5), channel_id=1, source_target_pairs={{0,8},{4,20},{8,0},{12,28},{16,24},{20,4},{24,16},{28,12},{1,9},{5... | collective-permute-start | bytes 1572872 | tf_op jit(solution)/shard_map/ppermute | solution.py:100
  15.7 12.1 %collective-permute-start.1 = (bf16[768,512]{1,0:T(8,128)(2,1)S(1)}, bf16[768,512]{1,0:T(8,128)(2,1)S(1)}, u32[]{:S(2)}, u32[]{:S(2)}) collective-permute-start(bf16[768,512]{1,0:T(8,128)(2,1)S(1)} %pad_maximum_fusion.3), channel_id=1, source_target_pairs={{0,16},{4,12},{8,24},{12,4},{16,0},{20,28},{24,8},{28,20},{1,17},{... | collective-permute-start | bytes 2359304 | tf_op jit(solution)/shard_map/ppermute | solution.py:100
  29.3 3.2 %collective-permute-start.2 = (bf16[1280,512]{1,0:T(8,128)(2,1)}, bf16[1280,512]{1,0:T(8,128)(2,1)S(1)}, u32[]{:S(2)}, u32[]{:S(2)}) collective-permute-start(bf16[1280,512]{1,0:T(8,128)(2,1)} %pad_maximum_fusion.1), channel_id=1, source_target_pairs={{0,4},{4,0},{8,12},{12,8},{16,20},{20,16},{24,28},{28,24},{1,5},{5... | collective-permute-start | bytes 3932168 | tf_op jit(solution)/shard_map/ppermute | solution.py:100
  33.4 0.7 copy-start
  37.0 21.0 %copy-start.1 = (bf16[8,32,512]{2,1,0:T(8,128)(2,1)S(1)}, bf16[8,32,512]{2,1,0:T(8,128)(2,1)}, u32[]{:S(2)}) copy-start(bf16[8,32,512]{2,1,0:T(8,128)(2,1)} %copy-done) | copy-start | bytes 786436
  40.2 3.8 %collective-permute-start.3 = (f32[2,2048]{1,0:T(2,128)S(1)}, f32[2,2048]{1,0:T(2,128)S(1)}, u32[]{:S(2)}, u32[]{:S(2)}) collective-permute-start(f32[2,2048]{1,0:T(2,128)S(1)} %pad_maximum_fusion.9), channel_id=1, source_target_pairs={{0,8},{4,20},{8,0},{12,28},{16,24},{20,4},{24,16},{28,12},{1,9},{5... | collective-permute-start | bytes 49160 | tf_op jit(solution)/shard_map/ppermute | solution.py:133
  44.2 3.8 %collective-permute-start.4 = (f32[2,2048]{1,0:T(2,128)S(1)}, f32[2,2048]{1,0:T(2,128)S(1)}, u32[]{:S(2)}, u32[]{:S(2)}) collective-permute-start(f32[2,2048]{1,0:T(2,128)S(1)} %fusion.21), channel_id=1, source_target_pairs={{0,16},{4,12},{8,24},{12,4},{16,0},{20,28},{24,8},{28,20},{1,17},{... | collective-permute-start | bytes 49160 | tf_op jit(solution)/shard_map/ppermute | solution.py:133
  48.1 1.2 %collective-permute-start.5 = (f32[2,2048]{1,0:T(2,128)S(1)}, f32[2,2048]{1,0:T(2,128)S(1)}, u32[]{:S(2)}, u32[]{:S(2)}) collective-permute-start(f32[2,2048]{1,0:T(2,128)S(1)} %fusion.32), channel_id=1, source_target_pairs={{0,4},{4,0},{8,12},{12,8},{16,20},{20,16},{24,28},{28,24},{1,5},{5... | collective-permute-start | bytes 49160 | tf_op jit(solution)/shard_map/ppermute | solution.py:130
  49.5 6.1 %collective-permute-start.6 = (f32[2,2048]{1,0:T(2,128)S(1)}, f32[2,2048]{1,0:T(2,128)S(1)}, u32[]{:S(2)}, u32[]{:S(2)}) collective-permute-start(f32[2,2048]{1,0:T(2,128)S(1)} %add.83), channel_id=1, source_target_pairs={{0,1},{1,2},{2,3},{3,0},{4,5},{5,6},{6,7},{7,4},{8,9},{9,10},{10,1... | collective-permute-start | bytes 49160 | tf_op jit(solution)/shard_map/ppermute | solution.py:58
  51.6 4.9 %collective-permute-start.7 = (f32[2,2048]{1,0:T(2,128)S(1)}, f32[2,2048]{1,0:T(2,128)S(1)}, u32[]{:S(2)}, u32[]{:S(2)}) collective-permute-start(f32[2,2048]{1,0:T(2,128)S(1)} %add.83), channel_id=1, source_target_pairs={{0,2},{1,3},{2,0},{3,1},{4,6},{5,7},{6,4},{7,5},{8,10},{9,11},{10,... | collective-permute-start | bytes 49160 | tf_op jit(solution)/shard_map/ppermute | solution.py:58
  54.2 3.7 %collective-permute-start.8 = (f32[2,2048]{1,0:T(2,128)S(1)}, f32[2,2048]{1,0:T(2,128)S(1)}, u32[]{:S(2)}, u32[]{:S(2)}) collective-permute-start(f32[2,2048]{1,0:T(2,128)S(1)} %add.83), channel_id=1, source_target_pairs={{0,3},{1,0},{2,1},{3,2},{4,7},{5,4},{6,5},{7,6},{8,11},{9,8},{10,9... | collective-permute-start | bytes 49160 | tf_op jit(solution)/shard_map/ppermute | solution.py:58

commit v12 on v11

--- a/solution.py
+++ b/solution.py
@@ -97,7 +97,13 @@
         if 2 * bot == cols:
             flat_feats = feats.reshape(-1, 2 * bot)
             payload = jnp.concatenate([flat_feats, away.reshape(-1, cols)], axis=0)
-            got = lax.ppermute(payload, "dp", pairs)
+            if last:
+                got = lax.ppermute(payload, "dp", pairs)
+            else:
+                cut = payload.shape[0] // 2
+                got = jnp.concatenate(
+                    [lax.ppermute(payload[:cut], "dp", pairs), lax.ppermute(payload[cut:], "dp", pairs)]
+                )
             got_feats = got[: flat_feats.shape[0]].reshape(feats.shape)
             got_held = got[flat_feats.shape[0]:].reshape(away.shape)
         else:

time: 76.3 us -> 76.9 us (level)
  waiting for transfers between devices: 25.8 us -> 27.2 us
  starting transfers between devices: 15.4 us -> 14.6 us
    ppermute x3 -> x1, waiting for transfers between devices: 19.6 us -> 2.48 us  [feature_plan(): got = lax.ppermute(payload, 'dp', pairs)]
    ppermute x0 -> x4, waiting for transfers between devices: none -> 16.3 us  [the longest x2 9.48 us: feature_plan(): lax.ppermute(payload[cut:], 'dp', pairs)]
    ppermute x0 -> x4, starting transfers between devices: none -> 5.28 us  [the longest x2 5.12 us: feature_plan(): lax.ppermute(payload[cut:], 'dp', pairs)]
    ppermute x3 -> x1, starting transfers between devices: 5.12 us -> 0.01 us  [feature_plan(): got = lax.ppermute(payload, 'dp', pairs)]
    ppermute x3, waiting for transfers between devices: 2.37 us -> 4.51 us  [exchange_all(): total = total + lax.ppermute(x, axis, [(i, (i + k) % n) for i in range(n)])]
    ppermute x3, starting transfers between devices: 6.06 us -> 5.16 us  [exchange_all(): total = total + lax.ppermute(x, axis, [(i, (i + k) % n) for i in range(n)])]
  transfers between devices with their start and end apart: 9 -> 11, of which waited for: 8 -> 10; matrix products, arithmetic and copies ran while one was open for 2% -> 3% of each run, Pallas kernels for 0% -> 0%
where the time goes in v12:
time: 76.9 us; the launch traced here: 76.6 us
  waiting for transfers between devices  27.2 us (35%)
  starting transfers between devices  14.6 us (19%)
  matrix products  11.2 us (15%)
  blocking collectives  11.2 us (15%)
  other arithmetic  6.38 us (8%)
  local copies, waits for them, and re-layouts  4.97 us (6%)
  between operations  1.09 us (1%)
    all_to_all x1, blocking collectives, feature_plan(): got = lax.all_to_all(sent, 'dp', 0, 2, tiled=True)  11.2 us
    ppermute x2, waiting for transfers between devices, feature_plan(): lax.ppermute(payload[cut:], 'dp', pairs)  9.48 us
    ppermute x2, waiting for transfers between devices, feature_plan(): lax.ppermute(payload[:cut], 'dp', pairs)  6.82 us
    ppermute x3, starting transfers between devices, exchange_all(): total = total + lax.ppermute(x, axis, [(i, (i + k) % n) for i in range(n)])  5.16 us
    ppermute x2, starting transfers between devices, feature_plan(): lax.ppermute(payload[cut:], 'dp', pairs)  5.12 us
    dot_general x1, matrix products, feature_plan(): lax.dot_general(zs, dlog, (((0,), (0,)), ((), ())), preferred_element_typ...  5.09 us
    ppermute x3, waiting for transfers between devices, exchange_all(): total = total + lax.ppermute(x, axis, [(i, (i + k) % n) for i in range(n)])  4.51 us
    ppermute x2, starting transfers between devices, feature_plan(): got = lax.ppermute(totals, 'dp', swap(up[r], down[r])).reshape(shape)  4.11 us
  transfers between devices with their start and end apart: 11, of which 10 were waited for; matrix products, arithmetic and copies ran while one was open for 3% of the time, Pallas kernels for 0%

profile of v12, /device:TPU:0, one launch (start us, length us, event | category | flops | bytes accessed | tf_op | source)
XLA Modules:
  0.0 76.6 jit_solution(11460045701494567245)
XLA Ops:
  0.7 2.0 %fusion.25 = (bf16[32,4096]{1,0:T(8,128)(2,1)S(1)}, f32[32,4096]{1,0:T(8,128)}) fusion(bf16[32,4096]{1,0:T(8,128)(2,1)} %param.8, f32[32,4096]{1,0:T(8,128)} %param.7), kind=kLoop, calls=%fused_computation.76 | loop fusion | flops 655360 | bytes 1572864 | tf_op jit(solution)/shard_map/convert_element_type | solution.py:75
  2.9 1.0 %copy.36 = bf16[4,8,8,512]{3,2,1,0:T(8,128)(2,1)S(1)} copy(bf16[4,8,8,512]{3,1,2,0:T(8,128)(2,1)} %bitcast.86) | data formatting | bytes 524288
  4.1 0.6 gather_fusion
  4.9 3.0 %collective-permute-start.2 = (bf16[256,512]{1,0:T(8,128)(2,1)S(1)}, bf16[256,512]{1,0:T(8,128)(2,1)S(1)}, u32[]{:S(2)}, u32[]{:S(2)}) collective-permute-start(bf16[256,512]{1,0:T(8,128)(2,1)S(1)} %bitcast.91), channel_id=1, source_target_pairs={{0,8},{4,20},{8,0},{12,28},{16,24},{20,4},{24,16},{28,12},{1,9},{5... | collective-permute-start | bytes 786440 | tf_op jit(solution)/shard_map/ppermute | solution.py:105
  8.1 0.1 fusion.14
  8.4 3.8 %collective-permute-done.2 = bf16[256,512]{1,0:T(8,128)(2,1)S(1)} collective-permute-done((bf16[256,512]{1,0:T(8,128)(2,1)S(1)}, bf16[256,512]{1,0:T(8,128)(2,1)S(1)}, u32[]{:S(2)}, u32[]{:S(2)}) %collective-permute-start.2) | collective-permute-done | bytes 262176 | tf_op jit(solution)/shard_map/ppermute | solution.py:105
  12.3 2.8 %collective-permute-done = bf16[256,512]{1,0:T(8,128)(2,1)S(1)} collective-permute-done((bf16[256,512]{1,0:T(8,128)(2,1)S(1)}, bf16[256,512]{1,0:T(8,128)(2,1)S(1)}, u32[]{:S(2)}, u32[]{:S(2)}) %collective-permute-start) | collective-permute-done | bytes 262176 | tf_op jit(solution)/shard_map/ppermute | solution.py:105
  15.2 2.1 %collective-permute-start.3 = (bf16[384,512]{1,0:T(8,128)(2,1)S(1)}, bf16[384,512]{1,0:T(8,128)(2,1)S(1)}, u32[]{:S(2)}, u32[]{:S(2)}) collective-permute-start(bf16[384,512]{1,0:T(8,128)(2,1)S(1)} %get-tuple-element.23), channel_id=1, source_target_pairs={{0,16},{4,12},{8,24},{12,4},{16,0},{20,28},{24,8},{28,20},{1,17},{... | collective-permute-start | bytes 1179656 | tf_op jit(solution)/shard_map/ppermute | solution.py:105
  17.4 5.7 %collective-permute-done.3 = bf16[384,512]{1,0:T(8,128)(2,1)S(1)} collective-permute-done((bf16[384,512]{1,0:T(8,128)(2,1)S(1)}, bf16[384,512]{1,0:T(8,128)(2,1)S(1)}, u32[]{:S(2)}, u32[]{:S(2)}) %collective-permute-start.3) | collective-permute-done | bytes 393248 | tf_op jit(solution)/shard_map/ppermute | solution.py:105
  23.2 4.1 %collective-permute-done.1 = bf16[384,512]{1,0:T(8,128)(2,1)S(1)} collective-permute-done((bf16[384,512]{1,0:T(8,128)(2,1)S(1)}, bf16[384,512]{1,0:T(8,128)(2,1)S(1)}, u32[]{:S(2)}, u32[]{:S(2)}) %collective-permute-start.1) | collective-permute-done | bytes 393248 | tf_op jit(solution)/shard_map/ppermute | solution.py:105
  27.4 1.2 %pad_maximum_fusion.1 = bf16[1280,512]{1,0:T(8,128)(2,1)} fusion(bf16[256,512]{1,0:T(8,128)(2,1)S(1)} %bitcast.80, bf16[1024,512]{1,0:T(8,128)(2,1)S(1)} %bitcast.67), kind=kLoop, calls=%fused_computation.9 | loop fusion | flops 2621440 | bytes 2621440 | tf_op jit(solution)/shard_map/concatenate | solution.py:99
  28.6 0.8 dynamic_slice.3
  29.4 2.5 %collective-permute-done.4 = bf16[1280,512]{1,0:T(8,128)(2,1)S(1)} collective-permute-done((bf16[1280,512]{1,0:T(8,128)(2,1)}, bf16[1280,512]{1,0:T(8,128)(2,1)S(1)}, u32[]{:S(2)}, u32[]{:S(2)}) %collective-permute-start.4) | collective-permute-done | bytes 1310752 | tf_op jit(solution)/shard_map/ppermute | solution.py:101
  32.0 0.6 gather_fusion.1
  33.0 0.2 pad_maximum_fusion
  33.2 0.2 copy-done
  33.4 3.0 %fusion.31 = (f32[2048]{0:T(1024)S(1)}, f32[2048,512]{0,1:T(8,128)}) fusion(f32[512]{0:T(512)S(1)} %add_sqrt_fusion.1, bf16[256,512]{1,0:T(8,128)(2,1)S(1)} %bitcast.89, bf16[2048,512]{1,0:T(8,128)(2,1)S(1)} %bitcast.71), kind=kOutput, calls=%fused_computation.82 | convolution fusion | flops 540014592 | bytes 5515264 | tf_op jit(solution)/shard_map/dot_general | solution.py:129
  36.4 3.2 %fusion = (f32[2048]{0:T(1024)S(1)}, f32[512]{0:T(512)S(1)}, f32[2048,512]{0,1:T(8,128)}) fusion(f32[512]{0:T(512)S(1)} %dynamic_slice.3, f32[512]{0:T(512)S(1)} %add_sqrt_fusion, bf16[256,512]{1,0:T(8,128)(2,1)S(1)} %bitcast.92, bf16[2048,512]{1,0:T(8,128)(2,1)S(1)} %bitcast.72), kind=kOutput, calls=%fused_computation.5 | convolution fusion | flops 542111232 | bytes 5519360 | tf_op jit(solution)/shard_map/dot_general | solution.py:128
  39.6 2.0 %collective-permute-start.5 = (f32[2,2048]{1,0:T(2,128)S(1)}, f32[2,2048]{1,0:T(2,128)S(1)}, u32[]{:S(2)}, u32[]{:S(2)}) collective-permute-start(f32[2,2048]{1,0:T(2,128)S(1)} %pad_maximum_fusion.10), channel_id=1, source_target_pairs={{0,8},{4,20},{8,0},{12,28},{16,24},{20,4},{24,16},{28,12},{1,9},{5... | collective-permute-start | bytes 49160 | tf_op jit(solution)/shard_map/ppermute | solution.py:139
  41.6 1.8 %collective-permute-done.5 = f32[2,2048]{1,0:T(2,128)S(1)} collective-permute-done((f32[2,2048]{1,0:T(2,128)S(1)}, f32[2,2048]{1,0:T(2,128)S(1)}, u32[]{:S(2)}, u32[]{:S(2)}) %collective-permute-start.5) | collective-permute-done | bytes 16416 | tf_op jit(solution)/shard_map/ppermute | solution.py:139
  43.6 2.1 %collective-permute-start.6 = (f32[2,2048]{1,0:T(2,128)S(1)}, f32[2,2048]{1,0:T(2,128)S(1)}, u32[]{:S(2)}, u32[]{:S(2)}) collective-permute-start(f32[2,2048]{1,0:T(2,128)S(1)} %fusion.21), channel_id=1, source_target_pairs={{0,16},{4,12},{8,24},{12,4},{16,0},{20,28},{24,8},{28,20},{1,17},{... | collective-permute-start | bytes 49160 | tf_op jit(solution)/shard_map/ppermute | solution.py:139
  45.7 1.7 %collective-permute-done.6 = f32[2,2048]{1,0:T(2,128)S(1)} collective-permute-done((f32[2,2048]{1,0:T(2,128)S(1)}, f32[2,2048]{1,0:T(2,128)S(1)}, u32[]{:S(2)}, u32[]{:S(2)}) %collective-permute-start.6) | collective-permute-done | bytes 16416 | tf_op jit(solution)/shard_map/ppermute | solution.py:139
  47.6 0.8 %fusion.18 = (bf16[512]{0:T(512)(128)(2,1)S(1)}, bf16[512]{0:T(512)(128)(2,1)S(1)}) fusion(f32[512]{0:T(512)S(1)} %get-tuple-element.5, f32[4096]{0:T(1024)} %param.11, s32[]{:T(128)S(6)} %select_n.27), kind=kLoop, calls=%fused_computation.69 | loop fusion | flops 3584 | bytes 6148 | tf_op jit(solution)/shard_map/convert_element_type | solution.py:152
  48.4 0.4 collective-permute-done.7
  48.9 4.1 %collective-permute-start.10 = (f32[2,2048]{1,0:T(2,128)S(1)}, f32[2,2048]{1,0:T(2,128)S(1)}, u32[]{:S(2)}, u32[]{:S(2)}) collective-permute-start(f32[2,2048]{1,0:T(2,128)S(1)} %add.83), channel_id=1, source_target_pairs={{0,3},{1,0},{2,1},{3,2},{4,7},{5,4},{6,5},{7,6},{8,11},{9,8},{10,9... | collective-permute-start | bytes 49160 | tf_op jit(solution)/shard_map/ppermute | solution.py:58
  53.0 1.0 %collective-permute-start.9 = (f32[2,2048]{1,0:T(2,128)S(1)}, f32[2,2048]{1,0:T(2,128)S(1)}, u32[]{:S(2)}, u32[]{:S(2)}) collective-permute-start(f32[2,2048]{1,0:T(2,128)S(1)} %add.83), channel_id=1, source_target_pairs={{0,2},{1,3},{2,0},{3,1},{4,6},{5,7},{6,4},{7,5},{8,10},{9,11},{10,... | collective-permute-start | bytes 49160 | tf_op jit(solution)/shard_map/ppermute | solution.py:58
  54.0 0.4 collective-permute-done.10
  54.5 4.1 %collective-permute-done.8 = f32[2,2048]{1,0:T(2,128)S(1)} collective-permute-done((f32[2,2048]{1,0:T(2,128)S(1)}, f32[2,2048]{1,0:T(2,128)S(1)}, u32[]{:S(2)}, u32[]{:S(2)}) %collective-permute-start.8) | collective-permute-done | bytes 16416 | tf_op jit(solution)/shard_map/ppermute | solution.py:58
  58.6 5.1 %fusion.7 = (f32[512]{0:T(512)S(1)}, f32[256,512]{1,0:T(8,128)S(1)}) fusion(bf16[8,32,512]{2,1,0:T(8,128)(2,1)S(1)} %copy-done.1, f32[2048,512]{0,1:T(8,128)} %get-tuple-element.34, f32[2048,512]{0,1:T(8,128)} %get-tuple-element.32, f32[2048]{0:T(1024)S(1)} %bitcast.103, f32[2048]{0:T(1024)S(1)} %bitcast.102, f32[512]{0:T(512)S(1)} %dynamic_slice.3, ...), kind=kOutput, calls=%fused_computation.23 | convolution fusion | flops 544603648 | bytes 10244096 | tf_op jit(solution)/shard_map/dot_general | solution.py:146
  63.9 11.2 %all_to_all.4 = bf16[8,34,512]{2,1,0:T(8,128)(2,1)S(1)} all-to-all(bf16[8,34,512]{2,1,0:T(8,128)(2,1)S(1)} %pad_maximum_fusion.8), channel_id=1, replica_groups=mesh['dp'=8,'tensor'=4] {'dp'}, dimensions={0} | all-to-all | bytes 557056 | tf_op jit(solution)/shard_map/all_to_all | solution.py:161
  75.2 0.6 slice_add_fusion
  75.8 0.8 %copy.38 = f32[4,8,8,512]{3,1,2,0:T(8,128)} copy(f32[4,8,8,512]{3,1,0,2:T(8,128)S(1)} %slice_bitcast_fusion.1) | data formatting | bytes 1048576
  (72 shorter events, 2.7 us)
Async XLA Ops:
  0.6 7.2 %copy-start.3 = (bf16[256,256]{1,0:T(8,128)(2,1)S(1)}, bf16[256,256]{1,0:T(8,128)(2,1)}, u32[]{:S(2)}) copy-start(bf16[256,256]{1,0:T(8,128)(2,1)} %param.10) | copy-start | bytes 393220
  0.6 7.4 %copy-start.2 = (bf16[256,256]{1,0:T(8,128)(2,1)S(1)}, bf16[256,256]{1,0:T(8,128)(2,1)}, u32[]{:S(2)}) copy-start(bf16[256,256]{1,0:T(8,128)(2,1)} %param.9) | copy-start | bytes 393220
  4.9 7.4 %collective-permute-start.2 = (bf16[256,512]{1,0:T(8,128)(2,1)S(1)}, bf16[256,512]{1,0:T(8,128)(2,1)S(1)}, u32[]{:S(2)}, u32[]{:S(2)}) collective-permute-start(bf16[256,512]{1,0:T(8,128)(2,1)S(1)} %bitcast.91), channel_id=1, source_target_pairs={{0,8},{4,20},{8,0},{12,28},{16,24},{20,4},{24,16},{28,12},{1,9},{5... | collective-permute-start | bytes 786440 | tf_op jit(solution)/shard_map/ppermute | solution.py:105
  8.3 6.7 %collective-permute-start = (bf16[256,512]{1,0:T(8,128)(2,1)S(1)}, bf16[256,512]{1,0:T(8,128)(2,1)S(1)}, u32[]{:S(2)}, u32[]{:S(2)}) collective-permute-start(bf16[256,512]{1,0:T(8,128)(2,1)S(1)} %get-tuple-element.27), channel_id=1, source_target_pairs={{0,8},{4,20},{8,0},{12,28},{16,24},{20,4},{24,16},{28,12},{1,9},{5... | collective-permute-start | bytes 786440 | tf_op jit(solution)/shard_map/ppermute | solution.py:105
  15.2 7.9 %collective-permute-start.3 = (bf16[384,512]{1,0:T(8,128)(2,1)S(1)}, bf16[384,512]{1,0:T(8,128)(2,1)S(1)}, u32[]{:S(2)}, u32[]{:S(2)}) collective-permute-start(bf16[384,512]{1,0:T(8,128)(2,1)S(1)} %get-tuple-element.23), channel_id=1, source_target_pairs={{0,16},{4,12},{8,24},{12,4},{16,0},{20,28},{24,8},{28,20},{1,17},{... | collective-permute-start | bytes 1179656 | tf_op jit(solution)/shard_map/ppermute | solution.py:105
  17.3 10.0 %collective-permute-start.1 = (bf16[384,512]{1,0:T(8,128)(2,1)S(1)}, bf16[384,512]{1,0:T(8,128)(2,1)S(1)}, u32[]{:S(2)}, u32[]{:S(2)}) collective-permute-start(bf16[384,512]{1,0:T(8,128)(2,1)S(1)} %get-tuple-element.22), channel_id=1, source_target_pairs={{0,16},{4,12},{8,24},{12,4},{16,0},{20,28},{24,8},{28,20},{1,17},{... | collective-permute-start | bytes 1179656 | tf_op jit(solution)/shard_map/ppermute | solution.py:105
  28.6 3.2 %collective-permute-start.4 = (bf16[1280,512]{1,0:T(8,128)(2,1)}, bf16[1280,512]{1,0:T(8,128)(2,1)S(1)}, u32[]{:S(2)}, u32[]{:S(2)}) collective-permute-start(bf16[1280,512]{1,0:T(8,128)(2,1)} %pad_maximum_fusion.1), channel_id=1, source_target_pairs={{0,4},{4,0},{8,12},{12,8},{16,20},{20,16},{24,28},{28,24},{1,5},{5... | collective-permute-start | bytes 3932168 | tf_op jit(solution)/shard_map/ppermute | solution.py:101
  32.7 0.7 copy-start
  36.4 22.2 %copy-start.1 = (bf16[8,32,512]{2,1,0:T(8,128)(2,1)S(1)}, bf16[8,32,512]{2,1,0:T(8,128)(2,1)}, u32[]{:S(2)}) copy-start(bf16[8,32,512]{2,1,0:T(8,128)(2,1)} %copy-done) | copy-start | bytes 786436
  39.6 3.8 %collective-permute-start.5 = (f32[2,2048]{1,0:T(2,128)S(1)}, f32[2,2048]{1,0:T(2,128)S(1)}, u32[]{:S(2)}, u32[]{:S(2)}) collective-permute-start(f32[2,2048]{1,0:T(2,128)S(1)} %pad_maximum_fusion.10), channel_id=1, source_target_pairs={{0,8},{4,20},{8,0},{12,28},{16,24},{20,4},{24,16},{28,12},{1,9},{5... | collective-permute-start | bytes 49160 | tf_op jit(solution)/shard_map/ppermute | solution.py:139
  43.6 3.8 %collective-permute-start.6 = (f32[2,2048]{1,0:T(2,128)S(1)}, f32[2,2048]{1,0:T(2,128)S(1)}, u32[]{:S(2)}, u32[]{:S(2)}) collective-permute-start(f32[2,2048]{1,0:T(2,128)S(1)} %fusion.21), channel_id=1, source_target_pairs={{0,16},{4,12},{8,24},{12,4},{16,0},{20,28},{24,8},{28,20},{1,17},{... | collective-permute-start | bytes 49160 | tf_op jit(solution)/shard_map/ppermute | solution.py:139
  47.5 1.2 %collective-permute-start.7 = (f32[2,2048]{1,0:T(2,128)S(1)}, f32[2,2048]{1,0:T(2,128)S(1)}, u32[]{:S(2)}, u32[]{:S(2)}) collective-permute-start(f32[2,2048]{1,0:T(2,128)S(1)} %fusion.34), channel_id=1, source_target_pairs={{0,4},{4,0},{8,12},{12,8},{16,20},{20,16},{24,28},{28,24},{1,5},{5... | collective-permute-start | bytes 49160 | tf_op jit(solution)/shard_map/ppermute | solution.py:136
  48.9 5.6 %collective-permute-start.10 = (f32[2,2048]{1,0:T(2,128)S(1)}, f32[2,2048]{1,0:T(2,128)S(1)}, u32[]{:S(2)}, u32[]{:S(2)}) collective-permute-start(f32[2,2048]{1,0:T(2,128)S(1)} %add.83), channel_id=1, source_target_pairs={{0,3},{1,0},{2,1},{3,2},{4,7},{5,4},{6,5},{7,6},{8,11},{9,8},{10,9... | collective-permute-start | bytes 49160 | tf_op jit(solution)/shard_map/ppermute | solution.py:58
  53.0 5.5 %collective-permute-start.8 = (f32[2,2048]{1,0:T(2,128)S(1)}, f32[2,2048]{1,0:T(2,128)S(1)}, u32[]{:S(2)}, u32[]{:S(2)}) collective-permute-start(f32[2,2048]{1,0:T(2,128)S(1)} %add.83), channel_id=1, source_target_pairs={{0,1},{1,2},{2,3},{3,0},{4,5},{5,6},{6,7},{7,4},{8,9},{9,10},{10,1... | collective-permute-start | bytes 49160 | tf_op jit(solution)/shard_map/ppermute | solution.py:58
  53.0 5.5 %collective-permute-start.9 = (f32[2,2048]{1,0:T(2,128)S(1)}, f32[2,2048]{1,0:T(2,128)S(1)}, u32[]{:S(2)}, u32[]{:S(2)}) collective-permute-start(f32[2,2048]{1,0:T(2,128)S(1)} %add.83), channel_id=1, source_target_pairs={{0,2},{1,3},{2,0},{3,1},{4,6},{5,7},{6,4},{7,5},{8,10},{9,11},{10,... | collective-permute-start | bytes 49160 | tf_op jit(solution)/shard_map/ppermute | solution.py:58

commit v13 on v11

--- a/solution.py
+++ b/solution.py
@@ -133,7 +133,7 @@
             got = lax.ppermute(totals, "dp", swap(up[r], down[r])).reshape(shape)
             got = jnp.flip(got, nbits - r)
         totals = totals + got.reshape(totals.shape)
-    totals = exchange_all(totals, "tensor", lax.axis_size("tensor"))
+    totals = exchange_sum(totals, "tensor", lax.axis_size("tensor"))
     t_total, s_total = totals[0][:, None], totals[1][:, None]
     part_center = 0.5 * c + 0.5 * (jnp.sum(t_cos, 0) / (images * n))
     dlog = ((s_exp / s_total - t_exp / t_total) / 0.1).astype(jnp.bfloat16)

time: 76.3 us -> 76.8 us (level)
  waiting for transfers between devices: 25.8 us -> 26.9 us
  starting transfers between devices: 15.4 us -> 14.6 us
    ppermute x3 -> x2, starting transfers between devices: 6.06 us -> 5.23 us  [exchange_sum(): x = x + lax.ppermute(x, axis, [(i, i ^ step) for i in range(n)])]
    ppermute x1, waiting for transfers between devices: 0.39 us -> 1.17 us  [feature_plan(): lax.ppermute(totals, 'dp', [(i, i ^ 1) for i in range(n)]).reshape(shape)]
    ppermute x3 -> x2, waiting for transfers between devices: 2.37 us -> 2.65 us  [exchange_sum(): x = x + lax.ppermute(x, axis, [(i, i ^ step) for i in range(n)])]
  transfers between devices with their start and end apart: 9 -> 8, of which waited for: 8 -> 8; matrix products, arithmetic and copies ran while one was open for 2% -> 2% of each run, Pallas kernels for 0% -> 0%
where the time goes in v13:
time: 76.8 us; the launch traced here: 76.6 us
  waiting for transfers between devices  26.9 us (35%)
  starting transfers between devices  14.6 us (19%)
  blocking collectives  11.5 us (15%)
  matrix products  11.2 us (15%)
  other arithmetic  6.35 us (8%)
  local copies, waits for them, and re-layouts  5 us (7%)
  between operations  1.1 us (1%)
    ppermute x3, waiting for transfers between devices, feature_plan(): got = lax.ppermute(payload, 'dp', pairs)  19.6 us
    all_to_all x1, blocking collectives, feature_plan(): got = lax.all_to_all(sent, 'dp', 0, 2, tiled=True)  11.5 us
    ppermute x2, starting transfers between devices, exchange_sum(): x = x + lax.ppermute(x, axis, [(i, i ^ step) for i in range(n)])  5.23 us
    ppermute x3, starting transfers between devices, feature_plan(): got = lax.ppermute(payload, 'dp', pairs)  5.12 us
    dot_general x1, matrix products, feature_plan(): lax.dot_general(zs, dlog, (((0,), (0,)), ((), ())), preferred_element_typ...  5.09 us
    ppermute x2, starting transfers between devices, feature_plan(): got = lax.ppermute(totals, 'dp', swap(up[r], down[r])).reshape(shape)  4.13 us
    ppermute x2, waiting for transfers between devices, feature_plan(): got = lax.ppermute(totals, 'dp', swap(up[r], down[r])).reshape(shape)  3.48 us
    dot_general x1, matrix products, feature_plan(): t_cos = jnp.dot(zt, tw, preferred_element_type=jnp.float32) / t_norm  3.18 us
  transfers between devices with their start and end apart: 8, of which 8 were waited for; matrix products, arithmetic and copies ran while one was open for 2% of the time, Pallas kernels for 0%

profile of v13, /device:TPU:0, one launch (start us, length us, event | category | flops | bytes accessed | tf_op | source)
XLA Modules:
  0.0 76.6 jit_solution(451062515323067575)
XLA Ops:
  0.7 2.0 %fusion.24 = (bf16[32,4096]{1,0:T(8,128)(2,1)S(1)}, f32[32,4096]{1,0:T(8,128)}) fusion(bf16[32,4096]{1,0:T(8,128)(2,1)} %param.8, f32[32,4096]{1,0:T(8,128)} %param.7), kind=kLoop, calls=%fused_computation.75 | loop fusion | flops 655360 | bytes 1572864 | tf_op jit(solution)/shard_map/convert_element_type | solution.py:75
  2.9 1.0 %copy.27 = bf16[4,8,8,512]{3,2,1,0:T(8,128)(2,1)S(1)} copy(bf16[4,8,8,512]{3,1,2,0:T(8,128)(2,1)} %bitcast.87) | data formatting | bytes 524288
  4.1 0.6 gather_fusion
  5.1 0.1 fusion.14
  5.3 3.0 %collective-permute-start = (bf16[512,512]{1,0:T(8,128)(2,1)S(1)}, bf16[512,512]{1,0:T(8,128)(2,1)S(1)}, u32[]{:S(2)}, u32[]{:S(2)}) collective-permute-start(bf16[512,512]{1,0:T(8,128)(2,1)S(1)} %pad_maximum_fusion.5), channel_id=1, source_target_pairs={{0,8},{4,20},{8,0},{12,28},{16,24},{20,4},{24,16},{28,12},{1,9},{5... | collective-permute-start | bytes 1572872 | tf_op jit(solution)/shard_map/ppermute | solution.py:100
  8.4 7.1 %collective-permute-done = bf16[512,512]{1,0:T(8,128)(2,1)S(1)} collective-permute-done((bf16[512,512]{1,0:T(8,128)(2,1)S(1)}, bf16[512,512]{1,0:T(8,128)(2,1)S(1)}, u32[]{:S(2)}, u32[]{:S(2)}) %collective-permute-start) | collective-permute-done | bytes 524320 | tf_op jit(solution)/shard_map/ppermute | solution.py:100
  15.7 2.1 %collective-permute-start.1 = (bf16[768,512]{1,0:T(8,128)(2,1)S(1)}, bf16[768,512]{1,0:T(8,128)(2,1)S(1)}, u32[]{:S(2)}, u32[]{:S(2)}) collective-permute-start(bf16[768,512]{1,0:T(8,128)(2,1)S(1)} %pad_maximum_fusion.3), channel_id=1, source_target_pairs={{0,16},{4,12},{8,24},{12,4},{16,0},{20,28},{24,8},{28,20},{1,17},{... | collective-permute-start | bytes 2359304 | tf_op jit(solution)/shard_map/ppermute | solution.py:100
  17.8 10.0 %collective-permute-done.1 = bf16[768,512]{1,0:T(8,128)(2,1)S(1)} collective-permute-done((bf16[768,512]{1,0:T(8,128)(2,1)S(1)}, bf16[768,512]{1,0:T(8,128)(2,1)S(1)}, u32[]{:S(2)}, u32[]{:S(2)}) %collective-permute-start.1) | collective-permute-done | bytes 786464 | tf_op jit(solution)/shard_map/ppermute | solution.py:100
  28.0 0.1 fusion.23
  28.1 1.1 %pad_maximum_fusion.1 = bf16[1280,512]{1,0:T(8,128)(2,1)} fusion(bf16[256,512]{1,0:T(8,128)(2,1)S(1)} %bitcast.81, bf16[1024,512]{1,0:T(8,128)(2,1)S(1)} %bitcast.67), kind=kLoop, calls=%fused_computation.9 | loop fusion | flops 2621440 | bytes 2621440 | tf_op jit(solution)/shard_map/concatenate | solution.py:99
  29.3 0.8 dynamic_slice.3
  30.0 2.5 %collective-permute-done.2 = bf16[1280,512]{1,0:T(8,128)(2,1)S(1)} collective-permute-done((bf16[1280,512]{1,0:T(8,128)(2,1)}, bf16[1280,512]{1,0:T(8,128)(2,1)S(1)}, u32[]{:S(2)}, u32[]{:S(2)}) %collective-permute-start.2) | collective-permute-done | bytes 1310752 | tf_op jit(solution)/shard_map/ppermute | solution.py:100
  32.6 0.6 gather_fusion.1
  33.4 0.1 multiply_reduce_fusion.1
  33.7 0.2 pad_maximum_fusion
  33.9 0.2 copy-done
  34.1 2.9 %fusion.29 = (f32[2048]{0:T(1024)S(1)}, f32[2048,512]{0,1:T(8,128)}) fusion(f32[512]{0:T(512)S(1)} %add_sqrt_fusion.1, bf16[256,512]{1,0:T(8,128)(2,1)S(1)} %bitcast.90, bf16[2048,512]{1,0:T(8,128)(2,1)S(1)} %bitcast.73), kind=kOutput, calls=%fused_computation.80 | convolution fusion | flops 540014592 | bytes 5515264 | tf_op jit(solution)/shard_map/dot_general | solution.py:123
  37.0 3.2 %fusion = (f32[2048]{0:T(1024)S(1)}, f32[512]{0:T(512)S(1)}, f32[2048,512]{0,1:T(8,128)}) fusion(f32[512]{0:T(512)S(1)} %dynamic_slice.3, f32[512]{0:T(512)S(1)} %add_sqrt_fusion, bf16[256,512]{1,0:T(8,128)(2,1)S(1)} %bitcast.93, bf16[2048,512]{1,0:T(8,128)(2,1)S(1)} %bitcast.74), kind=kOutput, calls=%fused_computation.5 | convolution fusion | flops 542111232 | bytes 5519360 | tf_op jit(solution)/shard_map/dot_general | solution.py:122
  40.2 2.1 %collective-permute-start.3 = (f32[2,2048]{1,0:T(2,128)S(1)}, f32[2,2048]{1,0:T(2,128)S(1)}, u32[]{:S(2)}, u32[]{:S(2)}) collective-permute-start(f32[2,2048]{1,0:T(2,128)S(1)} %pad_maximum_fusion.9), channel_id=1, source_target_pairs={{0,8},{4,20},{8,0},{12,28},{16,24},{20,4},{24,16},{28,12},{1,9},{5... | collective-permute-start | bytes 49160 | tf_op jit(solution)/shard_map/ppermute | solution.py:133
  42.3 1.7 %collective-permute-done.3 = f32[2,2048]{1,0:T(2,128)S(1)} collective-permute-done((f32[2,2048]{1,0:T(2,128)S(1)}, f32[2,2048]{1,0:T(2,128)S(1)}, u32[]{:S(2)}, u32[]{:S(2)}) %collective-permute-start.3) | collective-permute-done | bytes 16416 | tf_op jit(solution)/shard_map/ppermute | solution.py:133
  44.2 2.1 %collective-permute-start.4 = (f32[2,2048]{1,0:T(2,128)S(1)}, f32[2,2048]{1,0:T(2,128)S(1)}, u32[]{:S(2)}, u32[]{:S(2)}) collective-permute-start(f32[2,2048]{1,0:T(2,128)S(1)} %fusion.21), channel_id=1, source_target_pairs={{0,16},{4,12},{8,24},{12,4},{16,0},{20,28},{24,8},{28,20},{1,17},{... | collective-permute-start | bytes 49160 | tf_op jit(solution)/shard_map/ppermute | solution.py:133
  46.3 1.7 %collective-permute-done.4 = f32[2,2048]{1,0:T(2,128)S(1)} collective-permute-done((f32[2,2048]{1,0:T(2,128)S(1)}, f32[2,2048]{1,0:T(2,128)S(1)}, u32[]{:S(2)}, u32[]{:S(2)}) %collective-permute-start.4) | collective-permute-done | bytes 16416 | tf_op jit(solution)/shard_map/ppermute | solution.py:133
  48.2 1.2 %collective-permute-done.5 = f32[2,2048]{1,0:T(2,128)S(1)} collective-permute-done((f32[2,2048]{1,0:T(2,128)S(1)}, f32[2,2048]{1,0:T(2,128)S(1)}, u32[]{:S(2)}, u32[]{:S(2)}) %collective-permute-start.5) | collective-permute-done | bytes 16416 | tf_op jit(solution)/shard_map/ppermute | solution.py:130
  49.5 2.1 %collective-permute-start.6 = (f32[2,2048]{1,0:T(2,128)S(1)}, f32[2,2048]{1,0:T(2,128)S(1)}, u32[]{:S(2)}, u32[]{:S(2)}) collective-permute-start(f32[2,2048]{1,0:T(2,128)S(1)} %add.80), channel_id=1, source_target_pairs={{0,1},{1,0},{2,3},{3,2},{4,5},{5,4},{6,7},{7,6},{8,9},{9,8},{10,11... | collective-permute-start | bytes 49160 | tf_op jit(solution)/shard_map/ppermute | solution.py:50
  51.6 0.8 fusion.18
  52.4 0.9 %collective-permute-done.6 = f32[2,2048]{1,0:T(2,128)S(1)} collective-permute-done((f32[2,2048]{1,0:T(2,128)S(1)}, f32[2,2048]{1,0:T(2,128)S(1)}, u32[]{:S(2)}, u32[]{:S(2)}) %collective-permute-start.6) | collective-permute-done | bytes 16416 | tf_op jit(solution)/shard_map/ppermute | solution.py:50
  53.4 3.1 %collective-permute-start.7 = (f32[2,2048]{1,0:T(2,128)S(1)}, f32[2,2048]{1,0:T(2,128)S(1)}, u32[]{:S(2)}, u32[]{:S(2)}) collective-permute-start(f32[2,2048]{1,0:T(2,128)S(1)} %add.81), channel_id=1, source_target_pairs={{0,2},{1,3},{2,0},{3,1},{4,6},{5,7},{6,4},{7,5},{8,10},{9,11},{10,... | collective-permute-start | bytes 49160 | tf_op jit(solution)/shard_map/ppermute | solution.py:50
  56.5 1.7 %collective-permute-done.7 = f32[2,2048]{1,0:T(2,128)S(1)} collective-permute-done((f32[2,2048]{1,0:T(2,128)S(1)}, f32[2,2048]{1,0:T(2,128)S(1)}, u32[]{:S(2)}, u32[]{:S(2)}) %collective-permute-start.7) | collective-permute-done | bytes 16416 | tf_op jit(solution)/shard_map/ppermute | solution.py:50
  58.2 5.1 %fusion.7 = (f32[512]{0:T(512)S(1)}, f32[256,512]{1,0:T(8,128)S(1)}) fusion(bf16[8,32,512]{2,1,0:T(8,128)(2,1)S(1)} %copy-done.1, f32[2048,512]{0,1:T(8,128)} %get-tuple-element.32, f32[2048,512]{0,1:T(8,128)} %get-tuple-element.30, f32[2048]{0:T(1024)S(1)} %bitcast.103, f32[2048]{0:T(1024)S(1)} %bitcast.102, f32[512]{0:T(512)S(1)} %dynamic_slice.3, ...), kind=kOutput, calls=%fused_computation.24 | convolution fusion | flops 544603648 | bytes 10244096 | tf_op jit(solution)/shard_map/dot_general | solution.py:140
  63.5 11.5 %all_to_all.4 = bf16[8,34,512]{2,1,0:T(8,128)(2,1)S(1)} all-to-all(bf16[8,34,512]{2,1,0:T(8,128)(2,1)S(1)} %pad_maximum_fusion.8), channel_id=1, replica_groups=mesh['dp'=8,'tensor'=4] {'dp'}, dimensions={0} | all-to-all | bytes 557056 | tf_op jit(solution)/shard_map/all_to_all | solution.py:155
  75.1 0.6 slice_add_fusion
  75.7 0.8 %copy.29 = f32[4,8,8,512]{3,1,2,0:T(8,128)} copy(f32[4,8,8,512]{3,1,0,2:T(8,128)S(1)} %slice_bitcast_fusion.1) | data formatting | bytes 1048576
  (67 shorter events, 2.3 us)
Async XLA Ops:
  0.6 4.2 %copy-start.3 = (bf16[256,256]{1,0:T(8,128)(2,1)S(1)}, bf16[256,256]{1,0:T(8,128)(2,1)}, u32[]{:S(2)}) copy-start(bf16[256,256]{1,0:T(8,128)(2,1)} %param.10) | copy-start | bytes 393220
  0.6 4.4 %copy-start.2 = (bf16[256,256]{1,0:T(8,128)(2,1)S(1)}, bf16[256,256]{1,0:T(8,128)(2,1)}, u32[]{:S(2)}) copy-start(bf16[256,256]{1,0:T(8,128)(2,1)} %param.9) | copy-start | bytes 393220
  5.3 10.2 %collective-permute-start = (bf16[512,512]{1,0:T(8,128)(2,1)S(1)}, bf16[512,512]{1,0:T(8,128)(2,1)S(1)}, u32[]{:S(2)}, u32[]{:S(2)}) collective-permute-start(bf16[512,512]{1,0:T(8,128)(2,1)S(1)} %pad_maximum_fusion.5), channel_id=1, source_target_pairs={{0,8},{4,20},{8,0},{12,28},{16,24},{20,4},{24,16},{28,12},{1,9},{5... | collective-permute-start | bytes 1572872 | tf_op jit(solution)/shard_map/ppermute | solution.py:100
  15.7 12.1 %collective-permute-start.1 = (bf16[768,512]{1,0:T(8,128)(2,1)S(1)}, bf16[768,512]{1,0:T(8,128)(2,1)S(1)}, u32[]{:S(2)}, u32[]{:S(2)}) collective-permute-start(bf16[768,512]{1,0:T(8,128)(2,1)S(1)} %pad_maximum_fusion.3), channel_id=1, source_target_pairs={{0,16},{4,12},{8,24},{12,4},{16,0},{20,28},{24,8},{28,20},{1,17},{... | collective-permute-start | bytes 2359304 | tf_op jit(solution)/shard_map/ppermute | solution.py:100
  29.3 3.2 %collective-permute-start.2 = (bf16[1280,512]{1,0:T(8,128)(2,1)}, bf16[1280,512]{1,0:T(8,128)(2,1)S(1)}, u32[]{:S(2)}, u32[]{:S(2)}) collective-permute-start(bf16[1280,512]{1,0:T(8,128)(2,1)} %pad_maximum_fusion.1), channel_id=1, source_target_pairs={{0,4},{4,0},{8,12},{12,8},{16,20},{20,16},{24,28},{28,24},{1,5},{5... | collective-permute-start | bytes 3932168 | tf_op jit(solution)/shard_map/ppermute | solution.py:100
  33.4 0.7 copy-start
  37.0 21.2 %copy-start.1 = (bf16[8,32,512]{2,1,0:T(8,128)(2,1)S(1)}, bf16[8,32,512]{2,1,0:T(8,128)(2,1)}, u32[]{:S(2)}) copy-start(bf16[8,32,512]{2,1,0:T(8,128)(2,1)} %copy-done) | copy-start | bytes 786436
  40.2 3.8 %collective-permute-start.3 = (f32[2,2048]{1,0:T(2,128)S(1)}, f32[2,2048]{1,0:T(2,128)S(1)}, u32[]{:S(2)}, u32[]{:S(2)}) collective-permute-start(f32[2,2048]{1,0:T(2,128)S(1)} %pad_maximum_fusion.9), channel_id=1, source_target_pairs={{0,8},{4,20},{8,0},{12,28},{16,24},{20,4},{24,16},{28,12},{1,9},{5... | collective-permute-start | bytes 49160 | tf_op jit(solution)/shard_map/ppermute | solution.py:133
  44.2 3.8 %collective-permute-start.4 = (f32[2,2048]{1,0:T(2,128)S(1)}, f32[2,2048]{1,0:T(2,128)S(1)}, u32[]{:S(2)}, u32[]{:S(2)}) collective-permute-start(f32[2,2048]{1,0:T(2,128)S(1)} %fusion.21), channel_id=1, source_target_pairs={{0,16},{4,12},{8,24},{12,4},{16,0},{20,28},{24,8},{28,20},{1,17},{... | collective-permute-start | bytes 49160 | tf_op jit(solution)/shard_map/ppermute | solution.py:133
  48.1 1.2 %collective-permute-start.5 = (f32[2,2048]{1,0:T(2,128)S(1)}, f32[2,2048]{1,0:T(2,128)S(1)}, u32[]{:S(2)}, u32[]{:S(2)}) collective-permute-start(f32[2,2048]{1,0:T(2,128)S(1)} %fusion.32), channel_id=1, source_target_pairs={{0,4},{4,0},{8,12},{12,8},{16,20},{20,16},{24,28},{28,24},{1,5},{5... | collective-permute-start | bytes 49160 | tf_op jit(solution)/shard_map/ppermute | solution.py:130
  49.5 3.9 %collective-permute-start.6 = (f32[2,2048]{1,0:T(2,128)S(1)}, f32[2,2048]{1,0:T(2,128)S(1)}, u32[]{:S(2)}, u32[]{:S(2)}) collective-permute-start(f32[2,2048]{1,0:T(2,128)S(1)} %add.80), channel_id=1, source_target_pairs={{0,1},{1,0},{2,3},{3,2},{4,5},{5,4},{6,7},{7,6},{8,9},{9,8},{10,11... | collective-permute-start | bytes 49160 | tf_op jit(solution)/shard_map/ppermute | solution.py:50
  53.4 4.8 %collective-permute-start.7 = (f32[2,2048]{1,0:T(2,128)S(1)}, f32[2,2048]{1,0:T(2,128)S(1)}, u32[]{:S(2)}, u32[]{:S(2)}) collective-permute-start(f32[2,2048]{1,0:T(2,128)S(1)} %add.81), channel_id=1, source_target_pairs={{0,2},{1,3},{2,0},{3,1},{4,6},{5,7},{6,4},{7,5},{8,10},{9,11},{10,... | collective-permute-start | bytes 49160 | tf_op jit(solution)/shard_map/ppermute | solution.py:50

commit v14 on v11

--- a/solution.py
+++ b/solution.py
@@ -72,13 +72,18 @@
     down = up[::-1]
     dim_bits = [jnp.where(odd == 1, down[r], up[r]) for r in range(nbits - 1)][::-1]
     master_new = 0.996 * teacher_master + 0.004 * student_weight.astype(jnp.float32)
-    both = jnp.stack([student_weight, master_new.astype(jnp.bfloat16)])
-    both = both.reshape(2, rows, n, cols).transpose(2, 0, 1, 3).reshape(n, 2 * rows, cols)
+
+    def by_destination(weight):
+        return weight.reshape(rows, n, cols).transpose(1, 0, 2)
+
     pos = jnp.arange(n)
     rel = (pos >> (nbits - 1)) & 1
     for d, bit in enumerate(dim_bits):
         rel = rel | (((pos >> (nbits - 2 - d)) & 1) << bit)
-    held = jnp.take(both, me ^ rel, axis=0).reshape((2,) * nbits + (2 * rows, cols))
+    held = [
+        jnp.take(by_destination(w), me ^ rel, axis=0).reshape((2,) * nbits + (rows, cols))
+        for w in (student_weight, master_new.astype(jnp.bfloat16))
+    ]
     feats = jnp.concatenate([unit_rows(teacher_feat), unit_rows(student_feat)], axis=1)
     cross_rev = list(range(nbits - 2, -1, -1))
 
@@ -88,33 +93,36 @@
     for r in range(nbits):
         last = r == nbits - 1
         dim = 0 if last else nbits - 1 - r
-        keep = lax.index_in_dim(held, 0, dim, keepdims=False)
-        away = lax.index_in_dim(held, 1, dim, keepdims=False)
+        keep = [lax.index_in_dim(h, 0, dim, keepdims=False) for h in held]
+        away = [lax.index_in_dim(h, 1, dim, keepdims=False) for h in held]
         if last:
             pairs = [(i, i ^ 1) for i in range(n)]
         else:
             pairs = swap(up[r], down[r])
-        if 2 * bot == cols:
-            flat_feats = feats.reshape(-1, 2 * bot)
-            payload = jnp.concatenate([flat_feats, away.reshape(-1, cols)], axis=0)
-            got = lax.ppermute(payload, "dp", pairs)
-            got_feats = got[: flat_feats.shape[0]].reshape(feats.shape)
-            got_held = got[flat_feats.shape[0]:].reshape(away.shape)
+        flat = [feats.reshape(-1, 2 * bot)] + [a.reshape(-1, cols) for a in away]
+        if 2 * bot == cols and r == 0:
+            got = lax.ppermute(jnp.concatenate(flat[:2], axis=0), "dp", pairs)
+            got = [got[: flat[0].shape[0]], got[flat[0].shape[0]:]]
+            got = got + [lax.ppermute(flat[2], "dp", pairs)]
+        elif 2 * bot == cols:
+            got = lax.ppermute(jnp.concatenate(flat, axis=0), "dp", pairs)
+            cut = [flat[0].shape[0], flat[0].shape[0] + flat[1].shape[0]]
+            got = [got[: cut[0]], got[cut[0]: cut[1]], got[cut[1]:]]
         else:
-            got_feats, got_held = lax.ppermute((feats, away), "dp", pairs)
+            got = list(lax.ppermute(tuple(flat), "dp", pairs))
+        got_feats = got[0].reshape(feats.shape)
+        got_held = [g.reshape(a.shape) for g, a in zip(got[1:], away)]
         if last:
             got_feats = jnp.transpose(got_feats, cross_rev + [nbits - 1, nbits])
-            got_held = jnp.transpose(got_held, cross_rev + [nbits - 1, nbits])
+            got_held = [jnp.transpose(g, cross_rev + [nbits - 1, nbits]) for g in got_held]
         feats = jnp.stack([feats, got_feats])
-        held = jnp.stack([keep, got_held], axis=dim)
+        held = [jnp.stack([k, g], axis=dim) for k, g in zip(keep, got_held)]
     feats = feats.reshape(-1, 2 * bot)
     src = me ^ pos
     where = src & 1
     for d, bit in enumerate(dim_bits):
         where = (where << 1) | ((src >> bit) & 1)
-    held = jnp.take(held.reshape(n, 2 * rows, cols), where, axis=0)
-    sw = held[:, :rows].reshape(n * rows, cols)
-    tw = held[:, rows:].reshape(n * rows, cols)
+    sw, tw = [jnp.take(h.reshape(n, rows, cols), where, axis=0).reshape(n * rows, cols) for h in held]
     zt, zs = feats[:, :bot], feats[:, bot:]
     c = lax.dynamic_slice_in_dim(center, me * cols, cols)
     t_norm = jnp.sqrt(jnp.sum(jnp.square(tw.astype(jnp.float32)), 0) + 1e-06)

time: 76.3 us -> 78.7 us (1.031)
  local copies, waits for them, and re-layouts: 5 us -> 6.24 us
  other arithmetic: 6.37 us -> 7.23 us
    unnamed x12 -> x8, local copies, waits for them, and re-layouts: 2.2 us -> 0.89 us
    gather x2 -> x4, local copies, waits for them, and re-layouts: 1.16 us -> 2.25 us  [the longest x2 1.13 us: feature_plan(): jnp.take(by_destination(w), me ^ rel, axis=0)]
    reshape x2 -> x4, local copies, waits for them, and re-layouts: 0.09 us -> 1.07 us  [the longest x2 0.99 us: by_destination(): return weight.reshape(rows, n, cols).transpose(1, 0, 2)]
    another operation x4 -> x6, other arithmetic: 0.17 us -> 1.03 us  [feature_plan(): held = [jnp.stack([k, g], axis=dim) for k, g in zip(keep, got_held)]]
    ppermute x3 -> x4, waiting for transfers between devices: 19.6 us -> 19.5 us  [the longest x2 12.4 us: feature_plan(): got = lax.ppermute(jnp.concatenate(flat, axis=0), 'dp', pairs)]
    ppermute x3 -> x4, starting transfers between devices: 5.12 us -> 5.2 us  [the longest x1 3 us: feature_plan(): got = lax.ppermute(jnp.concatenate(flat[:2], axis=0), 'dp', pairs)]
  transfers between devices with their start and end apart: 9 -> 10, of which waited for: 8 -> 8; matrix products, arithmetic and copies ran while one was open for 2% -> 2% of each run, Pallas kernels for 0% -> 0%
where the time goes in v14:
time: 78.7 us; the launch traced here: 78.5 us
  waiting for transfers between devices  25.8 us (33%)
  starting transfers between devices  15.4 us (20%)
  matrix products  11.5 us (15%)
  blocking collectives  11.1 us (14%)
  other arithmetic  7.23 us (9%)
  local copies, waits for them, and re-layouts  6.24 us (8%)
  between operations  1.14 us (1%)
    ppermute x2, waiting for transfers between devices, feature_plan(): got = lax.ppermute(jnp.concatenate(flat, axis=0), 'dp', pairs)  12.4 us
    all_to_all x1, blocking collectives, feature_plan(): got = lax.all_to_all(sent, 'dp', 0, 2, tiled=True)  11.1 us
    ppermute x1, waiting for transfers between devices, feature_plan(): got = got + [lax.ppermute(flat[2], 'dp', pairs)]  7.03 us
    ppermute x3, starting transfers between devices, exchange_all(): total = total + lax.ppermute(x, axis, [(i, (i + k) % n) for i in range(n)])  6.05 us
    dot_general x1, matrix products, feature_plan(): lax.dot_general(zs, dlog, (((0,), (0,)), ((), ())), preferred_element_typ...  5.4 us
    ppermute x2, starting transfers between devices, feature_plan(): got = lax.ppermute(totals, 'dp', swap(up[r], down[r])).reshape(shape)  4.1 us
    ppermute x2, waiting for transfers between devices, feature_plan(): got = lax.ppermute(totals, 'dp', swap(up[r], down[r])).reshape(shape)  3.51 us
    dot_general x1, matrix products, feature_plan(): t_cos = jnp.dot(zt, tw, preferred_element_type=jnp.float32) / t_norm  3.18 us
  transfers between devices with their start and end apart: 10, of which 8 were waited for; matrix products, arithmetic and copies ran while one was open for 2% of the time, Pallas kernels for 0%

profile of v14, /device:TPU:0, one launch (start us, length us, event | category | flops | bytes accessed | tf_op | source)
XLA Modules:
  0.0 78.5 jit_solution(12834320490062227375)
XLA Ops:
  0.7 2.0 %fusion.29 = (bf16[32,4096]{1,0:T(8,128)(2,1)S(1)}, f32[32,4096]{1,0:T(8,128)}) fusion(bf16[32,4096]{1,0:T(8,128)(2,1)} %param.8, f32[32,4096]{1,0:T(8,128)} %param.7), kind=kLoop, calls=%fused_computation.91 | loop fusion | flops 655360 | bytes 1572864 | tf_op jit(solution)/shard_map/convert_element_type | solution.py:85
  2.8 1.0 %copy.53 = bf16[4,8,8,512]{3,2,0,1:T(8,128)(2,1)S(1)} copy(bf16[4,8,8,512]{3,2,1,0:T(8,128)(2,1)} %bitcast.103) | data formatting | bytes 524288 | tf_op jit(solution)/shard_map/reshape | solution.py:77
  3.7 0.6 gather_fusion.1
  4.3 0.6 gather_fusion
  5.5 3.0 %collective-permute-start = (bf16[384,512]{1,0:T(8,128)(2,1)S(1)}, bf16[384,512]{1,0:T(8,128)(2,1)S(1)}, u32[]{:S(2)}, u32[]{:S(2)}) collective-permute-start(bf16[384,512]{1,0:T(8,128)(2,1)S(1)} %pad_maximum_fusion.5), channel_id=1, source_target_pairs={{0,8},{4,20},{8,0},{12,28},{16,24},{20,4},{24,16},{28,12},{1,9},{5... | collective-permute-start | bytes 1179656 | tf_op jit(solution)/shard_map/ppermute | solution.py:104
  8.6 7.0 %collective-permute-done.1 = bf16[128,512]{1,0:T(8,128)(2,1)S(1)} collective-permute-done((bf16[128,512]{1,0:T(8,128)(2,1)S(1)}, bf16[128,512]{1,0:T(8,128)(2,1)S(1)}, u32[]{:S(2)}, u32[]{:S(2)}) %collective-permute-start.1) | collective-permute-done | bytes 131104 | tf_op jit(solution)/shard_map/ppermute | solution.py:106
  15.9 2.1 %collective-permute-start.2 = (bf16[768,512]{1,0:T(8,128)(2,1)S(1)}, bf16[768,512]{1,0:T(8,128)(2,1)S(1)}, u32[]{:S(2)}, u32[]{:S(2)}) collective-permute-start(bf16[768,512]{1,0:T(8,128)(2,1)S(1)} %pad_maximum_fusion.3), channel_id=1, source_target_pairs={{0,16},{4,12},{8,24},{12,4},{16,0},{20,28},{24,8},{28,20},{1,17},{... | collective-permute-start | bytes 2359304 | tf_op jit(solution)/shard_map/ppermute | solution.py:108
  18.0 10.0 %collective-permute-done.2 = bf16[768,512]{1,0:T(8,128)(2,1)S(1)} collective-permute-done((bf16[768,512]{1,0:T(8,128)(2,1)S(1)}, bf16[768,512]{1,0:T(8,128)(2,1)S(1)}, u32[]{:S(2)}, u32[]{:S(2)}) %collective-permute-start.2) | collective-permute-done | bytes 786464 | tf_op jit(solution)/shard_map/ppermute | solution.py:108
  28.1 0.7 fusion.33
  29.0 1.2 %pad_maximum_fusion.1 = bf16[1280,512]{1,0:T(8,128)(2,1)} fusion(bf16[128,512]{1,0:T(8,128)(2,1)S(1)} %bitcast.112, bf16[128,512]{1,0:T(8,128)(2,1)S(1)} %bitcast.114, bf16[1024,512]{1,0:T(8,128)(2,1)S(1)} %bitcast.88), kind=kLoop, calls=%fused_computation.11 | loop fusion | flops 3932160 | bytes 2621440 | tf_op jit(solution)/shard_map/concatenate | solution.py:108
  30.1 0.8 dynamic_slice.3
  30.9 2.5 %collective-permute-done.3 = bf16[1280,512]{1,0:T(8,128)(2,1)S(1)} collective-permute-done((bf16[1280,512]{1,0:T(8,128)(2,1)}, bf16[1280,512]{1,0:T(8,128)(2,1)S(1)}, u32[]{:S(2)}, u32[]{:S(2)}) %collective-permute-start.3) | collective-permute-done | bytes 1310752 | tf_op jit(solution)/shard_map/ppermute | solution.py:108
  33.6 0.9 %pad_maximum_fusion.8 = bf16[2,2,2,32,512]{4,3,1,0,2:T(8,128)(2,1)S(1)} fusion(bf16[1,2,2,32,512]{4,3,1,0,2:T(8,128)(2,1)S(1)} %bitcast.120, bf16[1,2,2,32,512]{4,3,1,0,2:T(8,128)(2,1)} %get-tuple-element.26), kind=kLoop, calls=%fused_computation.58 | loop fusion | flops 131072 | bytes 524288 | tf_op jit(solution)/shard_map/stack | solution.py:119
  34.6 0.6 gather_fusion.3
  35.2 0.6 gather_fusion.2
  36.2 3.0 %fusion.37 = (f32[2048]{0:T(1024)S(1)}, f32[2048,512]{0,1:T(8,128)}) fusion(f32[512]{0:T(512)S(1)} %add_sqrt_fusion.1, bf16[256,512]{1,0:T(8,128)(2,1)S(1)} %bitcast.107, bf16[2048,512]{1,0:T(8,128)(2,1)S(1)} %bitcast.92), kind=kOutput, calls=%fused_computation.99 | convolution fusion | flops 540014592 | bytes 5515264 | tf_op jit(solution)/shard_map/dot_general | solution.py:131
  39.2 3.2 %fusion = (f32[2048]{0:T(1024)S(1)}, f32[512]{0:T(512)S(1)}, f32[2048,512]{0,1:T(8,128)}) fusion(f32[512]{0:T(512)S(1)} %dynamic_slice.3, f32[512]{0:T(512)S(1)} %add_sqrt_fusion, bf16[256,512]{1,0:T(8,128)(2,1)S(1)} %bitcast.121, bf16[2048,512]{1,0:T(8,128)(2,1)S(1)} %bitcast.93), kind=kOutput, calls=%fused_computation.7 | convolution fusion | flops 542111232 | bytes 5519360 | tf_op jit(solution)/shard_map/dot_general | solution.py:130
  42.4 2.0 %collective-permute-start.4 = (f32[2,2048]{1,0:T(2,128)S(1)}, f32[2,2048]{1,0:T(2,128)S(1)}, u32[]{:S(2)}, u32[]{:S(2)}) collective-permute-start(f32[2,2048]{1,0:T(2,128)S(1)} %pad_maximum_fusion.9), channel_id=1, source_target_pairs={{0,8},{4,20},{8,0},{12,28},{16,24},{20,4},{24,16},{28,12},{1,9},{5... | collective-permute-start | bytes 49160 | tf_op jit(solution)/shard_map/ppermute | solution.py:141
  44.4 1.8 %collective-permute-done.4 = f32[2,2048]{1,0:T(2,128)S(1)} collective-permute-done((f32[2,2048]{1,0:T(2,128)S(1)}, f32[2,2048]{1,0:T(2,128)S(1)}, u32[]{:S(2)}, u32[]{:S(2)}) %collective-permute-start.4) | collective-permute-done | bytes 16416 | tf_op jit(solution)/shard_map/ppermute | solution.py:141
  46.4 2.1 %collective-permute-start.5 = (f32[2,2048]{1,0:T(2,128)S(1)}, f32[2,2048]{1,0:T(2,128)S(1)}, u32[]{:S(2)}, u32[]{:S(2)}) collective-permute-start(f32[2,2048]{1,0:T(2,128)S(1)} %fusion.26), channel_id=1, source_target_pairs={{0,16},{4,12},{8,24},{12,4},{16,0},{20,28},{24,8},{28,20},{1,17},{... | collective-permute-start | bytes 49160 | tf_op jit(solution)/shard_map/ppermute | solution.py:141
  48.4 1.7 %collective-permute-done.5 = f32[2,2048]{1,0:T(2,128)S(1)} collective-permute-done((f32[2,2048]{1,0:T(2,128)S(1)}, f32[2,2048]{1,0:T(2,128)S(1)}, u32[]{:S(2)}, u32[]{:S(2)}) %collective-permute-start.5) | collective-permute-done | bytes 16416 | tf_op jit(solution)/shard_map/ppermute | solution.py:141
  50.4 0.8 fusion.23
  51.1 0.4 collective-permute-done.6
  51.6 2.1 %collective-permute-start.7 = (f32[2,2048]{1,0:T(2,128)S(1)}, f32[2,2048]{1,0:T(2,128)S(1)}, u32[]{:S(2)}, u32[]{:S(2)}) collective-permute-start(f32[2,2048]{1,0:T(2,128)S(1)} %add.83), channel_id=1, source_target_pairs={{0,1},{1,2},{2,3},{3,0},{4,5},{5,6},{6,7},{7,4},{8,9},{9,10},{10,1... | collective-permute-start | bytes 49160 | tf_op jit(solution)/shard_map/ppermute | solution.py:58
  53.8 2.6 %collective-permute-start.8 = (f32[2,2048]{1,0:T(2,128)S(1)}, f32[2,2048]{1,0:T(2,128)S(1)}, u32[]{:S(2)}, u32[]{:S(2)}) collective-permute-start(f32[2,2048]{1,0:T(2,128)S(1)} %add.83), channel_id=1, source_target_pairs={{0,2},{1,3},{2,0},{3,1},{4,6},{5,7},{6,4},{7,5},{8,10},{9,11},{10,... | collective-permute-start | bytes 49160 | tf_op jit(solution)/shard_map/ppermute | solution.py:58
  56.4 1.3 %collective-permute-start.9 = (f32[2,2048]{1,0:T(2,128)S(1)}, f32[2,2048]{1,0:T(2,128)S(1)}, u32[]{:S(2)}, u32[]{:S(2)}) collective-permute-start(f32[2,2048]{1,0:T(2,128)S(1)} %add.83), channel_id=1, source_target_pairs={{0,3},{1,0},{2,1},{3,2},{4,7},{5,4},{6,5},{7,6},{8,11},{9,8},{10,9... | collective-permute-start | bytes 49160 | tf_op jit(solution)/shard_map/ppermute | solution.py:58
  57.7 0.9 %collective-permute-done.8 = f32[2,2048]{1,0:T(2,128)S(1)} collective-permute-done((f32[2,2048]{1,0:T(2,128)S(1)}, f32[2,2048]{1,0:T(2,128)S(1)}, u32[]{:S(2)}, u32[]{:S(2)}) %collective-permute-start.8) | collective-permute-done | bytes 16416 | tf_op jit(solution)/shard_map/ppermute | solution.py:58
  58.6 1.5 %collective-permute-done.9 = f32[2,2048]{1,0:T(2,128)S(1)} collective-permute-done((f32[2,2048]{1,0:T(2,128)S(1)}, f32[2,2048]{1,0:T(2,128)S(1)}, u32[]{:S(2)}, u32[]{:S(2)}) %collective-permute-start.9) | collective-permute-done | bytes 16416 | tf_op jit(solution)/shard_map/ppermute | solution.py:58
  60.1 5.4 %fusion.5 = (f32[512]{0:T(512)S(1)}, f32[256,512]{1,0:T(8,128)S(1)}) fusion(bf16[8,32,512]{2,1,0:T(8,128)(2,1)S(1)} %get-tuple-element.7, f32[2048,512]{0,1:T(8,128)} %get-tuple-element.42, f32[2048,512]{0,1:T(8,128)} %get-tuple-element.40, f32[2048]{0:T(1024)S(1)} %bitcast.132, f32[2048]{0:T(1024)S(1)} %bitcast.131, f32[512]{0:T(512)S(1)} %dynamic_slice.3, ...), kind=kOutput, calls=%fused_computation.21 | convolution fusion | flops 544603648 | bytes 10244096 | tf_op jit(solution)/shard_map/dot_general | solution.py:148
  65.7 11.1 %all_to_all.4 = bf16[8,34,512]{2,1,0:T(8,128)(2,1)S(1)} all-to-all(bf16[8,34,512]{2,1,0:T(8,128)(2,1)S(1)} %pad_maximum_fusion.6), channel_id=1, replica_groups=mesh['dp'=8,'tensor'=4] {'dp'}, dimensions={0} | all-to-all | bytes 557056 | tf_op jit(solution)/shard_map/all_to_all | solution.py:163
  77.0 0.6 slice_add_fusion
  77.6 0.8 %copy.42 = f32[4,8,8,512]{3,1,2,0:T(8,128)} copy(f32[4,8,8,512]{3,1,0,2:T(8,128)S(1)} %slice_bitcast_fusion.2) | data formatting | bytes 1048576
  (74 shorter events, 2.6 us)
Async XLA Ops:
  0.6 4.4 %copy-start.2 = (bf16[256,256]{1,0:T(8,128)(2,1)S(1)}, bf16[256,256]{1,0:T(8,128)(2,1)}, u32[]{:S(2)}) copy-start(bf16[256,256]{1,0:T(8,128)(2,1)} %param.10) | copy-start | bytes 393220
  0.6 4.5 %copy-start.1 = (bf16[256,256]{1,0:T(8,128)(2,1)S(1)}, bf16[256,256]{1,0:T(8,128)(2,1)}, u32[]{:S(2)}) copy-start(bf16[256,256]{1,0:T(8,128)(2,1)} %param.9) | copy-start | bytes 393220
  5.5 10.2 %collective-permute-start = (bf16[384,512]{1,0:T(8,128)(2,1)S(1)}, bf16[384,512]{1,0:T(8,128)(2,1)S(1)}, u32[]{:S(2)}, u32[]{:S(2)}) collective-permute-start(bf16[384,512]{1,0:T(8,128)(2,1)S(1)} %pad_maximum_fusion.5), channel_id=1, source_target_pairs={{0,8},{4,20},{8,0},{12,28},{16,24},{20,4},{24,16},{28,12},{1,9},{5... | collective-permute-start | bytes 1179656 | tf_op jit(solution)/shard_map/ppermute | solution.py:104
  8.5 7.1 %collective-permute-start.1 = (bf16[128,512]{1,0:T(8,128)(2,1)S(1)}, bf16[128,512]{1,0:T(8,128)(2,1)S(1)}, u32[]{:S(2)}, u32[]{:S(2)}) collective-permute-start(bf16[128,512]{1,0:T(8,128)(2,1)S(1)} %bitcast.122), channel_id=1, source_target_pairs={{0,8},{4,20},{8,0},{12,28},{16,24},{20,4},{24,16},{28,12},{1,9},{5... | collective-permute-start | bytes 393224 | tf_op jit(solution)/shard_map/ppermute | solution.py:106
  15.9 12.1 %collective-permute-start.2 = (bf16[768,512]{1,0:T(8,128)(2,1)S(1)}, bf16[768,512]{1,0:T(8,128)(2,1)S(1)}, u32[]{:S(2)}, u32[]{:S(2)}) collective-permute-start(bf16[768,512]{1,0:T(8,128)(2,1)S(1)} %pad_maximum_fusion.3), channel_id=1, source_target_pairs={{0,16},{4,12},{8,24},{12,4},{16,0},{20,28},{24,8},{28,20},{1,17},{... | collective-permute-start | bytes 2359304 | tf_op jit(solution)/shard_map/ppermute | solution.py:108
  30.1 3.2 %collective-permute-start.3 = (bf16[1280,512]{1,0:T(8,128)(2,1)}, bf16[1280,512]{1,0:T(8,128)(2,1)S(1)}, u32[]{:S(2)}, u32[]{:S(2)}) collective-permute-start(bf16[1280,512]{1,0:T(8,128)(2,1)} %pad_maximum_fusion.1), channel_id=1, source_target_pairs={{0,4},{4,0},{8,12},{12,8},{16,20},{20,16},{24,28},{28,24},{1,5},{5... | collective-permute-start | bytes 3932168 | tf_op jit(solution)/shard_map/ppermute | solution.py:108
  36.2 3.0 %copy-start = (bf16[2,2,2,256,512]{4,3,2,1,0:T(8,128)(2,1)}, bf16[2,2,2,256,512]{4,3,2,1,0:T(8,128)(2,1)S(1)}, u32[]{:S(2)}) copy-start(bf16[2,2,2,256,512]{4,3,2,1,0:T(8,128)(2,1)S(1)} %pad_maximum_fusion) | copy-start | bytes 6291460
  42.4 3.8 %collective-permute-start.4 = (f32[2,2048]{1,0:T(2,128)S(1)}, f32[2,2048]{1,0:T(2,128)S(1)}, u32[]{:S(2)}, u32[]{:S(2)}) collective-permute-start(f32[2,2048]{1,0:T(2,128)S(1)} %pad_maximum_fusion.9), channel_id=1, source_target_pairs={{0,8},{4,20},{8,0},{12,28},{16,24},{20,4},{24,16},{28,12},{1,9},{5... | collective-permute-start | bytes 49160 | tf_op jit(solution)/shard_map/ppermute | solution.py:141
  46.4 3.8 %collective-permute-start.5 = (f32[2,2048]{1,0:T(2,128)S(1)}, f32[2,2048]{1,0:T(2,128)S(1)}, u32[]{:S(2)}, u32[]{:S(2)}) collective-permute-start(f32[2,2048]{1,0:T(2,128)S(1)} %fusion.26), channel_id=1, source_target_pairs={{0,16},{4,12},{8,24},{12,4},{16,0},{20,28},{24,8},{28,20},{1,17},{... | collective-permute-start | bytes 49160 | tf_op jit(solution)/shard_map/ppermute | solution.py:141
  50.3 1.2 %collective-permute-start.6 = (f32[2,2048]{1,0:T(2,128)S(1)}, f32[2,2048]{1,0:T(2,128)S(1)}, u32[]{:S(2)}, u32[]{:S(2)}) collective-permute-start(f32[2,2048]{1,0:T(2,128)S(1)} %fusion.40), channel_id=1, source_target_pairs={{0,4},{4,0},{8,12},{12,8},{16,20},{20,16},{24,28},{28,24},{1,5},{5... | collective-permute-start | bytes 49160 | tf_op jit(solution)/shard_map/ppermute | solution.py:138
  51.6 6.1 %collective-permute-start.7 = (f32[2,2048]{1,0:T(2,128)S(1)}, f32[2,2048]{1,0:T(2,128)S(1)}, u32[]{:S(2)}, u32[]{:S(2)}) collective-permute-start(f32[2,2048]{1,0:T(2,128)S(1)} %add.83), channel_id=1, source_target_pairs={{0,1},{1,2},{2,3},{3,0},{4,5},{5,6},{6,7},{7,4},{8,9},{9,10},{10,1... | collective-permute-start | bytes 49160 | tf_op jit(solution)/shard_map/ppermute | solution.py:58
  53.8 4.9 %collective-permute-start.8 = (f32[2,2048]{1,0:T(2,128)S(1)}, f32[2,2048]{1,0:T(2,128)S(1)}, u32[]{:S(2)}, u32[]{:S(2)}) collective-permute-start(f32[2,2048]{1,0:T(2,128)S(1)} %add.83), channel_id=1, source_target_pairs={{0,2},{1,3},{2,0},{3,1},{4,6},{5,7},{6,4},{7,5},{8,10},{9,11},{10,... | collective-permute-start | bytes 49160 | tf_op jit(solution)/shard_map/ppermute | solution.py:58
  56.4 3.7 %collective-permute-start.9 = (f32[2,2048]{1,0:T(2,128)S(1)}, f32[2,2048]{1,0:T(2,128)S(1)}, u32[]{:S(2)}, u32[]{:S(2)}) collective-permute-start(f32[2,2048]{1,0:T(2,128)S(1)} %add.83), channel_id=1, source_target_pairs={{0,3},{1,0},{2,1},{3,2},{4,7},{5,4},{6,5},{7,6},{8,11},{9,8},{10,9... | collective-permute-start | bytes 49160 | tf_op jit(solution)/shard_map/ppermute | solution.py:58

commit v15 on v11

--- a/solution.py
+++ b/solution.py
@@ -124,6 +124,8 @@
     t_exp = jnp.exp((t_cos - c) / 0.04)
     s_exp = jnp.exp(s_cos / 0.1)
     totals = jnp.stack([jnp.sum(t_exp, 1), jnp.sum(s_exp, 1)])
+    t_exp = t_exp.astype(jnp.bfloat16).astype(jnp.float32)
+    s_exp = s_exp.astype(jnp.bfloat16).astype(jnp.float32)
     shape = (2,) + (2,) * nbits + (images,)
     for r in range(nbits):
         if r == nbits - 1:

time: 76.3 us -> 75.2 us (0.986)
  matrix products: 11.2 us -> 10.1 us
where the time goes in v15:
time: 75.2 us; the launch traced here: 74.9 us
  waiting for transfers between devices  25.8 us (34%)
  starting transfers between devices  15.4 us (20%)
  blocking collectives  11.1 us (15%)
  matrix products  10.1 us (13%)
  other arithmetic  6.37 us (8%)
  local copies, waits for them, and re-layouts  5 us (7%)
  between operations  1.11 us (1%)
    ppermute x3, waiting for transfers between devices, feature_plan(): got = lax.ppermute(payload, 'dp', pairs)  19.6 us
    all_to_all x1, blocking collectives, feature_plan(): got = lax.all_to_all(sent, 'dp', 0, 2, tiled=True)  11.1 us
    ppermute x3, starting transfers between devices, exchange_all(): total = total + lax.ppermute(x, axis, [(i, (i + k) % n) for i in range(n)])  6.07 us
    ppermute x3, starting transfers between devices, feature_plan(): got = lax.ppermute(payload, 'dp', pairs)  5.12 us
    dot_general x1, matrix products, feature_plan(): lax.dot_general(zs, dlog, (((0,), (0,)), ((), ())), preferred_element_typ...  4.61 us
    ppermute x2, starting transfers between devices, feature_plan(): got = lax.ppermute(totals, 'dp', swap(up[r], down[r])).reshape(shape)  4.13 us
    ppermute x2, waiting for transfers between devices, feature_plan(): got = lax.ppermute(totals, 'dp', swap(up[r], down[r])).reshape(shape)  3.47 us
    dot_general x1, matrix products, feature_plan(): t_cos = jnp.dot(zt, tw, preferred_element_type=jnp.float32) / t_norm  3.16 us
  transfers between devices with their start and end apart: 9, of which 8 were waited for; matrix products, arithmetic and copies ran while one was open for 2% of the time, Pallas kernels for 0%

profile of v15, /device:TPU:0, one launch (start us, length us, event | category | flops | bytes accessed | tf_op | source)
XLA Modules:
  0.0 74.9 jit_solution(7787979435828009332)
XLA Ops:
  0.7 2.0 %fusion.25 = (bf16[32,4096]{1,0:T(8,128)(2,1)S(1)}, f32[32,4096]{1,0:T(8,128)}) fusion(bf16[32,4096]{1,0:T(8,128)(2,1)} %param.8, f32[32,4096]{1,0:T(8,128)} %param.7), kind=kLoop, calls=%fused_computation.77 | loop fusion | flops 655360 | bytes 1572864 | tf_op jit(solution)/shard_map/convert_element_type | solution.py:75
  2.9 1.0 %copy.27 = bf16[4,8,8,512]{3,2,1,0:T(8,128)(2,1)S(1)} copy(bf16[4,8,8,512]{3,1,2,0:T(8,128)(2,1)} %bitcast.87) | data formatting | bytes 524288
  4.1 0.6 gather_fusion
  5.1 0.1 fusion.15
  5.3 3.0 %collective-permute-start = (bf16[512,512]{1,0:T(8,128)(2,1)S(1)}, bf16[512,512]{1,0:T(8,128)(2,1)S(1)}, u32[]{:S(2)}, u32[]{:S(2)}) collective-permute-start(bf16[512,512]{1,0:T(8,128)(2,1)S(1)} %pad_maximum_fusion.5), channel_id=1, source_target_pairs={{0,8},{4,20},{8,0},{12,28},{16,24},{20,4},{24,16},{28,12},{1,9},{5... | collective-permute-start | bytes 1572872 | tf_op jit(solution)/shard_map/ppermute | solution.py:100
  8.4 7.1 %collective-permute-done = bf16[512,512]{1,0:T(8,128)(2,1)S(1)} collective-permute-done((bf16[512,512]{1,0:T(8,128)(2,1)S(1)}, bf16[512,512]{1,0:T(8,128)(2,1)S(1)}, u32[]{:S(2)}, u32[]{:S(2)}) %collective-permute-start) | collective-permute-done | bytes 524320 | tf_op jit(solution)/shard_map/ppermute | solution.py:100
  15.7 2.1 %collective-permute-start.1 = (bf16[768,512]{1,0:T(8,128)(2,1)S(1)}, bf16[768,512]{1,0:T(8,128)(2,1)S(1)}, u32[]{:S(2)}, u32[]{:S(2)}) collective-permute-start(bf16[768,512]{1,0:T(8,128)(2,1)S(1)} %pad_maximum_fusion.3), channel_id=1, source_target_pairs={{0,16},{4,12},{8,24},{12,4},{16,0},{20,28},{24,8},{28,20},{1,17},{... | collective-permute-start | bytes 2359304 | tf_op jit(solution)/shard_map/ppermute | solution.py:100
  17.8 10.0 %collective-permute-done.1 = bf16[768,512]{1,0:T(8,128)(2,1)S(1)} collective-permute-done((bf16[768,512]{1,0:T(8,128)(2,1)S(1)}, bf16[768,512]{1,0:T(8,128)(2,1)S(1)}, u32[]{:S(2)}, u32[]{:S(2)}) %collective-permute-start.1) | collective-permute-done | bytes 786464 | tf_op jit(solution)/shard_map/ppermute | solution.py:100
  28.0 0.1 fusion.24
  28.1 1.2 %pad_maximum_fusion.1 = bf16[1280,512]{1,0:T(8,128)(2,1)} fusion(bf16[256,512]{1,0:T(8,128)(2,1)S(1)} %bitcast.81, bf16[1024,512]{1,0:T(8,128)(2,1)S(1)} %bitcast.67), kind=kLoop, calls=%fused_computation.10 | loop fusion | flops 2621440 | bytes 2621440 | tf_op jit(solution)/shard_map/concatenate | solution.py:99
  29.3 0.8 %dynamic_slice.3 = f32[512]{0:T(512)S(1)} dynamic-slice(f32[4096]{0:T(1024)} %param.11, s32[]{:T(128)S(6)} %select_n.27), dynamic_slice_sizes={512} | dynamic-slice | bytes 4100 | tf_op jit(solution)/shard_map/dynamic_slice | solution.py:119
  30.0 2.5 %collective-permute-done.2 = bf16[1280,512]{1,0:T(8,128)(2,1)S(1)} collective-permute-done((bf16[1280,512]{1,0:T(8,128)(2,1)}, bf16[1280,512]{1,0:T(8,128)(2,1)S(1)}, u32[]{:S(2)}, u32[]{:S(2)}) %collective-permute-start.2) | collective-permute-done | bytes 1310752 | tf_op jit(solution)/shard_map/ppermute | solution.py:100
  32.6 0.6 gather_fusion.1
  33.7 0.2 pad_maximum_fusion
  33.9 0.2 copy-done
  34.1 2.3 %fusion.30 = (f32[2048]{0:T(1024)S(1)}, bf16[2048,512]{0,1:T(8,128)(2,1)}) fusion(f32[512]{0:T(512)S(1)} %add_sqrt_fusion.1, bf16[256,512]{1,0:T(8,128)(2,1)S(1)} %bitcast.90, bf16[2048,512]{1,0:T(8,128)(2,1)S(1)} %bitcast.73), kind=kOutput, calls=%fused_computation.82 | convolution fusion | flops 541063168 | bytes 3418112 | tf_op jit(solution)/shard_map/dot_general | solution.py:123
  36.4 3.2 %fusion.1 = (f32[2048]{0:T(1024)S(1)}, f32[512]{0:T(512)S(1)}, f32[2048,512]{0,1:T(8,128)}) fusion(f32[512]{0:T(512)S(1)} %dynamic_slice.3, f32[512]{0:T(512)S(1)} %add_sqrt_fusion, bf16[256,512]{1,0:T(8,128)(2,1)S(1)} %bitcast.93, bf16[2048,512]{1,0:T(8,128)(2,1)S(1)} %bitcast.74), kind=kOutput, calls=%fused_computation.6 | convolution fusion | flops 542111232 | bytes 5519360 | tf_op jit(solution)/shard_map/dot_general | solution.py:122
  39.6 2.0 %collective-permute-start.3 = (f32[2,2048]{1,0:T(2,128)S(1)}, f32[2,2048]{1,0:T(2,128)S(1)}, u32[]{:S(2)}, u32[]{:S(2)}) collective-permute-start(f32[2,2048]{1,0:T(2,128)S(1)} %pad_maximum_fusion.9), channel_id=1, source_target_pairs={{0,8},{4,20},{8,0},{12,28},{16,24},{20,4},{24,16},{28,12},{1,9},{5... | collective-permute-start | bytes 49160 | tf_op jit(solution)/shard_map/ppermute | solution.py:135
  41.7 1.8 %collective-permute-done.3 = f32[2,2048]{1,0:T(2,128)S(1)} collective-permute-done((f32[2,2048]{1,0:T(2,128)S(1)}, f32[2,2048]{1,0:T(2,128)S(1)}, u32[]{:S(2)}, u32[]{:S(2)}) %collective-permute-start.3) | collective-permute-done | bytes 16416 | tf_op jit(solution)/shard_map/ppermute | solution.py:135
  43.6 2.1 %collective-permute-start.4 = (f32[2,2048]{1,0:T(2,128)S(1)}, f32[2,2048]{1,0:T(2,128)S(1)}, u32[]{:S(2)}, u32[]{:S(2)}) collective-permute-start(f32[2,2048]{1,0:T(2,128)S(1)} %fusion.22), channel_id=1, source_target_pairs={{0,16},{4,12},{8,24},{12,4},{16,0},{20,28},{24,8},{28,20},{1,17},{... | collective-permute-start | bytes 49160 | tf_op jit(solution)/shard_map/ppermute | solution.py:135
  45.7 1.7 %collective-permute-done.4 = f32[2,2048]{1,0:T(2,128)S(1)} collective-permute-done((f32[2,2048]{1,0:T(2,128)S(1)}, f32[2,2048]{1,0:T(2,128)S(1)}, u32[]{:S(2)}, u32[]{:S(2)}) %collective-permute-start.4) | collective-permute-done | bytes 16416 | tf_op jit(solution)/shard_map/ppermute | solution.py:135
  47.6 0.8 %fusion.19 = (bf16[512]{0:T(512)(128)(2,1)S(1)}, bf16[512]{0:T(512)(128)(2,1)S(1)}) fusion(f32[512]{0:T(512)S(1)} %get-tuple-element.5, f32[4096]{0:T(1024)} %param.11, s32[]{:T(128)S(6)} %select_n.27), kind=kLoop, calls=%fused_computation.71 | loop fusion | flops 3584 | bytes 6148 | tf_op jit(solution)/shard_map/convert_element_type | solution.py:148
  48.4 0.4 collective-permute-done.5
  48.9 2.1 %collective-permute-start.6 = (f32[2,2048]{1,0:T(2,128)S(1)}, f32[2,2048]{1,0:T(2,128)S(1)}, u32[]{:S(2)}, u32[]{:S(2)}) collective-permute-start(f32[2,2048]{1,0:T(2,128)S(1)} %add.83), channel_id=1, source_target_pairs={{0,1},{1,2},{2,3},{3,0},{4,5},{5,6},{6,7},{7,4},{8,9},{9,10},{10,1... | collective-permute-start | bytes 49160 | tf_op jit(solution)/shard_map/ppermute | solution.py:58
  51.0 2.6 %collective-permute-start.7 = (f32[2,2048]{1,0:T(2,128)S(1)}, f32[2,2048]{1,0:T(2,128)S(1)}, u32[]{:S(2)}, u32[]{:S(2)}) collective-permute-start(f32[2,2048]{1,0:T(2,128)S(1)} %add.83), channel_id=1, source_target_pairs={{0,2},{1,3},{2,0},{3,1},{4,6},{5,7},{6,4},{7,5},{8,10},{9,11},{10,... | collective-permute-start | bytes 49160 | tf_op jit(solution)/shard_map/ppermute | solution.py:58
  53.6 1.3 %collective-permute-start.8 = (f32[2,2048]{1,0:T(2,128)S(1)}, f32[2,2048]{1,0:T(2,128)S(1)}, u32[]{:S(2)}, u32[]{:S(2)}) collective-permute-start(f32[2,2048]{1,0:T(2,128)S(1)} %add.83), channel_id=1, source_target_pairs={{0,3},{1,0},{2,1},{3,2},{4,7},{5,4},{6,5},{7,6},{8,11},{9,8},{10,9... | collective-permute-start | bytes 49160 | tf_op jit(solution)/shard_map/ppermute | solution.py:58
  55.0 0.9 %collective-permute-done.7 = f32[2,2048]{1,0:T(2,128)S(1)} collective-permute-done((f32[2,2048]{1,0:T(2,128)S(1)}, f32[2,2048]{1,0:T(2,128)S(1)}, u32[]{:S(2)}, u32[]{:S(2)}) %collective-permute-start.7) | collective-permute-done | bytes 16416 | tf_op jit(solution)/shard_map/ppermute | solution.py:58
  55.9 1.4 %collective-permute-done.8 = f32[2,2048]{1,0:T(2,128)S(1)} collective-permute-done((f32[2,2048]{1,0:T(2,128)S(1)}, f32[2,2048]{1,0:T(2,128)S(1)}, u32[]{:S(2)}, u32[]{:S(2)}) %collective-permute-start.8) | collective-permute-done | bytes 16416 | tf_op jit(solution)/shard_map/ppermute | solution.py:58
  57.4 4.6 %fusion.8 = (f32[512]{0:T(512)S(1)}, f32[256,512]{1,0:T(8,128)S(1)}) fusion(bf16[8,32,512]{2,1,0:T(8,128)(2,1)S(1)} %copy-done.1, f32[2048,512]{0,1:T(8,128)} %get-tuple-element.30, f32[2048]{0:T(1024)S(1)} %bitcast.103, f32[2048]{0:T(1024)S(1)} %bitcast.102, f32[512]{0:T(512)S(1)} %dynamic_slice.3, bf16[2048,512]{0,1:T(8,128)(2,1)} %get-tuple-element.32, ...), kind=kOutput, calls=%fused_computation.25 | convolution fusion | flops 547749376 | bytes 8146944 | tf_op jit(solution)/shard_map/dot_general | solution.py:142
  62.2 11.1 %all_to_all.4 = bf16[8,34,512]{2,1,0:T(8,128)(2,1)S(1)} all-to-all(bf16[8,34,512]{2,1,0:T(8,128)(2,1)S(1)} %pad_maximum_fusion.8), channel_id=1, replica_groups=mesh['dp'=8,'tensor'=4] {'dp'}, dimensions={0} | all-to-all | bytes 557056 | tf_op jit(solution)/shard_map/all_to_all | solution.py:157
  73.5 0.6 slice_add_fusion
  74.1 0.8 %copy.29 = f32[4,8,8,512]{3,1,2,0:T(8,128)} copy(f32[4,8,8,512]{3,1,0,2:T(8,128)S(1)} %slice_bitcast_fusion.1) | data formatting | bytes 1048576
  (68 shorter events, 2.4 us)
Async XLA Ops:
  0.6 4.2 %copy-start.3 = (bf16[256,256]{1,0:T(8,128)(2,1)S(1)}, bf16[256,256]{1,0:T(8,128)(2,1)}, u32[]{:S(2)}) copy-start(bf16[256,256]{1,0:T(8,128)(2,1)} %param.10) | copy-start | bytes 393220
  0.6 4.4 %copy-start.2 = (bf16[256,256]{1,0:T(8,128)(2,1)S(1)}, bf16[256,256]{1,0:T(8,128)(2,1)}, u32[]{:S(2)}) copy-start(bf16[256,256]{1,0:T(8,128)(2,1)} %param.9) | copy-start | bytes 393220
  5.3 10.2 %collective-permute-start = (bf16[512,512]{1,0:T(8,128)(2,1)S(1)}, bf16[512,512]{1,0:T(8,128)(2,1)S(1)}, u32[]{:S(2)}, u32[]{:S(2)}) collective-permute-start(bf16[512,512]{1,0:T(8,128)(2,1)S(1)} %pad_maximum_fusion.5), channel_id=1, source_target_pairs={{0,8},{4,20},{8,0},{12,28},{16,24},{20,4},{24,16},{28,12},{1,9},{5... | collective-permute-start | bytes 1572872 | tf_op jit(solution)/shard_map/ppermute | solution.py:100
  15.7 12.1 %collective-permute-start.1 = (bf16[768,512]{1,0:T(8,128)(2,1)S(1)}, bf16[768,512]{1,0:T(8,128)(2,1)S(1)}, u32[]{:S(2)}, u32[]{:S(2)}) collective-permute-start(bf16[768,512]{1,0:T(8,128)(2,1)S(1)} %pad_maximum_fusion.3), channel_id=1, source_target_pairs={{0,16},{4,12},{8,24},{12,4},{16,0},{20,28},{24,8},{28,20},{1,17},{... | collective-permute-start | bytes 2359304 | tf_op jit(solution)/shard_map/ppermute | solution.py:100
  29.3 3.2 %collective-permute-start.2 = (bf16[1280,512]{1,0:T(8,128)(2,1)}, bf16[1280,512]{1,0:T(8,128)(2,1)S(1)}, u32[]{:S(2)}, u32[]{:S(2)}) collective-permute-start(bf16[1280,512]{1,0:T(8,128)(2,1)} %pad_maximum_fusion.1), channel_id=1, source_target_pairs={{0,4},{4,0},{8,12},{12,8},{16,20},{20,16},{24,28},{28,24},{1,5},{5... | collective-permute-start | bytes 3932168 | tf_op jit(solution)/shard_map/ppermute | solution.py:100
  33.4 0.7 copy-start
  36.4 21.0 %copy-start.1 = (bf16[8,32,512]{2,1,0:T(8,128)(2,1)S(1)}, bf16[8,32,512]{2,1,0:T(8,128)(2,1)}, u32[]{:S(2)}) copy-start(bf16[8,32,512]{2,1,0:T(8,128)(2,1)} %copy-done) | copy-start | bytes 786436
  39.6 3.8 %collective-permute-start.3 = (f32[2,2048]{1,0:T(2,128)S(1)}, f32[2,2048]{1,0:T(2,128)S(1)}, u32[]{:S(2)}, u32[]{:S(2)}) collective-permute-start(f32[2,2048]{1,0:T(2,128)S(1)} %pad_maximum_fusion.9), channel_id=1, source_target_pairs={{0,8},{4,20},{8,0},{12,28},{16,24},{20,4},{24,16},{28,12},{1,9},{5... | collective-permute-start | bytes 49160 | tf_op jit(solution)/shard_map/ppermute | solution.py:135
  43.6 3.8 %collective-permute-start.4 = (f32[2,2048]{1,0:T(2,128)S(1)}, f32[2,2048]{1,0:T(2,128)S(1)}, u32[]{:S(2)}, u32[]{:S(2)}) collective-permute-start(f32[2,2048]{1,0:T(2,128)S(1)} %fusion.22), channel_id=1, source_target_pairs={{0,16},{4,12},{8,24},{12,4},{16,0},{20,28},{24,8},{28,20},{1,17},{... | collective-permute-start | bytes 49160 | tf_op jit(solution)/shard_map/ppermute | solution.py:135
  47.6 1.2 %collective-permute-start.5 = (f32[2,2048]{1,0:T(2,128)S(1)}, f32[2,2048]{1,0:T(2,128)S(1)}, u32[]{:S(2)}, u32[]{:S(2)}) collective-permute-start(f32[2,2048]{1,0:T(2,128)S(1)} %fusion.33), channel_id=1, source_target_pairs={{0,4},{4,0},{8,12},{12,8},{16,20},{20,16},{24,28},{28,24},{1,5},{5... | collective-permute-start | bytes 49160 | tf_op jit(solution)/shard_map/ppermute | solution.py:132
  48.9 6.1 %collective-permute-start.6 = (f32[2,2048]{1,0:T(2,128)S(1)}, f32[2,2048]{1,0:T(2,128)S(1)}, u32[]{:S(2)}, u32[]{:S(2)}) collective-permute-start(f32[2,2048]{1,0:T(2,128)S(1)} %add.83), channel_id=1, source_target_pairs={{0,1},{1,2},{2,3},{3,0},{4,5},{5,6},{6,7},{7,4},{8,9},{9,10},{10,1... | collective-permute-start | bytes 49160 | tf_op jit(solution)/shard_map/ppermute | solution.py:58
  51.0 4.9 %collective-permute-start.7 = (f32[2,2048]{1,0:T(2,128)S(1)}, f32[2,2048]{1,0:T(2,128)S(1)}, u32[]{:S(2)}, u32[]{:S(2)}) collective-permute-start(f32[2,2048]{1,0:T(2,128)S(1)} %add.83), channel_id=1, source_target_pairs={{0,2},{1,3},{2,0},{3,1},{4,6},{5,7},{6,4},{7,5},{8,10},{9,11},{10,... | collective-permute-start | bytes 49160 | tf_op jit(solution)/shard_map/ppermute | solution.py:58
  53.6 3.7 %collective-permute-start.8 = (f32[2,2048]{1,0:T(2,128)S(1)}, f32[2,2048]{1,0:T(2,128)S(1)}, u32[]{:S(2)}, u32[]{:S(2)}) collective-permute-start(f32[2,2048]{1,0:T(2,128)S(1)} %add.83), channel_id=1, source_target_pairs={{0,3},{1,0},{2,1},{3,2},{4,7},{5,4},{6,5},{7,6},{8,11},{9,8},{10,9... | collective-permute-start | bytes 49160 | tf_op jit(solution)/shard_map/ppermute | solution.py:58

commit v16 on v11

--- a/solution.py
+++ b/solution.py
@@ -124,6 +124,8 @@
     t_exp = jnp.exp((t_cos - c) / 0.04)
     s_exp = jnp.exp(s_cos / 0.1)
     totals = jnp.stack([jnp.sum(t_exp, 1), jnp.sum(s_exp, 1)])
+    t_exp, s_exp = lax.optimization_barrier((t_exp.astype(jnp.bfloat16), s_exp.astype(jnp.bfloat16)))
+    t_exp, s_exp = t_exp.astype(jnp.float32), s_exp.astype(jnp.float32)
     shape = (2,) + (2,) * nbits + (images,)
     for r in range(nbits):
         if r == nbits - 1:

time: 76.3 us -> 72.4 us (0.949)
  matrix products: 11.2 us -> 8.22 us
  local copies, waits for them, and re-layouts: 5 us -> 4.12 us
    dot_general x1, matrix products: 5.09 us -> 3.47 us  [feature_plan(): lax.dot_general(zs, dlog, (((0,), (0,)), ((), ())), preferred_element_typ...]
    unnamed x12 -> x14, local copies, waits for them, and re-layouts: 2.2 us -> 1.32 us
where the time goes in v16:
time: 72.4 us; the launch traced here: 72.2 us
  waiting for transfers between devices  25.8 us (36%)
  starting transfers between devices  15.4 us (21%)
  blocking collectives  11.2 us (15%)
  matrix products  8.22 us (11%)
  other arithmetic  6.35 us (9%)
  local copies, waits for them, and re-layouts  4.12 us (6%)
  between operations  1.12 us (2%)
    ppermute x3, waiting for transfers between devices, feature_plan(): got = lax.ppermute(payload, 'dp', pairs)  19.6 us
    all_to_all x1, blocking collectives, feature_plan(): got = lax.all_to_all(sent, 'dp', 0, 2, tiled=True)  11.2 us
    ppermute x3, starting transfers between devices, exchange_all(): total = total + lax.ppermute(x, axis, [(i, (i + k) % n) for i in range(n)])  6.07 us
    ppermute x3, starting transfers between devices, feature_plan(): got = lax.ppermute(payload, 'dp', pairs)  5.12 us
    ppermute x2, starting transfers between devices, feature_plan(): got = lax.ppermute(totals, 'dp', swap(up[r], down[r])).reshape(shape)  4.14 us
    ppermute x2, waiting for transfers between devices, feature_plan(): got = lax.ppermute(totals, 'dp', swap(up[r], down[r])).reshape(shape)  3.47 us
    dot_general x1, matrix products, feature_plan(): lax.dot_general(zs, dlog, (((0,), (0,)), ((), ())), preferred_element_typ...  3.47 us
    dot_general x1, matrix products, feature_plan(): t_cos = jnp.dot(zt, tw, preferred_element_type=jnp.float32) / t_norm  2.53 us
  transfers between devices with their start and end apart: 9, of which 8 were waited for; matrix products, arithmetic and copies ran while one was open for 2% of the time, Pallas kernels for 0%

profile of v16, /device:TPU:0, one launch (start us, length us, event | category | flops | bytes accessed | tf_op | source)
XLA Modules:
  0.0 72.2 jit_solution(5730765004240952965)
XLA Ops:
  0.7 2.0 %fusion.24 = (bf16[32,4096]{1,0:T(8,128)(2,1)S(1)}, f32[32,4096]{1,0:T(8,128)}) fusion(bf16[32,4096]{1,0:T(8,128)(2,1)} %param.8, f32[32,4096]{1,0:T(8,128)} %param.7), kind=kLoop, calls=%fused_computation.76 | loop fusion | flops 655360 | bytes 1572864 | tf_op jit(solution)/shard_map/convert_element_type | solution.py:75
  3.2 0.6 gather_fusion
  4.3 0.1 fusion.15
  4.5 3.0 %collective-permute-start = (bf16[512,512]{1,0:T(8,128)(2,1)S(1)}, bf16[512,512]{1,0:T(8,128)(2,1)S(1)}, u32[]{:S(2)}, u32[]{:S(2)}) collective-permute-start(bf16[512,512]{1,0:T(8,128)(2,1)S(1)} %pad_maximum_fusion.5), channel_id=1, source_target_pairs={{0,8},{4,20},{8,0},{12,28},{16,24},{20,4},{24,16},{28,12},{1,9},{5... | collective-permute-start | bytes 1572872 | tf_op jit(solution)/shard_map/ppermute | solution.py:100
  7.5 7.1 %collective-permute-done = bf16[512,512]{1,0:T(8,128)(2,1)S(1)} collective-permute-done((bf16[512,512]{1,0:T(8,128)(2,1)S(1)}, bf16[512,512]{1,0:T(8,128)(2,1)S(1)}, u32[]{:S(2)}, u32[]{:S(2)}) %collective-permute-start) | collective-permute-done | bytes 524320 | tf_op jit(solution)/shard_map/ppermute | solution.py:100
  14.8 2.1 %collective-permute-start.1 = (bf16[768,512]{1,0:T(8,128)(2,1)S(1)}, bf16[768,512]{1,0:T(8,128)(2,1)S(1)}, u32[]{:S(2)}, u32[]{:S(2)}) collective-permute-start(bf16[768,512]{1,0:T(8,128)(2,1)S(1)} %pad_maximum_fusion.3), channel_id=1, source_target_pairs={{0,16},{4,12},{8,24},{12,4},{16,0},{20,28},{24,8},{28,20},{1,17},{... | collective-permute-start | bytes 2359304 | tf_op jit(solution)/shard_map/ppermute | solution.py:100
  16.9 10.0 %collective-permute-done.1 = bf16[768,512]{1,0:T(8,128)(2,1)S(1)} collective-permute-done((bf16[768,512]{1,0:T(8,128)(2,1)S(1)}, bf16[768,512]{1,0:T(8,128)(2,1)S(1)}, u32[]{:S(2)}, u32[]{:S(2)}) %collective-permute-start.1) | collective-permute-done | bytes 786464 | tf_op jit(solution)/shard_map/ppermute | solution.py:100
  27.1 0.1 fusion.23
  27.2 1.2 %pad_maximum_fusion.1 = bf16[1280,512]{1,0:T(8,128)(2,1)} fusion(bf16[256,512]{1,0:T(8,128)(2,1)S(1)} %bitcast.81, bf16[1024,512]{1,0:T(8,128)(2,1)S(1)} %bitcast.67), kind=kLoop, calls=%fused_computation.10 | loop fusion | flops 2621440 | bytes 2621440 | tf_op jit(solution)/shard_map/concatenate | solution.py:99
  28.4 0.8 %dynamic_slice.3 = f32[512]{0:T(512)S(1)} dynamic-slice(f32[4096]{0:T(1024)} %param.11, s32[]{:T(128)S(6)} %select_n.27), dynamic_slice_sizes={512} | dynamic-slice | bytes 4100 | tf_op jit(solution)/shard_map/dynamic_slice | solution.py:119
  29.1 2.5 %collective-permute-done.2 = bf16[1280,512]{1,0:T(8,128)(2,1)S(1)} collective-permute-done((bf16[1280,512]{1,0:T(8,128)(2,1)}, bf16[1280,512]{1,0:T(8,128)(2,1)S(1)}, u32[]{:S(2)}, u32[]{:S(2)}) %collective-permute-start.2) | collective-permute-done | bytes 1310752 | tf_op jit(solution)/shard_map/ppermute | solution.py:100
  31.7 0.6 gather_fusion.1
  32.5 0.1 multiply_reduce_fusion
  32.8 0.2 pad_maximum_fusion
  33.0 0.2 copy-done.1
  33.2 2.2 %fusion.25 = (f32[2048]{0:T(1024)S(1)}, bf16[2048,512]{1,0:T(8,128)(2,1)}) fusion(f32[512]{0:T(512)S(1)} %add_sqrt_fusion, bf16[256,512]{1,0:T(8,128)(2,1)S(1)} %bitcast.90, bf16[2048,512]{1,0:T(8,128)(2,1)S(1)} %bitcast.73), kind=kOutput, calls=%fused_computation.77 | convolution fusion | flops 541063168 | bytes 3418112 | tf_op jit(solution)/shard_map/dot_general | solution.py:123
  35.4 2.5 %fusion = (f32[2048]{0:T(1024)S(1)}, f32[512]{0:T(512)S(1)}, bf16[2048,512]{1,0:T(8,128)(2,1)}) fusion(f32[512]{0:T(512)S(1)} %dynamic_slice.3, f32[512]{0:T(512)S(1)} %add_sqrt_fusion.1, bf16[256,512]{1,0:T(8,128)(2,1)S(1)} %bitcast.93, bf16[2048,512]{1,0:T(8,128)(2,1)S(1)} %bitcast.74), kind=kOutput, calls=%fused_computation.5 | convolution fusion | flops 543159808 | bytes 3422208 | tf_op jit(solution)/shard_map/dot_general | solution.py:122
  38.0 2.1 %collective-permute-start.3 = (f32[2,2048]{1,0:T(2,128)S(1)}, f32[2,2048]{1,0:T(2,128)S(1)}, u32[]{:S(2)}, u32[]{:S(2)}) collective-permute-start(f32[2,2048]{1,0:T(2,128)S(1)} %pad_maximum_fusion.9), channel_id=1, source_target_pairs={{0,8},{4,20},{8,0},{12,28},{16,24},{20,4},{24,16},{28,12},{1,9},{5... | collective-permute-start | bytes 49160 | tf_op jit(solution)/shard_map/ppermute | solution.py:135
  40.0 1.7 %collective-permute-done.3 = f32[2,2048]{1,0:T(2,128)S(1)} collective-permute-done((f32[2,2048]{1,0:T(2,128)S(1)}, f32[2,2048]{1,0:T(2,128)S(1)}, u32[]{:S(2)}, u32[]{:S(2)}) %collective-permute-start.3) | collective-permute-done | bytes 16416 | tf_op jit(solution)/shard_map/ppermute | solution.py:135
  42.0 2.1 %collective-permute-start.4 = (f32[2,2048]{1,0:T(2,128)S(1)}, f32[2,2048]{1,0:T(2,128)S(1)}, u32[]{:S(2)}, u32[]{:S(2)}) collective-permute-start(f32[2,2048]{1,0:T(2,128)S(1)} %fusion.21), channel_id=1, source_target_pairs={{0,16},{4,12},{8,24},{12,4},{16,0},{20,28},{24,8},{28,20},{1,17},{... | collective-permute-start | bytes 49160 | tf_op jit(solution)/shard_map/ppermute | solution.py:135
  44.1 1.7 %collective-permute-done.4 = f32[2,2048]{1,0:T(2,128)S(1)} collective-permute-done((f32[2,2048]{1,0:T(2,128)S(1)}, f32[2,2048]{1,0:T(2,128)S(1)}, u32[]{:S(2)}, u32[]{:S(2)}) %collective-permute-start.4) | collective-permute-done | bytes 16416 | tf_op jit(solution)/shard_map/ppermute | solution.py:135
  46.0 0.8 %fusion.19 = (bf16[512]{0:T(512)(128)(2,1)S(1)}, bf16[512]{0:T(512)(128)(2,1)S(1)}) fusion(f32[512]{0:T(512)S(1)} %get-tuple-element.9, f32[4096]{0:T(1024)} %param.11, s32[]{:T(128)S(6)} %select_n.27), kind=kLoop, calls=%fused_computation.71 | loop fusion | flops 3584 | bytes 6148 | tf_op jit(solution)/shard_map/convert_element_type | solution.py:148
  46.8 0.4 collective-permute-done.5
  47.3 2.1 %collective-permute-start.6 = (f32[2,2048]{1,0:T(2,128)S(1)}, f32[2,2048]{1,0:T(2,128)S(1)}, u32[]{:S(2)}, u32[]{:S(2)}) collective-permute-start(f32[2,2048]{1,0:T(2,128)S(1)} %add.83), channel_id=1, source_target_pairs={{0,1},{1,2},{2,3},{3,0},{4,5},{5,6},{6,7},{7,4},{8,9},{9,10},{10,1... | collective-permute-start | bytes 49160 | tf_op jit(solution)/shard_map/ppermute | solution.py:58
  49.4 2.6 %collective-permute-start.7 = (f32[2,2048]{1,0:T(2,128)S(1)}, f32[2,2048]{1,0:T(2,128)S(1)}, u32[]{:S(2)}, u32[]{:S(2)}) collective-permute-start(f32[2,2048]{1,0:T(2,128)S(1)} %add.83), channel_id=1, source_target_pairs={{0,2},{1,3},{2,0},{3,1},{4,6},{5,7},{6,4},{7,5},{8,10},{9,11},{10,... | collective-permute-start | bytes 49160 | tf_op jit(solution)/shard_map/ppermute | solution.py:58
  52.0 1.3 %collective-permute-start.8 = (f32[2,2048]{1,0:T(2,128)S(1)}, f32[2,2048]{1,0:T(2,128)S(1)}, u32[]{:S(2)}, u32[]{:S(2)}) collective-permute-start(f32[2,2048]{1,0:T(2,128)S(1)} %add.83), channel_id=1, source_target_pairs={{0,3},{1,0},{2,1},{3,2},{4,7},{5,4},{6,5},{7,6},{8,11},{9,8},{10,9... | collective-permute-start | bytes 49160 | tf_op jit(solution)/shard_map/ppermute | solution.py:58
  53.4 0.9 %collective-permute-done.7 = f32[2,2048]{1,0:T(2,128)S(1)} collective-permute-done((f32[2,2048]{1,0:T(2,128)S(1)}, f32[2,2048]{1,0:T(2,128)S(1)}, u32[]{:S(2)}, u32[]{:S(2)}) %collective-permute-start.7) | collective-permute-done | bytes 16416 | tf_op jit(solution)/shard_map/ppermute | solution.py:58
  54.3 1.4 %collective-permute-done.8 = f32[2,2048]{1,0:T(2,128)S(1)} collective-permute-done((f32[2,2048]{1,0:T(2,128)S(1)}, f32[2,2048]{1,0:T(2,128)S(1)}, u32[]{:S(2)}, u32[]{:S(2)}) %collective-permute-start.8) | collective-permute-done | bytes 16416 | tf_op jit(solution)/shard_map/ppermute | solution.py:58
  55.8 3.5 %fusion.8 = (f32[512]{0:T(512)S(1)}, f32[256,512]{1,0:T(8,128)S(1)}) fusion(bf16[8,32,512]{2,1,0:T(8,128)(2,1)S(1)} %copy-done.2, bf16[2048,512]{1,0:T(8,128)(2,1)} %get-tuple-element.7, bf16[2048,512]{1,0:T(8,128)(2,1)} %get-tuple-element.6, f32[2048]{0:T(1024)S(1)} %bitcast.103, f32[2048]{0:T(1024)S(1)} %bitcast.102, bf16[2048,512]{1,0:T(8,128)(2,1)S(1)} %bitcast.75), kind=kOutput, calls=%fused_computation.25 | convolution fusion | flops 544603648 | bytes 6047744 | tf_op jit(solution)/shard_map/dot_general | solution.py:142
  59.4 11.2 %all_to_all.4 = bf16[8,34,512]{2,1,0:T(8,128)(2,1)S(1)} all-to-all(bf16[8,34,512]{2,1,0:T(8,128)(2,1)S(1)} %pad_maximum_fusion.8), channel_id=1, replica_groups=mesh['dp'=8,'tensor'=4] {'dp'}, dimensions={0} | all-to-all | bytes 557056 | tf_op jit(solution)/shard_map/all_to_all | solution.py:157
  70.7 0.6 slice_add_fusion
  71.4 0.8 %copy.29 = f32[4,8,8,512]{3,1,2,0:T(8,128)} copy(f32[4,8,8,512]{3,1,0,2:T(8,128)S(1)} %slice_bitcast_fusion.1) | data formatting | bytes 1048576
  (70 shorter events, 2.4 us)
Async XLA Ops:
  0.6 2.3 %copy-start = (bf16[32,4096]{1,0:T(8,128)(2,1)S(1)}, bf16[32,4096]{1,0:T(8,128)(2,1)}, u32[]{:S(2)}) copy-start(bf16[32,4096]{1,0:T(8,128)(2,1)} %param.8) | copy-start | bytes 786436
  3.1 0.9 %copy-start.4 = (bf16[256,256]{1,0:T(8,128)(2,1)S(1)}, bf16[256,256]{1,0:T(8,128)(2,1)}, u32[]{:S(2)}) copy-start(bf16[256,256]{1,0:T(8,128)(2,1)} %param.10) | copy-start | bytes 393220
  3.1 1.0 %copy-start.3 = (bf16[256,256]{1,0:T(8,128)(2,1)S(1)}, bf16[256,256]{1,0:T(8,128)(2,1)}, u32[]{:S(2)}) copy-start(bf16[256,256]{1,0:T(8,128)(2,1)} %param.9) | copy-start | bytes 393220
  4.5 10.2 %collective-permute-start = (bf16[512,512]{1,0:T(8,128)(2,1)S(1)}, bf16[512,512]{1,0:T(8,128)(2,1)S(1)}, u32[]{:S(2)}, u32[]{:S(2)}) collective-permute-start(bf16[512,512]{1,0:T(8,128)(2,1)S(1)} %pad_maximum_fusion.5), channel_id=1, source_target_pairs={{0,8},{4,20},{8,0},{12,28},{16,24},{20,4},{24,16},{28,12},{1,9},{5... | collective-permute-start | bytes 1572872 | tf_op jit(solution)/shard_map/ppermute | solution.py:100
  14.8 12.1 %collective-permute-start.1 = (bf16[768,512]{1,0:T(8,128)(2,1)S(1)}, bf16[768,512]{1,0:T(8,128)(2,1)S(1)}, u32[]{:S(2)}, u32[]{:S(2)}) collective-permute-start(bf16[768,512]{1,0:T(8,128)(2,1)S(1)} %pad_maximum_fusion.3), channel_id=1, source_target_pairs={{0,16},{4,12},{8,24},{12,4},{16,0},{20,28},{24,8},{28,20},{1,17},{... | collective-permute-start | bytes 2359304 | tf_op jit(solution)/shard_map/ppermute | solution.py:100
  28.4 3.2 %collective-permute-start.2 = (bf16[1280,512]{1,0:T(8,128)(2,1)}, bf16[1280,512]{1,0:T(8,128)(2,1)S(1)}, u32[]{:S(2)}, u32[]{:S(2)}) collective-permute-start(bf16[1280,512]{1,0:T(8,128)(2,1)} %pad_maximum_fusion.1), channel_id=1, source_target_pairs={{0,4},{4,0},{8,12},{12,8},{16,20},{20,16},{24,28},{28,24},{1,5},{5... | collective-permute-start | bytes 3932168 | tf_op jit(solution)/shard_map/ppermute | solution.py:100
  32.5 0.7 copy-start.1
  35.4 20.3 %copy-start.2 = (bf16[8,32,512]{2,1,0:T(8,128)(2,1)S(1)}, bf16[8,32,512]{2,1,0:T(8,128)(2,1)}, u32[]{:S(2)}) copy-start(bf16[8,32,512]{2,1,0:T(8,128)(2,1)} %copy-done.1) | copy-start | bytes 786436
  38.0 3.8 %collective-permute-start.3 = (f32[2,2048]{1,0:T(2,128)S(1)}, f32[2,2048]{1,0:T(2,128)S(1)}, u32[]{:S(2)}, u32[]{:S(2)}) collective-permute-start(f32[2,2048]{1,0:T(2,128)S(1)} %pad_maximum_fusion.9), channel_id=1, source_target_pairs={{0,8},{4,20},{8,0},{12,28},{16,24},{20,4},{24,16},{28,12},{1,9},{5... | collective-permute-start | bytes 49160 | tf_op jit(solution)/shard_map/ppermute | solution.py:135
  42.0 3.8 %collective-permute-start.4 = (f32[2,2048]{1,0:T(2,128)S(1)}, f32[2,2048]{1,0:T(2,128)S(1)}, u32[]{:S(2)}, u32[]{:S(2)}) collective-permute-start(f32[2,2048]{1,0:T(2,128)S(1)} %fusion.21), channel_id=1, source_target_pairs={{0,16},{4,12},{8,24},{12,4},{16,0},{20,28},{24,8},{28,20},{1,17},{... | collective-permute-start | bytes 49160 | tf_op jit(solution)/shard_map/ppermute | solution.py:135
  45.9 1.2 %collective-permute-start.5 = (f32[2,2048]{1,0:T(2,128)S(1)}, f32[2,2048]{1,0:T(2,128)S(1)}, u32[]{:S(2)}, u32[]{:S(2)}) collective-permute-start(f32[2,2048]{1,0:T(2,128)S(1)} %fusion.32), channel_id=1, source_target_pairs={{0,4},{4,0},{8,12},{12,8},{16,20},{20,16},{24,28},{28,24},{1,5},{5... | collective-permute-start | bytes 49160 | tf_op jit(solution)/shard_map/ppermute | solution.py:132
  47.3 6.1 %collective-permute-start.6 = (f32[2,2048]{1,0:T(2,128)S(1)}, f32[2,2048]{1,0:T(2,128)S(1)}, u32[]{:S(2)}, u32[]{:S(2)}) collective-permute-start(f32[2,2048]{1,0:T(2,128)S(1)} %add.83), channel_id=1, source_target_pairs={{0,1},{1,2},{2,3},{3,0},{4,5},{5,6},{6,7},{7,4},{8,9},{9,10},{10,1... | collective-permute-start | bytes 49160 | tf_op jit(solution)/shard_map/ppermute | solution.py:58
  49.4 4.9 %collective-permute-start.7 = (f32[2,2048]{1,0:T(2,128)S(1)}, f32[2,2048]{1,0:T(2,128)S(1)}, u32[]{:S(2)}, u32[]{:S(2)}) collective-permute-start(f32[2,2048]{1,0:T(2,128)S(1)} %add.83), channel_id=1, source_target_pairs={{0,2},{1,3},{2,0},{3,1},{4,6},{5,7},{6,4},{7,5},{8,10},{9,11},{10,... | collective-permute-start | bytes 49160 | tf_op jit(solution)/shard_map/ppermute | solution.py:58
  52.0 3.7 %collective-permute-start.8 = (f32[2,2048]{1,0:T(2,128)S(1)}, f32[2,2048]{1,0:T(2,128)S(1)}, u32[]{:S(2)}, u32[]{:S(2)}) collective-permute-start(f32[2,2048]{1,0:T(2,128)S(1)} %add.83), channel_id=1, source_target_pairs={{0,3},{1,0},{2,1},{3,2},{4,7},{5,4},{6,5},{7,6},{8,11},{9,8},{10,9... | collective-permute-start | bytes 49160 | tf_op jit(solution)/shard_map/ppermute | solution.py:58

commit v17 on v16

--- a/solution.py
+++ b/solution.py
@@ -59,6 +59,11 @@
     return total
 
 
+def teacher_rows(teacher_master, student_weight):
+    master, student = lax.optimization_barrier((teacher_master, student_weight))
+    return (0.996 * master + 0.004 * student.astype(jnp.float32)).astype(jnp.bfloat16)
+
+
 def feature_plan(teacher_master, student_weight, teacher_feat, student_feat, center):
     n = lax.axis_size("dp")
     me = lax.axis_index("dp")
@@ -72,7 +77,7 @@
     down = up[::-1]
     dim_bits = [jnp.where(odd == 1, down[r], up[r]) for r in range(nbits - 1)][::-1]
     master_new = 0.996 * teacher_master + 0.004 * student_weight.astype(jnp.float32)
-    both = jnp.stack([student_weight, master_new.astype(jnp.bfloat16)])
+    both = jnp.stack([student_weight, teacher_rows(teacher_master, student_weight)])
     both = both.reshape(2, rows, n, cols).transpose(2, 0, 1, 3).reshape(n, 2 * rows, cols)
     pos = jnp.arange(n)
     rel = (pos >> (nbits - 1)) & 1

time: 72.4 us -> 74.7 us (1.032)
  blocking collectives: 11.2 us -> 0 us
  waiting for transfers between devices: 25.8 us -> 32.6 us
  starting transfers between devices: 15.4 us -> 19.1 us
  local copies, waits for them, and re-layouts: 4.12 us -> 6.06 us
  other arithmetic: 6.35 us -> 7.17 us
    all_to_all x1 -> x0, blocking collectives: 11.2 us -> none  [feature_plan(): got = lax.all_to_all(sent, 'dp', 0, 2, tiled=True)]
    all_to_all x0 -> x1, waiting for transfers between devices: none -> 6.76 us  [feature_plan(): got = lax.all_to_all(sent, 'dp', 0, 2, tiled=True)]
    all_to_all x0 -> x1, starting transfers between devices: none -> 3.72 us  [feature_plan(): got = lax.all_to_all(sent, 'dp', 0, 2, tiled=True)]
    unnamed x14 -> x20, local copies, waits for them, and re-layouts: 1.32 us -> 3.27 us
    add x0 -> x1, other arithmetic: none -> 0.87 us  [feature_plan(): 0.996 * teacher_master + 0.004 * student_weight.astype(jnp.float32)]
    convert_element_type x1, other arithmetic: 2.03 us -> 1.23 us  [teacher_rows(): (0.996 * master + 0.004 * student.astype(jnp.float32)).astype(jnp.bfloat16)]
  transfers between devices with their start and end apart: 9 -> 10, of which waited for: 8 -> 9; matrix products, arithmetic and copies ran while one was open for 2% -> 3% of each run, Pallas kernels for 0% -> 0%
where the time goes in v17:
time: 74.7 us; the launch traced here: 74.3 us
  waiting for transfers between devices  32.6 us (44%)
  starting transfers between devices  19.1 us (26%)
  matrix products  8.26 us (11%)
  other arithmetic  7.17 us (10%)
  local copies, waits for them, and re-layouts  6.06 us (8%)
  between operations  1.14 us (2%)
    ppermute x3, waiting for transfers between devices, feature_plan(): got = lax.ppermute(payload, 'dp', pairs)  19.6 us
    all_to_all x1, waiting for transfers between devices, feature_plan(): got = lax.all_to_all(sent, 'dp', 0, 2, tiled=True)  6.76 us
    ppermute x3, starting transfers between devices, exchange_all(): total = total + lax.ppermute(x, axis, [(i, (i + k) % n) for i in range(n)])  6.06 us
    ppermute x3, starting transfers between devices, feature_plan(): got = lax.ppermute(payload, 'dp', pairs)  5.12 us
    ppermute x2, starting transfers between devices, feature_plan(): got = lax.ppermute(totals, 'dp', swap(up[r], down[r])).reshape(shape)  4.12 us
    all_to_all x1, starting transfers between devices, feature_plan(): got = lax.all_to_all(sent, 'dp', 0, 2, tiled=True)  3.72 us
    ppermute x2, waiting for transfers between devices, feature_plan(): got = lax.ppermute(totals, 'dp', swap(up[r], down[r])).reshape(shape)  3.49 us
    dot_general x1, matrix products, feature_plan(): lax.dot_general(zs, dlog, (((0,), (0,)), ((), ())), preferred_element_typ...  3.48 us
  transfers between devices with their start and end apart: 10, of which 9 were waited for; matrix products, arithmetic and copies ran while one was open for 3% of the time, Pallas kernels for 0%

profile of v17, /device:TPU:0, one launch (start us, length us, event | category | flops | bytes accessed | tf_op | source)
XLA Modules:
  0.0 74.3 jit_solution(14488047063809233311)
XLA Ops:
  0.7 1.2 %add_convert_fusion = bf16[32,4096]{1,0:T(8,128)(2,1)S(1)} fusion(bf16[32,4096]{1,0:T(8,128)(2,1)} %param.8, f32[32,4096]{1,0:T(8,128)} %param.7), kind=kLoop, calls=%fused_computation.37 | loop fusion | flops 655360 | bytes 1048576 | tf_op jit(solution)/shard_map/convert_element_type | solution.py:64
  2.4 0.6 gather_fusion
  3.7 3.0 %collective-permute-start = (bf16[512,512]{1,0:T(8,128)(2,1)S(1)}, bf16[512,512]{1,0:T(8,128)(2,1)S(1)}, u32[]{:S(2)}, u32[]{:S(2)}) collective-permute-start(bf16[512,512]{1,0:T(8,128)(2,1)S(1)} %pad_maximum_fusion.5), channel_id=1, source_target_pairs={{0,8},{4,20},{8,0},{12,28},{16,24},{20,4},{24,16},{28,12},{1,9},{5... | collective-permute-start | bytes 1572872 | tf_op jit(solution)/shard_map/ppermute | solution.py:105
  6.7 7.1 %collective-permute-done = bf16[512,512]{1,0:T(8,128)(2,1)S(1)} collective-permute-done((bf16[512,512]{1,0:T(8,128)(2,1)S(1)}, bf16[512,512]{1,0:T(8,128)(2,1)S(1)}, u32[]{:S(2)}, u32[]{:S(2)}) %collective-permute-start) | collective-permute-done | bytes 524320 | tf_op jit(solution)/shard_map/ppermute | solution.py:105
  14.0 2.1 %collective-permute-start.1 = (bf16[768,512]{1,0:T(8,128)(2,1)S(1)}, bf16[768,512]{1,0:T(8,128)(2,1)S(1)}, u32[]{:S(2)}, u32[]{:S(2)}) collective-permute-start(bf16[768,512]{1,0:T(8,128)(2,1)S(1)} %pad_maximum_fusion.3), channel_id=1, source_target_pairs={{0,16},{4,12},{8,24},{12,4},{16,0},{20,28},{24,8},{28,20},{1,17},{... | collective-permute-start | bytes 2359304 | tf_op jit(solution)/shard_map/ppermute | solution.py:105
  16.2 10.0 %collective-permute-done.1 = bf16[768,512]{1,0:T(8,128)(2,1)S(1)} collective-permute-done((bf16[768,512]{1,0:T(8,128)(2,1)S(1)}, bf16[768,512]{1,0:T(8,128)(2,1)S(1)}, u32[]{:S(2)}, u32[]{:S(2)}) %collective-permute-start.1) | collective-permute-done | bytes 786464 | tf_op jit(solution)/shard_map/ppermute | solution.py:105
  26.4 1.2 %pad_maximum_fusion.1 = bf16[1280,512]{1,0:T(8,128)(2,1)} fusion(bf16[256,512]{1,0:T(8,128)(2,1)S(1)} %bitcast.82, bf16[1024,512]{1,0:T(8,128)(2,1)S(1)} %bitcast.67), kind=kLoop, calls=%fused_computation.10 | loop fusion | flops 2621440 | bytes 2621440 | tf_op jit(solution)/shard_map/concatenate | solution.py:104
  27.6 0.8 %dynamic_slice.3 = f32[512]{0:T(512)S(1)} dynamic-slice(f32[4096]{0:T(1024)} %param.11, s32[]{:T(128)S(6)} %select_n.27), dynamic_slice_sizes={512} | dynamic-slice | bytes 4100 | tf_op jit(solution)/shard_map/dynamic_slice | solution.py:124
  28.4 2.5 %collective-permute-done.2 = bf16[1280,512]{1,0:T(8,128)(2,1)S(1)} collective-permute-done((bf16[1280,512]{1,0:T(8,128)(2,1)}, bf16[1280,512]{1,0:T(8,128)(2,1)S(1)}, u32[]{:S(2)}, u32[]{:S(2)}) %collective-permute-start.2) | collective-permute-done | bytes 1310752 | tf_op jit(solution)/shard_map/ppermute | solution.py:105
  30.9 1.0 %copy-done.2 = bf16[1280,512]{1,0:T(8,128)(2,1)} copy-done((bf16[1280,512]{1,0:T(8,128)(2,1)}, bf16[1280,512]{1,0:T(8,128)(2,1)S(1)}, u32[]{:S(2)}) %copy-start.2) | copy-done | bytes 1310744
  32.0 0.6 gather_fusion.1
  32.9 1.1 %copy-done.3 = bf16[1280,512]{1,0:T(8,128)(2,1)S(1)} copy-done((bf16[1280,512]{1,0:T(8,128)(2,1)S(1)}, bf16[1280,512]{1,0:T(8,128)(2,1)}, u32[]{:S(2)}) %copy-start.3) | copy-done | bytes 1310744
  34.4 2.3 %fusion.24 = (f32[2048]{0:T(1024)S(1)}, bf16[2048,512]{1,0:T(8,128)(2,1)}) fusion(f32[512]{0:T(512)S(1)} %add_sqrt_fusion, bf16[256,512]{1,0:T(8,128)(2,1)S(1)} %bitcast.90, bf16[2048,512]{1,0:T(8,128)(2,1)S(1)} %bitcast.74), kind=kOutput, calls=%fused_computation.77 | convolution fusion | flops 541063168 | bytes 3418112 | tf_op jit(solution)/shard_map/dot_general | solution.py:128
  36.6 2.5 %fusion = (f32[2048]{0:T(1024)S(1)}, f32[512]{0:T(512)S(1)}, bf16[2048,512]{1,0:T(8,128)(2,1)}) fusion(f32[512]{0:T(512)S(1)} %dynamic_slice.3, f32[512]{0:T(512)S(1)} %add_sqrt_fusion.1, bf16[256,512]{1,0:T(8,128)(2,1)S(1)} %bitcast.93, bf16[2048,512]{1,0:T(8,128)(2,1)S(1)} %bitcast.75), kind=kOutput, calls=%fused_computation.5 | convolution fusion | flops 543159808 | bytes 3422208 | tf_op jit(solution)/shard_map/dot_general | solution.py:127
  39.2 2.0 %collective-permute-start.3 = (f32[2,2048]{1,0:T(2,128)S(1)}, f32[2,2048]{1,0:T(2,128)S(1)}, u32[]{:S(2)}, u32[]{:S(2)}) collective-permute-start(f32[2,2048]{1,0:T(2,128)S(1)} %pad_maximum_fusion.9), channel_id=1, source_target_pairs={{0,8},{4,20},{8,0},{12,28},{16,24},{20,4},{24,16},{28,12},{1,9},{5... | collective-permute-start | bytes 49160 | tf_op jit(solution)/shard_map/ppermute | solution.py:140
  41.2 1.8 %collective-permute-done.3 = f32[2,2048]{1,0:T(2,128)S(1)} collective-permute-done((f32[2,2048]{1,0:T(2,128)S(1)}, f32[2,2048]{1,0:T(2,128)S(1)}, u32[]{:S(2)}, u32[]{:S(2)}) %collective-permute-start.3) | collective-permute-done | bytes 16416 | tf_op jit(solution)/shard_map/ppermute | solution.py:140
  43.2 2.1 %collective-permute-start.4 = (f32[2,2048]{1,0:T(2,128)S(1)}, f32[2,2048]{1,0:T(2,128)S(1)}, u32[]{:S(2)}, u32[]{:S(2)}) collective-permute-start(f32[2,2048]{1,0:T(2,128)S(1)} %fusion.21), channel_id=1, source_target_pairs={{0,16},{4,12},{8,24},{12,4},{16,0},{20,28},{24,8},{28,20},{1,17},{... | collective-permute-start | bytes 49160 | tf_op jit(solution)/shard_map/ppermute | solution.py:140
  45.3 1.7 %collective-permute-done.4 = f32[2,2048]{1,0:T(2,128)S(1)} collective-permute-done((f32[2,2048]{1,0:T(2,128)S(1)}, f32[2,2048]{1,0:T(2,128)S(1)}, u32[]{:S(2)}, u32[]{:S(2)}) %collective-permute-start.4) | collective-permute-done | bytes 16416 | tf_op jit(solution)/shard_map/ppermute | solution.py:140
  47.2 0.8 %fusion.19 = (bf16[512]{0:T(512)(128)(2,1)S(1)}, bf16[512]{0:T(512)(128)(2,1)S(1)}) fusion(f32[512]{0:T(512)S(1)} %get-tuple-element.13, f32[4096]{0:T(1024)} %param.11, s32[]{:T(128)S(6)} %select_n.27), kind=kLoop, calls=%fused_computation.72 | loop fusion | flops 3584 | bytes 6148 | tf_op jit(solution)/shard_map/convert_element_type | solution.py:153
  48.0 0.4 collective-permute-done.5
  48.5 2.1 %collective-permute-start.6 = (f32[2,2048]{1,0:T(2,128)S(1)}, f32[2,2048]{1,0:T(2,128)S(1)}, u32[]{:S(2)}, u32[]{:S(2)}) collective-permute-start(f32[2,2048]{1,0:T(2,128)S(1)} %add.87), channel_id=1, source_target_pairs={{0,1},{1,2},{2,3},{3,0},{4,5},{5,6},{6,7},{7,4},{8,9},{9,10},{10,1... | collective-permute-start | bytes 49160 | tf_op jit(solution)/shard_map/ppermute | solution.py:58
  50.6 2.6 %collective-permute-start.7 = (f32[2,2048]{1,0:T(2,128)S(1)}, f32[2,2048]{1,0:T(2,128)S(1)}, u32[]{:S(2)}, u32[]{:S(2)}) collective-permute-start(f32[2,2048]{1,0:T(2,128)S(1)} %add.87), channel_id=1, source_target_pairs={{0,2},{1,3},{2,0},{3,1},{4,6},{5,7},{6,4},{7,5},{8,10},{9,11},{10,... | collective-permute-start | bytes 49160 | tf_op jit(solution)/shard_map/ppermute | solution.py:58
  53.2 1.3 %collective-permute-start.8 = (f32[2,2048]{1,0:T(2,128)S(1)}, f32[2,2048]{1,0:T(2,128)S(1)}, u32[]{:S(2)}, u32[]{:S(2)}) collective-permute-start(f32[2,2048]{1,0:T(2,128)S(1)} %add.87), channel_id=1, source_target_pairs={{0,3},{1,0},{2,1},{3,2},{4,7},{5,4},{6,5},{7,6},{8,11},{9,8},{10,9... | collective-permute-start | bytes 49160 | tf_op jit(solution)/shard_map/ppermute | solution.py:58
  54.5 0.9 %collective-permute-done.7 = f32[2,2048]{1,0:T(2,128)S(1)} collective-permute-done((f32[2,2048]{1,0:T(2,128)S(1)}, f32[2,2048]{1,0:T(2,128)S(1)}, u32[]{:S(2)}, u32[]{:S(2)}) %collective-permute-start.7) | collective-permute-done | bytes 16416 | tf_op jit(solution)/shard_map/ppermute | solution.py:58
  55.5 1.4 %collective-permute-done.8 = f32[2,2048]{1,0:T(2,128)S(1)} collective-permute-done((f32[2,2048]{1,0:T(2,128)S(1)}, f32[2,2048]{1,0:T(2,128)S(1)}, u32[]{:S(2)}, u32[]{:S(2)}) %collective-permute-start.8) | collective-permute-done | bytes 16416 | tf_op jit(solution)/shard_map/ppermute | solution.py:58
  57.0 3.5 %fusion.8 = (f32[512]{0:T(512)S(1)}, f32[256,512]{1,0:T(8,128)S(1)}) fusion(bf16[8,32,512]{2,1,0:T(8,128)(2,1)S(1)} %copy-done.5, bf16[2048,512]{1,0:T(8,128)(2,1)} %get-tuple-element.11, bf16[2048,512]{1,0:T(8,128)(2,1)} %get-tuple-element.10, f32[2048]{0:T(1024)S(1)} %bitcast.103, f32[2048]{0:T(1024)S(1)} %bitcast.102, bf16[2048,512]{1,0:T(8,128)(2,1)S(1)} %bitcast.76), kind=kOutput, calls=%fused_computation.25 | convolution fusion | flops 544603648 | bytes 6047744 | tf_op jit(solution)/shard_map/dot_general | solution.py:147
  60.6 0.8 %pad_maximum_fusion.8 = bf16[8,34,512]{2,1,0:T(8,128)(2,1)} fusion(bf16[8,2,512]{2,1,0:T(2,128)(2,1)S(1)} %broadcast_in_dim.11, bf16[8,32,512]{2,1,0:T(8,128)(2,1)S(1)} %bitcast.87), kind=kLoop, calls=%fused_computation.45 | loop fusion | flops 557056 | bytes 557056 | tf_op jit(solution)/shard_map/concatenate | solution.py:155
  61.4 3.7 %all-to-all-start = ((bf16[8,34,512]{2,1,0:T(8,128)(2,1)}), bf16[8,34,512]{2,1,0:T(8,128)(2,1)S(1)}, u32[]{:S(2)}, u32[]{:S(2)}) async-start(bf16[8,34,512]{2,1,0:T(8,128)(2,1)} %pad_maximum_fusion.8), calls=%async_computation | async-start | bytes 655360 | tf_op jit(solution)/shard_map/all_to_all | solution.py:162
  65.1 0.9 %multiply_add_fusion = f32[32,4096]{1,0:T(8,128)} fusion(bf16[32,4096]{1,0:T(8,128)(2,1)S(1)} %copy-done, f32[32,4096]{1,0:T(8,128)S(1)} %copy-done.1), kind=kLoop, calls=%fused_computation.38 | loop fusion | flops 524288 | bytes 1310720 | tf_op jit(solution)/shard_map/add | solution.py:79
  66.0 6.8 %all-to-all-done = bf16[8,34,512]{2,1,0:T(8,128)(2,1)S(1)} async-done(((bf16[8,34,512]{2,1,0:T(8,128)(2,1)}), bf16[8,34,512]{2,1,0:T(8,128)(2,1)S(1)}, u32[]{:S(2)}, u32[]{:S(2)}) %all-to-all-start) | async-done | bytes 278560 | tf_op jit(solution)/shard_map/all_to_all | solution.py:162
  72.9 0.6 slice_add_fusion
  73.5 0.8 %copy.29 = f32[4,8,8,512]{3,1,2,0:T(8,128)} copy(f32[4,8,8,512]{3,1,0,2:T(8,128)S(1)} %slice_bitcast_fusion.1) | data formatting | bytes 1048576
  (78 shorter events, 3.0 us)
Async XLA Ops:
  0.6 1.5 %copy-start = (bf16[32,4096]{1,0:T(8,128)(2,1)S(1)}, bf16[32,4096]{1,0:T(8,128)(2,1)}, u32[]{:S(2)}) copy-start(bf16[32,4096]{1,0:T(8,128)(2,1)} %param.8) | copy-start | bytes 786436
  2.3 0.9 %copy-start.7 = (bf16[256,256]{1,0:T(8,128)(2,1)S(1)}, bf16[256,256]{1,0:T(8,128)(2,1)}, u32[]{:S(2)}) copy-start(bf16[256,256]{1,0:T(8,128)(2,1)} %param.10) | copy-start | bytes 393220
  2.3 1.0 %copy-start.6 = (bf16[256,256]{1,0:T(8,128)(2,1)S(1)}, bf16[256,256]{1,0:T(8,128)(2,1)}, u32[]{:S(2)}) copy-start(bf16[256,256]{1,0:T(8,128)(2,1)} %param.9) | copy-start | bytes 393220
  3.7 10.2 %collective-permute-start = (bf16[512,512]{1,0:T(8,128)(2,1)S(1)}, bf16[512,512]{1,0:T(8,128)(2,1)S(1)}, u32[]{:S(2)}, u32[]{:S(2)}) collective-permute-start(bf16[512,512]{1,0:T(8,128)(2,1)S(1)} %pad_maximum_fusion.5), channel_id=1, source_target_pairs={{0,8},{4,20},{8,0},{12,28},{16,24},{20,4},{24,16},{28,12},{1,9},{5... | collective-permute-start | bytes 1572872 | tf_op jit(solution)/shard_map/ppermute | solution.py:105
  14.0 12.1 %collective-permute-start.1 = (bf16[768,512]{1,0:T(8,128)(2,1)S(1)}, bf16[768,512]{1,0:T(8,128)(2,1)S(1)}, u32[]{:S(2)}, u32[]{:S(2)}) collective-permute-start(bf16[768,512]{1,0:T(8,128)(2,1)S(1)} %pad_maximum_fusion.3), channel_id=1, source_target_pairs={{0,16},{4,12},{8,24},{12,4},{16,0},{20,28},{24,8},{28,20},{1,17},{... | collective-permute-start | bytes 2359304 | tf_op jit(solution)/shard_map/ppermute | solution.py:105
  27.6 3.2 %collective-permute-start.2 = (bf16[1280,512]{1,0:T(8,128)(2,1)}, bf16[1280,512]{1,0:T(8,128)(2,1)S(1)}, u32[]{:S(2)}, u32[]{:S(2)}) collective-permute-start(bf16[1280,512]{1,0:T(8,128)(2,1)} %pad_maximum_fusion.1), channel_id=1, source_target_pairs={{0,4},{4,0},{8,12},{12,8},{16,20},{20,16},{24,28},{28,24},{1,5},{5... | collective-permute-start | bytes 3932168 | tf_op jit(solution)/shard_map/ppermute | solution.py:105
  30.9 1.1 %copy-start.2 = (bf16[1280,512]{1,0:T(8,128)(2,1)}, bf16[1280,512]{1,0:T(8,128)(2,1)S(1)}, u32[]{:S(2)}) copy-start(bf16[1280,512]{1,0:T(8,128)(2,1)S(1)} %collective-permute-done.2) | copy-start | bytes 3932164
  32.6 1.4 %copy-start.3 = (bf16[1280,512]{1,0:T(8,128)(2,1)S(1)}, bf16[1280,512]{1,0:T(8,128)(2,1)}, u32[]{:S(2)}) copy-start(bf16[1280,512]{1,0:T(8,128)(2,1)} %copy-done.2) | copy-start | bytes 3932164
  32.8 1.6 %copy-start.4 = (bf16[8,32,512]{2,1,0:T(8,128)(2,1)}, bf16[8,32,512]{2,1,0:T(8,128)(2,1)S(1)}, u32[]{:S(2)}) copy-start(bf16[8,32,512]{2,1,0:T(8,128)(2,1)S(1)} %get-tuple-element.25) | copy-start | bytes 786436
  36.6 20.3 %copy-start.5 = (bf16[8,32,512]{2,1,0:T(8,128)(2,1)S(1)}, bf16[8,32,512]{2,1,0:T(8,128)(2,1)}, u32[]{:S(2)}) copy-start(bf16[8,32,512]{2,1,0:T(8,128)(2,1)} %copy-done.4) | copy-start | bytes 786436
  39.2 3.8 %collective-permute-start.3 = (f32[2,2048]{1,0:T(2,128)S(1)}, f32[2,2048]{1,0:T(2,128)S(1)}, u32[]{:S(2)}, u32[]{:S(2)}) collective-permute-start(f32[2,2048]{1,0:T(2,128)S(1)} %pad_maximum_fusion.9), channel_id=1, source_target_pairs={{0,8},{4,20},{8,0},{12,28},{16,24},{20,4},{24,16},{28,12},{1,9},{5... | collective-permute-start | bytes 49160 | tf_op jit(solution)/shard_map/ppermute | solution.py:140
  43.2 3.8 %collective-permute-start.4 = (f32[2,2048]{1,0:T(2,128)S(1)}, f32[2,2048]{1,0:T(2,128)S(1)}, u32[]{:S(2)}, u32[]{:S(2)}) collective-permute-start(f32[2,2048]{1,0:T(2,128)S(1)} %fusion.21), channel_id=1, source_target_pairs={{0,16},{4,12},{8,24},{12,4},{16,0},{20,28},{24,8},{28,20},{1,17},{... | collective-permute-start | bytes 49160 | tf_op jit(solution)/shard_map/ppermute | solution.py:140
  47.1 1.2 %collective-permute-start.5 = (f32[2,2048]{1,0:T(2,128)S(1)}, f32[2,2048]{1,0:T(2,128)S(1)}, u32[]{:S(2)}, u32[]{:S(2)}) collective-permute-start(f32[2,2048]{1,0:T(2,128)S(1)} %fusion.31), channel_id=1, source_target_pairs={{0,4},{4,0},{8,12},{12,8},{16,20},{20,16},{24,28},{28,24},{1,5},{5... | collective-permute-start | bytes 49160 | tf_op jit(solution)/shard_map/ppermute | solution.py:137
  48.5 6.1 %collective-permute-start.6 = (f32[2,2048]{1,0:T(2,128)S(1)}, f32[2,2048]{1,0:T(2,128)S(1)}, u32[]{:S(2)}, u32[]{:S(2)}) collective-permute-start(f32[2,2048]{1,0:T(2,128)S(1)} %add.87), channel_id=1, source_target_pairs={{0,1},{1,2},{2,3},{3,0},{4,5},{5,6},{6,7},{7,4},{8,9},{9,10},{10,1... | collective-permute-start | bytes 49160 | tf_op jit(solution)/shard_map/ppermute | solution.py:58
  50.6 4.9 %collective-permute-start.7 = (f32[2,2048]{1,0:T(2,128)S(1)}, f32[2,2048]{1,0:T(2,128)S(1)}, u32[]{:S(2)}, u32[]{:S(2)}) collective-permute-start(f32[2,2048]{1,0:T(2,128)S(1)} %add.87), channel_id=1, source_target_pairs={{0,2},{1,3},{2,0},{3,1},{4,6},{5,7},{6,4},{7,5},{8,10},{9,11},{10,... | collective-permute-start | bytes 49160 | tf_op jit(solution)/shard_map/ppermute | solution.py:58
  53.2 3.7 %collective-permute-start.8 = (f32[2,2048]{1,0:T(2,128)S(1)}, f32[2,2048]{1,0:T(2,128)S(1)}, u32[]{:S(2)}, u32[]{:S(2)}) collective-permute-start(f32[2,2048]{1,0:T(2,128)S(1)} %add.87), channel_id=1, source_target_pairs={{0,3},{1,0},{2,1},{3,2},{4,7},{5,4},{6,5},{7,6},{8,11},{9,8},{10,9... | collective-permute-start | bytes 49160 | tf_op jit(solution)/shard_map/ppermute | solution.py:58
  60.5 4.6 %copy-start.1 = (f32[32,4096]{1,0:T(8,128)S(1)}, f32[32,4096]{1,0:T(8,128)}, u32[]{:S(2)}) copy-start(f32[32,4096]{1,0:T(8,128)} %param.7) | copy-start | bytes 1572868
  61.4 11.4 %all-to-all-start = ((bf16[8,34,512]{2,1,0:T(8,128)(2,1)}), bf16[8,34,512]{2,1,0:T(8,128)(2,1)S(1)}, u32[]{:S(2)}, u32[]{:S(2)}) async-start(bf16[8,34,512]{2,1,0:T(8,128)(2,1)} %pad_maximum_fusion.8), calls=%async_computation | async-start | bytes 655360 | tf_op jit(solution)/shard_map/all_to_all | solution.py:162

commit v18 on v16

--- a/solution.py
+++ b/solution.py
@@ -147,16 +147,20 @@
     grad = (product - wide * scaled) / s_norm
     high = part_center.astype(jnp.bfloat16)
     low = (part_center - high.astype(jnp.float32)).astype(jnp.bfloat16)
+    lanes = 128 if (rows * cols) % 128 == 0 and (2 * cols) % 128 == 0 else cols
+    grad_rows = rows * cols // lanes
     sent = jnp.concatenate(
         [
-            grad.astype(jnp.bfloat16).reshape(n, rows, cols),
-            jnp.broadcast_to(jnp.stack([high, low]), (n, 2, cols)),
+            grad.astype(jnp.bfloat16).reshape(n, grad_rows, lanes),
+            jnp.broadcast_to(jnp.stack([high, low]), (n, 2, cols)).reshape(n, -1, lanes),
         ],
         axis=1,
     )
-    got = lax.all_to_all(sent, "dp", 0, 2, tiled=True)
-    got = got.reshape(rows + 2, n * cols).astype(jnp.float32)
-    return (master_new, got[:rows], got[rows] + got[rows + 1])
+    got = lax.all_to_all(sent, "dp", 0, 0, tiled=True)
+    student_grad = got[:, :grad_rows].reshape(n, rows, cols).transpose(1, 0, 2)
+    student_grad = student_grad.reshape(rows, n * cols).astype(jnp.float32)
+    parts = got[:, grad_rows:].reshape(n, 2, cols).astype(jnp.float32)
+    return (master_new, student_grad, (parts[:, 0] + parts[:, 1]).reshape(n * cols))
 
 
 def solution(mesh):

time: 72.4 us -> 72.1 us (level)
  no operation moved by 1% of the time
where the time goes in v18:
time: 72.1 us; the launch traced here: 71.9 us
  waiting for transfers between devices  25.8 us (36%)
  starting transfers between devices  15.4 us (21%)
  blocking collectives  10.6 us (15%)
  matrix products  8.22 us (11%)
  other arithmetic  6.32 us (9%)
  local copies, waits for them, and re-layouts  4.35 us (6%)
  between operations  1.13 us (2%)
    ppermute x3, waiting for transfers between devices, feature_plan(): got = lax.ppermute(payload, 'dp', pairs)  19.6 us
    all_to_all x1, blocking collectives, feature_plan(): got = lax.all_to_all(sent, 'dp', 0, 0, tiled=True)  10.6 us
    ppermute x3, starting transfers between devices, exchange_all(): total = total + lax.ppermute(x, axis, [(i, (i + k) % n) for i in range(n)])  6.07 us
    ppermute x3, starting transfers between devices, feature_plan(): got = lax.ppermute(payload, 'dp', pairs)  5.12 us
    ppermute x2, starting transfers between devices, feature_plan(): got = lax.ppermute(totals, 'dp', swap(up[r], down[r])).reshape(shape)  4.14 us
    ppermute x2, waiting for transfers between devices, feature_plan(): got = lax.ppermute(totals, 'dp', swap(up[r], down[r])).reshape(shape)  3.47 us
    dot_general x1, matrix products, feature_plan(): lax.dot_general(zs, dlog, (((0,), (0,)), ((), ())), preferred_element_typ...  3.47 us
    dot_general x1, matrix products, feature_plan(): t_cos = jnp.dot(zt, tw, preferred_element_type=jnp.float32) / t_norm  2.53 us
  transfers between devices with their start and end apart: 9, of which 8 were waited for; matrix products, arithmetic and copies ran while one was open for 2% of the time, Pallas kernels for 0%

profile of v18, /device:TPU:0, one launch (start us, length us, event | category | flops | bytes accessed | tf_op | source)
XLA Modules:
  0.0 71.9 jit_solution(16814078990677868478)
XLA Ops:
  0.7 2.0 %fusion.24 = (bf16[32,4096]{1,0:T(8,128)(2,1)S(1)}, f32[32,4096]{1,0:T(8,128)}) fusion(bf16[32,4096]{1,0:T(8,128)(2,1)} %param.8, f32[32,4096]{1,0:T(8,128)} %param.7), kind=kLoop, calls=%fused_computation.77 | loop fusion | flops 655360 | bytes 1572864 | tf_op jit(solution)/shard_map/convert_element_type | solution.py:75
  3.2 0.6 gather_fusion
  4.3 0.1 fusion.15
  4.5 3.0 %collective-permute-start = (bf16[512,512]{1,0:T(8,128)(2,1)S(1)}, bf16[512,512]{1,0:T(8,128)(2,1)S(1)}, u32[]{:S(2)}, u32[]{:S(2)}) collective-permute-start(bf16[512,512]{1,0:T(8,128)(2,1)S(1)} %pad_maximum_fusion.5), channel_id=1, source_target_pairs={{0,8},{4,20},{8,0},{12,28},{16,24},{20,4},{24,16},{28,12},{1,9},{5... | collective-permute-start | bytes 1572872 | tf_op jit(solution)/shard_map/ppermute | solution.py:100
  7.5 7.1 %collective-permute-done = bf16[512,512]{1,0:T(8,128)(2,1)S(1)} collective-permute-done((bf16[512,512]{1,0:T(8,128)(2,1)S(1)}, bf16[512,512]{1,0:T(8,128)(2,1)S(1)}, u32[]{:S(2)}, u32[]{:S(2)}) %collective-permute-start) | collective-permute-done | bytes 524320 | tf_op jit(solution)/shard_map/ppermute | solution.py:100
  14.8 2.1 %collective-permute-start.1 = (bf16[768,512]{1,0:T(8,128)(2,1)S(1)}, bf16[768,512]{1,0:T(8,128)(2,1)S(1)}, u32[]{:S(2)}, u32[]{:S(2)}) collective-permute-start(bf16[768,512]{1,0:T(8,128)(2,1)S(1)} %pad_maximum_fusion.3), channel_id=1, source_target_pairs={{0,16},{4,12},{8,24},{12,4},{16,0},{20,28},{24,8},{28,20},{1,17},{... | collective-permute-start | bytes 2359304 | tf_op jit(solution)/shard_map/ppermute | solution.py:100
  16.9 10.0 %collective-permute-done.1 = bf16[768,512]{1,0:T(8,128)(2,1)S(1)} collective-permute-done((bf16[768,512]{1,0:T(8,128)(2,1)S(1)}, bf16[768,512]{1,0:T(8,128)(2,1)S(1)}, u32[]{:S(2)}, u32[]{:S(2)}) %collective-permute-start.1) | collective-permute-done | bytes 786464 | tf_op jit(solution)/shard_map/ppermute | solution.py:100
  27.1 0.1 fusion.23
  27.2 1.2 %pad_maximum_fusion.1 = bf16[1280,512]{1,0:T(8,128)(2,1)} fusion(bf16[256,512]{1,0:T(8,128)(2,1)S(1)} %bitcast.75, bf16[1024,512]{1,0:T(8,128)(2,1)S(1)} %bitcast.60), kind=kLoop, calls=%fused_computation.10 | loop fusion | flops 2621440 | bytes 2621440 | tf_op jit(solution)/shard_map/concatenate | solution.py:99
  28.4 0.8 %dynamic_slice.3 = f32[512]{0:T(512)S(1)} dynamic-slice(f32[4096]{0:T(1024)} %param.11, s32[]{:T(128)S(6)} %select_n.27), dynamic_slice_sizes={512} | dynamic-slice | bytes 4100 | tf_op jit(solution)/shard_map/dynamic_slice | solution.py:119
  29.1 2.5 %collective-permute-done.2 = bf16[1280,512]{1,0:T(8,128)(2,1)S(1)} collective-permute-done((bf16[1280,512]{1,0:T(8,128)(2,1)}, bf16[1280,512]{1,0:T(8,128)(2,1)S(1)}, u32[]{:S(2)}, u32[]{:S(2)}) %collective-permute-start.2) | collective-permute-done | bytes 1310752 | tf_op jit(solution)/shard_map/ppermute | solution.py:100
  31.7 0.6 gather_fusion.1
  32.8 0.2 pad_maximum_fusion
  33.0 0.2 copy-done.1
  33.2 2.2 %fusion.25 = (f32[2048]{0:T(1024)S(1)}, bf16[2048,512]{1,0:T(8,128)(2,1)}) fusion(f32[512]{0:T(512)S(1)} %add_sqrt_fusion, bf16[256,512]{1,0:T(8,128)(2,1)S(1)} %bitcast.83, bf16[2048,512]{1,0:T(8,128)(2,1)S(1)} %bitcast.66), kind=kOutput, calls=%fused_computation.78 | convolution fusion | flops 541063168 | bytes 3418112 | tf_op jit(solution)/shard_map/dot_general | solution.py:123
  35.4 2.5 %fusion = (f32[2048]{0:T(1024)S(1)}, f32[512]{0:T(512)S(1)}, bf16[2048,512]{1,0:T(8,128)(2,1)}) fusion(f32[512]{0:T(512)S(1)} %dynamic_slice.3, f32[512]{0:T(512)S(1)} %add_sqrt_fusion.1, bf16[256,512]{1,0:T(8,128)(2,1)S(1)} %bitcast.86, bf16[2048,512]{1,0:T(8,128)(2,1)S(1)} %bitcast.67), kind=kOutput, calls=%fused_computation.5 | convolution fusion | flops 543159808 | bytes 3422208 | tf_op jit(solution)/shard_map/dot_general | solution.py:122
  38.0 2.1 %collective-permute-start.3 = (f32[2,2048]{1,0:T(2,128)S(1)}, f32[2,2048]{1,0:T(2,128)S(1)}, u32[]{:S(2)}, u32[]{:S(2)}) collective-permute-start(f32[2,2048]{1,0:T(2,128)S(1)} %pad_maximum_fusion.9), channel_id=1, source_target_pairs={{0,8},{4,20},{8,0},{12,28},{16,24},{20,4},{24,16},{28,12},{1,9},{5... | collective-permute-start | bytes 49160 | tf_op jit(solution)/shard_map/ppermute | solution.py:135
  40.0 1.7 %collective-permute-done.3 = f32[2,2048]{1,0:T(2,128)S(1)} collective-permute-done((f32[2,2048]{1,0:T(2,128)S(1)}, f32[2,2048]{1,0:T(2,128)S(1)}, u32[]{:S(2)}, u32[]{:S(2)}) %collective-permute-start.3) | collective-permute-done | bytes 16416 | tf_op jit(solution)/shard_map/ppermute | solution.py:135
  42.0 2.1 %collective-permute-start.4 = (f32[2,2048]{1,0:T(2,128)S(1)}, f32[2,2048]{1,0:T(2,128)S(1)}, u32[]{:S(2)}, u32[]{:S(2)}) collective-permute-start(f32[2,2048]{1,0:T(2,128)S(1)} %fusion.21), channel_id=1, source_target_pairs={{0,16},{4,12},{8,24},{12,4},{16,0},{20,28},{24,8},{28,20},{1,17},{... | collective-permute-start | bytes 49160 | tf_op jit(solution)/shard_map/ppermute | solution.py:135
  44.1 1.7 %collective-permute-done.4 = f32[2,2048]{1,0:T(2,128)S(1)} collective-permute-done((f32[2,2048]{1,0:T(2,128)S(1)}, f32[2,2048]{1,0:T(2,128)S(1)}, u32[]{:S(2)}, u32[]{:S(2)}) %collective-permute-start.4) | collective-permute-done | bytes 16416 | tf_op jit(solution)/shard_map/ppermute | solution.py:135
  46.0 0.8 %fusion.19 = (bf16[512]{0:T(512)(128)(2,1)S(1)}, bf16[512]{0:T(512)(128)(2,1)S(1)}) fusion(f32[512]{0:T(512)S(1)} %get-tuple-element.9, f32[4096]{0:T(1024)} %param.11, s32[]{:T(128)S(6)} %select_n.27), kind=kLoop, calls=%fused_computation.72 | loop fusion | flops 3584 | bytes 6148 | tf_op jit(solution)/shard_map/convert_element_type | solution.py:148
  46.8 0.4 collective-permute-done.5
  47.3 2.1 %collective-permute-start.6 = (f32[2,2048]{1,0:T(2,128)S(1)}, f32[2,2048]{1,0:T(2,128)S(1)}, u32[]{:S(2)}, u32[]{:S(2)}) collective-permute-start(f32[2,2048]{1,0:T(2,128)S(1)} %add.83), channel_id=1, source_target_pairs={{0,1},{1,2},{2,3},{3,0},{4,5},{5,6},{6,7},{7,4},{8,9},{9,10},{10,1... | collective-permute-start | bytes 49160 | tf_op jit(solution)/shard_map/ppermute | solution.py:58
  49.4 2.6 %collective-permute-start.7 = (f32[2,2048]{1,0:T(2,128)S(1)}, f32[2,2048]{1,0:T(2,128)S(1)}, u32[]{:S(2)}, u32[]{:S(2)}) collective-permute-start(f32[2,2048]{1,0:T(2,128)S(1)} %add.83), channel_id=1, source_target_pairs={{0,2},{1,3},{2,0},{3,1},{4,6},{5,7},{6,4},{7,5},{8,10},{9,11},{10,... | collective-permute-start | bytes 49160 | tf_op jit(solution)/shard_map/ppermute | solution.py:58
  52.0 1.3 %collective-permute-start.8 = (f32[2,2048]{1,0:T(2,128)S(1)}, f32[2,2048]{1,0:T(2,128)S(1)}, u32[]{:S(2)}, u32[]{:S(2)}) collective-permute-start(f32[2,2048]{1,0:T(2,128)S(1)} %add.83), channel_id=1, source_target_pairs={{0,3},{1,0},{2,1},{3,2},{4,7},{5,4},{6,5},{7,6},{8,11},{9,8},{10,9... | collective-permute-start | bytes 49160 | tf_op jit(solution)/shard_map/ppermute | solution.py:58
  53.4 0.9 %collective-permute-done.7 = f32[2,2048]{1,0:T(2,128)S(1)} collective-permute-done((f32[2,2048]{1,0:T(2,128)S(1)}, f32[2,2048]{1,0:T(2,128)S(1)}, u32[]{:S(2)}, u32[]{:S(2)}) %collective-permute-start.7) | collective-permute-done | bytes 16416 | tf_op jit(solution)/shard_map/ppermute | solution.py:58
  54.3 1.4 %collective-permute-done.8 = f32[2,2048]{1,0:T(2,128)S(1)} collective-permute-done((f32[2,2048]{1,0:T(2,128)S(1)}, f32[2,2048]{1,0:T(2,128)S(1)}, u32[]{:S(2)}, u32[]{:S(2)}) %collective-permute-start.8) | collective-permute-done | bytes 16416 | tf_op jit(solution)/shard_map/ppermute | solution.py:58
  55.8 3.5 %fusion.8 = (f32[512]{0:T(512)S(1)}, f32[256,512]{1,0:T(8,128)S(1)}) fusion(bf16[8,32,512]{2,1,0:T(8,128)(2,1)S(1)} %copy-done.2, bf16[2048,512]{1,0:T(8,128)(2,1)} %get-tuple-element.7, bf16[2048,512]{1,0:T(8,128)(2,1)} %get-tuple-element.6, f32[2048]{0:T(1024)S(1)} %bitcast.96, f32[2048]{0:T(1024)S(1)} %bitcast.95, bf16[2048,512]{1,0:T(8,128)(2,1)S(1)} %bitcast.68), kind=kOutput, calls=%fused_computation.24 | convolution fusion | flops 544603648 | bytes 6047744 | tf_op jit(solution)/shard_map/dot_general | solution.py:142
  59.4 0.2 reshape.127
  59.6 10.6 %all_to_all.5 = bf16[8,136,128]{2,1,0:T(8,128)(2,1)S(1)} all-to-all(bf16[8,136,128]{2,1,0:T(8,128)(2,1)S(1)} %pad_maximum_fusion.8), channel_id=1, replica_groups=mesh['dp'=8,'tensor'=4] {'dp'}, dimensions={0} | all-to-all | bytes 557056 | tf_op jit(solution)/shard_map/all_to_all | solution.py:159
  70.4 0.8 %copy.29 = f32[4,8,8,512]{3,1,2,0:T(8,128)} copy(f32[4,8,8,512]{3,1,0,2:T(8,128)S(1)} %bitcast.72) | data formatting | bytes 1048576
  71.2 0.6 slice_add_fusion
  (74 shorter events, 2.6 us)
Async XLA Ops:
  0.6 2.3 %copy-start = (bf16[32,4096]{1,0:T(8,128)(2,1)S(1)}, bf16[32,4096]{1,0:T(8,128)(2,1)}, u32[]{:S(2)}) copy-start(bf16[32,4096]{1,0:T(8,128)(2,1)} %param.8) | copy-start | bytes 786436
  3.1 0.9 %copy-start.4 = (bf16[256,256]{1,0:T(8,128)(2,1)S(1)}, bf16[256,256]{1,0:T(8,128)(2,1)}, u32[]{:S(2)}) copy-start(bf16[256,256]{1,0:T(8,128)(2,1)} %param.10) | copy-start | bytes 393220
  3.1 1.0 %copy-start.3 = (bf16[256,256]{1,0:T(8,128)(2,1)S(1)}, bf16[256,256]{1,0:T(8,128)(2,1)}, u32[]{:S(2)}) copy-start(bf16[256,256]{1,0:T(8,128)(2,1)} %param.9) | copy-start | bytes 393220
  4.5 10.2 %collective-permute-start = (bf16[512,512]{1,0:T(8,128)(2,1)S(1)}, bf16[512,512]{1,0:T(8,128)(2,1)S(1)}, u32[]{:S(2)}, u32[]{:S(2)}) collective-permute-start(bf16[512,512]{1,0:T(8,128)(2,1)S(1)} %pad_maximum_fusion.5), channel_id=1, source_target_pairs={{0,8},{4,20},{8,0},{12,28},{16,24},{20,4},{24,16},{28,12},{1,9},{5... | collective-permute-start | bytes 1572872 | tf_op jit(solution)/shard_map/ppermute | solution.py:100
  14.8 12.1 %collective-permute-start.1 = (bf16[768,512]{1,0:T(8,128)(2,1)S(1)}, bf16[768,512]{1,0:T(8,128)(2,1)S(1)}, u32[]{:S(2)}, u32[]{:S(2)}) collective-permute-start(bf16[768,512]{1,0:T(8,128)(2,1)S(1)} %pad_maximum_fusion.3), channel_id=1, source_target_pairs={{0,16},{4,12},{8,24},{12,4},{16,0},{20,28},{24,8},{28,20},{1,17},{... | collective-permute-start | bytes 2359304 | tf_op jit(solution)/shard_map/ppermute | solution.py:100
  28.4 3.2 %collective-permute-start.2 = (bf16[1280,512]{1,0:T(8,128)(2,1)}, bf16[1280,512]{1,0:T(8,128)(2,1)S(1)}, u32[]{:S(2)}, u32[]{:S(2)}) collective-permute-start(bf16[1280,512]{1,0:T(8,128)(2,1)} %pad_maximum_fusion.1), channel_id=1, source_target_pairs={{0,4},{4,0},{8,12},{12,8},{16,20},{20,16},{24,28},{28,24},{1,5},{5... | collective-permute-start | bytes 3932168 | tf_op jit(solution)/shard_map/ppermute | solution.py:100
  32.5 0.7 copy-start.1
  35.4 20.3 %copy-start.2 = (bf16[8,32,512]{2,1,0:T(8,128)(2,1)S(1)}, bf16[8,32,512]{2,1,0:T(8,128)(2,1)}, u32[]{:S(2)}) copy-start(bf16[8,32,512]{2,1,0:T(8,128)(2,1)} %copy-done.1) | copy-start | bytes 786436
  38.0 3.8 %collective-permute-start.3 = (f32[2,2048]{1,0:T(2,128)S(1)}, f32[2,2048]{1,0:T(2,128)S(1)}, u32[]{:S(2)}, u32[]{:S(2)}) collective-permute-start(f32[2,2048]{1,0:T(2,128)S(1)} %pad_maximum_fusion.9), channel_id=1, source_target_pairs={{0,8},{4,20},{8,0},{12,28},{16,24},{20,4},{24,16},{28,12},{1,9},{5... | collective-permute-start | bytes 49160 | tf_op jit(solution)/shard_map/ppermute | solution.py:135
  42.0 3.8 %collective-permute-start.4 = (f32[2,2048]{1,0:T(2,128)S(1)}, f32[2,2048]{1,0:T(2,128)S(1)}, u32[]{:S(2)}, u32[]{:S(2)}) collective-permute-start(f32[2,2048]{1,0:T(2,128)S(1)} %fusion.21), channel_id=1, source_target_pairs={{0,16},{4,12},{8,24},{12,4},{16,0},{20,28},{24,8},{28,20},{1,17},{... | collective-permute-start | bytes 49160 | tf_op jit(solution)/shard_map/ppermute | solution.py:135
  45.9 1.2 %collective-permute-start.5 = (f32[2,2048]{1,0:T(2,128)S(1)}, f32[2,2048]{1,0:T(2,128)S(1)}, u32[]{:S(2)}, u32[]{:S(2)}) collective-permute-start(f32[2,2048]{1,0:T(2,128)S(1)} %fusion.32), channel_id=1, source_target_pairs={{0,4},{4,0},{8,12},{12,8},{16,20},{20,16},{24,28},{28,24},{1,5},{5... | collective-permute-start | bytes 49160 | tf_op jit(solution)/shard_map/ppermute | solution.py:132
  47.3 6.1 %collective-permute-start.6 = (f32[2,2048]{1,0:T(2,128)S(1)}, f32[2,2048]{1,0:T(2,128)S(1)}, u32[]{:S(2)}, u32[]{:S(2)}) collective-permute-start(f32[2,2048]{1,0:T(2,128)S(1)} %add.83), channel_id=1, source_target_pairs={{0,1},{1,2},{2,3},{3,0},{4,5},{5,6},{6,7},{7,4},{8,9},{9,10},{10,1... | collective-permute-start | bytes 49160 | tf_op jit(solution)/shard_map/ppermute | solution.py:58
  49.4 4.9 %collective-permute-start.7 = (f32[2,2048]{1,0:T(2,128)S(1)}, f32[2,2048]{1,0:T(2,128)S(1)}, u32[]{:S(2)}, u32[]{:S(2)}) collective-permute-start(f32[2,2048]{1,0:T(2,128)S(1)} %add.83), channel_id=1, source_target_pairs={{0,2},{1,3},{2,0},{3,1},{4,6},{5,7},{6,4},{7,5},{8,10},{9,11},{10,... | collective-permute-start | bytes 49160 | tf_op jit(solution)/shard_map/ppermute | solution.py:58
  52.0 3.7 %collective-permute-start.8 = (f32[2,2048]{1,0:T(2,128)S(1)}, f32[2,2048]{1,0:T(2,128)S(1)}, u32[]{:S(2)}, u32[]{:S(2)}) collective-permute-start(f32[2,2048]{1,0:T(2,128)S(1)} %add.83), channel_id=1, source_target_pairs={{0,3},{1,0},{2,1},{3,2},{4,7},{5,4},{6,5},{7,6},{8,11},{9,8},{10,9... | collective-permute-start | bytes 49160 | tf_op jit(solution)/shard_map/ppermute | solution.py:58

commit v19 on v18

--- a/solution.py
+++ b/solution.py
@@ -159,8 +159,10 @@
     got = lax.all_to_all(sent, "dp", 0, 0, tiled=True)
     student_grad = got[:, :grad_rows].reshape(n, rows, cols).transpose(1, 0, 2)
     student_grad = student_grad.reshape(rows, n * cols).astype(jnp.float32)
-    parts = got[:, grad_rows:].reshape(n, 2, cols).astype(jnp.float32)
-    return (master_new, student_grad, (parts[:, 0] + parts[:, 1]).reshape(n * cols))
+    half = cols // lanes
+    high = got[:, grad_rows: grad_rows + half].astype(jnp.float32)
+    low = got[:, grad_rows + half:].astype(jnp.float32)
+    return (master_new, student_grad, (high + low).reshape(n * cols))
 
 
 def solution(mesh):

time: 72.1 us -> 72.1 us (level)
  no operation moved by 1% of the time
where the time goes in v19:
time: 72.1 us; the launch traced here: 71.8 us
  waiting for transfers between devices  25.8 us (36%)
  starting transfers between devices  15.4 us (21%)
  blocking collectives  10.6 us (15%)
  matrix products  8.22 us (11%)
  other arithmetic  6.3 us (9%)
  local copies, waits for them, and re-layouts  4.33 us (6%)
  between operations  1.13 us (2%)
    ppermute x3, waiting for transfers between devices, feature_plan(): got = lax.ppermute(payload, 'dp', pairs)  19.6 us
    all_to_all x1, blocking collectives, feature_plan(): got = lax.all_to_all(sent, 'dp', 0, 0, tiled=True)  10.6 us
    ppermute x3, starting transfers between devices, exchange_all(): total = total + lax.ppermute(x, axis, [(i, (i + k) % n) for i in range(n)])  6.07 us
    ppermute x3, starting transfers between devices, feature_plan(): got = lax.ppermute(payload, 'dp', pairs)  5.12 us
    ppermute x2, starting transfers between devices, feature_plan(): got = lax.ppermute(totals, 'dp', swap(up[r], down[r])).reshape(shape)  4.14 us
    ppermute x2, waiting for transfers between devices, feature_plan(): got = lax.ppermute(totals, 'dp', swap(up[r], down[r])).reshape(shape)  3.47 us
    dot_general x1, matrix products, feature_plan(): lax.dot_general(zs, dlog, (((0,), (0,)), ((), ())), preferred_element_typ...  3.47 us
    dot_general x1, matrix products, feature_plan(): t_cos = jnp.dot(zt, tw, preferred_element_type=jnp.float32) / t_norm  2.53 us
  transfers between devices with their start and end apart: 9, of which 8 were waited for; matrix products, arithmetic and copies ran while one was open for 2% of the time, Pallas kernels for 0%

profile of v19, /device:TPU:0, one launch (start us, length us, event | category | flops | bytes accessed | tf_op | source)
XLA Modules:
  0.0 71.8 jit_solution(12604403095151192665)
XLA Ops:
  0.7 2.0 %fusion.24 = (bf16[32,4096]{1,0:T(8,128)(2,1)S(1)}, f32[32,4096]{1,0:T(8,128)}) fusion(bf16[32,4096]{1,0:T(8,128)(2,1)} %param.8, f32[32,4096]{1,0:T(8,128)} %param.7), kind=kLoop, calls=%fused_computation.76 | loop fusion | flops 655360 | bytes 1572864 | tf_op jit(solution)/shard_map/convert_element_type | solution.py:75
  3.2 0.6 gather_fusion
  4.3 0.1 fusion.15
  4.5 3.0 %collective-permute-start = (bf16[512,512]{1,0:T(8,128)(2,1)S(1)}, bf16[512,512]{1,0:T(8,128)(2,1)S(1)}, u32[]{:S(2)}, u32[]{:S(2)}) collective-permute-start(bf16[512,512]{1,0:T(8,128)(2,1)S(1)} %pad_maximum_fusion.5), channel_id=1, source_target_pairs={{0,8},{4,20},{8,0},{12,28},{16,24},{20,4},{24,16},{28,12},{1,9},{5... | collective-permute-start | bytes 1572872 | tf_op jit(solution)/shard_map/ppermute | solution.py:100
  7.5 7.1 %collective-permute-done = bf16[512,512]{1,0:T(8,128)(2,1)S(1)} collective-permute-done((bf16[512,512]{1,0:T(8,128)(2,1)S(1)}, bf16[512,512]{1,0:T(8,128)(2,1)S(1)}, u32[]{:S(2)}, u32[]{:S(2)}) %collective-permute-start) | collective-permute-done | bytes 524320 | tf_op jit(solution)/shard_map/ppermute | solution.py:100
  14.8 2.1 %collective-permute-start.1 = (bf16[768,512]{1,0:T(8,128)(2,1)S(1)}, bf16[768,512]{1,0:T(8,128)(2,1)S(1)}, u32[]{:S(2)}, u32[]{:S(2)}) collective-permute-start(bf16[768,512]{1,0:T(8,128)(2,1)S(1)} %pad_maximum_fusion.3), channel_id=1, source_target_pairs={{0,16},{4,12},{8,24},{12,4},{16,0},{20,28},{24,8},{28,20},{1,17},{... | collective-permute-start | bytes 2359304 | tf_op jit(solution)/shard_map/ppermute | solution.py:100
  16.9 10.0 %collective-permute-done.1 = bf16[768,512]{1,0:T(8,128)(2,1)S(1)} collective-permute-done((bf16[768,512]{1,0:T(8,128)(2,1)S(1)}, bf16[768,512]{1,0:T(8,128)(2,1)S(1)}, u32[]{:S(2)}, u32[]{:S(2)}) %collective-permute-start.1) | collective-permute-done | bytes 786464 | tf_op jit(solution)/shard_map/ppermute | solution.py:100
  27.1 0.1 fusion.23
  27.2 1.2 %pad_maximum_fusion.1 = bf16[1280,512]{1,0:T(8,128)(2,1)} fusion(bf16[256,512]{1,0:T(8,128)(2,1)S(1)} %bitcast.75, bf16[1024,512]{1,0:T(8,128)(2,1)S(1)} %bitcast.60), kind=kLoop, calls=%fused_computation.10 | loop fusion | flops 2621440 | bytes 2621440 | tf_op jit(solution)/shard_map/concatenate | solution.py:99
  28.4 0.8 %dynamic_slice.3 = f32[512]{0:T(512)S(1)} dynamic-slice(f32[4096]{0:T(1024)} %param.11, s32[]{:T(128)S(6)} %select_n.27), dynamic_slice_sizes={512} | dynamic-slice | bytes 4100 | tf_op jit(solution)/shard_map/dynamic_slice | solution.py:119
  29.1 2.5 %collective-permute-done.2 = bf16[1280,512]{1,0:T(8,128)(2,1)S(1)} collective-permute-done((bf16[1280,512]{1,0:T(8,128)(2,1)}, bf16[1280,512]{1,0:T(8,128)(2,1)S(1)}, u32[]{:S(2)}, u32[]{:S(2)}) %collective-permute-start.2) | collective-permute-done | bytes 1310752 | tf_op jit(solution)/shard_map/ppermute | solution.py:100
  31.7 0.6 gather_fusion.1
  32.8 0.2 pad_maximum_fusion
  33.0 0.2 copy-done.1
  33.2 2.2 %fusion.25 = (f32[2048]{0:T(1024)S(1)}, bf16[2048,512]{1,0:T(8,128)(2,1)}) fusion(f32[512]{0:T(512)S(1)} %add_sqrt_fusion, bf16[256,512]{1,0:T(8,128)(2,1)S(1)} %bitcast.83, bf16[2048,512]{1,0:T(8,128)(2,1)S(1)} %bitcast.66), kind=kOutput, calls=%fused_computation.77 | convolution fusion | flops 541063168 | bytes 3418112 | tf_op jit(solution)/shard_map/dot_general | solution.py:123
  35.4 2.5 %fusion = (f32[2048]{0:T(1024)S(1)}, f32[512]{0:T(512)S(1)}, bf16[2048,512]{1,0:T(8,128)(2,1)}) fusion(f32[512]{0:T(512)S(1)} %dynamic_slice.3, f32[512]{0:T(512)S(1)} %add_sqrt_fusion.1, bf16[256,512]{1,0:T(8,128)(2,1)S(1)} %bitcast.86, bf16[2048,512]{1,0:T(8,128)(2,1)S(1)} %bitcast.67), kind=kOutput, calls=%fused_computation.5 | convolution fusion | flops 543159808 | bytes 3422208 | tf_op jit(solution)/shard_map/dot_general | solution.py:122
  38.0 2.1 %collective-permute-start.3 = (f32[2,2048]{1,0:T(2,128)S(1)}, f32[2,2048]{1,0:T(2,128)S(1)}, u32[]{:S(2)}, u32[]{:S(2)}) collective-permute-start(f32[2,2048]{1,0:T(2,128)S(1)} %pad_maximum_fusion.9), channel_id=1, source_target_pairs={{0,8},{4,20},{8,0},{12,28},{16,24},{20,4},{24,16},{28,12},{1,9},{5... | collective-permute-start | bytes 49160 | tf_op jit(solution)/shard_map/ppermute | solution.py:135
  40.0 1.7 %collective-permute-done.3 = f32[2,2048]{1,0:T(2,128)S(1)} collective-permute-done((f32[2,2048]{1,0:T(2,128)S(1)}, f32[2,2048]{1,0:T(2,128)S(1)}, u32[]{:S(2)}, u32[]{:S(2)}) %collective-permute-start.3) | collective-permute-done | bytes 16416 | tf_op jit(solution)/shard_map/ppermute | solution.py:135
  42.0 2.1 %collective-permute-start.4 = (f32[2,2048]{1,0:T(2,128)S(1)}, f32[2,2048]{1,0:T(2,128)S(1)}, u32[]{:S(2)}, u32[]{:S(2)}) collective-permute-start(f32[2,2048]{1,0:T(2,128)S(1)} %fusion.21), channel_id=1, source_target_pairs={{0,16},{4,12},{8,24},{12,4},{16,0},{20,28},{24,8},{28,20},{1,17},{... | collective-permute-start | bytes 49160 | tf_op jit(solution)/shard_map/ppermute | solution.py:135
  44.1 1.7 %collective-permute-done.4 = f32[2,2048]{1,0:T(2,128)S(1)} collective-permute-done((f32[2,2048]{1,0:T(2,128)S(1)}, f32[2,2048]{1,0:T(2,128)S(1)}, u32[]{:S(2)}, u32[]{:S(2)}) %collective-permute-start.4) | collective-permute-done | bytes 16416 | tf_op jit(solution)/shard_map/ppermute | solution.py:135
  46.0 0.8 %fusion.19 = (bf16[512]{0:T(512)(128)(2,1)S(1)}, bf16[512]{0:T(512)(128)(2,1)S(1)}) fusion(f32[512]{0:T(512)S(1)} %get-tuple-element.9, f32[4096]{0:T(1024)} %param.11, s32[]{:T(128)S(6)} %select_n.27), kind=kLoop, calls=%fused_computation.71 | loop fusion | flops 3584 | bytes 6148 | tf_op jit(solution)/shard_map/convert_element_type | solution.py:148
  46.8 0.4 collective-permute-done.5
  47.3 2.1 %collective-permute-start.6 = (f32[2,2048]{1,0:T(2,128)S(1)}, f32[2,2048]{1,0:T(2,128)S(1)}, u32[]{:S(2)}, u32[]{:S(2)}) collective-permute-start(f32[2,2048]{1,0:T(2,128)S(1)} %add.79), channel_id=1, source_target_pairs={{0,1},{1,2},{2,3},{3,0},{4,5},{5,6},{6,7},{7,4},{8,9},{9,10},{10,1... | collective-permute-start | bytes 49160 | tf_op jit(solution)/shard_map/ppermute | solution.py:58
  49.4 2.6 %collective-permute-start.7 = (f32[2,2048]{1,0:T(2,128)S(1)}, f32[2,2048]{1,0:T(2,128)S(1)}, u32[]{:S(2)}, u32[]{:S(2)}) collective-permute-start(f32[2,2048]{1,0:T(2,128)S(1)} %add.79), channel_id=1, source_target_pairs={{0,2},{1,3},{2,0},{3,1},{4,6},{5,7},{6,4},{7,5},{8,10},{9,11},{10,... | collective-permute-start | bytes 49160 | tf_op jit(solution)/shard_map/ppermute | solution.py:58
  52.0 1.3 %collective-permute-start.8 = (f32[2,2048]{1,0:T(2,128)S(1)}, f32[2,2048]{1,0:T(2,128)S(1)}, u32[]{:S(2)}, u32[]{:S(2)}) collective-permute-start(f32[2,2048]{1,0:T(2,128)S(1)} %add.79), channel_id=1, source_target_pairs={{0,3},{1,0},{2,1},{3,2},{4,7},{5,4},{6,5},{7,6},{8,11},{9,8},{10,9... | collective-permute-start | bytes 49160 | tf_op jit(solution)/shard_map/ppermute | solution.py:58
  53.4 0.9 %collective-permute-done.7 = f32[2,2048]{1,0:T(2,128)S(1)} collective-permute-done((f32[2,2048]{1,0:T(2,128)S(1)}, f32[2,2048]{1,0:T(2,128)S(1)}, u32[]{:S(2)}, u32[]{:S(2)}) %collective-permute-start.7) | collective-permute-done | bytes 16416 | tf_op jit(solution)/shard_map/ppermute | solution.py:58
  54.3 1.4 %collective-permute-done.8 = f32[2,2048]{1,0:T(2,128)S(1)} collective-permute-done((f32[2,2048]{1,0:T(2,128)S(1)}, f32[2,2048]{1,0:T(2,128)S(1)}, u32[]{:S(2)}, u32[]{:S(2)}) %collective-permute-start.8) | collective-permute-done | bytes 16416 | tf_op jit(solution)/shard_map/ppermute | solution.py:58
  55.8 3.5 %fusion.8 = (f32[512]{0:T(512)S(1)}, f32[256,512]{1,0:T(8,128)S(1)}) fusion(bf16[8,32,512]{2,1,0:T(8,128)(2,1)S(1)} %copy-done.2, bf16[2048,512]{1,0:T(8,128)(2,1)} %get-tuple-element.7, bf16[2048,512]{1,0:T(8,128)(2,1)} %get-tuple-element.6, f32[2048]{0:T(1024)S(1)} %bitcast.96, f32[2048]{0:T(1024)S(1)} %bitcast.95, bf16[2048,512]{1,0:T(8,128)(2,1)S(1)} %bitcast.68), kind=kOutput, calls=%fused_computation.24 | convolution fusion | flops 544603648 | bytes 6047744 | tf_op jit(solution)/shard_map/dot_general | solution.py:142
  59.4 0.2 reshape.123
  59.6 10.6 %all_to_all.5 = bf16[8,136,128]{2,1,0:T(8,128)(2,1)S(1)} all-to-all(bf16[8,136,128]{2,1,0:T(8,128)(2,1)S(1)} %pad_maximum_fusion.8), channel_id=1, replica_groups=mesh['dp'=8,'tensor'=4] {'dp'}, dimensions={0} | all-to-all | bytes 557056 | tf_op jit(solution)/shard_map/all_to_all | solution.py:159
  70.4 0.8 %copy.29 = f32[4,8,8,512]{3,1,2,0:T(8,128)} copy(f32[4,8,8,512]{3,1,0,2:T(8,128)S(1)} %bitcast.72) | data formatting | bytes 1048576
  71.2 0.6 convert_add_fusion
  (72 shorter events, 2.6 us)
Async XLA Ops:
  0.6 2.3 %copy-start = (bf16[32,4096]{1,0:T(8,128)(2,1)S(1)}, bf16[32,4096]{1,0:T(8,128)(2,1)}, u32[]{:S(2)}) copy-start(bf16[32,4096]{1,0:T(8,128)(2,1)} %param.8) | copy-start | bytes 786436
  3.1 0.9 %copy-start.4 = (bf16[256,256]{1,0:T(8,128)(2,1)S(1)}, bf16[256,256]{1,0:T(8,128)(2,1)}, u32[]{:S(2)}) copy-start(bf16[256,256]{1,0:T(8,128)(2,1)} %param.10) | copy-start | bytes 393220
  3.1 1.0 %copy-start.3 = (bf16[256,256]{1,0:T(8,128)(2,1)S(1)}, bf16[256,256]{1,0:T(8,128)(2,1)}, u32[]{:S(2)}) copy-start(bf16[256,256]{1,0:T(8,128)(2,1)} %param.9) | copy-start | bytes 393220
  4.5 10.2 %collective-permute-start = (bf16[512,512]{1,0:T(8,128)(2,1)S(1)}, bf16[512,512]{1,0:T(8,128)(2,1)S(1)}, u32[]{:S(2)}, u32[]{:S(2)}) collective-permute-start(bf16[512,512]{1,0:T(8,128)(2,1)S(1)} %pad_maximum_fusion.5), channel_id=1, source_target_pairs={{0,8},{4,20},{8,0},{12,28},{16,24},{20,4},{24,16},{28,12},{1,9},{5... | collective-permute-start | bytes 1572872 | tf_op jit(solution)/shard_map/ppermute | solution.py:100
  14.8 12.1 %collective-permute-start.1 = (bf16[768,512]{1,0:T(8,128)(2,1)S(1)}, bf16[768,512]{1,0:T(8,128)(2,1)S(1)}, u32[]{:S(2)}, u32[]{:S(2)}) collective-permute-start(bf16[768,512]{1,0:T(8,128)(2,1)S(1)} %pad_maximum_fusion.3), channel_id=1, source_target_pairs={{0,16},{4,12},{8,24},{12,4},{16,0},{20,28},{24,8},{28,20},{1,17},{... | collective-permute-start | bytes 2359304 | tf_op jit(solution)/shard_map/ppermute | solution.py:100
  28.4 3.2 %collective-permute-start.2 = (bf16[1280,512]{1,0:T(8,128)(2,1)}, bf16[1280,512]{1,0:T(8,128)(2,1)S(1)}, u32[]{:S(2)}, u32[]{:S(2)}) collective-permute-start(bf16[1280,512]{1,0:T(8,128)(2,1)} %pad_maximum_fusion.1), channel_id=1, source_target_pairs={{0,4},{4,0},{8,12},{12,8},{16,20},{20,16},{24,28},{28,24},{1,5},{5... | collective-permute-start | bytes 3932168 | tf_op jit(solution)/shard_map/ppermute | solution.py:100
  32.5 0.7 copy-start.1
  35.4 20.3 %copy-start.2 = (bf16[8,32,512]{2,1,0:T(8,128)(2,1)S(1)}, bf16[8,32,512]{2,1,0:T(8,128)(2,1)}, u32[]{:S(2)}) copy-start(bf16[8,32,512]{2,1,0:T(8,128)(2,1)} %copy-done.1) | copy-start | bytes 786436
  38.0 3.8 %collective-permute-start.3 = (f32[2,2048]{1,0:T(2,128)S(1)}, f32[2,2048]{1,0:T(2,128)S(1)}, u32[]{:S(2)}, u32[]{:S(2)}) collective-permute-start(f32[2,2048]{1,0:T(2,128)S(1)} %pad_maximum_fusion.9), channel_id=1, source_target_pairs={{0,8},{4,20},{8,0},{12,28},{16,24},{20,4},{24,16},{28,12},{1,9},{5... | collective-permute-start | bytes 49160 | tf_op jit(solution)/shard_map/ppermute | solution.py:135
  42.0 3.8 %collective-permute-start.4 = (f32[2,2048]{1,0:T(2,128)S(1)}, f32[2,2048]{1,0:T(2,128)S(1)}, u32[]{:S(2)}, u32[]{:S(2)}) collective-permute-start(f32[2,2048]{1,0:T(2,128)S(1)} %fusion.21), channel_id=1, source_target_pairs={{0,16},{4,12},{8,24},{12,4},{16,0},{20,28},{24,8},{28,20},{1,17},{... | collective-permute-start | bytes 49160 | tf_op jit(solution)/shard_map/ppermute | solution.py:135
  45.9 1.2 %collective-permute-start.5 = (f32[2,2048]{1,0:T(2,128)S(1)}, f32[2,2048]{1,0:T(2,128)S(1)}, u32[]{:S(2)}, u32[]{:S(2)}) collective-permute-start(f32[2,2048]{1,0:T(2,128)S(1)} %fusion.32), channel_id=1, source_target_pairs={{0,4},{4,0},{8,12},{12,8},{16,20},{20,16},{24,28},{28,24},{1,5},{5... | collective-permute-start | bytes 49160 | tf_op jit(solution)/shard_map/ppermute | solution.py:132
  47.3 6.1 %collective-permute-start.6 = (f32[2,2048]{1,0:T(2,128)S(1)}, f32[2,2048]{1,0:T(2,128)S(1)}, u32[]{:S(2)}, u32[]{:S(2)}) collective-permute-start(f32[2,2048]{1,0:T(2,128)S(1)} %add.79), channel_id=1, source_target_pairs={{0,1},{1,2},{2,3},{3,0},{4,5},{5,6},{6,7},{7,4},{8,9},{9,10},{10,1... | collective-permute-start | bytes 49160 | tf_op jit(solution)/shard_map/ppermute | solution.py:58
  49.4 4.9 %collective-permute-start.7 = (f32[2,2048]{1,0:T(2,128)S(1)}, f32[2,2048]{1,0:T(2,128)S(1)}, u32[]{:S(2)}, u32[]{:S(2)}) collective-permute-start(f32[2,2048]{1,0:T(2,128)S(1)} %add.79), channel_id=1, source_target_pairs={{0,2},{1,3},{2,0},{3,1},{4,6},{5,7},{6,4},{7,5},{8,10},{9,11},{10,... | collective-permute-start | bytes 49160 | tf_op jit(solution)/shard_map/ppermute | solution.py:58
  52.0 3.7 %collective-permute-start.8 = (f32[2,2048]{1,0:T(2,128)S(1)}, f32[2,2048]{1,0:T(2,128)S(1)}, u32[]{:S(2)}, u32[]{:S(2)}) collective-permute-start(f32[2,2048]{1,0:T(2,128)S(1)} %add.79), channel_id=1, source_target_pairs={{0,3},{1,0},{2,1},{3,2},{4,7},{5,4},{6,5},{7,6},{8,11},{9,8},{10,9... | collective-permute-start | bytes 49160 | tf_op jit(solution)/shard_map/ppermute | solution.py:58

commit v20 on v19

--- a/solution.py
+++ b/solution.py
@@ -135,7 +135,9 @@
             got = lax.ppermute(totals, "dp", swap(up[r], down[r])).reshape(shape)
             got = jnp.flip(got, nbits - r)
         totals = totals + got.reshape(totals.shape)
-    totals = exchange_all(totals, "tensor", lax.axis_size("tensor"))
+    width_t = lax.axis_size("tensor")
+    spread = jnp.broadcast_to(totals[None], (width_t,) + totals.shape)
+    totals = jnp.sum(lax.all_to_all(spread, "tensor", 0, 0, tiled=True), 0)
     t_total, s_total = totals[0][:, None], totals[1][:, None]
     part_center = 0.5 * c + 0.5 * (jnp.sum(t_cos, 0) / (images * n))
     dlog = ((s_exp / s_total - t_exp / t_total) / 0.1).astype(jnp.bfloat16)

time: 72.1 us -> 75.5 us (1.047)
  waiting for transfers between devices: 25.8 us -> 29.2 us
    ppermute x3 -> x0, starting transfers between devices: 6.07 us -> none  [exchange_all(): total = total + lax.ppermute(x, axis, [(i, (i + k) % n) for i in range(n)])]
    all_to_all x0 -> x1, waiting for transfers between devices: none -> 5.72 us  [feature_plan(): totals = jnp.sum(lax.all_to_all(spread, 'tensor', 0, 0, tiled=True), 0)]
    all_to_all x0 -> x1, starting transfers between devices: none -> 5.37 us  [feature_plan(): totals = jnp.sum(lax.all_to_all(spread, 'tensor', 0, 0, tiled=True), 0)]
    ppermute x3 -> x0, waiting for transfers between devices: 2.36 us -> none  [exchange_all(): total = total + lax.ppermute(x, axis, [(i, (i + k) % n) for i in range(n)])]
  transfers between devices with their start and end apart: 9 -> 7, of which waited for: 8 -> 7; matrix products, arithmetic and copies ran while one was open for 2% -> 2% of each run, Pallas kernels for 0% -> 0%
where the time goes in v20:
time: 75.5 us; the launch traced here: 75.1 us
  waiting for transfers between devices  29.2 us (39%)
  starting transfers between devices  14.7 us (19%)
  blocking collectives  10.6 us (14%)
  matrix products  8.24 us (11%)
  other arithmetic  6.31 us (8%)
  local copies, waits for them, and re-layouts  4.98 us (7%)
  between operations  1.12 us (1%)
    ppermute x3, waiting for transfers between devices, feature_plan(): got = lax.ppermute(payload, 'dp', pairs)  19.6 us
    all_to_all x1, blocking collectives, feature_plan(): got = lax.all_to_all(sent, 'dp', 0, 0, tiled=True)  10.6 us
    all_to_all x1, waiting for transfers between devices, feature_plan(): totals = jnp.sum(lax.all_to_all(spread, 'tensor', 0, 0, tiled=True), 0)  5.72 us
    all_to_all x1, starting transfers between devices, feature_plan(): totals = jnp.sum(lax.all_to_all(spread, 'tensor', 0, 0, tiled=True), 0)  5.37 us
    ppermute x3, starting transfers between devices, feature_plan(): got = lax.ppermute(payload, 'dp', pairs)  5.12 us
    ppermute x2, starting transfers between devices, feature_plan(): got = lax.ppermute(totals, 'dp', swap(up[r], down[r])).reshape(shape)  4.12 us
    ppermute x2, waiting for transfers between devices, feature_plan(): got = lax.ppermute(totals, 'dp', swap(up[r], down[r])).reshape(shape)  3.48 us
    dot_general x1, matrix products, feature_plan(): lax.dot_general(zs, dlog, (((0,), (0,)), ((), ())), preferred_element_typ...  3.47 us
  transfers between devices with their start and end apart: 7, of which 7 were waited for; matrix products, arithmetic and copies ran while one was open for 2% of the time, Pallas kernels for 0%

profile of v20, /device:TPU:0, one launch (start us, length us, event | category | flops | bytes accessed | tf_op | source)
XLA Modules:
  0.0 75.1 jit_solution(13071027885515995867)
XLA Ops:
  0.7 2.0 %fusion.24 = (bf16[32,4096]{1,0:T(8,128)(2,1)S(1)}, f32[32,4096]{1,0:T(8,128)}) fusion(bf16[32,4096]{1,0:T(8,128)(2,1)} %param.8, f32[32,4096]{1,0:T(8,128)} %param.7), kind=kLoop, calls=%fused_computation.75 | loop fusion | flops 655360 | bytes 1572864 | tf_op jit(solution)/shard_map/convert_element_type | solution.py:75
  3.2 0.6 gather_fusion
  4.3 0.1 fusion.15
  4.5 3.0 %collective-permute-start = (bf16[512,512]{1,0:T(8,128)(2,1)S(1)}, bf16[512,512]{1,0:T(8,128)(2,1)S(1)}, u32[]{:S(2)}, u32[]{:S(2)}) collective-permute-start(bf16[512,512]{1,0:T(8,128)(2,1)S(1)} %pad_maximum_fusion.5), channel_id=1, source_target_pairs={{0,8},{4,20},{8,0},{12,28},{16,24},{20,4},{24,16},{28,12},{1,9},{5... | collective-permute-start | bytes 1572872 | tf_op jit(solution)/shard_map/ppermute | solution.py:100
  7.5 7.1 %collective-permute-done = bf16[512,512]{1,0:T(8,128)(2,1)S(1)} collective-permute-done((bf16[512,512]{1,0:T(8,128)(2,1)S(1)}, bf16[512,512]{1,0:T(8,128)(2,1)S(1)}, u32[]{:S(2)}, u32[]{:S(2)}) %collective-permute-start) | collective-permute-done | bytes 524320 | tf_op jit(solution)/shard_map/ppermute | solution.py:100
  14.8 2.1 %collective-permute-start.1 = (bf16[768,512]{1,0:T(8,128)(2,1)S(1)}, bf16[768,512]{1,0:T(8,128)(2,1)S(1)}, u32[]{:S(2)}, u32[]{:S(2)}) collective-permute-start(bf16[768,512]{1,0:T(8,128)(2,1)S(1)} %pad_maximum_fusion.3), channel_id=1, source_target_pairs={{0,16},{4,12},{8,24},{12,4},{16,0},{20,28},{24,8},{28,20},{1,17},{... | collective-permute-start | bytes 2359304 | tf_op jit(solution)/shard_map/ppermute | solution.py:100
  16.9 10.0 %collective-permute-done.1 = bf16[768,512]{1,0:T(8,128)(2,1)S(1)} collective-permute-done((bf16[768,512]{1,0:T(8,128)(2,1)S(1)}, bf16[768,512]{1,0:T(8,128)(2,1)S(1)}, u32[]{:S(2)}, u32[]{:S(2)}) %collective-permute-start.1) | collective-permute-done | bytes 786464 | tf_op jit(solution)/shard_map/ppermute | solution.py:100
  27.1 0.1 fusion.23
  27.2 1.2 %pad_maximum_fusion.1 = bf16[1280,512]{1,0:T(8,128)(2,1)} fusion(bf16[256,512]{1,0:T(8,128)(2,1)S(1)} %bitcast.75, bf16[1024,512]{1,0:T(8,128)(2,1)S(1)} %bitcast.60), kind=kLoop, calls=%fused_computation.10 | loop fusion | flops 2621440 | bytes 2621440 | tf_op jit(solution)/shard_map/concatenate | solution.py:99
  28.4 0.8 %dynamic_slice.3 = f32[512]{0:T(512)S(1)} dynamic-slice(f32[4096]{0:T(1024)} %param.11, s32[]{:T(128)S(6)} %select_n.27), dynamic_slice_sizes={512} | dynamic-slice | bytes 4100 | tf_op jit(solution)/shard_map/dynamic_slice | solution.py:119
  29.1 2.5 %collective-permute-done.2 = bf16[1280,512]{1,0:T(8,128)(2,1)S(1)} collective-permute-done((bf16[1280,512]{1,0:T(8,128)(2,1)}, bf16[1280,512]{1,0:T(8,128)(2,1)S(1)}, u32[]{:S(2)}, u32[]{:S(2)}) %collective-permute-start.2) | collective-permute-done | bytes 1310752 | tf_op jit(solution)/shard_map/ppermute | solution.py:100
  31.7 0.6 gather_fusion.1
  32.5 0.1 multiply_reduce_fusion
  32.8 0.2 pad_maximum_fusion
  33.0 0.2 copy-done.1
  33.2 2.2 %fusion.25 = (f32[2048]{0:T(1024)S(1)}, bf16[2048,512]{1,0:T(8,128)(2,1)}) fusion(f32[512]{0:T(512)S(1)} %add_sqrt_fusion, bf16[256,512]{1,0:T(8,128)(2,1)S(1)} %bitcast.83, bf16[2048,512]{1,0:T(8,128)(2,1)S(1)} %bitcast.66), kind=kOutput, calls=%fused_computation.76 | convolution fusion | flops 541063168 | bytes 3418112 | tf_op jit(solution)/shard_map/dot_general | solution.py:123
  35.4 2.5 %fusion = (f32[2048]{0:T(1024)S(1)}, f32[512]{0:T(512)S(1)}, bf16[2048,512]{1,0:T(8,128)(2,1)}) fusion(f32[512]{0:T(512)S(1)} %dynamic_slice.3, f32[512]{0:T(512)S(1)} %add_sqrt_fusion.1, bf16[256,512]{1,0:T(8,128)(2,1)S(1)} %bitcast.86, bf16[2048,512]{1,0:T(8,128)(2,1)S(1)} %bitcast.67), kind=kOutput, calls=%fused_computation.5 | convolution fusion | flops 543159808 | bytes 3422208 | tf_op jit(solution)/shard_map/dot_general | solution.py:122
  38.0 2.1 %collective-permute-start.3 = (f32[2,2048]{1,0:T(2,128)S(1)}, f32[2,2048]{1,0:T(2,128)S(1)}, u32[]{:S(2)}, u32[]{:S(2)}) collective-permute-start(f32[2,2048]{1,0:T(2,128)S(1)} %pad_maximum_fusion.9), channel_id=1, source_target_pairs={{0,8},{4,20},{8,0},{12,28},{16,24},{20,4},{24,16},{28,12},{1,9},{5... | collective-permute-start | bytes 49160 | tf_op jit(solution)/shard_map/ppermute | solution.py:135
  40.0 1.8 %collective-permute-done.3 = f32[2,2048]{1,0:T(2,128)S(1)} collective-permute-done((f32[2,2048]{1,0:T(2,128)S(1)}, f32[2,2048]{1,0:T(2,128)S(1)}, u32[]{:S(2)}, u32[]{:S(2)}) %collective-permute-start.3) | collective-permute-done | bytes 16416 | tf_op jit(solution)/shard_map/ppermute | solution.py:135
  41.8 0.1 rev.12
  42.0 2.1 %collective-permute-start.4 = (f32[2,2048]{1,0:T(2,128)S(1)}, f32[2,2048]{1,0:T(2,128)S(1)}, u32[]{:S(2)}, u32[]{:S(2)}) collective-permute-start(f32[2,2048]{1,0:T(2,128)S(1)} %fusion.21), channel_id=1, source_target_pairs={{0,16},{4,12},{8,24},{12,4},{16,0},{20,28},{24,8},{28,20},{1,17},{... | collective-permute-start | bytes 49160 | tf_op jit(solution)/shard_map/ppermute | solution.py:135
  44.1 1.7 %collective-permute-done.4 = f32[2,2048]{1,0:T(2,128)S(1)} collective-permute-done((f32[2,2048]{1,0:T(2,128)S(1)}, f32[2,2048]{1,0:T(2,128)S(1)}, u32[]{:S(2)}, u32[]{:S(2)}) %collective-permute-start.4) | collective-permute-done | bytes 16416 | tf_op jit(solution)/shard_map/ppermute | solution.py:135
  46.0 0.8 %fusion.19 = (bf16[512]{0:T(512)(128)(2,1)S(1)}, bf16[512]{0:T(512)(128)(2,1)S(1)}) fusion(f32[512]{0:T(512)S(1)} %get-tuple-element.9, f32[4096]{0:T(1024)} %param.11, s32[]{:T(128)S(6)} %select_n.27), kind=kLoop, calls=%fused_computation.70 | loop fusion | flops 3584 | bytes 6148 | tf_op jit(solution)/shard_map/convert_element_type | solution.py:150
  46.8 0.4 collective-permute-done.5
  47.3 0.6 broadcast_in_dim.15
  47.9 5.4 %all-to-all-start = ((f32[4,2,2048]{2,1,0:T(2,128)}), f32[4,2,2048]{2,1,0:T(2,128)S(1)}, u32[]{:S(2)}, u32[]{:S(2)}) async-start(f32[4,2,2048]{2,1,0:T(2,128)} %broadcast_in_dim.15), calls=%async_computation | async-start | bytes 131072 | tf_op jit(solution)/shard_map/all_to_all | solution.py:140
  53.3 5.7 %all-to-all-done = f32[4,2,2048]{2,1,0:T(2,128)S(1)} async-done(((f32[4,2,2048]{2,1,0:T(2,128)}), f32[4,2,2048]{2,1,0:T(2,128)S(1)}, u32[]{:S(2)}, u32[]{:S(2)}) %all-to-all-start) | async-done | bytes 65568 | tf_op jit(solution)/shard_map/all_to_all | solution.py:140
  59.1 3.5 %fusion.8 = (f32[512]{0:T(512)S(1)}, f32[256,512]{1,0:T(8,128)S(1)}) fusion(bf16[8,32,512]{2,1,0:T(8,128)(2,1)S(1)} %copy-done.2, bf16[2048,512]{1,0:T(8,128)(2,1)} %get-tuple-element.7, bf16[2048,512]{1,0:T(8,128)(2,1)} %get-tuple-element.6, f32[2048]{0:T(1024)S(1)} %bitcast.96, f32[2048]{0:T(1024)S(1)} %bitcast.95, bf16[2048,512]{1,0:T(8,128)(2,1)S(1)} %bitcast.68), kind=kOutput, calls=%fused_computation.24 | convolution fusion | flops 544603648 | bytes 6047744 | tf_op jit(solution)/shard_map/dot_general | solution.py:144
  62.7 0.2 reshape.154
  62.9 10.6 %all_to_all.10 = bf16[8,136,128]{2,1,0:T(8,128)(2,1)S(1)} all-to-all(bf16[8,136,128]{2,1,0:T(8,128)(2,1)S(1)} %pad_maximum_fusion.8), channel_id=1, replica_groups=mesh['dp'=8,'tensor'=4] {'dp'}, dimensions={0} | all-to-all | bytes 557056 | tf_op jit(solution)/shard_map/all_to_all | solution.py:161
  73.7 0.8 %copy.49 = f32[4,8,8,512]{3,1,2,0:T(8,128)} copy(f32[4,8,8,512]{3,1,0,2:T(8,128)S(1)} %bitcast.72) | data formatting | bytes 1048576
  74.5 0.6 convert_add_fusion
  (69 shorter events, 2.3 us)
Async XLA Ops:
  0.6 2.3 %copy-start = (bf16[32,4096]{1,0:T(8,128)(2,1)S(1)}, bf16[32,4096]{1,0:T(8,128)(2,1)}, u32[]{:S(2)}) copy-start(bf16[32,4096]{1,0:T(8,128)(2,1)} %param.8) | copy-start | bytes 786436
  3.1 0.9 %copy-start.4 = (bf16[256,256]{1,0:T(8,128)(2,1)S(1)}, bf16[256,256]{1,0:T(8,128)(2,1)}, u32[]{:S(2)}) copy-start(bf16[256,256]{1,0:T(8,128)(2,1)} %param.10) | copy-start | bytes 393220
  3.1 1.0 %copy-start.3 = (bf16[256,256]{1,0:T(8,128)(2,1)S(1)}, bf16[256,256]{1,0:T(8,128)(2,1)}, u32[]{:S(2)}) copy-start(bf16[256,256]{1,0:T(8,128)(2,1)} %param.9) | copy-start | bytes 393220
  4.5 10.2 %collective-permute-start = (bf16[512,512]{1,0:T(8,128)(2,1)S(1)}, bf16[512,512]{1,0:T(8,128)(2,1)S(1)}, u32[]{:S(2)}, u32[]{:S(2)}) collective-permute-start(bf16[512,512]{1,0:T(8,128)(2,1)S(1)} %pad_maximum_fusion.5), channel_id=1, source_target_pairs={{0,8},{4,20},{8,0},{12,28},{16,24},{20,4},{24,16},{28,12},{1,9},{5... | collective-permute-start | bytes 1572872 | tf_op jit(solution)/shard_map/ppermute | solution.py:100
  14.8 12.1 %collective-permute-start.1 = (bf16[768,512]{1,0:T(8,128)(2,1)S(1)}, bf16[768,512]{1,0:T(8,128)(2,1)S(1)}, u32[]{:S(2)}, u32[]{:S(2)}) collective-permute-start(bf16[768,512]{1,0:T(8,128)(2,1)S(1)} %pad_maximum_fusion.3), channel_id=1, source_target_pairs={{0,16},{4,12},{8,24},{12,4},{16,0},{20,28},{24,8},{28,20},{1,17},{... | collective-permute-start | bytes 2359304 | tf_op jit(solution)/shard_map/ppermute | solution.py:100
  28.4 3.2 %collective-permute-start.2 = (bf16[1280,512]{1,0:T(8,128)(2,1)}, bf16[1280,512]{1,0:T(8,128)(2,1)S(1)}, u32[]{:S(2)}, u32[]{:S(2)}) collective-permute-start(bf16[1280,512]{1,0:T(8,128)(2,1)} %pad_maximum_fusion.1), channel_id=1, source_target_pairs={{0,4},{4,0},{8,12},{12,8},{16,20},{20,16},{24,28},{28,24},{1,5},{5... | collective-permute-start | bytes 3932168 | tf_op jit(solution)/shard_map/ppermute | solution.py:100
  32.5 0.7 copy-start.1
  35.4 23.7 %copy-start.2 = (bf16[8,32,512]{2,1,0:T(8,128)(2,1)S(1)}, bf16[8,32,512]{2,1,0:T(8,128)(2,1)}, u32[]{:S(2)}) copy-start(bf16[8,32,512]{2,1,0:T(8,128)(2,1)} %copy-done.1) | copy-start | bytes 786436
  38.0 3.8 %collective-permute-start.3 = (f32[2,2048]{1,0:T(2,128)S(1)}, f32[2,2048]{1,0:T(2,128)S(1)}, u32[]{:S(2)}, u32[]{:S(2)}) collective-permute-start(f32[2,2048]{1,0:T(2,128)S(1)} %pad_maximum_fusion.9), channel_id=1, source_target_pairs={{0,8},{4,20},{8,0},{12,28},{16,24},{20,4},{24,16},{28,12},{1,9},{5... | collective-permute-start | bytes 49160 | tf_op jit(solution)/shard_map/ppermute | solution.py:135
  42.0 3.8 %collective-permute-start.4 = (f32[2,2048]{1,0:T(2,128)S(1)}, f32[2,2048]{1,0:T(2,128)S(1)}, u32[]{:S(2)}, u32[]{:S(2)}) collective-permute-start(f32[2,2048]{1,0:T(2,128)S(1)} %fusion.21), channel_id=1, source_target_pairs={{0,16},{4,12},{8,24},{12,4},{16,0},{20,28},{24,8},{28,20},{1,17},{... | collective-permute-start | bytes 49160 | tf_op jit(solution)/shard_map/ppermute | solution.py:135
  45.9 1.2 %collective-permute-start.5 = (f32[2,2048]{1,0:T(2,128)S(1)}, f32[2,2048]{1,0:T(2,128)S(1)}, u32[]{:S(2)}, u32[]{:S(2)}) collective-permute-start(f32[2,2048]{1,0:T(2,128)S(1)} %fusion.32), channel_id=1, source_target_pairs={{0,4},{4,0},{8,12},{12,8},{16,20},{20,16},{24,28},{28,24},{1,5},{5... | collective-permute-start | bytes 49160 | tf_op jit(solution)/shard_map/ppermute | solution.py:132
  47.9 11.1 %all-to-all-start = ((f32[4,2,2048]{2,1,0:T(2,128)}), f32[4,2,2048]{2,1,0:T(2,128)S(1)}, u32[]{:S(2)}, u32[]{:S(2)}) async-start(f32[4,2,2048]{2,1,0:T(2,128)} %broadcast_in_dim.15), calls=%async_computation | async-start | bytes 131072 | tf_op jit(solution)/shard_map/all_to_all | solution.py:140

commit v21 on v19

--- a/solution.py
+++ b/solution.py
@@ -71,8 +71,8 @@
     up = list(range(1, nbits))
     down = up[::-1]
     dim_bits = [jnp.where(odd == 1, down[r], up[r]) for r in range(nbits - 1)][::-1]
-    master_new = 0.996 * teacher_master + 0.004 * student_weight.astype(jnp.float32)
-    both = jnp.stack([student_weight, master_new.astype(jnp.bfloat16)])
+    rebuilt = 0.996 * teacher_master + 0.004 * student_weight.astype(jnp.float32)
+    both = jnp.stack([student_weight, rebuilt.astype(jnp.bfloat16)])
     both = both.reshape(2, rows, n, cols).transpose(2, 0, 1, 3).reshape(n, 2 * rows, cols)
     pos = jnp.arange(n)
     rel = (pos >> (nbits - 1)) & 1
@@ -97,10 +97,17 @@
         if 2 * bot == cols:
             flat_feats = feats.reshape(-1, 2 * bot)
             payload = jnp.concatenate([flat_feats, away.reshape(-1, cols)], axis=0)
+            if r == min(1, nbits - 1):
+                master, student, payload = lax.optimization_barrier(
+                    (teacher_master, student_weight, payload)
+                )
+                master_new = 0.996 * master + 0.004 * student.astype(jnp.float32)
             got = lax.ppermute(payload, "dp", pairs)
             got_feats = got[: flat_feats.shape[0]].reshape(feats.shape)
             got_held = got[flat_feats.shape[0]:].reshape(away.shape)
         else:
+            if r == min(1, nbits - 1):
+                master_new = rebuilt
             got_feats, got_held = lax.ppermute((feats, away), "dp", pairs)
         if last:
             got_feats = jnp.transpose(got_feats, cross_rev + [nbits - 1, nbits])
@@ -126,6 +133,7 @@
     totals = jnp.stack([jnp.sum(t_exp, 1), jnp.sum(s_exp, 1)])
     t_exp, s_exp = lax.optimization_barrier((t_exp.astype(jnp.bfloat16), s_exp.astype(jnp.bfloat16)))
     t_exp, s_exp = t_exp.astype(jnp.float32), s_exp.astype(jnp.float32)
+    totals, master_new = lax.optimization_barrier((totals, master_new))
     shape = (2,) + (2,) * nbits + (images,)
     for r in range(nbits):
         if r == nbits - 1:

time: 72.1 us -> 71.3 us (0.989)
  waiting for transfers between devices: 25.8 us -> 24.9 us
    ppermute x3, waiting for transfers between devices: 19.6 us -> 18.7 us  [feature_plan(): got = lax.ppermute(payload, 'dp', pairs)]
    add x0 -> x1, other arithmetic: none -> 0.87 us  [feature_plan(): master_new = 0.996 * master + 0.004 * student.astype(jnp.float32)]
    convert_element_type x1, other arithmetic: 2.03 us -> 1.23 us  [feature_plan(): both = jnp.stack([student_weight, rebuilt.astype(jnp.bfloat16)])]
  transfers between devices with their start and end apart: 9 -> 9, of which waited for: 8 -> 8; matrix products, arithmetic and copies ran while one was open for 2% -> 3% of each run, Pallas kernels for 0% -> 0%
where the time goes in v21:
time: 71.3 us; the launch traced here: 71 us
  waiting for transfers between devices  24.9 us (35%)
  starting transfers between devices  15.4 us (22%)
  blocking collectives  10.6 us (15%)
  matrix products  8.24 us (12%)
  other arithmetic  6.35 us (9%)
  local copies, waits for them, and re-layouts  4.34 us (6%)
  between operations  1.15 us (2%)
    ppermute x3, waiting for transfers between devices, feature_plan(): got = lax.ppermute(payload, 'dp', pairs)  18.7 us
    all_to_all x1, blocking collectives, feature_plan(): got = lax.all_to_all(sent, 'dp', 0, 0, tiled=True)  10.6 us
    ppermute x3, starting transfers between devices, exchange_all(): total = total + lax.ppermute(x, axis, [(i, (i + k) % n) for i in range(n)])  6.07 us
    ppermute x3, starting transfers between devices, feature_plan(): got = lax.ppermute(payload, 'dp', pairs)  5.12 us
    ppermute x2, starting transfers between devices, feature_plan(): got = lax.ppermute(totals, 'dp', swap(up[r], down[r])).reshape(shape)  4.13 us
    ppermute x2, waiting for transfers between devices, feature_plan(): got = lax.ppermute(totals, 'dp', swap(up[r], down[r])).reshape(shape)  3.48 us
    dot_general x1, matrix products, feature_plan(): lax.dot_general(zs, dlog, (((0,), (0,)), ((), ())), preferred_element_typ...  3.47 us
    dot_general x1, matrix products, feature_plan(): t_cos = jnp.dot(zt, tw, preferred_element_type=jnp.float32) / t_norm  2.53 us
  transfers between devices with their start and end apart: 9, of which 8 were waited for; matrix products, arithmetic and copies ran while one was open for 3% of the time, Pallas kernels for 0%

profile of v21, /device:TPU:0, one launch (start us, length us, event | category | flops | bytes accessed | tf_op | source)
XLA Modules:
  0.0 71.0 jit_solution(5145865209992548006)
XLA Ops:
  0.7 1.2 %add_convert_fusion = bf16[32,4096]{1,0:T(8,128)(2,1)S(1)} fusion(bf16[32,4096]{1,0:T(8,128)(2,1)} %param.8, f32[32,4096]{1,0:T(8,128)} %param.7), kind=kLoop, calls=%fused_computation.37 | loop fusion | flops 655360 | bytes 1048576 | tf_op jit(solution)/shard_map/convert_element_type | solution.py:75
  2.4 0.6 gather_fusion
  3.5 0.1 fusion.15
  3.7 3.0 %collective-permute-start = (bf16[512,512]{1,0:T(8,128)(2,1)S(1)}, bf16[512,512]{1,0:T(8,128)(2,1)S(1)}, u32[]{:S(2)}, u32[]{:S(2)}) collective-permute-start(bf16[512,512]{1,0:T(8,128)(2,1)S(1)} %pad_maximum_fusion.5), channel_id=1, source_target_pairs={{0,8},{4,20},{8,0},{12,28},{16,24},{20,4},{24,16},{28,12},{1,9},{5... | collective-permute-start | bytes 1572872 | tf_op jit(solution)/shard_map/ppermute | solution.py:105
  6.7 7.1 %collective-permute-done = bf16[512,512]{1,0:T(8,128)(2,1)S(1)} collective-permute-done((bf16[512,512]{1,0:T(8,128)(2,1)S(1)}, bf16[512,512]{1,0:T(8,128)(2,1)S(1)}, u32[]{:S(2)}, u32[]{:S(2)}) %collective-permute-start) | collective-permute-done | bytes 524320 | tf_op jit(solution)/shard_map/ppermute | solution.py:105
  14.0 2.1 %collective-permute-start.1 = (bf16[768,512]{1,0:T(8,128)(2,1)S(1)}, bf16[768,512]{1,0:T(8,128)(2,1)S(1)}, u32[]{:S(2)}, u32[]{:S(2)}) collective-permute-start(bf16[768,512]{1,0:T(8,128)(2,1)S(1)} %pad_maximum_fusion.3), channel_id=1, source_target_pairs={{0,16},{4,12},{8,24},{12,4},{16,0},{20,28},{24,8},{28,20},{1,17},{... | collective-permute-start | bytes 2359304 | tf_op jit(solution)/shard_map/ppermute | solution.py:105
  16.2 10.0 %collective-permute-done.1 = bf16[768,512]{1,0:T(8,128)(2,1)S(1)} collective-permute-done((bf16[768,512]{1,0:T(8,128)(2,1)S(1)}, bf16[768,512]{1,0:T(8,128)(2,1)S(1)}, u32[]{:S(2)}, u32[]{:S(2)}) %collective-permute-start.1) | collective-permute-done | bytes 786464 | tf_op jit(solution)/shard_map/ppermute | solution.py:105
  26.4 1.2 %pad_maximum_fusion.1 = bf16[1280,512]{1,0:T(8,128)(2,1)} fusion(bf16[256,512]{1,0:T(8,128)(2,1)S(1)} %bitcast.76, bf16[1024,512]{1,0:T(8,128)(2,1)S(1)} %bitcast.60), kind=kLoop, calls=%fused_computation.10 | loop fusion | flops 2621440 | bytes 2621440 | tf_op jit(solution)/shard_map/concatenate | solution.py:99
  27.6 0.8 %dynamic_slice.3 = f32[512]{0:T(512)S(1)} dynamic-slice(f32[4096]{0:T(1024)} %param.11, s32[]{:T(128)S(6)} %select_n.27), dynamic_slice_sizes={512} | dynamic-slice | bytes 4100 | tf_op jit(solution)/shard_map/dynamic_slice | solution.py:126
  28.4 0.9 %multiply_add_fusion = f32[32,4096]{1,0:T(8,128)} fusion(bf16[32,4096]{1,0:T(8,128)(2,1)S(1)} %copy-done, f32[32,4096]{1,0:T(8,128)S(1)} %copy-done.1), kind=kLoop, calls=%fused_computation.34 | loop fusion | flops 524288 | bytes 1310720 | tf_op jit(solution)/shard_map/add | solution.py:104
  29.2 1.6 %collective-permute-done.2 = bf16[1280,512]{1,0:T(8,128)(2,1)S(1)} collective-permute-done((bf16[1280,512]{1,0:T(8,128)(2,1)}, bf16[1280,512]{1,0:T(8,128)(2,1)S(1)}, u32[]{:S(2)}, u32[]{:S(2)}) %collective-permute-start.2) | collective-permute-done | bytes 1310752 | tf_op jit(solution)/shard_map/ppermute | solution.py:105
  31.0 0.6 gather_fusion.1
  32.0 0.2 pad_maximum_fusion
  32.2 0.2 copy-done.2
  32.4 2.2 %fusion.24 = (bf16[2048,512]{1,0:T(8,128)(2,1)}, f32[2048]{0:T(1024)S(1)}) fusion(f32[512]{0:T(512)S(1)} %add_sqrt_fusion, bf16[256,512]{1,0:T(8,128)(2,1)S(1)} %bitcast.83, bf16[2048,512]{1,0:T(8,128)(2,1)S(1)} %bitcast.67), kind=kOutput, calls=%fused_computation.77 | convolution fusion | flops 541063168 | bytes 3418112 | tf_op jit(solution)/shard_map/dot_general | solution.py:130
  34.7 2.5 %fusion.23 = (f32[512]{0:T(512)S(1)}, f32[2048]{0:T(1024)S(1)}, bf16[2048,512]{1,0:T(8,128)(2,1)}) fusion(f32[512]{0:T(512)S(1)} %dynamic_slice.3, f32[512]{0:T(512)S(1)} %add_sqrt_fusion.1, bf16[256,512]{1,0:T(8,128)(2,1)S(1)} %bitcast.86, bf16[2048,512]{1,0:T(8,128)(2,1)S(1)} %bitcast.68), kind=kOutput, calls=%fused_computation.76 | convolution fusion | flops 543159808 | bytes 3422208 | tf_op jit(solution)/shard_map/dot_general | solution.py:129
  37.2 2.1 %collective-permute-start.3 = (f32[2,2048]{1,0:T(2,128)S(1)}, f32[2,2048]{1,0:T(2,128)S(1)}, u32[]{:S(2)}, u32[]{:S(2)}) collective-permute-start(f32[2,2048]{1,0:T(2,128)S(1)} %pad_maximum_fusion.9), channel_id=1, source_target_pairs={{0,8},{4,20},{8,0},{12,28},{16,24},{20,4},{24,16},{28,12},{1,9},{5... | collective-permute-start | bytes 49160 | tf_op jit(solution)/shard_map/ppermute | solution.py:143
  39.3 1.8 %collective-permute-done.3 = f32[2,2048]{1,0:T(2,128)S(1)} collective-permute-done((f32[2,2048]{1,0:T(2,128)S(1)}, f32[2,2048]{1,0:T(2,128)S(1)}, u32[]{:S(2)}, u32[]{:S(2)}) %collective-permute-start.3) | collective-permute-done | bytes 16416 | tf_op jit(solution)/shard_map/ppermute | solution.py:143
  41.2 2.1 %collective-permute-start.4 = (f32[2,2048]{1,0:T(2,128)S(1)}, f32[2,2048]{1,0:T(2,128)S(1)}, u32[]{:S(2)}, u32[]{:S(2)}) collective-permute-start(f32[2,2048]{1,0:T(2,128)S(1)} %add.81), channel_id=1, source_target_pairs={{0,16},{4,12},{8,24},{12,4},{16,0},{20,28},{24,8},{28,20},{1,17},{... | collective-permute-start | bytes 49160 | tf_op jit(solution)/shard_map/ppermute | solution.py:143
  43.3 1.7 %collective-permute-done.4 = f32[2,2048]{1,0:T(2,128)S(1)} collective-permute-done((f32[2,2048]{1,0:T(2,128)S(1)}, f32[2,2048]{1,0:T(2,128)S(1)}, u32[]{:S(2)}, u32[]{:S(2)}) %collective-permute-start.4) | collective-permute-done | bytes 16416 | tf_op jit(solution)/shard_map/ppermute | solution.py:143
  45.2 0.8 %fusion.19 = (bf16[512]{0:T(512)(128)(2,1)S(1)}, bf16[512]{0:T(512)(128)(2,1)S(1)}) fusion(f32[512]{0:T(512)S(1)} %get-tuple-element.18, f32[4096]{0:T(1024)} %param.11, s32[]{:T(128)S(6)} %select_n.27), kind=kLoop, calls=%fused_computation.72 | loop fusion | flops 3584 | bytes 6148 | tf_op jit(solution)/shard_map/convert_element_type | solution.py:156
  46.0 0.4 collective-permute-done.5
  46.5 2.1 %collective-permute-start.6 = (f32[2,2048]{1,0:T(2,128)S(1)}, f32[2,2048]{1,0:T(2,128)S(1)}, u32[]{:S(2)}, u32[]{:S(2)}) collective-permute-start(f32[2,2048]{1,0:T(2,128)S(1)} %add.83), channel_id=1, source_target_pairs={{0,1},{1,2},{2,3},{3,0},{4,5},{5,6},{6,7},{7,4},{8,9},{9,10},{10,1... | collective-permute-start | bytes 49160 | tf_op jit(solution)/shard_map/ppermute | solution.py:58
  48.6 2.6 %collective-permute-start.7 = (f32[2,2048]{1,0:T(2,128)S(1)}, f32[2,2048]{1,0:T(2,128)S(1)}, u32[]{:S(2)}, u32[]{:S(2)}) collective-permute-start(f32[2,2048]{1,0:T(2,128)S(1)} %add.83), channel_id=1, source_target_pairs={{0,2},{1,3},{2,0},{3,1},{4,6},{5,7},{6,4},{7,5},{8,10},{9,11},{10,... | collective-permute-start | bytes 49160 | tf_op jit(solution)/shard_map/ppermute | solution.py:58
  51.2 1.3 %collective-permute-start.8 = (f32[2,2048]{1,0:T(2,128)S(1)}, f32[2,2048]{1,0:T(2,128)S(1)}, u32[]{:S(2)}, u32[]{:S(2)}) collective-permute-start(f32[2,2048]{1,0:T(2,128)S(1)} %add.83), channel_id=1, source_target_pairs={{0,3},{1,0},{2,1},{3,2},{4,7},{5,4},{6,5},{7,6},{8,11},{9,8},{10,9... | collective-permute-start | bytes 49160 | tf_op jit(solution)/shard_map/ppermute | solution.py:58
  52.6 0.9 %collective-permute-done.7 = f32[2,2048]{1,0:T(2,128)S(1)} collective-permute-done((f32[2,2048]{1,0:T(2,128)S(1)}, f32[2,2048]{1,0:T(2,128)S(1)}, u32[]{:S(2)}, u32[]{:S(2)}) %collective-permute-start.7) | collective-permute-done | bytes 16416 | tf_op jit(solution)/shard_map/ppermute | solution.py:58
  53.5 1.4 %collective-permute-done.8 = f32[2,2048]{1,0:T(2,128)S(1)} collective-permute-done((f32[2,2048]{1,0:T(2,128)S(1)}, f32[2,2048]{1,0:T(2,128)S(1)}, u32[]{:S(2)}, u32[]{:S(2)}) %collective-permute-start.8) | collective-permute-done | bytes 16416 | tf_op jit(solution)/shard_map/ppermute | solution.py:58
  55.0 3.5 %fusion.8 = (f32[512]{0:T(512)S(1)}, f32[256,512]{1,0:T(8,128)S(1)}) fusion(bf16[8,32,512]{2,1,0:T(8,128)(2,1)S(1)} %copy-done.3, bf16[2048,512]{1,0:T(8,128)(2,1)} %get-tuple-element.17, bf16[2048,512]{1,0:T(8,128)(2,1)} %get-tuple-element.15, f32[2048]{0:T(1024)S(1)} %bitcast.91, f32[2048]{0:T(1024)S(1)} %bitcast.90, bf16[2048,512]{1,0:T(8,128)(2,1)S(1)} %bitcast.69), kind=kOutput, calls=%fused_computation.24 | convolution fusion | flops 544603648 | bytes 6047744 | tf_op jit(solution)/shard_map/dot_general | solution.py:150
  58.6 0.2 reshape.123
  58.8 10.6 %all_to_all.5 = bf16[8,136,128]{2,1,0:T(8,128)(2,1)S(1)} all-to-all(bf16[8,136,128]{2,1,0:T(8,128)(2,1)S(1)} %pad_maximum_fusion.8), channel_id=1, replica_groups=mesh['dp'=8,'tensor'=4] {'dp'}, dimensions={0} | all-to-all | bytes 557056 | tf_op jit(solution)/shard_map/all_to_all | solution.py:167
  69.6 0.8 %copy.29 = f32[4,8,8,512]{3,1,2,0:T(8,128)} copy(f32[4,8,8,512]{3,1,0,2:T(8,128)S(1)} %bitcast.73) | data formatting | bytes 1048576
  70.4 0.6 convert_add_fusion
  (75 shorter events, 2.7 us)
Async XLA Ops:
  0.6 1.5 %copy-start = (bf16[32,4096]{1,0:T(8,128)(2,1)S(1)}, bf16[32,4096]{1,0:T(8,128)(2,1)}, u32[]{:S(2)}) copy-start(bf16[32,4096]{1,0:T(8,128)(2,1)} %param.8) | copy-start | bytes 786436
  2.3 0.9 %copy-start.5 = (bf16[256,256]{1,0:T(8,128)(2,1)S(1)}, bf16[256,256]{1,0:T(8,128)(2,1)}, u32[]{:S(2)}) copy-start(bf16[256,256]{1,0:T(8,128)(2,1)} %param.10) | copy-start | bytes 393220
  2.3 1.0 %copy-start.4 = (bf16[256,256]{1,0:T(8,128)(2,1)S(1)}, bf16[256,256]{1,0:T(8,128)(2,1)}, u32[]{:S(2)}) copy-start(bf16[256,256]{1,0:T(8,128)(2,1)} %param.9) | copy-start | bytes 393220
  3.7 10.2 %collective-permute-start = (bf16[512,512]{1,0:T(8,128)(2,1)S(1)}, bf16[512,512]{1,0:T(8,128)(2,1)S(1)}, u32[]{:S(2)}, u32[]{:S(2)}) collective-permute-start(bf16[512,512]{1,0:T(8,128)(2,1)S(1)} %pad_maximum_fusion.5), channel_id=1, source_target_pairs={{0,8},{4,20},{8,0},{12,28},{16,24},{20,4},{24,16},{28,12},{1,9},{5... | collective-permute-start | bytes 1572872 | tf_op jit(solution)/shard_map/ppermute | solution.py:105
  14.0 12.1 %collective-permute-start.1 = (bf16[768,512]{1,0:T(8,128)(2,1)S(1)}, bf16[768,512]{1,0:T(8,128)(2,1)S(1)}, u32[]{:S(2)}, u32[]{:S(2)}) collective-permute-start(bf16[768,512]{1,0:T(8,128)(2,1)S(1)} %pad_maximum_fusion.3), channel_id=1, source_target_pairs={{0,16},{4,12},{8,24},{12,4},{16,0},{20,28},{24,8},{28,20},{1,17},{... | collective-permute-start | bytes 2359304 | tf_op jit(solution)/shard_map/ppermute | solution.py:105
  26.4 1.9 %copy-start.1 = (f32[32,4096]{1,0:T(8,128)S(1)}, f32[32,4096]{1,0:T(8,128)}, u32[]{:S(2)}) copy-start(f32[32,4096]{1,0:T(8,128)} %param.7) | copy-start | bytes 1572868
  27.6 3.2 %collective-permute-start.2 = (bf16[1280,512]{1,0:T(8,128)(2,1)}, bf16[1280,512]{1,0:T(8,128)(2,1)S(1)}, u32[]{:S(2)}, u32[]{:S(2)}) collective-permute-start(bf16[1280,512]{1,0:T(8,128)(2,1)} %pad_maximum_fusion.1), channel_id=1, source_target_pairs={{0,4},{4,0},{8,12},{12,8},{16,20},{20,16},{24,28},{28,24},{1,5},{5... | collective-permute-start | bytes 3932168 | tf_op jit(solution)/shard_map/ppermute | solution.py:105
  31.7 0.7 %copy-start.2 = (bf16[8,32,512]{2,1,0:T(8,128)(2,1)}, bf16[8,32,512]{2,1,0:T(8,128)(2,1)S(1)}, u32[]{:S(2)}) copy-start(bf16[8,32,512]{2,1,0:T(8,128)(2,1)S(1)} %get-tuple-element.32) | copy-start | bytes 786436
  34.7 20.3 %copy-start.3 = (bf16[8,32,512]{2,1,0:T(8,128)(2,1)S(1)}, bf16[8,32,512]{2,1,0:T(8,128)(2,1)}, u32[]{:S(2)}) copy-start(bf16[8,32,512]{2,1,0:T(8,128)(2,1)} %copy-done.2) | copy-start | bytes 786436
  37.2 3.8 %collective-permute-start.3 = (f32[2,2048]{1,0:T(2,128)S(1)}, f32[2,2048]{1,0:T(2,128)S(1)}, u32[]{:S(2)}, u32[]{:S(2)}) collective-permute-start(f32[2,2048]{1,0:T(2,128)S(1)} %pad_maximum_fusion.9), channel_id=1, source_target_pairs={{0,8},{4,20},{8,0},{12,28},{16,24},{20,4},{24,16},{28,12},{1,9},{5... | collective-permute-start | bytes 49160 | tf_op jit(solution)/shard_map/ppermute | solution.py:143
  41.2 3.8 %collective-permute-start.4 = (f32[2,2048]{1,0:T(2,128)S(1)}, f32[2,2048]{1,0:T(2,128)S(1)}, u32[]{:S(2)}, u32[]{:S(2)}) collective-permute-start(f32[2,2048]{1,0:T(2,128)S(1)} %add.81), channel_id=1, source_target_pairs={{0,16},{4,12},{8,24},{12,4},{16,0},{20,28},{24,8},{28,20},{1,17},{... | collective-permute-start | bytes 49160 | tf_op jit(solution)/shard_map/ppermute | solution.py:143
  45.1 1.2 %collective-permute-start.5 = (f32[2,2048]{1,0:T(2,128)S(1)}, f32[2,2048]{1,0:T(2,128)S(1)}, u32[]{:S(2)}, u32[]{:S(2)}) collective-permute-start(f32[2,2048]{1,0:T(2,128)S(1)} %add.82), channel_id=1, source_target_pairs={{0,4},{4,0},{8,12},{12,8},{16,20},{20,16},{24,28},{28,24},{1,5},{5... | collective-permute-start | bytes 49160 | tf_op jit(solution)/shard_map/ppermute | solution.py:140
  46.5 6.1 %collective-permute-start.6 = (f32[2,2048]{1,0:T(2,128)S(1)}, f32[2,2048]{1,0:T(2,128)S(1)}, u32[]{:S(2)}, u32[]{:S(2)}) collective-permute-start(f32[2,2048]{1,0:T(2,128)S(1)} %add.83), channel_id=1, source_target_pairs={{0,1},{1,2},{2,3},{3,0},{4,5},{5,6},{6,7},{7,4},{8,9},{9,10},{10,1... | collective-permute-start | bytes 49160 | tf_op jit(solution)/shard_map/ppermute | solution.py:58
  48.6 4.9 %collective-permute-start.7 = (f32[2,2048]{1,0:T(2,128)S(1)}, f32[2,2048]{1,0:T(2,128)S(1)}, u32[]{:S(2)}, u32[]{:S(2)}) collective-permute-start(f32[2,2048]{1,0:T(2,128)S(1)} %add.83), channel_id=1, source_target_pairs={{0,2},{1,3},{2,0},{3,1},{4,6},{5,7},{6,4},{7,5},{8,10},{9,11},{10,... | collective-permute-start | bytes 49160 | tf_op jit(solution)/shard_map/ppermute | solution.py:58
  51.2 3.7 %collective-permute-start.8 = (f32[2,2048]{1,0:T(2,128)S(1)}, f32[2,2048]{1,0:T(2,128)S(1)}, u32[]{:S(2)}, u32[]{:S(2)}) collective-permute-start(f32[2,2048]{1,0:T(2,128)S(1)} %add.83), channel_id=1, source_target_pairs={{0,3},{1,0},{2,1},{3,2},{4,7},{5,4},{6,5},{7,6},{8,11},{9,8},{10,9... | collective-permute-start | bytes 49160 | tf_op jit(solution)/shard_map/ppermute | solution.py:58

commit v22 on v21

--- a/solution.py
+++ b/solution.py
@@ -97,14 +97,20 @@
         if 2 * bot == cols:
             flat_feats = feats.reshape(-1, 2 * bot)
             payload = jnp.concatenate([flat_feats, away.reshape(-1, cols)], axis=0)
+            if last:
+                payload = away
             if r == min(1, nbits - 1):
                 master, student, payload = lax.optimization_barrier(
                     (teacher_master, student_weight, payload)
                 )
                 master_new = 0.996 * master + 0.004 * student.astype(jnp.float32)
             got = lax.ppermute(payload, "dp", pairs)
-            got_feats = got[: flat_feats.shape[0]].reshape(feats.shape)
-            got_held = got[flat_feats.shape[0]:].reshape(away.shape)
+            if last:
+                got_held = got
+                got_feats = lax.ppermute(feats, "dp", pairs)
+            else:
+                got_feats = got[: flat_feats.shape[0]].reshape(feats.shape)
+                got_held = got[flat_feats.shape[0]:].reshape(away.shape)
         else:
             if r == min(1, nbits - 1):
                 master_new = rebuilt
@@ -112,6 +118,8 @@
         if last:
             got_feats = jnp.transpose(got_feats, cross_rev + [nbits - 1, nbits])
             got_held = jnp.transpose(got_held, cross_rev + [nbits - 1, nbits])
+        if last:
+            halves = [feats.reshape(-1, 2 * bot), got_feats.reshape(-1, 2 * bot)]
         feats = jnp.stack([feats, got_feats])
         held = jnp.stack([keep, got_held], axis=dim)
     feats = feats.reshape(-1, 2 * bot)
@@ -122,17 +130,22 @@
     held = jnp.take(held.reshape(n, 2 * rows, cols), where, axis=0)
     sw = held[:, :rows].reshape(n * rows, cols)
     tw = held[:, rows:].reshape(n * rows, cols)
-    zt, zs = feats[:, :bot], feats[:, bot:]
     c = lax.dynamic_slice_in_dim(center, me * cols, cols)
     t_norm = jnp.sqrt(jnp.sum(jnp.square(tw.astype(jnp.float32)), 0) + 1e-06)
     s_norm = jnp.sqrt(jnp.sum(jnp.square(sw.astype(jnp.float32)), 0) + 1e-06)
-    t_cos = jnp.dot(zt, tw, preferred_element_type=jnp.float32) / t_norm
-    s_cos = jnp.dot(zs, sw, preferred_element_type=jnp.float32) / s_norm
-    t_exp = jnp.exp((t_cos - c) / 0.04)
-    s_exp = jnp.exp(s_cos / 0.1)
-    totals = jnp.stack([jnp.sum(t_exp, 1), jnp.sum(s_exp, 1)])
-    t_exp, s_exp = lax.optimization_barrier((t_exp.astype(jnp.bfloat16), s_exp.astype(jnp.bfloat16)))
-    t_exp, s_exp = t_exp.astype(jnp.float32), s_exp.astype(jnp.float32)
+
+    def passes(part):
+        t_cos = jnp.dot(part[:, :bot], tw, preferred_element_type=jnp.float32) / t_norm
+        s_cos = jnp.dot(part[:, bot:], sw, preferred_element_type=jnp.float32) / s_norm
+        t_exp = jnp.exp((t_cos - c) / 0.04)
+        s_exp = jnp.exp(s_cos / 0.1)
+        sums = jnp.stack([jnp.sum(t_exp, 1), jnp.sum(s_exp, 1)])
+        return sums, jnp.sum(t_cos, 0), t_exp.astype(jnp.bfloat16), s_exp.astype(jnp.bfloat16)
+
+    outs = [passes(part) for part in halves]
+    totals = jnp.concatenate([o[0] for o in outs], axis=1)
+    cos_sum = outs[0][1] + outs[1][1]
+    exps = lax.optimization_barrier([(o[2], o[3]) for o in outs])
     totals, master_new = lax.optimization_barrier((totals, master_new))
     shape = (2,) + (2,) * nbits + (images,)
     for r in range(nbits):
@@ -144,12 +157,17 @@
             got = jnp.flip(got, nbits - r)
         totals = totals + got.reshape(totals.shape)
     totals = exchange_all(totals, "tensor", lax.axis_size("tensor"))
-    t_total, s_total = totals[0][:, None], totals[1][:, None]
-    part_center = 0.5 * c + 0.5 * (jnp.sum(t_cos, 0) / (images * n))
-    dlog = ((s_exp / s_total - t_exp / t_total) / 0.1).astype(jnp.bfloat16)
-    product = lax.dot_general(
-        zs, dlog, (((0,), (0,)), ((), ())), preferred_element_type=jnp.float32
-    )
+    part_center = 0.5 * c + 0.5 * (cos_sum / (images * n))
+    count = halves[0].shape[0]
+    product = 0.0
+    for h, (t_exp, s_exp) in enumerate(exps):
+        t_total = totals[0][h * count: (h + 1) * count, None]
+        s_total = totals[1][h * count: (h + 1) * count, None]
+        dlog = ((s_exp.astype(jnp.float32) / s_total - t_exp.astype(jnp.float32) / t_total) / 0.1)
+        product = product + lax.dot_general(
+            halves[h][:, bot:], dlog.astype(jnp.bfloat16), (((0,), (0,)), ((), ())),
+            preferred_element_type=jnp.float32,
+        )
     wide = sw.astype(jnp.float32)
     scaled = jnp.sum(wide * product, 0) / s_norm / s_norm
     grad = (product - wide * scaled) / s_norm

time: 71.3 us -> 70.2 us (0.985)
  waiting for transfers between devices: 24.9 us -> 22.6 us
  other arithmetic: 6.35 us -> 4.96 us
  matrix products: 8.24 us -> 9.32 us
  local copies, waits for them, and re-layouts: 4.34 us -> 5.29 us
    ppermute x3, waiting for transfers between devices: 18.7 us -> 16.3 us  [feature_plan(): got = lax.ppermute(payload, 'dp', pairs)]
    transpose x0 -> x1, local copies, waits for them, and re-layouts: none -> 1.29 us  [feature_plan(): got_feats = jnp.transpose(got_feats, cross_rev + [nbits - 1, nbits])]
    concatenate x3 -> x2, other arithmetic: 1.24 us -> 0.09 us  [feature_plan(): payload = jnp.concatenate([flat_feats, away.reshape(-1, cols)], axis=0)]
    dot_general x3 -> x6, matrix products: 8.24 us -> 9.32 us  [the longest x2 3.54 us: feature_plan(): lax.dot_general(halves[h][:, bot:], dlog.astype(jnp.bfloat16), (((0,), (0...]
  transfers between devices with their start and end apart: 9 -> 10, of which waited for: 8 -> 7; matrix products, arithmetic and copies ran while one was open for 3% -> 7% of each run, Pallas kernels for 0% -> 0%
where the time goes in v22:
time: 70.2 us; the launch traced here: 69.9 us
  waiting for transfers between devices  22.6 us (32%)
  starting transfers between devices  16 us (23%)
  blocking collectives  10.6 us (15%)
  matrix products  9.32 us (13%)
  local copies, waits for them, and re-layouts  5.29 us (8%)
  other arithmetic  4.96 us (7%)
  between operations  1.15 us (2%)
    ppermute x3, waiting for transfers between devices, feature_plan(): got = lax.ppermute(payload, 'dp', pairs)  16.3 us
    all_to_all x1, blocking collectives, feature_plan(): got = lax.all_to_all(sent, 'dp', 0, 0, tiled=True)  10.6 us
    ppermute x3, starting transfers between devices, exchange_all(): total = total + lax.ppermute(x, axis, [(i, (i + k) % n) for i in range(n)])  6.05 us
    ppermute x3, starting transfers between devices, feature_plan(): got = lax.ppermute(payload, 'dp', pairs)  5.19 us
    ppermute x2, starting transfers between devices, feature_plan(): got = lax.ppermute(totals, 'dp', swap(up[r], down[r])).reshape(shape)  4.16 us
    dot_general x2, matrix products, feature_plan(): lax.dot_general(halves[h][:, bot:], dlog.astype(jnp.bfloat16), (((0,), (0...  3.54 us
    ppermute x2, waiting for transfers between devices, feature_plan(): got = lax.ppermute(totals, 'dp', swap(up[r], down[r])).reshape(shape)  3.45 us
    dot_general x2, matrix products, passes(): jnp.dot(part[:, bot:], sw, preferred_element_type=jnp.float32) / s_norm  3.11 us
  transfers between devices with their start and end apart: 10, of which 7 were waited for; matrix products, arithmetic and copies ran while one was open for 7% of the time, Pallas kernels for 0%

profile of v22, /device:TPU:0, one launch (start us, length us, event | category | flops | bytes accessed | tf_op | source)
XLA Modules:
  0.0 69.9 jit_solution(11678761727753004171)
XLA Ops:
  0.7 1.2 %add_convert_fusion = bf16[32,4096]{1,0:T(8,128)(2,1)S(1)} fusion(bf16[32,4096]{1,0:T(8,128)(2,1)} %param.8, f32[32,4096]{1,0:T(8,128)} %param.7), kind=kLoop, calls=%fused_computation.40 | loop fusion | flops 655360 | bytes 1048576 | tf_op jit(solution)/shard_map/convert_element_type | solution.py:75
  2.4 0.6 gather_fusion
  3.7 3.0 %collective-permute-start = (bf16[512,512]{1,0:T(8,128)(2,1)S(1)}, bf16[512,512]{1,0:T(8,128)(2,1)S(1)}, u32[]{:S(2)}, u32[]{:S(2)}) collective-permute-start(bf16[512,512]{1,0:T(8,128)(2,1)S(1)} %pad_maximum_fusion.3), channel_id=1, source_target_pairs={{0,8},{4,20},{8,0},{12,28},{16,24},{20,4},{24,16},{28,12},{1,9},{5... | collective-permute-start | bytes 1572872 | tf_op jit(solution)/shard_map/ppermute | solution.py:107
  6.7 7.1 %collective-permute-done = bf16[512,512]{1,0:T(8,128)(2,1)S(1)} collective-permute-done((bf16[512,512]{1,0:T(8,128)(2,1)S(1)}, bf16[512,512]{1,0:T(8,128)(2,1)S(1)}, u32[]{:S(2)}, u32[]{:S(2)}) %collective-permute-start) | collective-permute-done | bytes 524320 | tf_op jit(solution)/shard_map/ppermute | solution.py:107
  14.1 2.1 %collective-permute-start.1 = (bf16[768,512]{1,0:T(8,128)(2,1)S(1)}, bf16[768,512]{1,0:T(8,128)(2,1)S(1)}, u32[]{:S(2)}, u32[]{:S(2)}) collective-permute-start(bf16[768,512]{1,0:T(8,128)(2,1)S(1)} %pad_maximum_fusion.1), channel_id=1, source_target_pairs={{0,16},{4,12},{8,24},{12,4},{16,0},{20,28},{24,8},{28,20},{1,17},{... | collective-permute-start | bytes 2359304 | tf_op jit(solution)/shard_map/ppermute | solution.py:107
  16.2 0.8 %dynamic_slice.3 = f32[512]{0:T(512)S(1)} dynamic-slice(f32[4096]{0:T(1024)} %param.11, s32[]{:T(128)S(6)} %select_n.27), dynamic_slice_sizes={512} | dynamic-slice | bytes 4100 | tf_op jit(solution)/shard_map/dynamic_slice | solution.py:133
  16.9 9.2 %collective-permute-done.1 = bf16[768,512]{1,0:T(8,128)(2,1)S(1)} collective-permute-done((bf16[768,512]{1,0:T(8,128)(2,1)S(1)}, bf16[768,512]{1,0:T(8,128)(2,1)S(1)}, u32[]{:S(2)}, u32[]{:S(2)}) %collective-permute-start.1) | collective-permute-done | bytes 786464 | tf_op jit(solution)/shard_map/ppermute | solution.py:107
  26.3 0.9 %multiply_add_fusion = f32[32,4096]{1,0:T(8,128)} fusion(bf16[32,4096]{1,0:T(8,128)(2,1)S(1)} %copy-done, f32[32,4096]{1,0:T(8,128)S(1)} %copy-done.1), kind=kLoop, calls=%fused_computation.37 | loop fusion | flops 524288 | bytes 1310720 | tf_op jit(solution)/shard_map/add | solution.py:106
  27.4 0.6 collective-permute-start.3
  28.0 0.6 gather_fusion.1
  28.9 1.5 %fusion.31 = (bf16[1024,512]{1,0:T(8,128)(2,1)}, f32[1024]{0:T(1024)S(1)}) fusion(f32[512]{0:T(512)S(1)} %add_sqrt_fusion, bf16[256,512]{1,0:T(8,128)(2,1)S(1)} %bitcast.77, bf16[1024,512]{1,0:T(8,128)(2,1)S(1)} %bitcast.67), kind=kOutput, calls=%fused_computation.86 | convolution fusion | flops 270531584 | bytes 1841152 | tf_op jit(solution)/shard_map/dot_general | solution.py:139
  30.4 1.3 %copy.28 = bf16[2,2,256,512]{3,2,1,0:T(8,128)(2,1)S(1)} copy(bf16[2,2,256,512]{3,2,0,1:T(8,128)(2,1)} %bitcast.22) | data formatting | bytes 2097152 | tf_op jit(solution)/shard_map/transpose | solution.py:119
  31.7 1.6 %fusion.30 = (bf16[1024,512]{1,0:T(8,128)(2,1)}, f32[1024]{0:T(1024)S(1)}) fusion(f32[512]{0:T(512)S(1)} %add_sqrt_fusion, bf16[256,512]{1,0:T(8,128)(2,1)S(1)} %bitcast.78, bf16[1024,512]{1,0:T(8,128)(2,1)S(1)} %bitcast.70), kind=kOutput, calls=%fused_computation.85 | convolution fusion | flops 270531584 | bytes 1841152 | tf_op jit(solution)/shard_map/dot_general | solution.py:139
  33.3 0.4 convolution_divide_fusion
  33.8 2.2 %fusion.29 = (f32[512]{0:T(512)S(1)}, f32[1024]{0:T(1024)S(1)}, bf16[1024,512]{1,0:T(8,128)(2,1)}, bf16[1024,512]{1,0:T(8,128)(2,1)}, f32[1024]{0:T(1024)S(1)}, /*index=5*/f32[512]{0:T(512)S(1)}) fusion(f32[512]{0:T(512)S(1)} %dynamic_slice.3, f32[1024,512]{1,0:T(8,128)S(1)} %convolution_divide_fusion, f32[512]{0:T(512)S(1)} %add_sqrt_fusion.1, ...), kind=kOutput, calls=%fused_computation.84 | convolution fusion | flops 274199552 | bytes 4997120 | tf_op jit(solution)/shard_map/dot_general | solution.py:138
  36.0 2.1 %collective-permute-start.4 = (f32[2,2048]{1,0:T(2,128)S(1)}, f32[2,2048]{1,0:T(2,128)S(1)}, u32[]{:S(2)}, u32[]{:S(2)}) collective-permute-start(f32[2,2048]{1,0:T(2,128)S(1)} %maximum_maximum_fusion), channel_id=1, source_target_pairs={{0,8},{4,20},{8,0},{12,28},{16,24},{20,4},{24,16},{28,12},{1,9},{5... | collective-permute-start | bytes 49160 | tf_op jit(solution)/shard_map/ppermute | solution.py:156
  38.1 1.7 %collective-permute-done.4 = f32[2,2048]{1,0:T(2,128)S(1)} collective-permute-done((f32[2,2048]{1,0:T(2,128)S(1)}, f32[2,2048]{1,0:T(2,128)S(1)}, u32[]{:S(2)}, u32[]{:S(2)}) %collective-permute-start.4) | collective-permute-done | bytes 16416 | tf_op jit(solution)/shard_map/ppermute | solution.py:156
  40.0 2.1 %collective-permute-start.5 = (f32[2,2048]{1,0:T(2,128)S(1)}, f32[2,2048]{1,0:T(2,128)S(1)}, u32[]{:S(2)}, u32[]{:S(2)}) collective-permute-start(f32[2,2048]{1,0:T(2,128)S(1)} %add.87), channel_id=1, source_target_pairs={{0,16},{4,12},{8,24},{12,4},{16,0},{20,28},{24,8},{28,20},{1,17},{... | collective-permute-start | bytes 49160 | tf_op jit(solution)/shard_map/ppermute | solution.py:156
  42.1 1.7 %collective-permute-done.5 = f32[2,2048]{1,0:T(2,128)S(1)} collective-permute-done((f32[2,2048]{1,0:T(2,128)S(1)}, f32[2,2048]{1,0:T(2,128)S(1)}, u32[]{:S(2)}, u32[]{:S(2)}) %collective-permute-start.5) | collective-permute-done | bytes 16416 | tf_op jit(solution)/shard_map/ppermute | solution.py:156
  44.0 0.8 %fusion.26 = (bf16[512]{0:T(512)(128)(2,1)S(1)}, bf16[512]{0:T(512)(128)(2,1)S(1)}) fusion(f32[512]{0:T(512)S(1)} %get-tuple-element.24, f32[512]{0:T(512)S(1)} %get-tuple-element.56, f32[4096]{0:T(1024)} %param.11, s32[]{:T(128)S(6)} %select_n.27), kind=kLoop, calls=%fused_computation.81 | loop fusion | flops 4096 | bytes 8196 | tf_op jit(solution)/shard_map/convert_element_type | solution.py:174
  44.8 0.4 collective-permute-done.6
  45.3 2.1 %collective-permute-start.7 = (f32[2,2048]{1,0:T(2,128)S(1)}, f32[2,2048]{1,0:T(2,128)S(1)}, u32[]{:S(2)}, u32[]{:S(2)}) collective-permute-start(f32[2,2048]{1,0:T(2,128)S(1)} %add.89), channel_id=1, source_target_pairs={{0,1},{1,2},{2,3},{3,0},{4,5},{5,6},{6,7},{7,4},{8,9},{9,10},{10,1... | collective-permute-start | bytes 49160 | tf_op jit(solution)/shard_map/ppermute | solution.py:58
  47.4 2.6 %collective-permute-start.8 = (f32[2,2048]{1,0:T(2,128)S(1)}, f32[2,2048]{1,0:T(2,128)S(1)}, u32[]{:S(2)}, u32[]{:S(2)}) collective-permute-start(f32[2,2048]{1,0:T(2,128)S(1)} %add.89), channel_id=1, source_target_pairs={{0,2},{1,3},{2,0},{3,1},{4,6},{5,7},{6,4},{7,5},{8,10},{9,11},{10,... | collective-permute-start | bytes 49160 | tf_op jit(solution)/shard_map/ppermute | solution.py:58
  50.0 1.3 %collective-permute-start.9 = (f32[2,2048]{1,0:T(2,128)S(1)}, f32[2,2048]{1,0:T(2,128)S(1)}, u32[]{:S(2)}, u32[]{:S(2)}) collective-permute-start(f32[2,2048]{1,0:T(2,128)S(1)} %add.89), channel_id=1, source_target_pairs={{0,3},{1,0},{2,1},{3,2},{4,7},{5,4},{6,5},{7,6},{8,11},{9,8},{10,9... | collective-permute-start | bytes 49160 | tf_op jit(solution)/shard_map/ppermute | solution.py:58
  51.4 0.9 %collective-permute-done.8 = f32[2,2048]{1,0:T(2,128)S(1)} collective-permute-done((f32[2,2048]{1,0:T(2,128)S(1)}, f32[2,2048]{1,0:T(2,128)S(1)}, u32[]{:S(2)}, u32[]{:S(2)}) %collective-permute-start.8) | collective-permute-done | bytes 16416 | tf_op jit(solution)/shard_map/ppermute | solution.py:58
  52.3 1.4 %collective-permute-done.9 = f32[2,2048]{1,0:T(2,128)S(1)} collective-permute-done((f32[2,2048]{1,0:T(2,128)S(1)}, f32[2,2048]{1,0:T(2,128)S(1)}, u32[]{:S(2)}, u32[]{:S(2)}) %collective-permute-start.9) | collective-permute-done | bytes 16416 | tf_op jit(solution)/shard_map/ppermute | solution.py:58
  53.8 2.6 %fusion.6 = f32[256,512]{1,0:T(8,128)S(1)} fusion(bf16[1024,512]{1,0:T(8,128)(2,1)} %get-tuple-element.19, bf16[1024,512]{1,0:T(8,128)(2,1)} %get-tuple-element.17, f32[1024]{0:T(1024)S(1)} %bitcast.92, f32[1024]{0:T(1024)S(1)} %bitcast.93, bf16[1024,512]{1,0:T(8,128)(2,1)S(1)} %bitcast.69), kind=kOutput, calls=%fused_computation.19 | convolution fusion | flops 272105472 | bytes 3153920 | tf_op jit(solution)/shard_map/dot_general | solution.py:167
  56.4 1.0 %fusion.7 = (f32[512]{0:T(512)S(1)}, f32[256,512]{1,0:T(8,128)S(1)}) fusion(bf16[8,32,512]{2,1,0:T(8,128)(2,1)S(1)} %get-tuple-element.39, f32[256,512]{1,0:T(8,128)S(1)} %fusion.6, bf16[1024,512]{1,0:T(8,128)(2,1)S(1)} %copy-done.5, bf16[1024,512]{1,0:T(8,128)(2,1)S(1)} %copy-done.4, f32[1024]{0:T(1024)S(1)} %bitcast.89, f32[1024]{0:T(1024)S(1)} %bitcast.88, ...), kind=kOutput, calls=%fused_computation.25 | convolution fusion | flops 272629248 | bytes 3942400 | tf_op jit(solution)/shard_map/dot_general | solution.py:167
  57.5 0.2 reshape.125
  57.7 10.6 %all_to_all.5 = bf16[8,136,128]{2,1,0:T(8,128)(2,1)S(1)} all-to-all(bf16[8,136,128]{2,1,0:T(8,128)(2,1)S(1)} %pad_maximum_fusion.6), channel_id=1, replica_groups=mesh['dp'=8,'tensor'=4] {'dp'}, dimensions={0} | all-to-all | bytes 557056 | tf_op jit(solution)/shard_map/all_to_all | solution.py:185
  68.5 0.8 %copy.37 = f32[4,8,8,512]{3,1,2,0:T(8,128)} copy(f32[4,8,8,512]{3,1,0,2:T(8,128)S(1)} %bitcast.64) | data formatting | bytes 1048576
  69.3 0.6 convert_add_fusion
  (76 shorter events, 2.7 us)
Async XLA Ops:
  0.6 1.5 %copy-start = (bf16[32,4096]{1,0:T(8,128)(2,1)S(1)}, bf16[32,4096]{1,0:T(8,128)(2,1)}, u32[]{:S(2)}) copy-start(bf16[32,4096]{1,0:T(8,128)(2,1)} %param.8) | copy-start | bytes 786436
  2.3 0.9 %copy-start.3 = (bf16[256,256]{1,0:T(8,128)(2,1)S(1)}, bf16[256,256]{1,0:T(8,128)(2,1)}, u32[]{:S(2)}) copy-start(bf16[256,256]{1,0:T(8,128)(2,1)} %param.10) | copy-start | bytes 393220
  2.3 1.0 %copy-start.2 = (bf16[256,256]{1,0:T(8,128)(2,1)S(1)}, bf16[256,256]{1,0:T(8,128)(2,1)}, u32[]{:S(2)}) copy-start(bf16[256,256]{1,0:T(8,128)(2,1)} %param.9) | copy-start | bytes 393220
  3.7 10.2 %collective-permute-start = (bf16[512,512]{1,0:T(8,128)(2,1)S(1)}, bf16[512,512]{1,0:T(8,128)(2,1)S(1)}, u32[]{:S(2)}, u32[]{:S(2)}) collective-permute-start(bf16[512,512]{1,0:T(8,128)(2,1)S(1)} %pad_maximum_fusion.3), channel_id=1, source_target_pairs={{0,8},{4,20},{8,0},{12,28},{16,24},{20,4},{24,16},{28,12},{1,9},{5... | collective-permute-start | bytes 1572872 | tf_op jit(solution)/shard_map/ppermute | solution.py:107
  14.0 12.4 %copy-start.1 = (f32[32,4096]{1,0:T(8,128)S(1)}, f32[32,4096]{1,0:T(8,128)}, u32[]{:S(2)}) copy-start(f32[32,4096]{1,0:T(8,128)} %param.7) | copy-start | bytes 1572868
  14.1 12.1 %collective-permute-start.1 = (bf16[768,512]{1,0:T(8,128)(2,1)S(1)}, bf16[768,512]{1,0:T(8,128)(2,1)S(1)}, u32[]{:S(2)}, u32[]{:S(2)}) collective-permute-start(bf16[768,512]{1,0:T(8,128)(2,1)S(1)} %pad_maximum_fusion.1), channel_id=1, source_target_pairs={{0,16},{4,12},{8,24},{12,4},{16,0},{20,28},{24,8},{28,20},{1,17},{... | collective-permute-start | bytes 2359304 | tf_op jit(solution)/shard_map/ppermute | solution.py:107
  26.3 1.7 %collective-permute-start.2 = (bf16[2,2,64,512]{3,2,1,0:T(8,128)(2,1)S(1)}, bf16[2,2,64,512]{3,2,1,0:T(8,128)(2,1)S(1)}, u32[]{:S(2)}, u32[]{:S(2)}) collective-permute-start(bf16[2,2,64,512]{3,2,1,0:T(8,128)(2,1)S(1)} %get-tuple-element.43), channel_id=1, source_target_pairs={{0,4},{4,0},{8,12},{12,8},{16,20},{20,16},{24,28},{28,24},{1,5},{5... | collective-permute-start | bytes 786440 | tf_op jit(solution)/shard_map/ppermute | solution.py:107
  27.4 3.1 %collective-permute-start.3 = (bf16[2,2,256,512]{3,2,1,0:T(8,128)(2,1)S(1)}, bf16[2,2,256,512]{3,2,1,0:T(8,128)(2,1)}, u32[]{:S(2)}, u32[]{:S(2)}) collective-permute-start(bf16[2,2,256,512]{3,2,1,0:T(8,128)(2,1)S(1)} %pad_maximum_fusion), channel_id=1, source_target_pairs={{0,4},{4,0},{8,12},{12,8},{16,20},{20,16},{24,28},{28,24},{1,5},{5... | collective-permute-start | bytes 3145736 | tf_op jit(solution)/shard_map/ppermute | solution.py:110
  36.0 3.8 %collective-permute-start.4 = (f32[2,2048]{1,0:T(2,128)S(1)}, f32[2,2048]{1,0:T(2,128)S(1)}, u32[]{:S(2)}, u32[]{:S(2)}) collective-permute-start(f32[2,2048]{1,0:T(2,128)S(1)} %maximum_maximum_fusion), channel_id=1, source_target_pairs={{0,8},{4,20},{8,0},{12,28},{16,24},{20,4},{24,16},{28,12},{1,9},{5... | collective-permute-start | bytes 49160 | tf_op jit(solution)/shard_map/ppermute | solution.py:156
  40.0 3.8 %collective-permute-start.5 = (f32[2,2048]{1,0:T(2,128)S(1)}, f32[2,2048]{1,0:T(2,128)S(1)}, u32[]{:S(2)}, u32[]{:S(2)}) collective-permute-start(f32[2,2048]{1,0:T(2,128)S(1)} %add.87), channel_id=1, source_target_pairs={{0,16},{4,12},{8,24},{12,4},{16,0},{20,28},{24,8},{28,20},{1,17},{... | collective-permute-start | bytes 49160 | tf_op jit(solution)/shard_map/ppermute | solution.py:156
  43.9 1.2 %collective-permute-start.6 = (f32[2,2048]{1,0:T(2,128)S(1)}, f32[2,2048]{1,0:T(2,128)S(1)}, u32[]{:S(2)}, u32[]{:S(2)}) collective-permute-start(f32[2,2048]{1,0:T(2,128)S(1)} %add.88), channel_id=1, source_target_pairs={{0,4},{4,0},{8,12},{12,8},{16,20},{20,16},{24,28},{28,24},{1,5},{5... | collective-permute-start | bytes 49160 | tf_op jit(solution)/shard_map/ppermute | solution.py:153
  45.3 6.1 %collective-permute-start.7 = (f32[2,2048]{1,0:T(2,128)S(1)}, f32[2,2048]{1,0:T(2,128)S(1)}, u32[]{:S(2)}, u32[]{:S(2)}) collective-permute-start(f32[2,2048]{1,0:T(2,128)S(1)} %add.89), channel_id=1, source_target_pairs={{0,1},{1,2},{2,3},{3,0},{4,5},{5,6},{6,7},{7,4},{8,9},{9,10},{10,1... | collective-permute-start | bytes 49160 | tf_op jit(solution)/shard_map/ppermute | solution.py:58
  47.4 4.9 %collective-permute-start.8 = (f32[2,2048]{1,0:T(2,128)S(1)}, f32[2,2048]{1,0:T(2,128)S(1)}, u32[]{:S(2)}, u32[]{:S(2)}) collective-permute-start(f32[2,2048]{1,0:T(2,128)S(1)} %add.89), channel_id=1, source_target_pairs={{0,2},{1,3},{2,0},{3,1},{4,6},{5,7},{6,4},{7,5},{8,10},{9,11},{10,... | collective-permute-start | bytes 49160 | tf_op jit(solution)/shard_map/ppermute | solution.py:58
  50.0 3.7 %collective-permute-start.9 = (f32[2,2048]{1,0:T(2,128)S(1)}, f32[2,2048]{1,0:T(2,128)S(1)}, u32[]{:S(2)}, u32[]{:S(2)}) collective-permute-start(f32[2,2048]{1,0:T(2,128)S(1)} %add.89), channel_id=1, source_target_pairs={{0,3},{1,0},{2,1},{3,2},{4,7},{5,4},{6,5},{7,6},{8,11},{9,8},{10,9... | collective-permute-start | bytes 49160 | tf_op jit(solution)/shard_map/ppermute | solution.py:58
  53.8 2.6 %copy-start.4 = (bf16[1024,512]{1,0:T(8,128)(2,1)S(1)}, bf16[1024,512]{1,0:T(8,128)(2,1)}, u32[]{:S(2)}) copy-start(bf16[1024,512]{1,0:T(8,128)(2,1)} %get-tuple-element.20) | copy-start | bytes 3145732
  53.8 2.6 %copy-start.5 = (bf16[1024,512]{1,0:T(8,128)(2,1)S(1)}, bf16[1024,512]{1,0:T(8,128)(2,1)}, u32[]{:S(2)}) copy-start(bf16[1024,512]{1,0:T(8,128)(2,1)} %get-tuple-element.21) | copy-start | bytes 3145732

commit v23 on v22

--- a/solution.py
+++ b/solution.py
@@ -107,7 +107,8 @@
             got = lax.ppermute(payload, "dp", pairs)
             if last:
                 got_held = got
-                got_feats = lax.ppermute(feats, "dp", pairs)
+                pieces = [lax.ppermute(feats[k], "dp", pairs) for k in range(2)]
+                got_feats = jnp.stack(pieces)
             else:
                 got_feats = got[: flat_feats.shape[0]].reshape(feats.shape)
                 got_held = got[flat_feats.shape[0]:].reshape(away.shape)
@@ -142,9 +143,16 @@
         sums = jnp.stack([jnp.sum(t_exp, 1), jnp.sum(s_exp, 1)])
         return sums, jnp.sum(t_cos, 0), t_exp.astype(jnp.bfloat16), s_exp.astype(jnp.bfloat16)
 
+    split = nbits == 3 and 2 * bot == cols
+    if split:
+        halves = [halves[0]] + [p.reshape(-1, 2 * bot) for p in pieces]
     outs = [passes(part) for part in halves]
-    totals = jnp.concatenate([o[0] for o in outs], axis=1)
-    cos_sum = outs[0][1] + outs[1][1]
+    if split:
+        remote = jnp.stack([o[0].reshape(2, 2, images) for o in outs[1:]], axis=2)
+        totals = jnp.concatenate([outs[0][0], remote.reshape(2, -1)], axis=1)
+    else:
+        totals = jnp.concatenate([o[0] for o in outs], axis=1)
+    cos_sum = sum(o[1] for o in outs)
     exps = lax.optimization_barrier([(o[2], o[3]) for o in outs])
     totals, master_new = lax.optimization_barrier((totals, master_new))
     shape = (2,) + (2,) * nbits + (images,)
@@ -159,10 +167,15 @@
     totals = exchange_all(totals, "tensor", lax.axis_size("tensor"))
     part_center = 0.5 * c + 0.5 * (cos_sum / (images * n))
     count = halves[0].shape[0]
+    if split:
+        remote = totals[:, count:].reshape(2, 2, 2, images)
+        part_totals = [totals[:, :count]] + [remote[:, :, k].reshape(2, -1) for k in range(2)]
+    else:
+        part_totals = [totals[:, h * count: (h + 1) * count] for h in range(len(exps))]
     product = 0.0
     for h, (t_exp, s_exp) in enumerate(exps):
-        t_total = totals[0][h * count: (h + 1) * count, None]
-        s_total = totals[1][h * count: (h + 1) * count, None]
+        t_total = part_totals[h][0][:, None]
+        s_total = part_totals[h][1][:, None]
         dlog = ((s_exp.astype(jnp.float32) / s_total - t_exp.astype(jnp.float32) / t_total) / 0.1)
         product = product + lax.dot_general(
             halves[h][:, bot:], dlog.astype(jnp.bfloat16), (((0,), (0,)), ((), ())),

time: 70.2 us -> 78.3 us (1.12)
  matrix products: 9.32 us -> 16.1 us
  waiting for transfers between devices: 22.6 us -> 24.7 us
  starting transfers between devices: 16 us -> 14.6 us
    dot_general x2 -> x3, matrix products: 2.66 us -> 5.44 us  [passes(): jnp.dot(part[:, :bot], tw, preferred_element_type=jnp.float32) / t_norm]
    ppermute x3, waiting for transfers between devices: 2.36 us -> 4.51 us  [exchange_all(): total = total + lax.ppermute(x, axis, [(i, (i + k) % n) for i in range(n)])]
    dot_general x2 -> x3, matrix products: 3.54 us -> 5.64 us  [feature_plan(): lax.dot_general(halves[h][:, bot:], dlog.astype(jnp.bfloat16), (((0,), (0...]
    dot_general x2 -> x3, matrix products: 3.11 us -> 5.01 us  [passes(): jnp.dot(part[:, bot:], sw, preferred_element_type=jnp.float32) / s_norm]
    unnamed x15 -> x17, local copies, waits for them, and re-layouts: 1.1 us -> 2.61 us
    transpose x1 -> x0, local copies, waits for them, and re-layouts: 1.29 us -> none  [feature_plan(): got_feats = jnp.transpose(got_feats, cross_rev + [nbits - 1, nbits])]
    ppermute x3, starting transfers between devices: 6.05 us -> 5.17 us  [exchange_all(): total = total + lax.ppermute(x, axis, [(i, (i + k) % n) for i in range(n)])]
  transfers between devices with their start and end apart: 10 -> 11, of which waited for: 7 -> 7; matrix products, arithmetic and copies ran while one was open for 7% -> 12% of each run, Pallas kernels for 0% -> 0%
where the time goes in v23:
time: 78.3 us; the launch traced here: 77.8 us
  waiting for transfers between devices  24.7 us (32%)
  matrix products  16.1 us (21%)
  starting transfers between devices  14.6 us (19%)
  blocking collectives  10.6 us (14%)
  local copies, waits for them, and re-layouts  5.55 us (7%)
  other arithmetic  4.97 us (6%)
  between operations  1.21 us (2%)
    ppermute x3, waiting for transfers between devices, feature_plan(): got = lax.ppermute(payload, 'dp', pairs)  16.3 us
    all_to_all x1, blocking collectives, feature_plan(): got = lax.all_to_all(sent, 'dp', 0, 0, tiled=True)  10.6 us
    dot_general x3, matrix products, feature_plan(): lax.dot_general(halves[h][:, bot:], dlog.astype(jnp.bfloat16), (((0,), (0...  5.64 us
    dot_general x3, matrix products, passes(): jnp.dot(part[:, :bot], tw, preferred_element_type=jnp.float32) / t_norm  5.44 us
    ppermute x3, starting transfers between devices, feature_plan(): got = lax.ppermute(payload, 'dp', pairs)  5.19 us
    ppermute x3, starting transfers between devices, exchange_all(): total = total + lax.ppermute(x, axis, [(i, (i + k) % n) for i in range(n)])  5.17 us
    dot_general x3, matrix products, passes(): jnp.dot(part[:, bot:], sw, preferred_element_type=jnp.float32) / s_norm  5.01 us
    ppermute x3, waiting for transfers between devices, exchange_all(): total = total + lax.ppermute(x, axis, [(i, (i + k) % n) for i in range(n)])  4.51 us
  transfers between devices with their start and end apart: 11, of which 7 were waited for; matrix products, arithmetic and copies ran while one was open for 12% of the time, Pallas kernels for 0%

profile of v23, /device:TPU:0, one launch (start us, length us, event | category | flops | bytes accessed | tf_op | source)
XLA Modules:
  0.0 77.8 jit_solution(391183042567380888)
XLA Ops:
  0.7 1.2 %add_convert_fusion = bf16[32,4096]{1,0:T(8,128)(2,1)S(1)} fusion(bf16[32,4096]{1,0:T(8,128)(2,1)} %param.8, f32[32,4096]{1,0:T(8,128)} %param.7), kind=kLoop, calls=%fused_computation.56 | loop fusion | flops 655360 | bytes 1048576 | tf_op jit(solution)/shard_map/convert_element_type | solution.py:75
  2.4 0.6 gather_fusion
  3.2 0.7 copy-done.3
  4.3 3.0 %collective-permute-start = (bf16[512,512]{1,0:T(8,128)(2,1)S(1)}, bf16[512,512]{1,0:T(8,128)(2,1)S(1)}, u32[]{:S(2)}, u32[]{:S(2)}) collective-permute-start(bf16[512,512]{1,0:T(8,128)(2,1)S(1)} %pad_maximum_fusion.3), channel_id=1, source_target_pairs={{0,8},{4,20},{8,0},{12,28},{16,24},{20,4},{24,16},{28,12},{1,9},{5... | collective-permute-start | bytes 1572872 | tf_op jit(solution)/shard_map/ppermute | solution.py:107
  7.4 7.1 %collective-permute-done = bf16[512,512]{1,0:T(8,128)(2,1)S(1)} collective-permute-done((bf16[512,512]{1,0:T(8,128)(2,1)S(1)}, bf16[512,512]{1,0:T(8,128)(2,1)S(1)}, u32[]{:S(2)}, u32[]{:S(2)}) %collective-permute-start) | collective-permute-done | bytes 524320 | tf_op jit(solution)/shard_map/ppermute | solution.py:107
  14.7 2.1 %collective-permute-start.1 = (bf16[768,512]{1,0:T(8,128)(2,1)S(1)}, bf16[768,512]{1,0:T(8,128)(2,1)S(1)}, u32[]{:S(2)}, u32[]{:S(2)}) collective-permute-start(bf16[768,512]{1,0:T(8,128)(2,1)S(1)} %pad_maximum_fusion.1), channel_id=1, source_target_pairs={{0,16},{4,12},{8,24},{12,4},{16,0},{20,28},{24,8},{28,20},{1,17},{... | collective-permute-start | bytes 2359304 | tf_op jit(solution)/shard_map/ppermute | solution.py:107
  16.8 0.8 dynamic_slice.3
  17.6 9.2 %collective-permute-done.1 = bf16[768,512]{1,0:T(8,128)(2,1)S(1)} collective-permute-done((bf16[768,512]{1,0:T(8,128)(2,1)S(1)}, bf16[768,512]{1,0:T(8,128)(2,1)S(1)}, u32[]{:S(2)}, u32[]{:S(2)}) %collective-permute-start.1) | collective-permute-done | bytes 786464 | tf_op jit(solution)/shard_map/ppermute | solution.py:107
  27.0 0.9 %copy-done.1 = f32[32,4096]{1,0:T(8,128)S(1)} copy-done((f32[32,4096]{1,0:T(8,128)S(1)}, f32[32,4096]{1,0:T(8,128)}, u32[]{:S(2)}) %copy-start.1) | copy-done | bytes 524312
  27.9 0.9 %multiply_add_fusion = f32[32,4096]{1,0:T(8,128)} fusion(bf16[32,4096]{1,0:T(8,128)(2,1)S(1)} %copy-done, f32[32,4096]{1,0:T(8,128)S(1)} %copy-done.1), kind=kLoop, calls=%fused_computation.51 | loop fusion | flops 524288 | bytes 1310720 | tf_op jit(solution)/shard_map/add | solution.py:106
  29.0 0.6 gather_fusion.1
  29.9 1.5 %fusion.46 = (bf16[1024,512]{1,0:T(8,128)(2,1)}, f32[1024]{0:T(1024)S(1)}) fusion(f32[512]{0:T(512)S(1)} %add_sqrt_fusion, bf16[256,512]{1,0:T(8,128)(2,1)S(1)} %bitcast.82, bf16[1024,512]{1,0:T(8,128)(2,1)S(1)} %bitcast.75), kind=kOutput, calls=%fused_computation.107 | convolution fusion | flops 270531584 | bytes 1841152 | tf_op jit(solution)/shard_map/dot_general | solution.py:140
  31.5 2.1 %fusion.48 = (bf16[512,512]{1,0:T(8,128)(2,1)}, f32[512]{0:T(512)S(1)}) fusion(f32[512]{0:T(512)S(1)} %add_sqrt_fusion, bf16[256,512]{1,0:T(8,128)(2,1)S(1)} %bitcast.83, bf16[512,512]{1,0:T(8,128)(2,1)} %bitcast.22), kind=kOutput, calls=%fused_computation.109 | convolution fusion | flops 135265792 | bytes 1052672 | tf_op jit(solution)/shard_map/dot_general | solution.py:140
  33.6 1.7 %fusion.43 = (f32[512]{0:T(512)S(1)}, f32[1024]{0:T(1024)S(1)}, bf16[1024,512]{1,0:T(8,128)(2,1)}) fusion(f32[512]{0:T(512)S(1)} %dynamic_slice.3, f32[512]{0:T(512)S(1)} %add_sqrt_fusion.1, bf16[256,512]{1,0:T(8,128)(2,1)S(1)} %bitcast.87, bf16[1024,512]{1,0:T(8,128)(2,1)S(1)} %bitcast.76), kind=kOutput, calls=%fused_computation.104 | convolution fusion | flops 271579648 | bytes 1845248 | tf_op jit(solution)/shard_map/dot_general | solution.py:139
  35.3 1.2 %convolution_divide_fusion.2 = f32[512,512]{1,0:T(8,128)S(1)} fusion(bf16[256,512]{1,0:T(8,128)(2,1)S(1)} %bitcast.88, f32[512]{0:T(512)S(1)} %add_sqrt_fusion.1, bf16[512,512]{1,0:T(8,128)(2,1)} %bitcast.26), kind=kOutput, calls=%fused_computation.11 | convolution fusion | flops 134479872 | bytes 1574912 | tf_op jit(solution)/shard_map/dot_general | solution.py:139
  36.6 1.4 %fusion.47 = (bf16[512,512]{1,0:T(8,128)(2,1)S(1)}, f32[512]{0:T(512)S(1)}) fusion(f32[512]{0:T(512)S(1)} %add_sqrt_fusion, bf16[256,512]{1,0:T(8,128)(2,1)S(1)} %bitcast.84, bf16[512,512]{1,0:T(8,128)(2,1)} %bitcast.26), kind=kOutput, calls=%fused_computation.108 | convolution fusion | flops 135265792 | bytes 1052672 | tf_op jit(solution)/shard_map/dot_general | solution.py:140
  37.9 2.5 %fusion.44 = (f32[512]{0:T(512)S(1)}, f32[512]{0:T(512)S(1)}, bf16[512,512]{1,0:T(8,128)(2,1)}, bf16[512,512]{1,0:T(8,128)(2,1)}, f32[512]{0:T(512)S(1)}, /*index=5*/f32[512]{0:T(512)S(1)}) fusion(f32[512]{0:T(512)S(1)} %dynamic_slice.3, f32[512,512]{1,0:T(8,128)S(1)} %convolution_divide_fusion.2, f32[512]{0:T(512)S(1)} %add_sqrt_fusion.1, ...), kind=kOutput, calls=%fused_computation.105 | convolution fusion | flops 137099264 | bytes 2633728 | tf_op jit(solution)/shard_map/dot_general | solution.py:139
  40.5 2.0 %collective-permute-start.5 = (f32[2,2048]{1,0:T(2,128)S(1)}, f32[2,2048]{1,0:T(2,128)S(1)}, u32[]{:S(2)}, u32[]{:S(2)}) collective-permute-start(f32[2,2048]{1,0:T(2,128)S(1)} %pad_maximum_fusion.7), channel_id=1, source_target_pairs={{0,8},{4,20},{8,0},{12,28},{16,24},{20,4},{24,16},{28,12},{1,9},{5... | collective-permute-start | bytes 49160 | tf_op jit(solution)/shard_map/ppermute | solution.py:164
  42.5 1.8 %collective-permute-done.5 = f32[2,2048]{1,0:T(2,128)S(1)} collective-permute-done((f32[2,2048]{1,0:T(2,128)S(1)}, f32[2,2048]{1,0:T(2,128)S(1)}, u32[]{:S(2)}, u32[]{:S(2)}) %collective-permute-start.5) | collective-permute-done | bytes 16416 | tf_op jit(solution)/shard_map/ppermute | solution.py:164
  44.5 2.1 %collective-permute-start.6 = (f32[2,2048]{1,0:T(2,128)S(1)}, f32[2,2048]{1,0:T(2,128)S(1)}, u32[]{:S(2)}, u32[]{:S(2)}) collective-permute-start(f32[2,2048]{1,0:T(2,128)S(1)} %add.93), channel_id=1, source_target_pairs={{0,16},{4,12},{8,24},{12,4},{16,0},{20,28},{24,8},{28,20},{1,17},{... | collective-permute-start | bytes 49160 | tf_op jit(solution)/shard_map/ppermute | solution.py:164
  46.6 1.7 %collective-permute-done.6 = f32[2,2048]{1,0:T(2,128)S(1)} collective-permute-done((f32[2,2048]{1,0:T(2,128)S(1)}, f32[2,2048]{1,0:T(2,128)S(1)}, u32[]{:S(2)}, u32[]{:S(2)}) %collective-permute-start.6) | collective-permute-done | bytes 16416 | tf_op jit(solution)/shard_map/ppermute | solution.py:164
  48.5 0.8 subtract_convert_fusion
  49.7 4.2 %collective-permute-start.10 = (f32[2,2048]{1,0:T(2,128)S(1)}, f32[2,2048]{1,0:T(2,128)S(1)}, u32[]{:S(2)}, u32[]{:S(2)}) collective-permute-start(f32[2,2048]{1,0:T(2,128)S(1)} %add.95), channel_id=1, source_target_pairs={{0,3},{1,0},{2,1},{3,2},{4,7},{5,4},{6,5},{7,6},{8,11},{9,8},{10,9... | collective-permute-start | bytes 49160 | tf_op jit(solution)/shard_map/ppermute | solution.py:58
  53.9 1.0 %collective-permute-start.9 = (f32[2,2048]{1,0:T(2,128)S(1)}, f32[2,2048]{1,0:T(2,128)S(1)}, u32[]{:S(2)}, u32[]{:S(2)}) collective-permute-start(f32[2,2048]{1,0:T(2,128)S(1)} %add.95), channel_id=1, source_target_pairs={{0,2},{1,3},{2,0},{3,1},{4,6},{5,7},{6,4},{7,5},{8,10},{9,11},{10,... | collective-permute-start | bytes 49160 | tf_op jit(solution)/shard_map/ppermute | solution.py:58
  54.9 0.4 collective-permute-done.10
  55.3 4.1 %collective-permute-done.8 = f32[2,2048]{1,0:T(2,128)S(1)} collective-permute-done((f32[2,2048]{1,0:T(2,128)S(1)}, f32[2,2048]{1,0:T(2,128)S(1)}, u32[]{:S(2)}, u32[]{:S(2)}) %collective-permute-start.8) | collective-permute-done | bytes 16416 | tf_op jit(solution)/shard_map/ppermute | solution.py:58
  59.6 2.5 %fusion.8 = f32[256,512]{1,0:T(8,128)S(1)} fusion(bf16[1024,512]{1,0:T(8,128)(2,1)} %get-tuple-element.21, bf16[1024,512]{1,0:T(8,128)(2,1)} %get-tuple-element.19, f32[1024]{0:T(1024)S(1)} %bitcast.94, f32[1024]{0:T(1024)S(1)} %bitcast.93, bf16[1024,512]{1,0:T(8,128)(2,1)S(1)} %bitcast.77), kind=kOutput, calls=%fused_computation.26 | convolution fusion | flops 272105472 | bytes 3153920 | tf_op jit(solution)/shard_map/dot_general | solution.py:180
  62.1 1.6 %convolution_add_fusion.1 = f32[256,512]{1,0:T(8,128)S(1)} fusion(f32[256,512]{1,0:T(8,128)S(1)} %fusion.8, bf16[512,512]{1,0:T(8,128)(2,1)S(1)} %copy-done.6, bf16[512,512]{1,0:T(8,128)(2,1)S(1)} %copy-done.4, f32[512]{0:T(512)S(1)} %bitcast.100, f32[512]{0:T(512)S(1)} %bitcast.101, bf16[512,512]{1,0:T(8,128)(2,1)} %bitcast.22), kind=kOutput, calls=%fused_computation.17 | convolution fusion | flops 136183808 | bytes 2363392 | tf_op jit(solution)/shard_map/dot_general | solution.py:180
  63.7 1.5 %fusion.13 = (f32[512]{0:T(512)S(1)}, f32[256,512]{1,0:T(8,128)S(1)}) fusion(bf16[8,32,512]{2,1,0:T(8,128)(2,1)S(1)} %get-tuple-element.52, f32[256,512]{1,0:T(8,128)S(1)} %convolution_add_fusion.1, bf16[512,512]{1,0:T(8,128)(2,1)S(1)} %copy-done.5, bf16[512,512]{1,0:T(8,128)(2,1)S(1)} %get-tuple-element.24, f32[512]{0:T(512)S(1)} %bitcast.99, ...), kind=kOutput, calls=%fused_computation.36 | convolution fusion | flops 136576512 | bytes 2627584 | tf_op jit(solution)/shard_map/dot_general | solution.py:180
  65.6 10.6 %all_to_all.5 = bf16[8,136,128]{2,1,0:T(8,128)(2,1)S(1)} all-to-all(bf16[8,136,128]{2,1,0:T(8,128)(2,1)S(1)} %pad_maximum_fusion.6), channel_id=1, replica_groups=mesh['dp'=8,'tensor'=4] {'dp'}, dimensions={0} | all-to-all | bytes 557056 | tf_op jit(solution)/shard_map/all_to_all | solution.py:198
  76.4 0.8 %copy.39 = f32[4,8,8,512]{3,1,2,0:T(8,128)} copy(f32[4,8,8,512]{3,1,0,2:T(8,128)S(1)} %bitcast.71) | data formatting | bytes 1048576
  77.2 0.6 convert_add_fusion
  (87 shorter events, 3.3 us)
Async XLA Ops:
  0.7 1.4 %copy-start = (bf16[32,4096]{1,0:T(8,128)(2,1)S(1)}, bf16[32,4096]{1,0:T(8,128)(2,1)}, u32[]{:S(2)}) copy-start(bf16[32,4096]{1,0:T(8,128)(2,1)} %param.8) | copy-start | bytes 786436
  3.0 0.9 %copy-start.3 = (bf16[256,256]{1,0:T(8,128)(2,1)S(1)}, bf16[256,256]{1,0:T(8,128)(2,1)}, u32[]{:S(2)}) copy-start(bf16[256,256]{1,0:T(8,128)(2,1)} %param.10) | copy-start | bytes 393220
  3.0 1.0 %copy-start.2 = (bf16[256,256]{1,0:T(8,128)(2,1)S(1)}, bf16[256,256]{1,0:T(8,128)(2,1)}, u32[]{:S(2)}) copy-start(bf16[256,256]{1,0:T(8,128)(2,1)} %param.9) | copy-start | bytes 393220
  4.3 10.2 %collective-permute-start = (bf16[512,512]{1,0:T(8,128)(2,1)S(1)}, bf16[512,512]{1,0:T(8,128)(2,1)S(1)}, u32[]{:S(2)}, u32[]{:S(2)}) collective-permute-start(bf16[512,512]{1,0:T(8,128)(2,1)S(1)} %pad_maximum_fusion.3), channel_id=1, source_target_pairs={{0,8},{4,20},{8,0},{12,28},{16,24},{20,4},{24,16},{28,12},{1,9},{5... | collective-permute-start | bytes 1572872 | tf_op jit(solution)/shard_map/ppermute | solution.py:107
  14.7 12.1 %collective-permute-start.1 = (bf16[768,512]{1,0:T(8,128)(2,1)S(1)}, bf16[768,512]{1,0:T(8,128)(2,1)S(1)}, u32[]{:S(2)}, u32[]{:S(2)}) collective-permute-start(bf16[768,512]{1,0:T(8,128)(2,1)S(1)} %pad_maximum_fusion.1), channel_id=1, source_target_pairs={{0,16},{4,12},{8,24},{12,4},{16,0},{20,28},{24,8},{28,20},{1,17},{... | collective-permute-start | bytes 2359304 | tf_op jit(solution)/shard_map/ppermute | solution.py:107
  17.6 13.9 %collective-permute-start.3 = (bf16[2,256,512]{2,1,0:T(8,128)(2,1)S(1)}, bf16[2,256,512]{2,1,0:T(8,128)(2,1)}, u32[]{:S(2)}, u32[]{:S(2)}) collective-permute-start(bf16[2,256,512]{2,1,0:T(8,128)(2,1)S(1)} %get-tuple-element.50), channel_id=1, source_target_pairs={{0,4},{4,0},{8,12},{12,8},{16,20},{20,16},{24,28},{28,24},{1,5},{5... | collective-permute-start | bytes 1572872 | tf_op jit(solution)/shard_map/ppermute | solution.py:110
  26.8 1.0 %copy-start.1 = (f32[32,4096]{1,0:T(8,128)S(1)}, f32[32,4096]{1,0:T(8,128)}, u32[]{:S(2)}) copy-start(f32[32,4096]{1,0:T(8,128)} %param.7) | copy-start | bytes 1572868
  26.9 2.0 %collective-permute-start.2 = (bf16[2,2,64,512]{3,2,1,0:T(8,128)(2,1)S(1)}, bf16[2,2,64,512]{3,2,1,0:T(8,128)(2,1)S(1)}, u32[]{:S(2)}, u32[]{:S(2)}) collective-permute-start(bf16[2,2,64,512]{3,2,1,0:T(8,128)(2,1)S(1)} %get-tuple-element.54), channel_id=1, source_target_pairs={{0,4},{4,0},{8,12},{12,8},{16,20},{20,16},{24,28},{28,24},{1,5},{5... | collective-permute-start | bytes 786440 | tf_op jit(solution)/shard_map/ppermute | solution.py:107
  28.8 6.6 %collective-permute-start.4 = (bf16[2,256,512]{2,1,0:T(8,128)(2,1)S(1)}, bf16[2,256,512]{2,1,0:T(8,128)(2,1)}, u32[]{:S(2)}, u32[]{:S(2)}) collective-permute-start(bf16[2,256,512]{2,1,0:T(8,128)(2,1)S(1)} %bitcast.72), channel_id=1, source_target_pairs={{0,4},{4,0},{8,12},{12,8},{16,20},{20,16},{24,28},{28,24},{1,5},{5... | collective-permute-start | bytes 1572872 | tf_op jit(solution)/shard_map/ppermute | solution.py:110
  40.5 3.8 %collective-permute-start.5 = (f32[2,2048]{1,0:T(2,128)S(1)}, f32[2,2048]{1,0:T(2,128)S(1)}, u32[]{:S(2)}, u32[]{:S(2)}) collective-permute-start(f32[2,2048]{1,0:T(2,128)S(1)} %pad_maximum_fusion.7), channel_id=1, source_target_pairs={{0,8},{4,20},{8,0},{12,28},{16,24},{20,4},{24,16},{28,12},{1,9},{5... | collective-permute-start | bytes 49160 | tf_op jit(solution)/shard_map/ppermute | solution.py:164
  44.5 3.8 %collective-permute-start.6 = (f32[2,2048]{1,0:T(2,128)S(1)}, f32[2,2048]{1,0:T(2,128)S(1)}, u32[]{:S(2)}, u32[]{:S(2)}) collective-permute-start(f32[2,2048]{1,0:T(2,128)S(1)} %add.93), channel_id=1, source_target_pairs={{0,16},{4,12},{8,24},{12,4},{16,0},{20,28},{24,8},{28,20},{1,17},{... | collective-permute-start | bytes 49160 | tf_op jit(solution)/shard_map/ppermute | solution.py:164
  48.4 1.2 %collective-permute-start.7 = (f32[2,2048]{1,0:T(2,128)S(1)}, f32[2,2048]{1,0:T(2,128)S(1)}, u32[]{:S(2)}, u32[]{:S(2)}) collective-permute-start(f32[2,2048]{1,0:T(2,128)S(1)} %add.94), channel_id=1, source_target_pairs={{0,4},{4,0},{8,12},{12,8},{16,20},{20,16},{24,28},{28,24},{1,5},{5... | collective-permute-start | bytes 49160 | tf_op jit(solution)/shard_map/ppermute | solution.py:161
  49.7 5.6 %collective-permute-start.10 = (f32[2,2048]{1,0:T(2,128)S(1)}, f32[2,2048]{1,0:T(2,128)S(1)}, u32[]{:S(2)}, u32[]{:S(2)}) collective-permute-start(f32[2,2048]{1,0:T(2,128)S(1)} %add.95), channel_id=1, source_target_pairs={{0,3},{1,0},{2,1},{3,2},{4,7},{5,4},{6,5},{7,6},{8,11},{9,8},{10,9... | collective-permute-start | bytes 49160 | tf_op jit(solution)/shard_map/ppermute | solution.py:58
  53.9 5.5 %collective-permute-start.8 = (f32[2,2048]{1,0:T(2,128)S(1)}, f32[2,2048]{1,0:T(2,128)S(1)}, u32[]{:S(2)}, u32[]{:S(2)}) collective-permute-start(f32[2,2048]{1,0:T(2,128)S(1)} %add.95), channel_id=1, source_target_pairs={{0,1},{1,2},{2,3},{3,0},{4,5},{5,6},{6,7},{7,4},{8,9},{9,10},{10,1... | collective-permute-start | bytes 49160 | tf_op jit(solution)/shard_map/ppermute | solution.py:58
  53.9 5.5 %collective-permute-start.9 = (f32[2,2048]{1,0:T(2,128)S(1)}, f32[2,2048]{1,0:T(2,128)S(1)}, u32[]{:S(2)}, u32[]{:S(2)}) collective-permute-start(f32[2,2048]{1,0:T(2,128)S(1)} %add.95), channel_id=1, source_target_pairs={{0,2},{1,3},{2,0},{3,1},{4,6},{5,7},{6,4},{7,5},{8,10},{9,11},{10,... | collective-permute-start | bytes 49160 | tf_op jit(solution)/shard_map/ppermute | solution.py:58
  59.5 2.5 %copy-start.4 = (bf16[512,512]{1,0:T(8,128)(2,1)S(1)}, bf16[512,512]{1,0:T(8,128)(2,1)}, u32[]{:S(2)}) copy-start(bf16[512,512]{1,0:T(8,128)(2,1)} %get-tuple-element.22) | copy-start | bytes 1572868
  59.5 2.5 %copy-start.6 = (bf16[512,512]{1,0:T(8,128)(2,1)S(1)}, bf16[512,512]{1,0:T(8,128)(2,1)}, u32[]{:S(2)}) copy-start(bf16[512,512]{1,0:T(8,128)(2,1)} %get-tuple-element.23) | copy-start | bytes 1572868
  62.1 1.6 %copy-start.5 = (bf16[512,512]{1,0:T(8,128)(2,1)S(1)}, bf16[512,512]{1,0:T(8,128)(2,1)}, u32[]{:S(2)}) copy-start(bf16[512,512]{1,0:T(8,128)(2,1)} %get-tuple-element.25) | copy-start | bytes 1572868
